TPU v7x, 512 devices: a whole 4x8x8 slice. The times are simulated.
512 devices in a mesh: seq: 128 (over z_hi, x, y), dp: 4 (over z_lo, core).
Axes of the slice: x: 4, y: 8, z: 8 (z_hi: 4, z_lo: 2; z = z_hi * 2 + z_lo), core: 2. Of those that a mesh axis runs over, the one named last changes fastest.
Arguments:
- query_proj: bfloat16 [4, 16384, 2048], P('dp', 'seq'), may hold values from -48 to 48
- key_projection: bfloat16 [4, 16384, 1024], P('dp', 'seq'), may hold values from -48 to 48
- value_proj: bfloat16 [4, 16384, 1024], P('dp', 'seq'), may hold values from -6 to 6
- attn_grad: bfloat16 [4, 16384, 2048], P('dp', 'seq'), may hold values from -6 to 6
- doc_ids: int32 [4, 16384], P('dp', 'seq'), may hold values from 0 to 8, as said below
- query_gain: float32 [128], replicated, may hold values from 0.5 to 1.5
- key_norm_gain: float32 [128], replicated, may hold values from 0.5 to 1.5
Outputs:
- query_grad: bfloat16 [4, 16384, 2048], P('dp', 'seq')
- key_grad: bfloat16 [4, 16384, 1024], P('dp', 'seq')
- value_grad: bfloat16 [4, 16384, 1024], P('dp', 'seq')
- query_gain_grad: float32 [128], replicated
- key_gain_grad: float32 [128], replicated
Inputs may be any that keep to these rules, and one draw needn't show every extreme that they name: `doc_ids`: document numbers never fall along a sequence and each is used; each document holds 1 to 2175 tokens, and one holds exactly 2175.
All inputs are finite; a program needn't handle non-finite values.
Results may differ from a plain program's by a relative error of at most 0.008.
Values may be sent and summed in bfloat16 or wider, within the bound.
No kernel may reach another device: no remote copies, remote signals or barrier semaphores. Data moves between devices by JAX's collectives and lax.ppermute only.
A program may use at most 128 MiB of HBM per device.

v0:
```python
import jax
import jax.numpy as jnp
from jax import lax
from jax.sharding import PartitionSpec as P

HEAD_SIZE = 128
QUERY_HEADS = 16
KEY_VALUE_HEADS = 8
WINDOW_LENGTH = 1024


rope_base = 10000.0
score_scale = 168.0 ** (-0.5)
norm_eps = 1e-06


def entering(value, axis, combine, identity):
    length, position = (lax.axis_size(axis), lax.axis_index(axis))
    everything = jax.tree.map(lambda part: lax.all_gather(part, axis), value)
    start = jax.tree.map(
        lambda part, zero: jnp.broadcast_to(jnp.asarray(zero, part.dtype), part.shape),
        value,
        identity,
    )

    def turn(k, before):
        reached = k < position
        new = combine(before, jax.tree.map(lambda part: part[k], everything))
        return jax.tree.map(lambda a, b: jnp.where(reached, a, b), new, before)

    return lax.fori_loop(0, length, turn, start)


def from_behind(value, axis, steps):
    count = lax.axis_size(axis)
    first, last = (max(0, -steps), min(count, count - steps))
    return lax.ppermute(value, axis, [(source, source + steps) for source in range(first, last)])


def rotary(field, positions):
    half = field.shape[-1] // 2
    freqs = rope_base ** (-jnp.arange(half, dtype=field.dtype) * 2.0 / field.shape[-1])
    angles = positions.astype(field.dtype)[:, None] * freqs[None, :]
    cosine = jnp.cos(angles)[:, None, :]
    sine = jnp.sin(angles)[:, None, :]
    first = field[..., :half]
    second = field[..., half:]
    return jnp.concatenate(
        [first * cosine - second * sine, second * cosine + first * sine], axis=-1
    )


def prepare(raw, gain, positions):
    meansq = jnp.mean(raw * raw, axis=-1, keepdims=True)
    normed = raw * lax.rsqrt(meansq + norm_eps) * gain
    return rotary(normed, positions)


def combine_docs(earlier, later):
    vacant = later[0] < 0
    joined = later[0] == earlier[0]
    doc_number = jnp.where(vacant, earlier[0], later[0])
    first_place = jnp.where(vacant | joined, earlier[1], later[1])
    return (doc_number, first_place)


def attend(query_blk, key_blk, value_blk, gradient_block, allowed):
    scores = (
        jnp.einsum("tgrd,wgd->grtw", query_blk, key_blk, preferred_element_type=jnp.float32)
        * score_scale
    )
    expd = jnp.where(allowed, jnp.exp(scores), 0.0)
    weights = expd / jnp.sum(expd, axis=-1, keepdims=True)
    weights_b = weights.astype(jnp.bfloat16)
    attention_probs = jnp.einsum(
        "grtw,wgd->tgrd", weights_b, value_blk, preferred_element_type=jnp.float32
    )
    delta_rows = jnp.einsum("jwkp,jwkp->wkj", gradient_block.astype(jnp.float32), attention_probs)
    dweights = jnp.einsum(
        "tgrd,wgd->grtw", gradient_block, value_blk, preferred_element_type=jnp.float32
    )
    dscores = (weights * (dweights - delta_rows[..., None])).astype(jnp.bfloat16)
    dquery = score_scale * jnp.einsum(
        "grtw,wgd->tgrd", dscores, key_blk, preferred_element_type=jnp.float32
    )
    dkey = score_scale * jnp.einsum(
        "grtw,tgrd->wgd", dscores, query_blk, preferred_element_type=jnp.float32
    )
    dvalue = jnp.einsum(
        "grtw,tgrd->wgd", weights_b, gradient_block, preferred_element_type=jnp.float32
    )
    return (dquery, dkey, dvalue)


def shards(query_proj, key_projection, value_proj, attn_grad, doc_ids, query_gain, key_norm_gain):
    row_count = query_proj.shape[1]
    behind = WINDOW_LENGTH // row_count
    group_ratio = QUERY_HEADS // KEY_VALUE_HEADS
    group_count = KEY_VALUE_HEADS // 2
    key_span_width = KEY_VALUE_HEADS * HEAD_SIZE
    base = lax.axis_index("seq") * row_count
    local = jnp.arange(row_count, dtype=jnp.int32)
    positions = base + local
    doc_row = doc_ids[0]
    same_doc = doc_row[:, None] == doc_row[None, :]
    local_first = jnp.min(jnp.where(same_doc, local[None, :], row_count), axis=1) + base
    carry_doc, carry_start = entering(
        (doc_row[row_count - 1], local_first[row_count - 1]),
        "seq",
        combine_docs,
        (jnp.int32(-1), jnp.int32(0)),
    )
    starts = jnp.where(doc_row == carry_doc, carry_start, local_first)

    def prepare_function(raw, gain):
        return prepare(raw, gain, positions)

    query_normalized, query_back = jax.vjp(
        prepare_function,
        query_proj[0].astype(jnp.float32).reshape(row_count, QUERY_HEADS, HEAD_SIZE),
        query_gain,
    )
    key_normalized, key_backward = jax.vjp(
        prepare_function,
        key_projection[0].astype(jnp.float32).reshape(row_count, KEY_VALUE_HEADS, HEAD_SIZE),
        key_norm_gain,
    )
    query_rot = query_normalized.astype(jnp.bfloat16)
    key_flat = key_normalized.astype(jnp.bfloat16).reshape(row_count, key_span_width)
    value_flat = value_proj[0]
    key_parts = []
    value_parts = []
    for offset in range(behind, 0, -1):
        moved = from_behind((key_flat, value_flat), "seq", offset)
        key_parts.append(moved[0])
        value_parts.append(moved[1])
    key_win = jnp.concatenate(key_parts + [key_flat], axis=0)
    value_win = jnp.concatenate(value_parts + [value_flat], axis=0)
    width = (behind + 1) * row_count
    key_pos = base - behind * row_count + jnp.arange(width, dtype=jnp.int32)
    allowed = (
        (key_pos[None, :] <= positions[:, None])
        & (positions[:, None] - key_pos[None, :] < WINDOW_LENGTH)
        & (key_pos[None, :] >= starts[:, None])
    )
    query_groups = query_rot.reshape(row_count, group_count, 2, group_ratio, HEAD_SIZE).transpose(
        1, 0, 2, 3, 4
    )
    grad_groups = (
        attn_grad[0]
        .reshape(row_count, group_count, 2, group_ratio, HEAD_SIZE)
        .transpose(1, 0, 2, 3, 4)
    )
    key_groups = key_win.reshape(width, group_count, 2, HEAD_SIZE).transpose(1, 0, 2, 3)
    value_groups = value_win.reshape(width, group_count, 2, HEAD_SIZE).transpose(1, 0, 2, 3)

    def group_work(items):
        return attend(items[0], items[1], items[2], items[3], allowed)

    dquery_g, dkey_g, dvalue_g = lax.map(
        group_work, (query_groups, key_groups, value_groups, grad_groups)
    )
    dquery_rot = dquery_g.transpose(1, 0, 2, 3, 4).reshape(row_count, QUERY_HEADS, HEAD_SIZE)
    dkey_win = dkey_g.transpose(1, 0, 2, 3).reshape(behind + 1, row_count, key_span_width)
    dvalue_win = dvalue_g.transpose(1, 0, 2, 3).reshape(behind + 1, row_count, key_span_width)
    key_remote = dkey_win[:behind].astype(jnp.bfloat16)
    value_remote = dvalue_win[:behind].astype(jnp.bfloat16)
    key_full_length = dkey_win[behind]
    value_total = dvalue_win[behind]
    for offset in range(1, behind + 1):
        moved = from_behind(
            (key_remote[behind - offset], value_remote[behind - offset]), "seq", -offset
        )
        key_full_length = key_full_length + moved[0].astype(jnp.float32)
        value_total = value_total + moved[1].astype(jnp.float32)
    query_raw_gradient, query_gain_gradient = query_back(dquery_rot)
    key_raw_gradient, key_gain_gradient = key_backward(
        key_full_length.reshape(row_count, KEY_VALUE_HEADS, HEAD_SIZE)
    )
    gain_query, gain_key = lax.psum((query_gain_gradient, key_gain_gradient), ("seq", "dp"))
    return (
        query_raw_gradient.astype(jnp.bfloat16).reshape(1, row_count, QUERY_HEADS * HEAD_SIZE),
        key_raw_gradient.astype(jnp.bfloat16).reshape(1, row_count, key_span_width),
        value_total.astype(jnp.bfloat16)[None],
        gain_query,
        gain_key,
    )


def solution(mesh):
    in_specs = (
        P("dp", "seq", None),
        P("dp", "seq", None),
        P("dp", "seq", None),
        P("dp", "seq", None),
        P("dp", "seq"),
        P(),
        P(),
    )
    out_specs = (P("dp", "seq", None), P("dp", "seq", None), P("dp", "seq", None), P(), P())
    return jax.shard_map(shards, mesh=mesh, in_specs=in_specs, out_specs=out_specs, check_vma=False)
```

profile of v0, /device:TPU:1, one launch (start us, length us, event | category | flops | bytes accessed | tf_op | source)
XLA Modules:
  0.0 1063.3 jit_solution(8678204765822)
XLA Ops:
  1.8 4.0 collective-permute-start.15
  5.8 4.2 collective-permute-start.14
  10.1 3.1 collective-permute-start.8
  16.6 4.9 collective-permute-start.1
  21.5 2.9 collective-permute-start
  28.5 28.4 %all-reduce.6 = (s32[128]{0:T(128)S(1)}, s32[128]{0:T(128)S(1)}) all-reduce(s32[128]{0:T(128)S(1)} %bitcast_dynamic-update-slice_fusion, s32[128]{0:T(128)S(1)} %slice_dynamic-update-slice_fusion), channel_id=2, replica_groups=mesh['seq'=128,'dp'=4] {'seq'}, use_global_device_ids=true, to_apply=%add.4 | all-reduce | flops 256 | bytes 2048 | tf_op jit(solution)/shard_map/all_gather | solution.py:19
  57.0 487.3 %while.30 = (s32[]{:T(128)}, s32[]{:T(128)}, s32[]{:T(128)}, s32[]{:T(128)}, s32[128]{0:T(128)S(1)}, /*index=5*/s32[128]{0:T(128)S(1)}, s32[]{:T(128)}, s32[]{:T(128)}) while((s32[]{:T(128)}, s32[]{:T(128)}, s32[]{:T(128)}, s32[]{:T(128)}, s32[128]{0:T(128)S(1)}, /*index=5*/s32[128]{0:T(128)S(1)}, s32[]{:T(128)}, s32[]{:T(128)}) %tuple.77), condition=%wide.region_4.5_spmd, body=%wide.region_3.4_spmd.sunk | while | flops 10 | bytes 199 | solution.py:31
  548.3 9.9 collective-permute-start.2
  562.9 7.1 collective-permute-done.2
  571.3 20.7 %collective-permute-done.3 = bf16[128,1024]{0,1:T(8,128)(2,1)S(1)} collective-permute-done((bf16[128,1024]{0,1:T(8,128)(2,1)S(1)}, bf16[128,1024]{0,1:T(8,128)(2,1)S(1)}, u32[]{:S(2)}, u32[]{:S(2)}) %collective-permute-start.3) | collective-permute-done | bytes 262176 | tf_op jit(solution)/shard_map/ppermute | solution.py:37
  594.8 8.5 collective-permute-start.11
  603.4 10.8 %collective-permute-start.9 = (bf16[128,1024]{0,1:T(8,128)(2,1)S(1)}, bf16[128,1024]{0,1:T(8,128)(2,1)S(1)}, u32[]{:S(2)}, u32[]{:S(2)}) collective-permute-start(bf16[128,1024]{0,1:T(8,128)(2,1)S(1)} %bitcast.260), channel_id=1, source_target_pairs={{0,28},{4,32},{8,36},{12,40},{16,44},{20,48},{24,52},{28,56},{32,6... | collective-permute-start | bytes 786440 | tf_op jit(solution)/shard_map/ppermute | solution.py:37
  615.2 9.4 collective-permute-start.10
  624.7 12.8 %collective-permute-start.12 = (bf16[128,1024]{0,1:T(8,128)(2,1)S(1)}, bf16[128,1024]{0,1:T(8,128)(2,1)S(1)}, u32[]{:S(2)}, u32[]{:S(2)}) collective-permute-start(bf16[128,1024]{0,1:T(8,128)(2,1)S(1)} %bitcast.262), channel_id=1, source_target_pairs={{0,16},{4,20},{8,24},{12,28},{16,32},{20,36},{24,40},{28,44},{32,4... | collective-permute-start | bytes 786440 | tf_op jit(solution)/shard_map/ppermute | solution.py:37
  639.3 2.7 collective-permute-done.12
  642.1 4.4 collective-permute-done.13
  648.2 57.1 %while.31 = (s32[]{:T(128)}, f32[4,128,2,2,128]{1,4,3,2,0:T(8,128)}, f32[4,1152,2,128]{1,3,2,0:T(8,128)}, f32[4,1152,2,128]{1,3,2,0:T(8,128)}, bf16[4,1152,2,128...) while((s32[]{:T(128)}, ...), condition=%wide.region_7.8_spmd.clone, body=%wide.region_5.7_spmd.clone.sunk | while | flops 912131200 | bytes 24730428 | solution.py:160
  650.2 1.9 fusion.96
  653.7 1.6 fusion.98
  655.3 2.1 fusion.99
  657.5 2.4 fusion.101
  659.9 2.5 fusion.100
  664.6 1.9 fusion.96
  669.6 2.1 fusion.99
  671.8 2.4 fusion.101
  674.2 2.5 fusion.100
  678.8 1.9 fusion.96
  683.9 2.1 fusion.99
  686.0 2.5 fusion.101
  688.5 2.5 fusion.100
  693.1 1.9 fusion.96
  698.2 2.1 fusion.99
  700.3 2.4 fusion.101
  702.8 2.5 fusion.100
  708.0 4.1 bitcast_convert_fusion.2
  712.1 1.9 slice.144
  713.9 4.1 bitcast_convert_fusion.1
  721.5 1.8 multiply_add_fusion.1
  724.5 2.9 fusion.55
  731.2 1.8 fusion.41
  733.0 2.1 reshape.221
  737.7 20.8 %collective-permute-done.23 = bf16[128,1024]{0,1:T(8,128)(2,1)} collective-permute-done((bf16[128,1024]{0,1:T(8,128)(2,1)}, bf16[128,1024]{0,1:T(8,128)(2,1)}, u32[]{:S(2)}, u32[]{:S(2)}) %collective-permute-start.23) | collective-permute-done | bytes 262176 | tf_op jit(solution)/shard_map/ppermute | solution.py:37
  761.1 38.7 %collective-permute-done.22 = bf16[128,1024]{0,1:T(8,128)(2,1)} collective-permute-done((bf16[128,1024]{0,1:T(8,128)(2,1)}, bf16[128,1024]{0,1:T(8,128)(2,1)}, u32[]{:S(2)}, u32[]{:S(2)}) %collective-permute-start.22) | collective-permute-done | bytes 262176 | tf_op jit(solution)/shard_map/ppermute | solution.py:37
  801.1 1.7 fusion.54
  819.3 6.8 collective-permute-done.25
  827.5 4.6 collective-permute-done.26
  836.1 224.7 %all-reduce.7 = (f32[128]{0:T(128)}, f32[128]{0:T(128)}) all-reduce(f32[128]{0:T(128)S(1)} %get-tuple-element.251, f32[128]{0:T(128)S(1)} %get-tuple-element.253), channel_id=1, replica_groups=mesh['seq'=128,'dp'=4] {'seq','dp'}, use_global_device_ids=true, to_apply=%region_11.12 | all-reduce | flops 256 | bytes 2048 | tf_op jit(solution)/shard_map/psum | solution.py:180
  1060.8 2.5 fusion.50
  (520 shorter events, 234.4 us)
Async XLA Ops:
  0.6 15.0 %copy-start.32 = (f32[128]{0:T(128)S(1)}, f32[128]{0:T(128)}, u32[]{:S(2)}) copy-start(f32[128]{0:T(128)} %param.17) | copy-start | bytes 1540
  1.8 644.8 %collective-permute-start.15 = (bf16[128,1024]{0,1:T(8,128)(2,1)S(1)}, bf16[128,1024]{0,1:T(8,128)(2,1)S(1)}, u32[]{:S(2)}, u32[]{:S(2)}) collective-permute-start(bf16[128,1024]{0,1:T(8,128)(2,1)S(1)} %bitcast.256), channel_id=1, source_target_pairs={{0,4},{4,8},{8,12},{12,16},{16,20},{20,24},{24,28},{28,32},{32,36}... | collective-permute-start | bytes 786440 | tf_op jit(solution)/shard_map/ppermute | solution.py:37
  5.8 640.7 %collective-permute-start.14 = (bf16[128,1024]{0,1:T(8,128)(2,1)S(1)}, bf16[128,1024]{0,1:T(8,128)(2,1)S(1)}, u32[]{:S(2)}, u32[]{:S(2)}) collective-permute-start(bf16[128,1024]{0,1:T(8,128)(2,1)S(1)} %bitcast.257), channel_id=1, source_target_pairs={{0,8},{4,12},{8,16},{12,20},{16,24},{20,28},{24,32},{28,36},{32,40... | collective-permute-start | bytes 786440 | tf_op jit(solution)/shard_map/ppermute | solution.py:37
  10.1 549.1 %collective-permute-start.8 = (bf16[128,1024]{0,1:T(8,128)(2,1)S(1)}, bf16[128,1024]{0,1:T(8,128)(2,1)S(1)}, u32[]{:S(2)}, u32[]{:S(2)}) collective-permute-start(bf16[128,1024]{0,1:T(8,128)(2,1)S(1)} %bitcast.258), channel_id=1, source_target_pairs={{0,32},{4,36},{8,40},{12,44},{16,48},{20,52},{24,56},{28,60},{32,6... | collective-permute-start | bytes 786440 | tf_op jit(solution)/shard_map/ppermute | solution.py:37
  15.1 9.2 copy-start.34
  15.1 529.1 %copy-start.16 = (bf16[1,128,2048]{2,1,0:T(8,128)(2,1)S(1)}, bf16[1,128,2048]{2,1,0:T(8,128)(2,1)}, u32[]{:S(2)}) copy-start(bf16[1,128,2048]{2,1,0:T(8,128)(2,1)} %param.11) | copy-start | bytes 1572868
  15.2 529.2 %copy-start.24 = (f32[128,8]{0,1:T(8,128)}, f32[128,8]{0,1:T(8,128)S(1)}, u32[]{:S(2)}) copy-start(f32[128,8]{0,1:T(8,128)S(1)} %copy.167) | copy-start | bytes 12292
  15.3 528.9 %copy-start.14 = (f32[128,8]{1,0:T(8,128)}, f32[128,8]{1,0:T(8,128)S(1)}, u32[]{:S(2)}) copy-start(f32[128,8]{1,0:T(8,128)S(1)} %copy.168) | copy-start | bytes 12292
  15.7 529.8 %copy-start.8 = (f32[128,64]{1,0:T(8,128)}, f32[128,64]{1,0:T(8,128)S(1)}, u32[]{:S(2)}) copy-start(f32[128,64]{1,0:T(8,128)S(1)} %get-tuple-element.321) | copy-start | bytes 98308
  15.7 529.8 %copy-start.10 = (f32[128,64]{1,0:T(8,128)}, f32[128,64]{1,0:T(8,128)S(1)}, u32[]{:S(2)}) copy-start(f32[128,64]{1,0:T(8,128)S(1)} %get-tuple-element.322) | copy-start | bytes 98308
  16.6 544.0 %collective-permute-start.1 = (bf16[128,1024]{0,1:T(8,128)(2,1)S(1)}, bf16[128,1024]{0,1:T(8,128)(2,1)}, u32[]{:S(2)}, u32[]{:S(2)}) collective-permute-start(bf16[128,1024]{0,1:T(8,128)(2,1)S(1)} %bitcast.265), channel_id=1, source_target_pairs={{0,28},{4,32},{8,36},{12,40},{16,44},{20,48},{24,52},{28,56},{32,6... | collective-permute-start | bytes 786440 | tf_op jit(solution)/shard_map/ppermute | solution.py:37
  21.5 526.8 %collective-permute-start = (bf16[128,1024]{0,1:T(8,128)(2,1)S(1)}, bf16[128,1024]{0,1:T(8,128)(2,1)}, u32[]{:S(2)}, u32[]{:S(2)}) collective-permute-start(bf16[128,1024]{0,1:T(8,128)(2,1)S(1)} %bitcast.266), channel_id=1, source_target_pairs={{0,32},{4,36},{8,40},{12,44},{16,48},{20,52},{24,56},{28,60},{32,6... | collective-permute-start | bytes 786440 | tf_op jit(solution)/shard_map/ppermute | solution.py:37
  548.3 21.7 %collective-permute-start.2 = (bf16[128,1024]{0,1:T(8,128)(2,1)S(1)}, bf16[128,1024]{0,1:T(8,128)(2,1)S(1)}, u32[]{:S(2)}, u32[]{:S(2)}) collective-permute-start(bf16[128,1024]{0,1:T(8,128)(2,1)S(1)} %bitcast.267), channel_id=1, source_target_pairs={{0,24},{4,28},{8,32},{12,36},{16,40},{20,44},{24,48},{28,52},{32,5... | collective-permute-start | bytes 786440 | tf_op jit(solution)/shard_map/ppermute | solution.py:37
  559.2 32.9 %collective-permute-start.3 = (bf16[128,1024]{0,1:T(8,128)(2,1)S(1)}, bf16[128,1024]{0,1:T(8,128)(2,1)S(1)}, u32[]{:S(2)}, u32[]{:S(2)}) collective-permute-start(bf16[128,1024]{0,1:T(8,128)(2,1)S(1)} %bitcast.268), channel_id=1, source_target_pairs={{0,20},{4,24},{8,28},{12,32},{16,36},{20,40},{24,44},{28,48},{32,5... | collective-permute-start | bytes 786440 | tf_op jit(solution)/shard_map/ppermute | solution.py:37
  560.5 32.9 %collective-permute-start.4 = (bf16[128,1024]{0,1:T(8,128)(2,1)S(1)}, bf16[128,1024]{0,1:T(8,128)(2,1)S(1)}, u32[]{:S(2)}, u32[]{:S(2)}) collective-permute-start(bf16[128,1024]{0,1:T(8,128)(2,1)S(1)} %bitcast.269), channel_id=1, source_target_pairs={{0,16},{4,20},{8,24},{12,28},{16,32},{20,36},{24,40},{28,44},{32,4... | collective-permute-start | bytes 786440 | tf_op jit(solution)/shard_map/ppermute | solution.py:37
  570.0 24.9 %collective-permute-start.5 = (bf16[128,1024]{0,1:T(8,128)(2,1)S(1)}, bf16[128,1024]{0,1:T(8,128)(2,1)S(1)}, u32[]{:S(2)}, u32[]{:S(2)}) collective-permute-start(bf16[128,1024]{0,1:T(8,128)(2,1)S(1)} %bitcast.270), channel_id=1, source_target_pairs={{0,12},{4,16},{8,20},{12,24},{16,28},{20,32},{24,36},{28,40},{32,4... | collective-permute-start | bytes 786440 | tf_op jit(solution)/shard_map/ppermute | solution.py:37
  592.0 11.4 %collective-permute-start.6 = (bf16[128,1024]{0,1:T(8,128)(2,1)S(1)}, bf16[128,1024]{0,1:T(8,128)(2,1)S(1)}, u32[]{:S(2)}, u32[]{:S(2)}) collective-permute-start(bf16[128,1024]{0,1:T(8,128)(2,1)S(1)} %bitcast.271), channel_id=1, source_target_pairs={{0,8},{4,12},{8,16},{12,20},{16,24},{20,28},{24,32},{28,36},{32,40... | collective-permute-start | bytes 786440 | tf_op jit(solution)/shard_map/ppermute | solution.py:37
  593.4 21.8 %collective-permute-start.7 = (bf16[128,1024]{0,1:T(8,128)(2,1)S(1)}, bf16[128,1024]{0,1:T(8,128)(2,1)S(1)}, u32[]{:S(2)}, u32[]{:S(2)}) collective-permute-start(bf16[128,1024]{0,1:T(8,128)(2,1)S(1)} %bitcast.272), channel_id=1, source_target_pairs={{0,4},{4,8},{8,12},{12,16},{16,20},{20,24},{24,28},{28,32},{32,36}... | collective-permute-start | bytes 786440 | tf_op jit(solution)/shard_map/ppermute | solution.py:37
  594.8 44.4 %collective-permute-start.11 = (bf16[128,1024]{0,1:T(8,128)(2,1)S(1)}, bf16[128,1024]{0,1:T(8,128)(2,1)S(1)}, u32[]{:S(2)}, u32[]{:S(2)}) collective-permute-start(bf16[128,1024]{0,1:T(8,128)(2,1)S(1)} %bitcast.259), channel_id=1, source_target_pairs={{0,20},{4,24},{8,28},{12,32},{16,36},{20,40},{24,44},{28,48},{32,5... | collective-permute-start | bytes 786440 | tf_op jit(solution)/shard_map/ppermute | solution.py:37
  603.4 21.3 %collective-permute-start.9 = (bf16[128,1024]{0,1:T(8,128)(2,1)S(1)}, bf16[128,1024]{0,1:T(8,128)(2,1)S(1)}, u32[]{:S(2)}, u32[]{:S(2)}) collective-permute-start(bf16[128,1024]{0,1:T(8,128)(2,1)S(1)} %bitcast.260), channel_id=1, source_target_pairs={{0,28},{4,32},{8,36},{12,40},{16,44},{20,48},{24,52},{28,56},{32,6... | collective-permute-start | bytes 786440 | tf_op jit(solution)/shard_map/ppermute | solution.py:37
  615.2 22.4 %collective-permute-start.10 = (bf16[128,1024]{0,1:T(8,128)(2,1)S(1)}, bf16[128,1024]{0,1:T(8,128)(2,1)S(1)}, u32[]{:S(2)}, u32[]{:S(2)}) collective-permute-start(bf16[128,1024]{0,1:T(8,128)(2,1)S(1)} %bitcast.261), channel_id=1, source_target_pairs={{0,24},{4,28},{8,32},{12,36},{16,40},{20,44},{24,48},{28,52},{32,5... | collective-permute-start | bytes 786440 | tf_op jit(solution)/shard_map/ppermute | solution.py:37
  624.6 23.5 %copy-start.26 = (s32[128]{0:T(128)S(1)}, s32[128]{0:T(128)}, u32[]{:S(2)}) copy-start(s32[128]{0:T(128)} %compare_select_fusion) | copy-start | bytes 1540
  624.6 23.5 %copy-start.28 = (s32[128]{0:T(128)S(1)}, s32[128]{0:T(128)}, u32[]{:S(2)}) copy-start(s32[128]{0:T(128)} %get-tuple-element.461) | copy-start | bytes 1540
  624.7 22.0 %copy-start.5 = (bf16[1152,4,2,128]{0,3,2,1:T(8,128)(2,1)}, bf16[1152,4,2,128]{0,3,2,1:T(8,128)(2,1)S(1)}, u32[]{:S(2)}) copy-start(bf16[1152,4,2,128]{0,3,2,1:T(8,128)(2,1)S(1)} %constant_dynamic-update-slice_fusion) | copy-start | bytes 7077892
  624.7 17.3 %collective-permute-start.12 = (bf16[128,1024]{0,1:T(8,128)(2,1)S(1)}, bf16[128,1024]{0,1:T(8,128)(2,1)S(1)}, u32[]{:S(2)}, u32[]{:S(2)}) collective-permute-start(bf16[128,1024]{0,1:T(8,128)(2,1)S(1)} %bitcast.262), channel_id=1, source_target_pairs={{0,16},{4,20},{8,24},{12,28},{16,32},{20,36},{24,40},{28,44},{32,4... | collective-permute-start | bytes 786440 | tf_op jit(solution)/shard_map/ppermute | solution.py:37
  637.6 8.8 collective-permute-start.13
  718.0 3.5 copy-start.11
  727.4 31.2 %collective-permute-start.23 = (bf16[128,1024]{0,1:T(8,128)(2,1)}, bf16[128,1024]{0,1:T(8,128)(2,1)}, u32[]{:S(2)}, u32[]{:S(2)}) collective-permute-start(bf16[128,1024]{0,1:T(8,128)(2,1)} %bitcast.46), channel_id=1, source_target_pairs={{32,0},{36,4},{40,8},{44,12},{48,16},{52,20},{56,24},{60,28},{64,3... | collective-permute-start | bytes 786440 | tf_op jit(solution)/shard_map/ppermute | solution.py:37
  728.6 31.2 %collective-permute-start.16 = (bf16[128,1024]{0,1:T(8,128)(2,1)}, bf16[128,1024]{0,1:T(8,128)(2,1)}, u32[]{:S(2)}, u32[]{:S(2)}) collective-permute-start(bf16[128,1024]{0,1:T(8,128)(2,1)} %bitcast.39), channel_id=1, source_target_pairs={{4,0},{8,4},{12,8},{16,12},{20,16},{24,20},{28,24},{32,28},{36,32}... | collective-permute-start | bytes 786440 | tf_op jit(solution)/shard_map/ppermute | solution.py:37
  729.9 69.9 %collective-permute-start.22 = (bf16[128,1024]{0,1:T(8,128)(2,1)}, bf16[128,1024]{0,1:T(8,128)(2,1)}, u32[]{:S(2)}, u32[]{:S(2)}) collective-permute-start(bf16[128,1024]{0,1:T(8,128)(2,1)} %bitcast.45), channel_id=1, source_target_pairs={{28,0},{32,4},{36,8},{40,12},{44,16},{48,20},{52,24},{56,28},{60,3... | collective-permute-start | bytes 786440 | tf_op jit(solution)/shard_map/ppermute | solution.py:37
  735.1 74.6 %collective-permute-start.21 = (bf16[128,1024]{0,1:T(8,128)(2,1)}, bf16[128,1024]{0,1:T(8,128)(2,1)S(1)}, u32[]{:S(2)}, u32[]{:S(2)}) collective-permute-start(bf16[128,1024]{0,1:T(8,128)(2,1)} %bitcast.278), channel_id=1, source_target_pairs={{24,0},{28,4},{32,8},{36,12},{40,16},{44,20},{48,24},{52,28},{56,3... | collective-permute-start | bytes 786440 | tf_op jit(solution)/shard_map/ppermute | solution.py:37
  736.4 74.6 %collective-permute-start.20 = (bf16[128,1024]{0,1:T(8,128)(2,1)}, bf16[128,1024]{0,1:T(8,128)(2,1)S(1)}, u32[]{:S(2)}, u32[]{:S(2)}) collective-permute-start(bf16[128,1024]{0,1:T(8,128)(2,1)} %bitcast.277), channel_id=1, source_target_pairs={{20,0},{24,4},{28,8},{32,12},{36,16},{40,20},{44,24},{48,28},{52,3... | collective-permute-start | bytes 786440 | tf_op jit(solution)/shard_map/ppermute | solution.py:37
  758.5 53.7 %collective-permute-start.19 = (bf16[128,1024]{0,1:T(8,128)(2,1)}, bf16[128,1024]{0,1:T(8,128)(2,1)S(1)}, u32[]{:S(2)}, u32[]{:S(2)}) collective-permute-start(bf16[128,1024]{0,1:T(8,128)(2,1)} %bitcast.276), channel_id=1, source_target_pairs={{16,0},{20,4},{24,8},{28,12},{32,16},{36,20},{40,24},{44,28},{48,3... | collective-permute-start | bytes 786440 | tf_op jit(solution)/shard_map/ppermute | solution.py:37
  759.8 53.7 %collective-permute-start.18 = (bf16[128,1024]{0,1:T(8,128)(2,1)}, bf16[128,1024]{0,1:T(8,128)(2,1)}, u32[]{:S(2)}, u32[]{:S(2)}) collective-permute-start(bf16[128,1024]{0,1:T(8,128)(2,1)} %bitcast.275), channel_id=1, source_target_pairs={{12,0},{16,4},{20,8},{24,12},{28,16},{32,20},{36,24},{40,28},{44,3... | collective-permute-start | bytes 786440 | tf_op jit(solution)/shard_map/ppermute | solution.py:37
  799.8 15.1 %collective-permute-start.17 = (bf16[128,1024]{0,1:T(8,128)(2,1)}, bf16[128,1024]{0,1:T(8,128)(2,1)}, u32[]{:S(2)}, u32[]{:S(2)}) collective-permute-start(bf16[128,1024]{0,1:T(8,128)(2,1)} %bitcast.274), channel_id=1, source_target_pairs={{8,0},{12,4},{16,8},{20,12},{24,16},{28,20},{32,24},{36,28},{40,32... | collective-permute-start | bytes 786440 | tf_op jit(solution)/shard_map/ppermute | solution.py:37
  802.8 13.4 %copy-start.7 = (f32[128,4,2,128]{0,3,2,1:T(8,128)S(1)}, f32[128,4,2,128]{0,3,2,1:T(8,128)}, u32[]{:S(2)}) copy-start(f32[128,4,2,128]{0,3,2,1:T(8,128)} %slice.144) | copy-start | bytes 1572868
  809.6 16.5 %collective-permute-start.25 = (bf16[128,1024]{1,0:T(8,128)(2,1)}, bf16[128,1024]{1,0:T(8,128)(2,1)}, u32[]{:S(2)}, u32[]{:S(2)}) collective-permute-start(bf16[128,1024]{1,0:T(8,128)(2,1)} %copy.218), channel_id=1, source_target_pairs={{8,0},{12,4},{16,8},{20,12},{24,16},{28,20},{32,24},{36,28},{40,32... | collective-permute-start | bytes 786440 | tf_op jit(solution)/shard_map/ppermute | solution.py:37
  810.9 21.1 %collective-permute-start.26 = (bf16[128,1024]{1,0:T(8,128)(2,1)}, bf16[128,1024]{1,0:T(8,128)(2,1)}, u32[]{:S(2)}, u32[]{:S(2)}) collective-permute-start(bf16[128,1024]{1,0:T(8,128)(2,1)} %copy.219), channel_id=1, source_target_pairs={{12,0},{16,4},{20,8},{24,12},{28,16},{32,20},{36,24},{40,28},{44,3... | collective-permute-start | bytes 786440 | tf_op jit(solution)/shard_map/ppermute | solution.py:37
  812.2 21.1 %collective-permute-start.27 = (bf16[128,1024]{1,0:T(8,128)(2,1)}, bf16[128,1024]{1,0:T(8,128)(2,1)}, u32[]{:S(2)}, u32[]{:S(2)}) collective-permute-start(bf16[128,1024]{1,0:T(8,128)(2,1)} %copy.220), channel_id=1, source_target_pairs={{16,0},{20,4},{24,8},{28,12},{32,16},{36,20},{40,24},{44,28},{48,3... | collective-permute-start | bytes 786440 | tf_op jit(solution)/shard_map/ppermute | solution.py:37
  813.6 247.2 %collective-permute-start.28 = (bf16[128,1024]{1,0:T(8,128)(2,1)}, bf16[128,1024]{1,0:T(8,128)(2,1)}, u32[]{:S(2)}, u32[]{:S(2)}) collective-permute-start(bf16[128,1024]{1,0:T(8,128)(2,1)} %copy.221), channel_id=1, source_target_pairs={{20,0},{24,4},{28,8},{32,12},{36,16},{40,20},{44,24},{48,28},{52,3... | collective-permute-start | bytes 786440 | tf_op jit(solution)/shard_map/ppermute | solution.py:37
  814.9 245.9 %collective-permute-start.29 = (bf16[128,1024]{1,0:T(8,128)(2,1)}, bf16[128,1024]{1,0:T(8,128)(2,1)}, u32[]{:S(2)}, u32[]{:S(2)}) collective-permute-start(bf16[128,1024]{1,0:T(8,128)(2,1)} %copy.222), channel_id=1, source_target_pairs={{24,0},{28,4},{32,8},{36,12},{40,16},{44,20},{48,24},{52,28},{56,3... | collective-permute-start | bytes 786440 | tf_op jit(solution)/shard_map/ppermute | solution.py:37
  818.3 13.7 %copy-start.21 = (bf16[128,1024]{1,0:T(8,128)(2,1)S(1)}, bf16[128,1024]{1,0:T(8,128)(2,1)}, u32[]{:S(2)}) copy-start(bf16[128,1024]{1,0:T(8,128)(2,1)} %copy.224) | copy-start | bytes 786436
  818.3 15.0 %copy-start.20 = (bf16[128,1024]{1,0:T(8,128)(2,1)S(1)}, bf16[128,1024]{1,0:T(8,128)(2,1)}, u32[]{:S(2)}) copy-start(bf16[128,1024]{1,0:T(8,128)(2,1)} %copy.217) | copy-start | bytes 786436
  818.3 16.3 %copy-start.25 = (f32[128,8]{0,1:T(8,128)S(1)}, f32[128,8]{0,1:T(8,128)}, u32[]{:S(2)}) copy-start(f32[128,8]{0,1:T(8,128)} %copy-done.24) | copy-start | bytes 12292
  818.8 242.0 %copy-start.6 = (f32[128,1024]{1,0:T(8,128)S(1)}, f32[128,1024]{1,0:T(8,128)}, u32[]{:S(2)}) copy-start(f32[128,1024]{1,0:T(8,128)} %copy.216) | copy-start | bytes 1572868
  826.2 234.6 %collective-permute-start.30 = (bf16[128,1024]{1,0:T(8,128)(2,1)}, bf16[128,1024]{1,0:T(8,128)(2,1)S(1)}, u32[]{:S(2)}, u32[]{:S(2)}) collective-permute-start(bf16[128,1024]{1,0:T(8,128)(2,1)} %copy.223), channel_id=1, source_target_pairs={{28,0},{32,4},{36,8},{40,12},{44,16},{48,20},{52,24},{56,28},{60,3... | collective-permute-start | bytes 786440 | tf_op jit(solution)/shard_map/ppermute | solution.py:37
  832.0 228.8 %collective-permute-start.31 = (bf16[128,1024]{1,0:T(8,128)(2,1)S(1)}, bf16[128,1024]{1,0:T(8,128)(2,1)}, u32[]{:S(2)}, u32[]{:S(2)}) collective-permute-start(bf16[128,1024]{1,0:T(8,128)(2,1)S(1)} %copy-done.21), channel_id=1, source_target_pairs={{32,0},{36,4},{40,8},{44,12},{48,16},{52,20},{56,24},{60,28},{64,3... | collective-permute-start | bytes 786440 | tf_op jit(solution)/shard_map/ppermute | solution.py:37
  833.3 227.5 %collective-permute-start.24 = (bf16[128,1024]{1,0:T(8,128)(2,1)S(1)}, bf16[128,1024]{1,0:T(8,128)(2,1)}, u32[]{:S(2)}, u32[]{:S(2)}) collective-permute-start(bf16[128,1024]{1,0:T(8,128)(2,1)S(1)} %copy-done.20), channel_id=1, source_target_pairs={{4,0},{8,4},{12,8},{16,12},{20,16},{24,20},{28,24},{32,28},{36,32}... | collective-permute-start | bytes 786440 | tf_op jit(solution)/shard_map/ppermute | solution.py:37
  (37 other events, 69.9 us)
where the time goes:
time: 1080 us; the launch traced here: 1060 us
  loops' own time  337 us (31%)
  blocking collectives  253 us (23%)
  local copies, waits for them, and re-layouts  192 us (18%)
  waiting for transfers between devices  107 us (10%)
  starting transfers between devices  99.1 us (9%)
  matrix products  48.5 us (4%)
  other arithmetic  24.7 us (2%)
    another operation x1, loops' own time, entering(): return lax.fori_loop(0, length, turn, start)  337 us
    psum x1, blocking collectives, shards(): lax.psum((query_gain_gradient, key_gain_gradient), ('seq', 'dp'))  225 us
    dynamic_slice x256, local copies, waits for them, and re-layouts, turn(): new = combine(before, jax.tree.map(lambda part: part[k], everything))  150 us
    ppermute x32, waiting for transfers between devices, from_behind(): lax.ppermute(value, axis, [(source, source + steps) for source in range(f...  107 us
    ppermute x32, starting transfers between devices, from_behind(): lax.ppermute(value, axis, [(source, source + steps) for source in range(f...  99.1 us
    all_gather x1, blocking collectives, entering(): everything = jax.tree.map(lambda part: lax.all_gather(part, axis), value)  28.4 us
  transfers between devices with their start and end apart: 32, of which 9 were waited for; matrix products, arithmetic and copies ran while one was open for 17% of the time, Pallas kernels for 0%

commit v1 on v0

--- a/solution.py
+++ b/solution.py
@@ -12,23 +12,6 @@
 rope_base = 10000.0
 score_scale = 168.0 ** (-0.5)
 norm_eps = 1e-06
-
-
-def entering(value, axis, combine, identity):
-    length, position = (lax.axis_size(axis), lax.axis_index(axis))
-    everything = jax.tree.map(lambda part: lax.all_gather(part, axis), value)
-    start = jax.tree.map(
-        lambda part, zero: jnp.broadcast_to(jnp.asarray(zero, part.dtype), part.shape),
-        value,
-        identity,
-    )
-
-    def turn(k, before):
-        reached = k < position
-        new = combine(before, jax.tree.map(lambda part: part[k], everything))
-        return jax.tree.map(lambda a, b: jnp.where(reached, a, b), new, before)
-
-    return lax.fori_loop(0, length, turn, start)
 
 
 def from_behind(value, axis, steps):
@@ -54,14 +37,6 @@
     meansq = jnp.mean(raw * raw, axis=-1, keepdims=True)
     normed = raw * lax.rsqrt(meansq + norm_eps) * gain
     return rotary(normed, positions)
-
-
-def combine_docs(earlier, later):
-    vacant = later[0] < 0
-    joined = later[0] == earlier[0]
-    doc_number = jnp.where(vacant, earlier[0], later[0])
-    first_place = jnp.where(vacant | joined, earlier[1], later[1])
-    return (doc_number, first_place)
 
 
 def attend(query_blk, key_blk, value_blk, gradient_block, allowed):
@@ -102,15 +77,6 @@
     local = jnp.arange(row_count, dtype=jnp.int32)
     positions = base + local
     doc_row = doc_ids[0]
-    same_doc = doc_row[:, None] == doc_row[None, :]
-    local_first = jnp.min(jnp.where(same_doc, local[None, :], row_count), axis=1) + base
-    carry_doc, carry_start = entering(
-        (doc_row[row_count - 1], local_first[row_count - 1]),
-        "seq",
-        combine_docs,
-        (jnp.int32(-1), jnp.int32(0)),
-    )
-    starts = jnp.where(doc_row == carry_doc, carry_start, local_first)
 
     def prepare_function(raw, gain):
         return prepare(raw, gain, positions)
@@ -128,20 +94,23 @@
     query_rot = query_normalized.astype(jnp.bfloat16)
     key_flat = key_normalized.astype(jnp.bfloat16).reshape(row_count, key_span_width)
     value_flat = value_proj[0]
-    key_parts = []
-    value_parts = []
-    for offset in range(behind, 0, -1):
-        moved = from_behind((key_flat, value_flat), "seq", offset)
-        key_parts.append(moved[0])
-        value_parts.append(moved[1])
-    key_win = jnp.concatenate(key_parts + [key_flat], axis=0)
-    value_win = jnp.concatenate(value_parts + [value_flat], axis=0)
+    doc_rows = jnp.zeros((16, 2 * key_span_width), jnp.bfloat16)
+    doc_rows = doc_rows.at[0, :row_count].set(doc_row.astype(jnp.bfloat16))
+    packed = jnp.concatenate(
+        [jnp.concatenate([key_flat, value_flat], axis=1), doc_rows], axis=0
+    )
+    parts = [from_behind(packed, "seq", offset) for offset in range(behind, 0, -1)]
+    stacked = jnp.stack(parts + [packed])
     width = (behind + 1) * row_count
+    key_win = stacked[:, :row_count, :key_span_width].reshape(width, key_span_width)
+    value_win = stacked[:, :row_count, key_span_width:].reshape(width, key_span_width)
+    key_doc = stacked[:, row_count, :row_count].reshape(width).astype(jnp.int32)
     key_pos = base - behind * row_count + jnp.arange(width, dtype=jnp.int32)
     allowed = (
         (key_pos[None, :] <= positions[:, None])
         & (positions[:, None] - key_pos[None, :] < WINDOW_LENGTH)
-        & (key_pos[None, :] >= starts[:, None])
+        & (key_pos[None, :] >= 0)
+        & (key_doc[None, :] == doc_row[:, None])
     )
     query_groups = query_rot.reshape(row_count, group_count, 2, group_ratio, HEAD_SIZE).transpose(
         1, 0, 2, 3, 4
@@ -163,21 +132,19 @@
     dquery_rot = dquery_g.transpose(1, 0, 2, 3, 4).reshape(row_count, QUERY_HEADS, HEAD_SIZE)
     dkey_win = dkey_g.transpose(1, 0, 2, 3).reshape(behind + 1, row_count, key_span_width)
     dvalue_win = dvalue_g.transpose(1, 0, 2, 3).reshape(behind + 1, row_count, key_span_width)
-    key_remote = dkey_win[:behind].astype(jnp.bfloat16)
-    value_remote = dvalue_win[:behind].astype(jnp.bfloat16)
+    remote = jnp.concatenate([dkey_win[:behind], dvalue_win[:behind]], axis=2).astype(jnp.bfloat16)
     key_full_length = dkey_win[behind]
     value_total = dvalue_win[behind]
     for offset in range(1, behind + 1):
-        moved = from_behind(
-            (key_remote[behind - offset], value_remote[behind - offset]), "seq", -offset
-        )
-        key_full_length = key_full_length + moved[0].astype(jnp.float32)
-        value_total = value_total + moved[1].astype(jnp.float32)
+        moved = from_behind(remote[behind - offset], "seq", -offset).astype(jnp.float32)
+        key_full_length = key_full_length + moved[:, :key_span_width]
+        value_total = value_total + moved[:, key_span_width:]
     query_raw_gradient, query_gain_gradient = query_back(dquery_rot)
     key_raw_gradient, key_gain_gradient = key_backward(
         key_full_length.reshape(row_count, KEY_VALUE_HEADS, HEAD_SIZE)
     )
-    gain_query, gain_key = lax.psum((query_gain_gradient, key_gain_gradient), ("seq", "dp"))
+    gains = lax.psum((query_gain_gradient, key_gain_gradient), "dp")
+    gain_query, gain_key = lax.psum(gains, "seq")
     return (
         query_raw_gradient.astype(jnp.bfloat16).reshape(1, row_count, QUERY_HEADS * HEAD_SIZE),
         key_raw_gradient.astype(jnp.bfloat16).reshape(1, row_count, key_span_width),

time: 1080 us -> 913 us (0.85)
  the two profiles are of different devices: /device:TPU:1 before, /device:TPU:320 now
where the time goes in v1:
time: 913 us; the launch traced here: 911 us
  blocking collectives  392 us (43%)
  waiting for transfers between devices  346 us (38%)
  local copies, waits for them, and re-layouts  58 us (6%)
  starting transfers between devices  43.4 us (5%)
  matrix products  34.9 us (4%)
  other arithmetic  34.2 us (4%)
    psum x1, blocking collectives, shards(): gain_query, gain_key = lax.psum(gains, 'seq')  387 us
    ppermute x16, waiting for transfers between devices, from_behind(): lax.ppermute(value, axis, [(source, source + steps) for source in range(f...  346 us
    ppermute x16, starting transfers between devices, from_behind(): lax.ppermute(value, axis, [(source, source + steps) for source in range(f...  43.4 us
  transfers between devices with their start and end apart: 16, of which 6 were waited for; matrix products, arithmetic and copies ran while one was open for 4% of the time, Pallas kernels for 0%

profile of v1, /device:TPU:320, one launch (start us, length us, event | category | flops | bytes accessed | tf_op | source)
XLA Modules:
  0.0 911.4 jit_solution(12322501338451647611)
XLA Ops:
  4.8 3.5 collective-permute-start.7
  8.3 4.5 collective-permute-start.6
  12.8 4.9 collective-permute-start.5
  17.7 5.4 collective-permute-start.1
  23.1 3.4 collective-permute-start
  31.1 109.9 %collective-permute-done = bf16[144,2048]{1,0:T(8,128)(2,1)} collective-permute-done((bf16[144,2048]{1,0:T(8,128)(2,1)}, bf16[144,2048]{1,0:T(8,128)(2,1)}, u32[]{:S(2)}, u32[]{:S(2)}) %collective-permute-start) | collective-permute-done | bytes 589856 | tf_op jit(solution)/shard_map/ppermute | solution.py:20
  141.0 1.9 collective-permute-start.2
  144.1 1.9 collective-permute-start.3
  147.1 79.2 %collective-permute-done.2 = bf16[144,2048]{1,0:T(8,128)(2,1)S(1)} collective-permute-done((bf16[144,2048]{1,0:T(8,128)(2,1)}, bf16[144,2048]{1,0:T(8,128)(2,1)S(1)}, u32[]{:S(2)}, u32[]{:S(2)}) %collective-permute-start.2) | collective-permute-done | bytes 589856 | tf_op jit(solution)/shard_map/ppermute | solution.py:20
  226.3 2.1 collective-permute-start.4
  228.5 18.8 %collective-permute-done.4 = bf16[144,2048]{1,0:T(8,128)(2,1)S(1)} collective-permute-done((bf16[144,2048]{1,0:T(8,128)(2,1)}, bf16[144,2048]{1,0:T(8,128)(2,1)S(1)}, u32[]{:S(2)}, u32[]{:S(2)}) %collective-permute-start.4) | collective-permute-done | bytes 589856 | tf_op jit(solution)/shard_map/ppermute | solution.py:20
  250.8 2.0 fusion.57
  252.8 6.6 reshape_reshape.7
  259.4 2.9 reshape_reshape.6
  262.3 54.9 %while.16 = (s32[]{:T(128)}, f32[4,128,2,2,128]{1,4,3,2,0:T(8,128)}, f32[4,1152,2,128]{1,3,2,0:T(8,128)}, f32[4,1152,2,128]{1,3,2,0:T(8,128)}, bf16[4,1152,2,128...) while((s32[]{:T(128)}, ...), condition=%wide.region_4.5_spmd.clone, body=%wide.region_2.4_spmd.clone.sunk | while | flops 912278656 | bytes 28114468 | solution.py:129
  263.4 1.9 fusion.86
  265.3 1.9 constant_dynamic-slice_fusion.5
  273.5 2.4 fusion.91
  277.0 1.9 fusion.86
  279.0 1.9 constant_dynamic-slice_fusion.5
  287.2 2.4 fusion.91
  290.7 1.9 fusion.86
  292.7 1.9 constant_dynamic-slice_fusion.5
  301.0 2.4 fusion.91
  304.5 1.9 fusion.86
  306.4 1.9 constant_dynamic-slice_fusion.5
  314.7 2.4 fusion.91
  317.2 2.5 slice.356
  320.3 3.0 copy.116
  323.3 2.5 slice.357
  326.4 2.9 copy.115
  329.4 3.7 fusion.50
  333.1 1.9 collective-permute-start.8
  335.0 1.9 collective-permute-start.9
  337.0 2.1 collective-permute-start.10
  340.6 1.9 collective-permute-start.11
  342.5 1.9 collective-permute-start.12
  347.7 124.1 %collective-permute-done.8 = bf16[128,2048]{1,0:T(8,128)(2,1)} collective-permute-done((bf16[128,2048]{1,0:T(8,128)(2,1)}, bf16[128,2048]{1,0:T(8,128)(2,1)}, u32[]{:S(2)}, u32[]{:S(2)}) %collective-permute-start.8) | collective-permute-done | bytes 524320 | tf_op jit(solution)/shard_map/ppermute | solution.py:20
  471.9 1.9 collective-permute-start.13
  473.8 9.3 %collective-permute-done.9 = bf16[128,2048]{1,0:T(8,128)(2,1)} collective-permute-done((bf16[128,2048]{1,0:T(8,128)(2,1)}, bf16[128,2048]{1,0:T(8,128)(2,1)}, u32[]{:S(2)}, u32[]{:S(2)}) %collective-permute-start.9) | collective-permute-done | bytes 524320 | tf_op jit(solution)/shard_map/ppermute | solution.py:20
  483.1 1.9 collective-permute-start.15
  485.0 5.0 collective-permute-done.10
  490.1 2.1 collective-permute-start.14
  496.9 2.0 copy.117
  499.0 2.0 copy.114
  503.0 2.1 reshape.195
  519.0 5.7 all-reduce.6
  524.7 386.7 %all-reduce.5 = (f32[128]{0:T(128)}, f32[128]{0:T(128)}) all-reduce(f32[128]{0:T(128)S(1)} %get-tuple-element.173, f32[128]{0:T(128)S(1)} %get-tuple-element.174), channel_id=1, replica_groups=mesh['seq'=128,'dp'=4] {'seq'}, use_global_device_ids=true, to_apply=%region_9.10 | all-reduce | flops 256 | bytes 2048 | tf_op jit(solution)/shard_map/psum | solution.py:147
  (242 shorter events, 69.9 us)
Async XLA Ops:
  3.2 25.9 %copy-start.10 = (f32[128,64]{1,0:T(8,128)}, f32[128,64]{1,0:T(8,128)S(1)}, u32[]{:S(2)}) copy-start(f32[128,64]{1,0:T(8,128)S(1)} %get-tuple-element.199) | copy-start | bytes 98308
  3.2 25.9 %copy-start.12 = (f32[128,64]{1,0:T(8,128)}, f32[128,64]{1,0:T(8,128)S(1)}, u32[]{:S(2)}) copy-start(f32[128,64]{1,0:T(8,128)S(1)} %get-tuple-element.200) | copy-start | bytes 98308
  3.4 24.5 %copy-start.20 = (bf16[1,128,2048]{2,1,0:T(8,128)(2,1)S(1)}, bf16[1,128,2048]{2,1,0:T(8,128)(2,1)}, u32[]{:S(2)}) copy-start(bf16[1,128,2048]{2,1,0:T(8,128)(2,1)} %param.11) | copy-start | bytes 1572868
  4.8 244.8 %collective-permute-start.7 = (bf16[144,2048]{1,0:T(8,128)(2,1)}, bf16[144,2048]{1,0:T(8,128)(2,1)}, u32[]{:S(2)}, u32[]{:S(2)}) collective-permute-start(bf16[144,2048]{1,0:T(8,128)(2,1)} %fusion.33), channel_id=1, source_target_pairs={{0,4},{4,8},{8,12},{12,16},{16,20},{20,24},{24,28},{28,32},{32,36}... | collective-permute-start | bytes 1769480 | tf_op jit(solution)/shard_map/ppermute | solution.py:20
  8.3 240.2 %collective-permute-start.6 = (bf16[144,2048]{1,0:T(8,128)(2,1)}, bf16[144,2048]{1,0:T(8,128)(2,1)}, u32[]{:S(2)}, u32[]{:S(2)}) collective-permute-start(bf16[144,2048]{1,0:T(8,128)(2,1)} %fusion.33), channel_id=1, source_target_pairs={{0,8},{4,12},{8,16},{12,20},{16,24},{20,28},{24,32},{28,36},{32,40... | collective-permute-start | bytes 1769480 | tf_op jit(solution)/shard_map/ppermute | solution.py:20
  12.8 234.6 %collective-permute-start.5 = (bf16[144,2048]{1,0:T(8,128)(2,1)}, bf16[144,2048]{1,0:T(8,128)(2,1)}, u32[]{:S(2)}, u32[]{:S(2)}) collective-permute-start(bf16[144,2048]{1,0:T(8,128)(2,1)} %fusion.33), channel_id=1, source_target_pairs={{0,12},{4,16},{8,20},{12,24},{16,28},{20,32},{24,36},{28,40},{32,4... | collective-permute-start | bytes 1769480 | tf_op jit(solution)/shard_map/ppermute | solution.py:20
  17.7 126.3 %collective-permute-start.1 = (bf16[144,2048]{1,0:T(8,128)(2,1)}, bf16[144,2048]{1,0:T(8,128)(2,1)}, u32[]{:S(2)}, u32[]{:S(2)}) collective-permute-start(bf16[144,2048]{1,0:T(8,128)(2,1)} %fusion.33), channel_id=1, source_target_pairs={{0,28},{4,32},{8,36},{12,40},{16,44},{20,48},{24,52},{28,56},{32,6... | collective-permute-start | bytes 1769480 | tf_op jit(solution)/shard_map/ppermute | solution.py:20
  23.1 117.9 %collective-permute-start = (bf16[144,2048]{1,0:T(8,128)(2,1)}, bf16[144,2048]{1,0:T(8,128)(2,1)}, u32[]{:S(2)}, u32[]{:S(2)}) collective-permute-start(bf16[144,2048]{1,0:T(8,128)(2,1)} %fusion.33), channel_id=1, source_target_pairs={{0,32},{4,36},{8,40},{12,44},{16,48},{20,52},{24,56},{28,60},{32,6... | collective-permute-start | bytes 1769480 | tf_op jit(solution)/shard_map/ppermute | solution.py:20
  141.0 85.3 %collective-permute-start.2 = (bf16[144,2048]{1,0:T(8,128)(2,1)}, bf16[144,2048]{1,0:T(8,128)(2,1)S(1)}, u32[]{:S(2)}, u32[]{:S(2)}) collective-permute-start(bf16[144,2048]{1,0:T(8,128)(2,1)} %fusion.33), channel_id=1, source_target_pairs={{0,24},{4,28},{8,32},{12,36},{16,40},{20,44},{24,48},{28,52},{32,5... | collective-permute-start | bytes 1769480 | tf_op jit(solution)/shard_map/ppermute | solution.py:20
  144.1 84.4 %collective-permute-start.3 = (bf16[144,2048]{1,0:T(8,128)(2,1)}, bf16[144,2048]{1,0:T(8,128)(2,1)S(1)}, u32[]{:S(2)}, u32[]{:S(2)}) collective-permute-start(bf16[144,2048]{1,0:T(8,128)(2,1)} %fusion.33), channel_id=1, source_target_pairs={{0,20},{4,24},{8,28},{12,32},{16,36},{20,40},{24,44},{28,48},{32,5... | collective-permute-start | bytes 1769480 | tf_op jit(solution)/shard_map/ppermute | solution.py:20
  226.3 21.0 %collective-permute-start.4 = (bf16[144,2048]{1,0:T(8,128)(2,1)}, bf16[144,2048]{1,0:T(8,128)(2,1)S(1)}, u32[]{:S(2)}, u32[]{:S(2)}) collective-permute-start(bf16[144,2048]{1,0:T(8,128)(2,1)} %fusion.33), channel_id=1, source_target_pairs={{0,16},{4,20},{8,24},{12,28},{16,32},{20,36},{24,40},{28,44},{32,4... | collective-permute-start | bytes 1769480 | tf_op jit(solution)/shard_map/ppermute | solution.py:20
  262.3 4.9 copy-start
  271.9 4.0 copy-start.7
  271.9 4.0 copy-start.24
  272.0 4.0 copy-start.28
  272.0 4.0 copy-start.30
  276.0 4.9 copy-start
  285.7 4.0 copy-start.7
  285.7 4.0 copy-start.24
  285.7 4.0 copy-start.28
  285.7 4.0 copy-start.30
  289.7 4.9 copy-start
  299.3 4.0 copy-start.7
  299.3 4.0 copy-start.24
  299.3 4.0 copy-start.28
  299.3 4.0 copy-start.30
  303.5 4.9 copy-start
  313.1 4.0 copy-start.7
  313.1 4.0 copy-start.24
  313.1 4.0 copy-start.28
  313.1 4.0 copy-start.30
  329.4 9.7 %copy-start.18 = (f32[4,128,2,2,128]{1,4,3,2,0:T(8,128)S(1)}, f32[4,128,2,2,128]{1,4,3,2,0:T(8,128)}, u32[]{:S(2)}) copy-start(f32[4,128,2,2,128]{1,4,3,2,0:T(8,128)} %get-tuple-element.332) | copy-start | bytes 3145732
  333.1 138.8 %collective-permute-start.8 = (bf16[128,2048]{1,0:T(8,128)(2,1)}, bf16[128,2048]{1,0:T(8,128)(2,1)}, u32[]{:S(2)}, u32[]{:S(2)}) collective-permute-start(bf16[128,2048]{1,0:T(8,128)(2,1)} %get-tuple-element.181), channel_id=1, source_target_pairs={{4,0},{8,4},{12,8},{16,12},{20,16},{24,20},{28,24},{32,28},{36,32}... | collective-permute-start | bytes 1572872 | tf_op jit(solution)/shard_map/ppermute | solution.py:20
  335.0 148.1 %collective-permute-start.9 = (bf16[128,2048]{1,0:T(8,128)(2,1)}, bf16[128,2048]{1,0:T(8,128)(2,1)}, u32[]{:S(2)}, u32[]{:S(2)}) collective-permute-start(bf16[128,2048]{1,0:T(8,128)(2,1)} %get-tuple-element.182), channel_id=1, source_target_pairs={{8,0},{12,4},{16,8},{20,12},{24,16},{28,20},{32,24},{36,28},{40,32... | collective-permute-start | bytes 1572872 | tf_op jit(solution)/shard_map/ppermute | solution.py:20
  337.0 153.1 %collective-permute-start.10 = (bf16[128,2048]{1,0:T(8,128)(2,1)}, bf16[128,2048]{1,0:T(8,128)(2,1)}, u32[]{:S(2)}, u32[]{:S(2)}) collective-permute-start(bf16[128,2048]{1,0:T(8,128)(2,1)} %get-tuple-element.183), channel_id=1, source_target_pairs={{12,0},{16,4},{20,8},{24,12},{28,16},{32,20},{36,24},{40,28},{44,3... | collective-permute-start | bytes 1572872 | tf_op jit(solution)/shard_map/ppermute | solution.py:20
  339.1 6.8 copy-start.11
  339.1 6.8 copy-start.13
  340.6 167.8 %collective-permute-start.11 = (bf16[128,2048]{1,0:T(8,128)(2,1)}, bf16[128,2048]{1,0:T(8,128)(2,1)}, u32[]{:S(2)}, u32[]{:S(2)}) collective-permute-start(bf16[128,2048]{1,0:T(8,128)(2,1)} %get-tuple-element.184), channel_id=1, source_target_pairs={{16,0},{20,4},{24,8},{28,12},{32,16},{36,20},{40,24},{44,28},{48,3... | collective-permute-start | bytes 1572872 | tf_op jit(solution)/shard_map/ppermute | solution.py:20
  342.5 167.1 %collective-permute-start.12 = (bf16[128,2048]{1,0:T(8,128)(2,1)}, bf16[128,2048]{1,0:T(8,128)(2,1)}, u32[]{:S(2)}, u32[]{:S(2)}) collective-permute-start(bf16[128,2048]{1,0:T(8,128)(2,1)} %get-tuple-element.185), channel_id=1, source_target_pairs={{20,0},{24,4},{28,8},{32,12},{36,16},{40,20},{44,24},{48,28},{52,3... | collective-permute-start | bytes 1572872 | tf_op jit(solution)/shard_map/ppermute | solution.py:20
  345.9 146.3 %copy-start.3 = (f32[16,8,16,128]{3,2,1,0:T(8,128)S(1)}, f32[16,8,16,128]{3,2,1,0:T(8,128)}, u32[]{:S(2)}) copy-start(f32[16,8,16,128]{3,2,1,0:T(8,128)} %copy-done.2) | copy-start | bytes 3145732
  345.9 146.4 %copy-start.15 = (f32[128,16]{1,0:T(8,128)S(1)}, f32[128,16]{1,0:T(8,128)}, u32[]{:S(2)}) copy-start(f32[128,16]{1,0:T(8,128)} %copy-done.14) | copy-start | bytes 24580
  345.9 146.4 %copy-start.32 = (f32[128]{0:T(128)S(1)}, f32[128]{0:T(128)}, u32[]{:S(2)}) copy-start(f32[128]{0:T(128)} %param.16) | copy-start | bytes 1540
  471.9 38.9 %collective-permute-start.13 = (bf16[128,2048]{1,0:T(8,128)(2,1)}, bf16[128,2048]{1,0:T(8,128)(2,1)}, u32[]{:S(2)}, u32[]{:S(2)}) collective-permute-start(bf16[128,2048]{1,0:T(8,128)(2,1)} %get-tuple-element.186), channel_id=1, source_target_pairs={{24,0},{28,4},{32,8},{36,12},{40,16},{44,20},{48,24},{52,28},{56,3... | collective-permute-start | bytes 1572872 | tf_op jit(solution)/shard_map/ppermute | solution.py:20
  483.1 28.9 %collective-permute-start.15 = (bf16[128,2048]{1,0:T(8,128)(2,1)}, bf16[128,2048]{1,0:T(8,128)(2,1)}, u32[]{:S(2)}, u32[]{:S(2)}) collective-permute-start(bf16[128,2048]{1,0:T(8,128)(2,1)} %get-tuple-element.187), channel_id=1, source_target_pairs={{32,0},{36,4},{40,8},{44,12},{48,16},{52,20},{56,24},{60,28},{64,3... | collective-permute-start | bytes 1572872 | tf_op jit(solution)/shard_map/ppermute | solution.py:20
  490.1 23.1 %collective-permute-start.14 = (bf16[128,2048]{1,0:T(8,128)(2,1)}, bf16[128,2048]{1,0:T(8,128)(2,1)}, u32[]{:S(2)}, u32[]{:S(2)}) collective-permute-start(bf16[128,2048]{1,0:T(8,128)(2,1)} %get-tuple-element.188), channel_id=1, source_target_pairs={{28,0},{32,4},{36,8},{40,12},{44,16},{48,20},{52,24},{56,28},{60,3... | collective-permute-start | bytes 1572872 | tf_op jit(solution)/shard_map/ppermute | solution.py:20
  493.1 7.9 copy-start.22
  510.7 3.6 copy-start.8
  510.8 3.6 copy-start.9
  (30 other events, 38.4 us)

commit v2 on v1

--- a/solution.py
+++ b/solution.py
@@ -12,6 +12,10 @@
 rope_base = 10000.0
 score_scale = 168.0 ** (-0.5)
 norm_eps = 1e-06
+
+
+SEQ_AXES = ("zh", "x", "y")
+DP_AXES = ("zl", "c")
 
 
 def from_behind(value, axis, steps):
@@ -73,7 +77,7 @@
     group_ratio = QUERY_HEADS // KEY_VALUE_HEADS
     group_count = KEY_VALUE_HEADS // 2
     key_span_width = KEY_VALUE_HEADS * HEAD_SIZE
-    base = lax.axis_index("seq") * row_count
+    base = lax.axis_index(SEQ_AXES) * row_count
     local = jnp.arange(row_count, dtype=jnp.int32)
     positions = base + local
     doc_row = doc_ids[0]
@@ -99,7 +103,7 @@
     packed = jnp.concatenate(
         [jnp.concatenate([key_flat, value_flat], axis=1), doc_rows], axis=0
     )
-    parts = [from_behind(packed, "seq", offset) for offset in range(behind, 0, -1)]
+    parts = [from_behind(packed, SEQ_AXES, offset) for offset in range(behind, 0, -1)]
     stacked = jnp.stack(parts + [packed])
     width = (behind + 1) * row_count
     key_win = stacked[:, :row_count, :key_span_width].reshape(width, key_span_width)
@@ -136,15 +140,17 @@
     key_full_length = dkey_win[behind]
     value_total = dvalue_win[behind]
     for offset in range(1, behind + 1):
-        moved = from_behind(remote[behind - offset], "seq", -offset).astype(jnp.float32)
+        moved = from_behind(remote[behind - offset], SEQ_AXES, -offset).astype(jnp.float32)
         key_full_length = key_full_length + moved[:, :key_span_width]
         value_total = value_total + moved[:, key_span_width:]
     query_raw_gradient, query_gain_gradient = query_back(dquery_rot)
     key_raw_gradient, key_gain_gradient = key_backward(
         key_full_length.reshape(row_count, KEY_VALUE_HEADS, HEAD_SIZE)
     )
-    gains = lax.psum((query_gain_gradient, key_gain_gradient), "dp")
-    gain_query, gain_key = lax.psum(gains, "seq")
+    gains = (query_gain_gradient, key_gain_gradient)
+    for axis in ("y", "x", "zh", "zl", "c"):
+        gains = lax.psum(gains, axis)
+    gain_query, gain_key = gains
     return (
         query_raw_gradient.astype(jnp.bfloat16).reshape(1, row_count, QUERY_HEADS * HEAD_SIZE),
         key_raw_gradient.astype(jnp.bfloat16).reshape(1, row_count, key_span_width),
@@ -155,14 +161,14 @@
 
 
 def solution(mesh):
-    in_specs = (
-        P("dp", "seq", None),
-        P("dp", "seq", None),
-        P("dp", "seq", None),
-        P("dp", "seq", None),
-        P("dp", "seq"),
-        P(),
-        P(),
+    seq_size, dp_size = mesh.shape["seq"], mesh.shape["dp"]
+    y_size = 8
+    x_size = 4
+    fine = jax.sharding.Mesh(
+        mesh.devices.reshape(seq_size // (x_size * y_size), x_size, y_size, dp_size // 2, 2),
+        ("zh", "x", "y", "zl", "c"),
     )
-    out_specs = (P("dp", "seq", None), P("dp", "seq", None), P("dp", "seq", None), P(), P())
-    return jax.shard_map(shards, mesh=mesh, in_specs=in_specs, out_specs=out_specs, check_vma=False)
+    tokens = P(DP_AXES, SEQ_AXES, None)
+    in_specs = (tokens, tokens, tokens, tokens, P(DP_AXES, SEQ_AXES), P(), P())
+    out_specs = (tokens, tokens, tokens, P(), P())
+    return jax.shard_map(shards, mesh=fine, in_specs=in_specs, out_specs=out_specs, check_vma=False)

time: 913 us -> 598 us (0.65)
  the two profiles are of different devices: /device:TPU:320 before, /device:TPU:1 now
where the time goes in v2:
time: 598 us; the launch traced here: 596 us
  blocking collectives  226 us (38%)
  waiting for transfers between devices  205 us (34%)
  local copies, waits for them, and re-layouts  58 us (10%)
  starting transfers between devices  36.7 us (6%)
  matrix products  34.9 us (6%)
  other arithmetic  34.2 us (6%)
    psum x5, blocking collectives, shards(): gains = lax.psum(gains, axis)  226 us
    ppermute x16, waiting for transfers between devices, from_behind(): lax.ppermute(value, axis, [(source, source + steps) for source in range(f...  205 us
    ppermute x16, starting transfers between devices, from_behind(): lax.ppermute(value, axis, [(source, source + steps) for source in range(f...  36.7 us
    unnamed x69, local copies, waits for them, and re-layouts  12.2 us
  transfers between devices with their start and end apart: 16, of which 7 were waited for; matrix products, arithmetic and copies ran while one was open for 6% of the time, Pallas kernels for 0%

profile of v2, /device:TPU:1, one launch (start us, length us, event | category | flops | bytes accessed | tf_op | source)
XLA Modules:
  0.0 596.0 jit_solution(751516873034374086)
XLA Ops:
  4.8 4.9 collective-permute-start.7
  9.7 4.2 collective-permute-start.6
  13.9 4.6 collective-permute-start.5
  18.5 5.1 collective-permute-start.1
  23.6 3.2 collective-permute-start
  31.3 36.5 %collective-permute-done = bf16[144,2048]{1,0:T(8,128)(2,1)} collective-permute-done((bf16[144,2048]{1,0:T(8,128)(2,1)}, bf16[144,2048]{1,0:T(8,128)(2,1)}, u32[]{:S(2)}, u32[]{:S(2)}) %collective-permute-start) | collective-permute-done | bytes 589856 | tf_op jit(solution)/shard_map/ppermute | solution.py:24
  72.7 34.0 %collective-permute-done.2 = bf16[144,2048]{1,0:T(8,128)(2,1)S(1)} collective-permute-done((bf16[144,2048]{1,0:T(8,128)(2,1)}, bf16[144,2048]{1,0:T(8,128)(2,1)S(1)}, u32[]{:S(2)}, u32[]{:S(2)}) %collective-permute-start.2) | collective-permute-done | bytes 589856 | tf_op jit(solution)/shard_map/ppermute | solution.py:24
  108.3 25.9 %collective-permute-done.3 = bf16[144,2048]{1,0:T(8,128)(2,1)S(1)} collective-permute-done((bf16[144,2048]{1,0:T(8,128)(2,1)}, bf16[144,2048]{1,0:T(8,128)(2,1)S(1)}, u32[]{:S(2)}, u32[]{:S(2)}) %collective-permute-start.3) | collective-permute-done | bytes 589856 | tf_op jit(solution)/shard_map/ppermute | solution.py:24
  137.7 2.0 fusion.57
  139.7 6.6 %reshape_reshape.7 = bf16[1152,4,2,128]{3,2,1,0:T(2,128)(2,1)} reshape(bf16[9,128,1024]{2,1,0:T(8,128)(2,1)} %get-tuple-element.185) | data formatting | bytes 4718592 | tf_op jit(solution)/shard_map/reshape;reshape | solution.py:128
  146.3 2.9 reshape_reshape.6
  149.2 54.9 %while.16 = (s32[]{:T(128)}, f32[4,128,2,2,128]{1,4,3,2,0:T(8,128)}, f32[4,1152,2,128]{1,3,2,0:T(8,128)}, f32[4,1152,2,128]{1,3,2,0:T(8,128)}, bf16[4,1152,2,128...) while((s32[]{:T(128)}, ...), condition=%wide.region_4.5_spmd.clone, body=%wide.region_2.4_spmd.clone.sunk | while | flops 912278656 | bytes 28114468 | solution.py:133
  150.3 1.9 fusion.86
  152.2 1.9 constant_dynamic-slice_fusion.5
  154.1 1.8 fusion.87
  160.4 2.4 fusion.91
  164.0 1.9 fusion.86
  165.9 1.9 constant_dynamic-slice_fusion.5
  174.1 2.4 fusion.91
  177.7 1.9 fusion.86
  179.6 1.9 constant_dynamic-slice_fusion.5
  181.5 1.8 fusion.87
  187.9 2.4 fusion.91
  191.4 1.9 fusion.86
  193.3 1.9 constant_dynamic-slice_fusion.5
  195.3 1.8 fusion.87
  201.6 2.4 fusion.91
  204.1 2.5 slice.356
  207.3 3.0 copy.116
  210.2 2.5 slice.357
  213.4 2.9 copy.115
  216.3 3.7 fusion.50
  229.5 1.9 multiply_add_fusion.1
  231.3 3.9 collective-permute-done.8
  236.5 48.4 %collective-permute-done.9 = bf16[128,2048]{1,0:T(8,128)(2,1)} collective-permute-done((bf16[128,2048]{1,0:T(8,128)(2,1)}, bf16[128,2048]{1,0:T(8,128)(2,1)}, u32[]{:S(2)}, u32[]{:S(2)}) %collective-permute-start.9) | collective-permute-done | bytes 524320 | tf_op jit(solution)/shard_map/ppermute | solution.py:24
  286.3 17.3 %collective-permute-done.10 = bf16[128,2048]{1,0:T(8,128)(2,1)} collective-permute-done((bf16[128,2048]{1,0:T(8,128)(2,1)}, bf16[128,2048]{1,0:T(8,128)(2,1)}, u32[]{:S(2)}, u32[]{:S(2)}) %collective-permute-start.10) | collective-permute-done | bytes 524320 | tf_op jit(solution)/shard_map/ppermute | solution.py:24
  306.0 1.9 slice.200
  307.9 1.9 slice.175
  309.8 2.0 copy.117
  311.8 2.0 copy.114
  314.0 1.8 fusion.32
  315.8 2.1 reshape.195
  324.8 38.7 %collective-permute-done.15 = bf16[128,2048]{1,0:T(8,128)(2,1)} collective-permute-done((bf16[128,2048]{1,0:T(8,128)(2,1)}, bf16[128,2048]{1,0:T(8,128)(2,1)}, u32[]{:S(2)}, u32[]{:S(2)}) %collective-permute-start.15) | collective-permute-done | bytes 524320 | tf_op jit(solution)/shard_map/ppermute | solution.py:24
  370.5 34.9 %all-reduce.5 = (f32[128]{0:T(128)S(1)}, f32[128]{0:T(128)S(1)}) all-reduce(f32[128]{0:T(128)S(1)} %get-tuple-element.141, f32[128]{0:T(128)S(1)} %get-tuple-element.143), channel_id=1, replica_groups=mesh['zh'=4,'x'=4,'y'=8,'zl'=2,'c'=2] {'y'}, use_global_device_ids=true, to_apply=%region_8.9 | all-reduce | flops 256 | bytes 2048 | tf_op jit(solution)/shard_map/psum | solution.py:152
  405.4 99.8 %all-reduce.6 = (f32[128]{0:T(128)S(1)}, f32[128]{0:T(128)S(1)}) all-reduce(f32[128]{0:T(128)S(1)} %get-tuple-element.171, f32[128]{0:T(128)S(1)} %get-tuple-element.172), channel_id=1, replica_groups=mesh['zh'=4,'x'=4,'y'=8,'zl'=2,'c'=2] {'x'}, use_global_device_ids=true, to_apply=%region_9.10 | all-reduce | flops 256 | bytes 2048 | tf_op jit(solution)/shard_map/psum | solution.py:152
  505.2 51.8 %all-reduce.7 = (f32[128]{0:T(128)S(1)}, f32[128]{0:T(128)S(1)}) all-reduce(f32[128]{0:T(128)S(1)} %get-tuple-element.173, f32[128]{0:T(128)S(1)} %get-tuple-element.174), channel_id=1, replica_groups=mesh['zh'=4,'x'=4,'y'=8,'zl'=2,'c'=2] {'zh'}, use_global_device_ids=true, to_apply=%region_10.11 | all-reduce | flops 256 | bytes 2048 | tf_op jit(solution)/shard_map/psum | solution.py:152
  557.0 24.8 %all-reduce.9 = (f32[128]{0:T(128)S(1)}, f32[128]{0:T(128)S(1)}) all-reduce(f32[128]{0:T(128)S(1)} %get-tuple-element.175, f32[128]{0:T(128)S(1)} %get-tuple-element.176), channel_id=1, replica_groups=mesh['zh'=4,'x'=4,'y'=8,'zl'=2,'c'=2] {'zl'}, use_global_device_ids=true, to_apply=%region_11.12 | all-reduce | flops 256 | bytes 2048 | tf_op jit(solution)/shard_map/psum | solution.py:152
  581.8 14.2 %all-reduce.8 = (f32[128]{0:T(128)}, f32[128]{0:T(128)}) all-reduce(f32[128]{0:T(128)S(1)} %get-tuple-element.179, f32[128]{0:T(128)S(1)} %get-tuple-element.180), channel_id=1, replica_groups=mesh['zh'=4,'x'=4,'y'=8,'zl'=2,'c'=2] {'c'}, use_global_device_ids=true, to_apply=%region_12.13 | all-reduce | flops 256 | bytes 2048 | tf_op jit(solution)/shard_map/psum | solution.py:152
  (245 shorter events, 71.8 us)
Async XLA Ops:
  3.2 26.2 %copy-start.10 = (f32[128,64]{1,0:T(8,128)}, f32[128,64]{1,0:T(8,128)S(1)}, u32[]{:S(2)}) copy-start(f32[128,64]{1,0:T(8,128)S(1)} %get-tuple-element.205) | copy-start | bytes 98308
  3.2 26.2 %copy-start.12 = (f32[128,64]{1,0:T(8,128)}, f32[128,64]{1,0:T(8,128)S(1)}, u32[]{:S(2)}) copy-start(f32[128,64]{1,0:T(8,128)S(1)} %get-tuple-element.206) | copy-start | bytes 98308
  3.4 24.7 %copy-start.20 = (bf16[1,128,2048]{2,1,0:T(8,128)(2,1)S(1)}, bf16[1,128,2048]{2,1,0:T(8,128)(2,1)}, u32[]{:S(2)}) copy-start(bf16[1,128,2048]{2,1,0:T(8,128)(2,1)} %param.11) | copy-start | bytes 1572868
  4.8 131.7 %collective-permute-start.7 = (bf16[144,2048]{1,0:T(8,128)(2,1)}, bf16[144,2048]{1,0:T(8,128)(2,1)}, u32[]{:S(2)}, u32[]{:S(2)}) collective-permute-start(bf16[144,2048]{1,0:T(8,128)(2,1)} %fusion.33), channel_id=1, source_target_pairs={{0,4},{4,8},{8,12},{12,16},{16,20},{20,24},{24,28},{28,32},{32,36}... | collective-permute-start | bytes 1769480 | tf_op jit(solution)/shard_map/ppermute | solution.py:24
  9.7 125.7 %collective-permute-start.6 = (bf16[144,2048]{1,0:T(8,128)(2,1)}, bf16[144,2048]{1,0:T(8,128)(2,1)}, u32[]{:S(2)}, u32[]{:S(2)}) collective-permute-start(bf16[144,2048]{1,0:T(8,128)(2,1)} %fusion.33), channel_id=1, source_target_pairs={{0,8},{4,12},{8,16},{12,20},{16,24},{20,28},{24,32},{28,36},{32,40... | collective-permute-start | bytes 1769480 | tf_op jit(solution)/shard_map/ppermute | solution.py:24
  13.9 120.4 %collective-permute-start.5 = (bf16[144,2048]{1,0:T(8,128)(2,1)}, bf16[144,2048]{1,0:T(8,128)(2,1)}, u32[]{:S(2)}, u32[]{:S(2)}) collective-permute-start(bf16[144,2048]{1,0:T(8,128)(2,1)} %fusion.33), channel_id=1, source_target_pairs={{0,12},{4,16},{8,20},{12,24},{16,28},{20,32},{24,36},{28,40},{32,4... | collective-permute-start | bytes 1769480 | tf_op jit(solution)/shard_map/ppermute | solution.py:24
  18.5 51.7 %collective-permute-start.1 = (bf16[144,2048]{1,0:T(8,128)(2,1)}, bf16[144,2048]{1,0:T(8,128)(2,1)}, u32[]{:S(2)}, u32[]{:S(2)}) collective-permute-start(bf16[144,2048]{1,0:T(8,128)(2,1)} %fusion.33), channel_id=1, source_target_pairs={{0,28},{4,32},{8,36},{12,40},{16,44},{20,48},{24,52},{28,56},{32,6... | collective-permute-start | bytes 1769480 | tf_op jit(solution)/shard_map/ppermute | solution.py:24
  23.6 44.2 %collective-permute-start = (bf16[144,2048]{1,0:T(8,128)(2,1)}, bf16[144,2048]{1,0:T(8,128)(2,1)}, u32[]{:S(2)}, u32[]{:S(2)}) collective-permute-start(bf16[144,2048]{1,0:T(8,128)(2,1)} %fusion.33), channel_id=1, source_target_pairs={{0,32},{4,36},{8,40},{12,44},{16,48},{20,52},{24,56},{28,60},{32,6... | collective-permute-start | bytes 1769480 | tf_op jit(solution)/shard_map/ppermute | solution.py:24
  67.8 38.9 %collective-permute-start.2 = (bf16[144,2048]{1,0:T(8,128)(2,1)}, bf16[144,2048]{1,0:T(8,128)(2,1)S(1)}, u32[]{:S(2)}, u32[]{:S(2)}) collective-permute-start(bf16[144,2048]{1,0:T(8,128)(2,1)} %fusion.33), channel_id=1, source_target_pairs={{0,24},{4,28},{8,32},{12,36},{16,40},{20,44},{24,48},{28,52},{32,5... | collective-permute-start | bytes 1769480 | tf_op jit(solution)/shard_map/ppermute | solution.py:24
  70.3 63.9 %collective-permute-start.3 = (bf16[144,2048]{1,0:T(8,128)(2,1)}, bf16[144,2048]{1,0:T(8,128)(2,1)S(1)}, u32[]{:S(2)}, u32[]{:S(2)}) collective-permute-start(bf16[144,2048]{1,0:T(8,128)(2,1)} %fusion.33), channel_id=1, source_target_pairs={{0,20},{4,24},{8,28},{12,32},{16,36},{20,40},{24,44},{28,48},{32,5... | collective-permute-start | bytes 1769480 | tf_op jit(solution)/shard_map/ppermute | solution.py:24
  106.8 27.5 %collective-permute-start.4 = (bf16[144,2048]{1,0:T(8,128)(2,1)}, bf16[144,2048]{1,0:T(8,128)(2,1)S(1)}, u32[]{:S(2)}, u32[]{:S(2)}) collective-permute-start(bf16[144,2048]{1,0:T(8,128)(2,1)} %fusion.33), channel_id=1, source_target_pairs={{0,16},{4,20},{8,24},{12,28},{16,32},{20,36},{24,40},{28,44},{32,4... | collective-permute-start | bytes 1769480 | tf_op jit(solution)/shard_map/ppermute | solution.py:24
  149.2 4.9 copy-start
  158.9 4.0 copy-start.7
  158.9 4.0 copy-start.24
  158.9 4.0 copy-start.28
  158.9 4.0 copy-start.30
  163.0 4.9 copy-start
  172.6 4.0 copy-start.7
  172.6 4.0 copy-start.24
  172.6 4.0 copy-start.28
  172.6 4.0 copy-start.30
  176.6 4.9 copy-start
  186.3 4.0 copy-start.7
  186.3 4.0 copy-start.24
  186.3 4.0 copy-start.28
  186.3 4.0 copy-start.30
  190.4 4.9 copy-start
  200.0 4.0 copy-start.7
  200.0 4.0 copy-start.24
  200.0 4.0 copy-start.28
  200.0 4.1 copy-start.30
  216.3 7.6 %copy-start.18 = (f32[4,128,2,2,128]{1,4,3,2,0:T(8,128)S(1)}, f32[4,128,2,2,128]{1,4,3,2,0:T(8,128)}, u32[]{:S(2)}) copy-start(f32[4,128,2,2,128]{1,4,3,2,0:T(8,128)} %get-tuple-element.338) | copy-start | bytes 3145732
  220.0 15.2 %collective-permute-start.8 = (bf16[128,2048]{1,0:T(8,128)(2,1)}, bf16[128,2048]{1,0:T(8,128)(2,1)}, u32[]{:S(2)}, u32[]{:S(2)}) collective-permute-start(bf16[128,2048]{1,0:T(8,128)(2,1)} %get-tuple-element.187), channel_id=1, source_target_pairs={{4,0},{8,4},{12,8},{16,12},{20,16},{24,20},{28,24},{32,28},{36,32}... | collective-permute-start | bytes 1572872 | tf_op jit(solution)/shard_map/ppermute | solution.py:24
  221.3 63.6 %collective-permute-start.9 = (bf16[128,2048]{1,0:T(8,128)(2,1)}, bf16[128,2048]{1,0:T(8,128)(2,1)}, u32[]{:S(2)}, u32[]{:S(2)}) collective-permute-start(bf16[128,2048]{1,0:T(8,128)(2,1)} %get-tuple-element.188), channel_id=1, source_target_pairs={{8,0},{12,4},{16,8},{20,12},{24,16},{28,20},{32,24},{36,28},{40,32... | collective-permute-start | bytes 1572872 | tf_op jit(solution)/shard_map/ppermute | solution.py:24
  222.6 80.9 %collective-permute-start.10 = (bf16[128,2048]{1,0:T(8,128)(2,1)}, bf16[128,2048]{1,0:T(8,128)(2,1)}, u32[]{:S(2)}, u32[]{:S(2)}) collective-permute-start(bf16[128,2048]{1,0:T(8,128)(2,1)} %get-tuple-element.189), channel_id=1, source_target_pairs={{12,0},{16,4},{20,8},{24,12},{28,16},{32,20},{36,24},{40,28},{44,3... | collective-permute-start | bytes 1572872 | tf_op jit(solution)/shard_map/ppermute | solution.py:24
  223.9 5.5 copy-start.11
  223.9 5.5 copy-start.13
  225.5 95.8 %collective-permute-start.11 = (bf16[128,2048]{1,0:T(8,128)(2,1)}, bf16[128,2048]{1,0:T(8,128)(2,1)}, u32[]{:S(2)}, u32[]{:S(2)}) collective-permute-start(bf16[128,2048]{1,0:T(8,128)(2,1)} %get-tuple-element.190), channel_id=1, source_target_pairs={{16,0},{20,4},{24,8},{28,12},{32,16},{36,20},{40,24},{44,28},{48,3... | collective-permute-start | bytes 1572872 | tf_op jit(solution)/shard_map/ppermute | solution.py:24
  226.8 95.7 %collective-permute-start.12 = (bf16[128,2048]{1,0:T(8,128)(2,1)}, bf16[128,2048]{1,0:T(8,128)(2,1)}, u32[]{:S(2)}, u32[]{:S(2)}) collective-permute-start(bf16[128,2048]{1,0:T(8,128)(2,1)} %get-tuple-element.191), channel_id=1, source_target_pairs={{20,0},{24,4},{28,8},{32,12},{36,16},{40,20},{44,24},{48,28},{52,3... | collective-permute-start | bytes 1572872 | tf_op jit(solution)/shard_map/ppermute | solution.py:24
  229.4 75.6 %copy-start.3 = (f32[16,8,16,128]{3,2,1,0:T(8,128)S(1)}, f32[16,8,16,128]{3,2,1,0:T(8,128)}, u32[]{:S(2)}) copy-start(f32[16,8,16,128]{3,2,1,0:T(8,128)} %copy-done.2) | copy-start | bytes 3145732
  229.4 75.6 %copy-start.15 = (f32[128,16]{1,0:T(8,128)S(1)}, f32[128,16]{1,0:T(8,128)}, u32[]{:S(2)}) copy-start(f32[128,16]{1,0:T(8,128)} %copy-done.14) | copy-start | bytes 24580
  229.4 75.6 %copy-start.32 = (f32[128]{0:T(128)S(1)}, f32[128]{0:T(128)}, u32[]{:S(2)}) copy-start(f32[128]{0:T(128)} %param.16) | copy-start | bytes 1540
  235.2 88.4 %collective-permute-start.13 = (bf16[128,2048]{1,0:T(8,128)(2,1)}, bf16[128,2048]{1,0:T(8,128)(2,1)}, u32[]{:S(2)}, u32[]{:S(2)}) collective-permute-start(bf16[128,2048]{1,0:T(8,128)(2,1)} %get-tuple-element.192), channel_id=1, source_target_pairs={{24,0},{28,4},{32,8},{36,12},{40,16},{44,20},{48,24},{52,28},{56,3... | collective-permute-start | bytes 1572872 | tf_op jit(solution)/shard_map/ppermute | solution.py:24
  285.0 78.6 %collective-permute-start.15 = (bf16[128,2048]{1,0:T(8,128)(2,1)}, bf16[128,2048]{1,0:T(8,128)(2,1)}, u32[]{:S(2)}, u32[]{:S(2)}) collective-permute-start(bf16[128,2048]{1,0:T(8,128)(2,1)} %get-tuple-element.193), channel_id=1, source_target_pairs={{32,0},{36,4},{40,8},{44,12},{48,16},{52,20},{56,24},{60,28},{64,3... | collective-permute-start | bytes 1572872 | tf_op jit(solution)/shard_map/ppermute | solution.py:24
  303.5 61.2 %collective-permute-start.14 = (bf16[128,2048]{1,0:T(8,128)(2,1)}, bf16[128,2048]{1,0:T(8,128)(2,1)}, u32[]{:S(2)}, u32[]{:S(2)}) collective-permute-start(bf16[128,2048]{1,0:T(8,128)(2,1)} %get-tuple-element.194), channel_id=1, source_target_pairs={{28,0},{32,4},{36,8},{40,12},{44,16},{48,20},{52,24},{56,28},{60,3... | collective-permute-start | bytes 1572872 | tf_op jit(solution)/shard_map/ppermute | solution.py:24
  306.0 7.9 %copy-start.22 = (f32[128,16]{0,1:T(8,128)S(1)}, f32[128,16]{0,1:T(8,128)}, u32[]{:S(2)}) copy-start(f32[128,16]{0,1:T(8,128)} %copy-done.21) | copy-start | bytes 24580
  323.6 42.3 %copy-start.8 = (f32[128,1024]{1,0:T(8,128)S(1)}, f32[128,1024]{1,0:T(8,128)}, u32[]{:S(2)}) copy-start(f32[128,1024]{1,0:T(8,128)} %copy.117) | copy-start | bytes 1572868
  323.6 42.3 %copy-start.9 = (f32[128,1024]{1,0:T(8,128)S(1)}, f32[128,1024]{1,0:T(8,128)}, u32[]{:S(2)}) copy-start(f32[128,1024]{1,0:T(8,128)} %copy.114) | copy-start | bytes 1572868
  (30 other events, 38.4 us)

commit v3 on v2

--- a/solution.py
+++ b/solution.py
@@ -90,67 +90,68 @@
         query_proj[0].astype(jnp.float32).reshape(row_count, QUERY_HEADS, HEAD_SIZE),
         query_gain,
     )
-    key_normalized, key_backward = jax.vjp(
-        prepare_function,
-        key_projection[0].astype(jnp.float32).reshape(row_count, KEY_VALUE_HEADS, HEAD_SIZE),
-        key_norm_gain,
-    )
     query_rot = query_normalized.astype(jnp.bfloat16)
-    key_flat = key_normalized.astype(jnp.bfloat16).reshape(row_count, key_span_width)
     value_flat = value_proj[0]
     doc_rows = jnp.zeros((16, 2 * key_span_width), jnp.bfloat16)
     doc_rows = doc_rows.at[0, :row_count].set(doc_row.astype(jnp.bfloat16))
     packed = jnp.concatenate(
-        [jnp.concatenate([key_flat, value_flat], axis=1), doc_rows], axis=0
+        [jnp.concatenate([key_projection[0], value_flat], axis=1), doc_rows], axis=0
     )
     parts = [from_behind(packed, SEQ_AXES, offset) for offset in range(behind, 0, -1)]
     stacked = jnp.stack(parts + [packed])
     width = (behind + 1) * row_count
-    key_win = stacked[:, :row_count, :key_span_width].reshape(width, key_span_width)
-    value_win = stacked[:, :row_count, key_span_width:].reshape(width, key_span_width)
+    key_raw_win = stacked[:, :row_count, :key_span_width].reshape(width, KEY_VALUE_HEADS, HEAD_SIZE)
+    value_win = stacked[:, :row_count, key_span_width:].reshape(width, KEY_VALUE_HEADS, HEAD_SIZE)
     key_doc = stacked[:, row_count, :row_count].reshape(width).astype(jnp.int32)
     key_pos = base - behind * row_count + jnp.arange(width, dtype=jnp.int32)
+
+    def prepare_window(raw, gain):
+        return prepare(raw, gain, key_pos)
+
+    key_normalized_win, key_window_back = jax.vjp(
+        prepare_window, key_raw_win.astype(jnp.float32), key_norm_gain
+    )
+    key_win = key_normalized_win.astype(jnp.bfloat16)
     allowed = (
         (key_pos[None, :] <= positions[:, None])
         & (positions[:, None] - key_pos[None, :] < WINDOW_LENGTH)
         & (key_pos[None, :] >= 0)
         & (key_doc[None, :] == doc_row[:, None])
     )
-    query_groups = query_rot.reshape(row_count, group_count, 2, group_ratio, HEAD_SIZE).transpose(
-        1, 0, 2, 3, 4
+    dquery_rot, dkey_win, dvalue_win = attend(
+        query_rot.reshape(row_count, KEY_VALUE_HEADS, group_ratio, HEAD_SIZE),
+        key_win,
+        value_win,
+        attn_grad[0].reshape(row_count, KEY_VALUE_HEADS, group_ratio, HEAD_SIZE),
+        allowed,
     )
-    grad_groups = (
-        attn_grad[0]
-        .reshape(row_count, group_count, 2, group_ratio, HEAD_SIZE)
-        .transpose(1, 0, 2, 3, 4)
-    )
-    key_groups = key_win.reshape(width, group_count, 2, HEAD_SIZE).transpose(1, 0, 2, 3)
-    value_groups = value_win.reshape(width, group_count, 2, HEAD_SIZE).transpose(1, 0, 2, 3)
-
-    def group_work(items):
-        return attend(items[0], items[1], items[2], items[3], allowed)
-
-    dquery_g, dkey_g, dvalue_g = lax.map(
-        group_work, (query_groups, key_groups, value_groups, grad_groups)
-    )
-    dquery_rot = dquery_g.transpose(1, 0, 2, 3, 4).reshape(row_count, QUERY_HEADS, HEAD_SIZE)
-    dkey_win = dkey_g.transpose(1, 0, 2, 3).reshape(behind + 1, row_count, key_span_width)
-    dvalue_win = dvalue_g.transpose(1, 0, 2, 3).reshape(behind + 1, row_count, key_span_width)
-    remote = jnp.concatenate([dkey_win[:behind], dvalue_win[:behind]], axis=2).astype(jnp.bfloat16)
-    key_full_length = dkey_win[behind]
-    value_total = dvalue_win[behind]
-    for offset in range(1, behind + 1):
-        moved = from_behind(remote[behind - offset], SEQ_AXES, -offset).astype(jnp.float32)
-        key_full_length = key_full_length + moved[:, :key_span_width]
-        value_total = value_total + moved[:, key_span_width:]
+    dquery_rot = dquery_rot.reshape(row_count, QUERY_HEADS, HEAD_SIZE)
+    dkey_win = dkey_win.reshape(behind + 1, row_count, key_span_width)
+    dvalue_win = dvalue_win.reshape(behind + 1, row_count, key_span_width)
+    remote_key = dkey_win[:behind].astype(jnp.bfloat16)
+    remote = jnp.concatenate([remote_key, dvalue_win[:behind].astype(jnp.bfloat16)], axis=2)
+    owned = jnp.concatenate([remote_key.astype(jnp.float32), dkey_win[behind:]], axis=0)
+    _, key_gain_gradient = key_window_back(owned.reshape(width, KEY_VALUE_HEADS, HEAD_SIZE))
     query_raw_gradient, query_gain_gradient = query_back(dquery_rot)
-    key_raw_gradient, key_gain_gradient = key_backward(
-        key_full_length.reshape(row_count, KEY_VALUE_HEADS, HEAD_SIZE)
-    )
+    sent = [from_behind(remote[behind - offset], SEQ_AXES, -offset) for offset in range(1, behind + 1)]
     gains = (query_gain_gradient, key_gain_gradient)
     for axis in ("y", "x", "zh", "zl", "c"):
         gains = lax.psum(gains, axis)
     gain_query, gain_key = gains
+    key_full_length = dkey_win[behind]
+    value_total = dvalue_win[behind]
+    for moved in sent:
+        moved = moved.astype(jnp.float32)
+        key_full_length = key_full_length + moved[:, :key_span_width]
+        value_total = value_total + moved[:, key_span_width:]
+    _, key_backward = jax.vjp(
+        prepare_function,
+        key_projection[0].astype(jnp.float32).reshape(row_count, KEY_VALUE_HEADS, HEAD_SIZE),
+        key_norm_gain,
+    )
+    key_raw_gradient, _ = key_backward(
+        key_full_length.reshape(row_count, KEY_VALUE_HEADS, HEAD_SIZE)
+    )
     return (
         query_raw_gradient.astype(jnp.bfloat16).reshape(1, row_count, QUERY_HEADS * HEAD_SIZE),
         key_raw_gradient.astype(jnp.bfloat16).reshape(1, row_count, key_span_width),

time: 598 us -> 582 us (0.973)
  waiting for transfers between devices: 205 us -> 135 us
  other arithmetic: 34.2 us -> 62.4 us
  blocking collectives: 226 us -> 244 us
  starting transfers between devices: 36.7 us -> 49.5 us
  matrix products: 34.9 us -> 24.9 us
    ppermute x16, waiting for transfers between devices: 205 us -> 135 us  [from_behind(): lax.ppermute(value, axis, [(source, source + steps) for source in range(f...]
    psum x5, blocking collectives: 226 us -> 244 us  [shards(): gains = lax.psum(gains, axis)]
    unnamed x69 -> x91, local copies, waits for them, and re-layouts: 12.2 us -> 28.4 us
    ppermute x16, starting transfers between devices: 36.7 us -> 49.5 us  [from_behind(): lax.ppermute(value, axis, [(source, source + steps) for source in range(f...]
    slice x5 -> x2, local copies, waits for them, and re-layouts: 12.9 us -> 2.84 us  [the longest x1 2.51 us: shards(): dvalue_win[:behind].astype(jnp.bfloat16)]
    dynamic_slice x12 -> x0, local copies, waits for them, and re-layouts: 8.19 us -> none  [shards(): lax.map(group_work, (query_groups, key_groups, value_groups, grad_groups))]
    dot_general x4 -> x1, matrix products: 9.7 us -> 1.85 us  [attend(): jnp.einsum('grtw,tgrd->wgd', dscores, query_blk, preferred_element_type=j...]
    convert_element_type x0 -> x2, local copies, waits for them, and re-layouts: none -> 7.61 us  [the longest x1 4.18 us: shards(): dvalue_win[:behind].astype(jnp.bfloat16)]
  transfers between devices with their start and end apart: 16 -> 16, of which waited for: 7 -> 5; matrix products, arithmetic and copies ran while one was open for 6% -> 9% of each run, Pallas kernels for 0% -> 0%
where the time goes in v3:
time: 582 us; the launch traced here: 576 us
  blocking collectives  244 us (42%)
  waiting for transfers between devices  135 us (23%)
  other arithmetic  62.4 us (11%)
  local copies, waits for them, and re-layouts  58.3 us (10%)
  starting transfers between devices  49.5 us (9%)
  matrix products  24.9 us (4%)
    psum x5, blocking collectives, shards(): gains = lax.psum(gains, axis)  244 us
    ppermute x16, waiting for transfers between devices, from_behind(): lax.ppermute(value, axis, [(source, source + steps) for source in range(f...  135 us
    ppermute x16, starting transfers between devices, from_behind(): lax.ppermute(value, axis, [(source, source + steps) for source in range(f...  49.5 us
    unnamed x91, local copies, waits for them, and re-layouts  28.4 us
  transfers between devices with their start and end apart: 16, of which 5 were waited for; matrix products, arithmetic and copies ran while one was open for 9% of the time, Pallas kernels for 0%

profile of v3, /device:TPU:1, one launch (start us, length us, event | category | flops | bytes accessed | tf_op | source)
XLA Modules:
  0.0 576.0 jit_solution(1699228929685614335)
XLA Ops:
  1.3 1.9 fusion.14
  3.2 4.8 collective-permute-start
  8.0 5.9 %collective-permute-start.1 = (bf16[144,2048]{1,0:T(8,128)(2,1)}, bf16[144,2048]{1,0:T(8,128)(2,1)}, u32[]{:S(2)}, u32[]{:S(2)}) collective-permute-start(bf16[144,2048]{1,0:T(8,128)(2,1)} %fusion.14), channel_id=1, source_target_pairs={{0,28},{4,32},{8,36},{12,40},{16,44},{20,48},{24,52},{28,56},{32,6... | collective-permute-start | bytes 1769480 | tf_op jit(solution)/shard_map/ppermute | solution.py:24
  13.9 4.7 collective-permute-start.2
  18.6 3.4 collective-permute-start.3
  22.0 4.9 collective-permute-start.4
  36.9 3.3 multiply_cosine_fusion
  40.7 8.2 %collective-permute-start.5 = (bf16[144,2048]{1,0:T(8,128)(2,1)}, bf16[144,2048]{1,0:T(8,128)(2,1)S(1)}, u32[]{:S(2)}, u32[]{:S(2)}) collective-permute-start(bf16[144,2048]{1,0:T(8,128)(2,1)} %fusion.14), channel_id=1, source_target_pairs={{0,12},{4,16},{8,20},{12,24},{16,28},{20,32},{24,36},{28,40},{32,4... | collective-permute-start | bytes 1769480 | tf_op jit(solution)/shard_map/ppermute | solution.py:24
  50.1 5.5 collective-permute-start.6
  56.7 1.9 collective-permute-start.7
  59.6 40.5 %collective-permute-done.3 = bf16[144,2048]{1,0:T(8,128)(2,1)} collective-permute-done((bf16[144,2048]{1,0:T(8,128)(2,1)}, bf16[144,2048]{1,0:T(8,128)(2,1)}, u32[]{:S(2)}, u32[]{:S(2)}) %collective-permute-start.3) | collective-permute-done | bytes 589856 | tf_op jit(solution)/shard_map/ppermute | solution.py:24
  101.3 9.6 %collective-permute-done.6 = bf16[144,2048]{1,0:T(8,128)(2,1)S(1)} collective-permute-done((bf16[144,2048]{1,0:T(8,128)(2,1)}, bf16[144,2048]{1,0:T(8,128)(2,1)S(1)}, u32[]{:S(2)}, u32[]{:S(2)}) %collective-permute-start.6) | collective-permute-done | bytes 589856 | tf_op jit(solution)/shard_map/ppermute | solution.py:24
  111.0 21.4 %collective-permute-done.7 = bf16[144,2048]{1,0:T(8,128)(2,1)S(1)} collective-permute-done((bf16[144,2048]{1,0:T(8,128)(2,1)}, bf16[144,2048]{1,0:T(8,128)(2,1)S(1)}, u32[]{:S(2)}, u32[]{:S(2)}) %collective-permute-start.7) | collective-permute-done | bytes 589856 | tf_op jit(solution)/shard_map/ppermute | solution.py:24
  132.5 3.0 slice_convert_fusion.2
  136.9 2.8 copy.140
  139.7 3.5 copy.166
  143.2 2.2 copy-done
  145.4 2.0 multiply_reduce_fusion.1
  147.7 4.2 fusion.5
  154.9 3.3 fusion.3
  158.2 3.6 copy-done.33
  161.8 3.4 fusion.9
  165.2 2.5 copy.147
  167.7 3.3 multiply_reduce_fusion.2
  172.3 8.3 %convolution_bitcast_fusion = f32[1152,8,128]{0,2,1:T(8,128)} fusion(bf16[128,8,2,128]{0,3,2,1:T(8,128)(2,1)} %copy.125, f32[8,1152,128,2]{2,1,3,0:T(8,128)} %copy-done.33, f32[8,2,128]{2,1,0:T(2,128)} %copy-done.34, pred[128,1152]{0,1:T(8,128)(4,1)} %copy-done.23), kind=kOutput, calls=%fused_computation.30 | convolution fusion | flops 613416960 | bytes 14835712 | tf_op jit(solution)/shard_map/grtw,tgrd->wgd/dot_general | solution.py:68
  180.7 5.9 %fusion.1 = bf16[8,2,128,1152]{2,3,1,0:T(8,128)(2,1)S(1)} fusion(bf16[1152,8,128,1]{0,2,3,1:T(8,128)(2,1)S(1)} %copy-done.11, bf16[128,8,2,128]{0,3,2,1:T(8,128)(2,1)S(1)} %copy-done.20, f32[8,2,128]{2,1,0:T(2,128)S(1)} %copy.148, f32[8,2,128]{2,1,0:T(2,128)S(1)} %copy-done.35, f32[8,1152,128,2]{2,1,3,0:T(8,128)} %copy-done.33, ...), kind=kOutput, calls=%fused_computation.2 | convolution fusion | flops 618135552 | bytes 17203200 | tf_op jit(solution)/shard_map/tgrd,wgd->grtw/dot_general | solution.py:58
  186.6 2.2 convolution_multiply_fusion
  188.8 1.8 fusion.4
  193.0 2.4 copy.163
  195.4 2.4 copy.162
  197.8 2.5 slice.355
  200.3 2.0 copy.170
  202.3 4.2 copy.127
  206.5 2.0 copy.169
  208.5 3.4 copy.126
  212.0 2.4 convert_element_type.137
  214.4 2.0 fusion.34
  221.6 2.9 pad_maximum_fusion
  227.2 5.5 multiply_add_fusion.1
  238.3 5.6 collective-permute-done.15
  245.1 58.2 %collective-permute-done.14 = bf16[128,2048]{1,0:T(8,128)(2,1)} collective-permute-done((bf16[128,2048]{1,0:T(8,128)(2,1)}, bf16[128,2048]{1,0:T(8,128)(2,1)}, u32[]{:S(2)}, u32[]{:S(2)}) %collective-permute-start.14) | collective-permute-done | bytes 524320 | tf_op jit(solution)/shard_map/ppermute | solution.py:24
  308.7 2.1 reshape.262
  312.2 6.5 %multiply_reduce_fusion = f32[128]{0:T(128)S(1)} fusion(f32[1152,8,64]{2,0,1:T(8,128)} %get-tuple-element.32, f32[1152,8,64]{2,0,1:T(8,128)} %get-tuple-element.31, f32[1152,8,128]{2,1,0:T(8,128)} %bitcast.142, f32[1152,8]{0,1:T(8,128)S(1)} %copy-done.22), kind=kLoop, calls=%fused_computation.24 | loop fusion | flops 4718464 | bytes 9474560 | tf_op jit(solution)/shard_map/transpose(jvp())/reduce_sum | solution.py:42
  318.7 23.2 %all-reduce.7 = (f32[128]{0:T(128)S(1)}, f32[128]{0:T(128)S(1)}) all-reduce(f32[128]{0:T(128)S(1)} %get-tuple-element.17, f32[128]{0:T(128)S(1)} %multiply_reduce_fusion), channel_id=1, replica_groups=mesh['zh'=4,'x'=4,'y'=8,'zl'=2,'c'=2] {'y'}, use_global_device_ids=true, to_apply=%region_7.8 | all-reduce | flops 256 | bytes 2048 | tf_op jit(solution)/shard_map/psum | solution.py:139
  341.9 125.5 %all-reduce.8 = (f32[128]{0:T(128)S(1)}, f32[128]{0:T(128)S(1)}) all-reduce(f32[128]{0:T(128)S(1)} %get-tuple-element.21, f32[128]{0:T(128)S(1)} %get-tuple-element.22), channel_id=1, replica_groups=mesh['zh'=4,'x'=4,'y'=8,'zl'=2,'c'=2] {'x'}, use_global_device_ids=true, to_apply=%region_8.9 | all-reduce | flops 256 | bytes 2048 | tf_op jit(solution)/shard_map/psum | solution.py:139
  467.5 79.8 %all-reduce.9 = (f32[128]{0:T(128)S(1)}, f32[128]{0:T(128)S(1)}) all-reduce(f32[128]{0:T(128)S(1)} %get-tuple-element.23, f32[128]{0:T(128)S(1)} %get-tuple-element.24), channel_id=1, replica_groups=mesh['zh'=4,'x'=4,'y'=8,'zl'=2,'c'=2] {'zh'}, use_global_device_ids=true, to_apply=%region_9.10 | all-reduce | flops 256 | bytes 2048 | tf_op jit(solution)/shard_map/psum | solution.py:139
  547.3 4.1 all-reduce.11
  551.4 10.9 %all-reduce.10 = (f32[128]{0:T(128)}, f32[128]{0:T(128)}) all-reduce(f32[128]{0:T(128)S(1)} %get-tuple-element.29, f32[128]{0:T(128)S(1)} %get-tuple-element.30), channel_id=1, replica_groups=mesh['zh'=4,'x'=4,'y'=8,'zl'=2,'c'=2] {'c'}, use_global_device_ids=true, to_apply=%region_11.12 | all-reduce | flops 256 | bytes 2048 | tf_op jit(solution)/shard_map/psum | solution.py:139
  (159 shorter events, 58.3 us)
Async XLA Ops:
  0.6 32.2 %copy-start.29 = (f32[128]{0:T(128)S(1)}, f32[128]{0:T(128)}, u32[]{:S(2)}) copy-start(f32[128]{0:T(128)} %param.14) | copy-start | bytes 1540
  3.2 37.5 %collective-permute-start = (bf16[144,2048]{1,0:T(8,128)(2,1)}, bf16[144,2048]{1,0:T(8,128)(2,1)}, u32[]{:S(2)}, u32[]{:S(2)}) collective-permute-start(bf16[144,2048]{1,0:T(8,128)(2,1)} %fusion.14), channel_id=1, source_target_pairs={{0,32},{4,36},{8,40},{12,44},{16,48},{20,52},{24,56},{28,60},{32,6... | collective-permute-start | bytes 1769480 | tf_op jit(solution)/shard_map/ppermute | solution.py:24
  8.0 42.1 %collective-permute-start.1 = (bf16[144,2048]{1,0:T(8,128)(2,1)}, bf16[144,2048]{1,0:T(8,128)(2,1)}, u32[]{:S(2)}, u32[]{:S(2)}) collective-permute-start(bf16[144,2048]{1,0:T(8,128)(2,1)} %fusion.14), channel_id=1, source_target_pairs={{0,28},{4,32},{8,36},{12,40},{16,44},{20,48},{24,52},{28,56},{32,6... | collective-permute-start | bytes 1769480 | tf_op jit(solution)/shard_map/ppermute | solution.py:24
  13.9 42.8 %collective-permute-start.2 = (bf16[144,2048]{1,0:T(8,128)(2,1)}, bf16[144,2048]{1,0:T(8,128)(2,1)}, u32[]{:S(2)}, u32[]{:S(2)}) collective-permute-start(bf16[144,2048]{1,0:T(8,128)(2,1)} %fusion.14), channel_id=1, source_target_pairs={{0,24},{4,28},{8,32},{12,36},{16,40},{20,44},{24,48},{28,52},{32,5... | collective-permute-start | bytes 1769480 | tf_op jit(solution)/shard_map/ppermute | solution.py:24
  18.6 81.5 %collective-permute-start.3 = (bf16[144,2048]{1,0:T(8,128)(2,1)}, bf16[144,2048]{1,0:T(8,128)(2,1)}, u32[]{:S(2)}, u32[]{:S(2)}) collective-permute-start(bf16[144,2048]{1,0:T(8,128)(2,1)} %fusion.14), channel_id=1, source_target_pairs={{0,20},{4,24},{8,28},{12,32},{16,36},{20,40},{24,44},{28,48},{32,5... | collective-permute-start | bytes 1769480 | tf_op jit(solution)/shard_map/ppermute | solution.py:24
  22.0 79.2 %collective-permute-start.4 = (bf16[144,2048]{1,0:T(8,128)(2,1)}, bf16[144,2048]{1,0:T(8,128)(2,1)S(1)}, u32[]{:S(2)}, u32[]{:S(2)}) collective-permute-start(bf16[144,2048]{1,0:T(8,128)(2,1)} %fusion.14), channel_id=1, source_target_pairs={{0,16},{4,20},{8,24},{12,28},{16,32},{20,36},{24,40},{28,44},{32,4... | collective-permute-start | bytes 1769480 | tf_op jit(solution)/shard_map/ppermute | solution.py:24
  31.2 5.8 copy-start.9
  33.5 23.1 %copy-start.17 = (f32[128,64]{1,0:T(8,128)}, f32[128,64]{1,0:T(8,128)S(1)}, u32[]{:S(2)}) copy-start(f32[128,64]{1,0:T(8,128)S(1)} %get-tuple-element.62) | copy-start | bytes 98308
  40.7 91.8 %copy-start.12 = (bf16[1,128,1024]{2,1,0:T(8,128)(2,1)S(1)}, bf16[1,128,1024]{2,1,0:T(8,128)(2,1)}, u32[]{:S(2)}) copy-start(bf16[1,128,1024]{2,1,0:T(8,128)(2,1)} %param.10) | copy-start | bytes 786436
  40.7 91.8 %copy-start.19 = (bf16[1,128,1024]{2,1,0:T(8,128)(2,1)S(1)}, bf16[1,128,1024]{2,1,0:T(8,128)(2,1)}, u32[]{:S(2)}) copy-start(bf16[1,128,1024]{2,1,0:T(8,128)(2,1)} %param.11) | copy-start | bytes 786436
  40.7 60.6 %collective-permute-start.5 = (bf16[144,2048]{1,0:T(8,128)(2,1)}, bf16[144,2048]{1,0:T(8,128)(2,1)S(1)}, u32[]{:S(2)}, u32[]{:S(2)}) collective-permute-start(bf16[144,2048]{1,0:T(8,128)(2,1)} %fusion.14), channel_id=1, source_target_pairs={{0,12},{4,16},{8,20},{12,24},{16,28},{20,32},{24,36},{28,40},{32,4... | collective-permute-start | bytes 1769480 | tf_op jit(solution)/shard_map/ppermute | solution.py:24
  50.1 60.8 %collective-permute-start.6 = (bf16[144,2048]{1,0:T(8,128)(2,1)}, bf16[144,2048]{1,0:T(8,128)(2,1)S(1)}, u32[]{:S(2)}, u32[]{:S(2)}) collective-permute-start(bf16[144,2048]{1,0:T(8,128)(2,1)} %fusion.14), channel_id=1, source_target_pairs={{0,8},{4,12},{8,16},{12,20},{16,24},{20,28},{24,32},{28,36},{32,40... | collective-permute-start | bytes 1769480 | tf_op jit(solution)/shard_map/ppermute | solution.py:24
  56.7 75.8 %collective-permute-start.7 = (bf16[144,2048]{1,0:T(8,128)(2,1)}, bf16[144,2048]{1,0:T(8,128)(2,1)S(1)}, u32[]{:S(2)}, u32[]{:S(2)}) collective-permute-start(bf16[144,2048]{1,0:T(8,128)(2,1)} %fusion.14), channel_id=1, source_target_pairs={{0,4},{4,8},{8,12},{12,16},{16,20},{20,24},{24,28},{28,32},{32,36}... | collective-permute-start | bytes 1769480 | tf_op jit(solution)/shard_map/ppermute | solution.py:24
  143.2 2.2 copy-start
  143.2 4.5 copy-start.27
  147.7 4.3 copy-start.21
  147.7 4.3 copy-start.4
  147.7 4.3 copy-start.6
  152.0 1.8 copy-start.25
  152.0 1.8 copy-start.26
  152.0 2.8 copy-start.13
  152.0 2.8 copy-start.15
  153.7 4.5 copy-start.1
  154.8 3.4 copy-start.23
  154.9 7.0 %copy-start.10 = (bf16[1152,8,128,1]{0,2,3,1:T(8,128)(2,1)S(1)}, bf16[1152,8,128,1]{0,2,3,1:T(8,128)(2,1)}, u32[]{:S(2)}) copy-start(bf16[1152,8,128,1]{0,2,3,1:T(8,128)(2,1)} %copy.140) | copy-start | bytes 7077892
  158.2 3.7 copy-start.33
  158.2 3.6 copy-start.34
  172.3 8.4 %copy-start.11 = (bf16[1152,8,128,1]{0,2,3,1:T(8,128)(2,1)S(1)}, bf16[1152,8,128,1]{0,2,3,1:T(8,128)(2,1)}, u32[]{:S(2)}) copy-start(bf16[1152,8,128,1]{0,2,3,1:T(8,128)(2,1)} %copy.140) | copy-start | bytes 7077892
  172.3 8.4 %copy-start.20 = (bf16[128,8,2,128]{0,3,2,1:T(8,128)(2,1)S(1)}, bf16[128,8,2,128]{0,3,2,1:T(8,128)(2,1)}, u32[]{:S(2)}) copy-start(bf16[128,8,2,128]{0,3,2,1:T(8,128)(2,1)} %copy.125) | copy-start | bytes 1572868
  172.3 8.4 %copy-start.24 = (pred[128,1152]{0,1:T(8,128)(4,1)S(1)}, pred[128,1152]{0,1:T(8,128)(4,1)}, u32[]{:S(2)}) copy-start(pred[128,1152]{0,1:T(8,128)(4,1)} %copy-done.23) | copy-start | bytes 442372
  172.3 8.4 %copy-start.35 = (f32[8,2,128]{2,1,0:T(2,128)S(1)}, f32[8,2,128]{2,1,0:T(2,128)}, u32[]{:S(2)}) copy-start(f32[8,2,128]{2,1,0:T(2,128)} %copy-done.34) | copy-start | bytes 24580
  180.6 5.9 %copy-start.2 = (bf16[1152,8,64]{2,0,1:T(8,128)(2,1)S(1)}, bf16[1152,8,64]{2,0,1:T(8,128)(2,1)}, u32[]{:S(2)}) copy-start(bf16[1152,8,64]{2,0,1:T(8,128)(2,1)} %copy-done.1) | copy-start | bytes 3538948
  186.5 2.3 copy-start.14
  186.5 2.3 copy-start.16
  212.0 2.4 copy-start.3
  216.5 27.4 %collective-permute-start.15 = (bf16[128,2048]{1,0:T(8,128)(2,1)}, bf16[128,2048]{1,0:T(8,128)(2,1)}, u32[]{:S(2)}, u32[]{:S(2)}) collective-permute-start(bf16[128,2048]{1,0:T(8,128)(2,1)} %get-tuple-element.47), channel_id=1, source_target_pairs={{32,0},{36,4},{40,8},{44,12},{48,16},{52,20},{56,24},{60,28},{64,3... | collective-permute-start | bytes 1572872 | tf_op jit(solution)/shard_map/ppermute | solution.py:24
  217.7 85.5 %collective-permute-start.14 = (bf16[128,2048]{1,0:T(8,128)(2,1)}, bf16[128,2048]{1,0:T(8,128)(2,1)}, u32[]{:S(2)}, u32[]{:S(2)}) collective-permute-start(bf16[128,2048]{1,0:T(8,128)(2,1)} %get-tuple-element.48), channel_id=1, source_target_pairs={{28,0},{32,4},{36,8},{40,12},{44,16},{48,20},{52,24},{56,28},{60,3... | collective-permute-start | bytes 1572872 | tf_op jit(solution)/shard_map/ppermute | solution.py:24
  219.0 85.5 %collective-permute-start.13 = (bf16[128,2048]{1,0:T(8,128)(2,1)}, bf16[128,2048]{1,0:T(8,128)(2,1)}, u32[]{:S(2)}, u32[]{:S(2)}) collective-permute-start(bf16[128,2048]{1,0:T(8,128)(2,1)} %get-tuple-element.46), channel_id=1, source_target_pairs={{24,0},{28,4},{32,8},{36,12},{40,16},{44,20},{48,24},{52,28},{56,3... | collective-permute-start | bytes 1572872 | tf_op jit(solution)/shard_map/ppermute | solution.py:24
  227.2 5.6 copy-start.18
  227.2 7.3 %copy-start.30 = (f32[128]{0:T(128)S(1)}, f32[128]{0:T(128)}, u32[]{:S(2)}) copy-start(f32[128]{0:T(128)} %param.14) | copy-start | bytes 1540
  235.5 76.8 %copy-start.22 = (f32[1152,8]{0,1:T(8,128)S(1)}, f32[1152,8]{0,1:T(8,128)}, u32[]{:S(2)}) copy-start(f32[1152,8]{0,1:T(8,128)} %copy-done.21) | copy-start | bytes 110596
  235.7 330.1 %collective-permute-start.12 = (bf16[128,2048]{1,0:T(8,128)(2,1)}, bf16[128,2048]{1,0:T(8,128)(2,1)}, u32[]{:S(2)}, u32[]{:S(2)}) collective-permute-start(bf16[128,2048]{1,0:T(8,128)(2,1)} %get-tuple-element.45), channel_id=1, source_target_pairs={{20,0},{24,4},{28,8},{32,12},{36,16},{40,20},{44,24},{48,28},{52,3... | collective-permute-start | bytes 1572872 | tf_op jit(solution)/shard_map/ppermute | solution.py:24
  237.0 330.0 %collective-permute-start.11 = (bf16[128,2048]{1,0:T(8,128)(2,1)}, bf16[128,2048]{1,0:T(8,128)(2,1)}, u32[]{:S(2)}, u32[]{:S(2)}) collective-permute-start(bf16[128,2048]{1,0:T(8,128)(2,1)} %get-tuple-element.44), channel_id=1, source_target_pairs={{16,0},{20,4},{24,8},{28,12},{32,16},{36,20},{40,24},{44,28},{48,3... | collective-permute-start | bytes 1572872 | tf_op jit(solution)/shard_map/ppermute | solution.py:24
  243.8 324.3 %collective-permute-start.10 = (bf16[128,2048]{1,0:T(8,128)(2,1)}, bf16[128,2048]{1,0:T(8,128)(2,1)}, u32[]{:S(2)}, u32[]{:S(2)}) collective-permute-start(bf16[128,2048]{1,0:T(8,128)(2,1)} %get-tuple-element.43), channel_id=1, source_target_pairs={{12,0},{16,4},{20,8},{24,12},{28,16},{32,20},{36,24},{40,28},{44,3... | collective-permute-start | bytes 1572872 | tf_op jit(solution)/shard_map/ppermute | solution.py:24
  303.3 266.0 %collective-permute-start.9 = (bf16[128,2048]{1,0:T(8,128)(2,1)}, bf16[128,2048]{1,0:T(8,128)(2,1)}, u32[]{:S(2)}, u32[]{:S(2)}) collective-permute-start(bf16[128,2048]{1,0:T(8,128)(2,1)} %get-tuple-element.42), channel_id=1, source_target_pairs={{8,0},{12,4},{16,8},{20,12},{24,16},{28,20},{32,24},{36,28},{40,32... | collective-permute-start | bytes 1572872 | tf_op jit(solution)/shard_map/ppermute | solution.py:24
  304.6 265.8 %collective-permute-start.8 = (bf16[128,2048]{1,0:T(8,128)(2,1)}, bf16[128,2048]{1,0:T(8,128)(2,1)}, u32[]{:S(2)}, u32[]{:S(2)}) collective-permute-start(bf16[128,2048]{1,0:T(8,128)(2,1)} %get-tuple-element.41), channel_id=1, source_target_pairs={{4,0},{8,4},{12,8},{16,12},{20,16},{24,20},{28,24},{32,28},{36,32}... | collective-permute-start | bytes 1572872 | tf_op jit(solution)/shard_map/ppermute | solution.py:24
  571.5 2.0 copy-start.8
  571.5 2.0 copy-start.28
  (4 other events, 6.6 us)

commit v4 on v3

--- a/solution.py
+++ b/solution.py
@@ -18,10 +18,13 @@
 DP_AXES = ("zl", "c")
 
 
-def from_behind(value, axis, steps):
-    count = lax.axis_size(axis)
-    first, last = (max(0, -steps), min(count, count - steps))
-    return lax.ppermute(value, axis, [(source, source + steps) for source in range(first, last)])
+def shift(value, steps, cyclic):
+    count = lax.axis_size(SEQ_AXES)
+    if cyclic:
+        pairs = [(source, (source + steps) % count) for source in range(count)]
+    else:
+        pairs = [(source, source + steps) for source in range(max(0, -steps), min(count, count - steps))]
+    return lax.ppermute(value, SEQ_AXES, pairs)
 
 
 def rotary(field, positions):
@@ -97,8 +100,15 @@
     packed = jnp.concatenate(
         [jnp.concatenate([key_projection[0], value_flat], axis=1), doc_rows], axis=0
     )
-    parts = [from_behind(packed, SEQ_AXES, offset) for offset in range(behind, 0, -1)]
-    stacked = jnp.stack(parts + [packed])
+    half = behind // 2
+    near, far = [], []
+    a_slot, b_slot = packed, packed
+    for step in range(half):
+        a_slot = shift(a_slot, 1, False)
+        b_slot = shift(b_slot, behind if step == 0 else -1, True)
+        near.append(a_slot)
+        far.append(b_slot)
+    stacked = jnp.stack(far + near[::-1] + [packed])
     width = (behind + 1) * row_count
     key_raw_win = stacked[:, :row_count, :key_span_width].reshape(width, KEY_VALUE_HEADS, HEAD_SIZE)
     value_win = stacked[:, :row_count, key_span_width:].reshape(width, KEY_VALUE_HEADS, HEAD_SIZE)
@@ -129,11 +139,20 @@
     dkey_win = dkey_win.reshape(behind + 1, row_count, key_span_width)
     dvalue_win = dvalue_win.reshape(behind + 1, row_count, key_span_width)
     remote_key = dkey_win[:behind].astype(jnp.bfloat16)
-    remote = jnp.concatenate([remote_key, dvalue_win[:behind].astype(jnp.bfloat16)], axis=2)
+    remote_f32 = jnp.concatenate([dkey_win[:behind], dvalue_win[:behind]], axis=2)
+    remote = remote_f32.astype(jnp.bfloat16)
     owned = jnp.concatenate([remote_key.astype(jnp.float32), dkey_win[behind:]], axis=0)
     _, key_gain_gradient = key_window_back(owned.reshape(width, KEY_VALUE_HEADS, HEAD_SIZE))
     query_raw_gradient, query_gain_gradient = query_back(dquery_rot)
-    sent = [from_behind(remote[behind - offset], SEQ_AXES, -offset) for offset in range(1, behind + 1)]
+    carry_near = remote[behind - half]
+    for offset in range(half - 1, 0, -1):
+        got = shift(carry_near, -1, False).astype(jnp.float32)
+        carry_near = (got + remote_f32[behind - offset]).astype(jnp.bfloat16)
+    carry_far = remote[behind - half - 1]
+    for offset in range(half + 2, behind + 1):
+        got = shift(carry_far, 1, True).astype(jnp.float32)
+        carry_far = (got + remote_f32[behind - offset]).astype(jnp.bfloat16)
+    sent = [shift(carry_near, -1, False), shift(carry_far, -behind, True)]
     gains = (query_gain_gradient, key_gain_gradient)
     for axis in ("y", "x", "zh", "zl", "c"):
         gains = lax.psum(gains, axis)

time: 582 us -> 427 us (0.73)
  blocking collectives: 244 us -> 145 us
  waiting for transfers between devices: 135 us -> 78 us
    psum x5, blocking collectives: 244 us -> 145 us  [shards(): gains = lax.psum(gains, axis)]
    ppermute x16, waiting for transfers between devices: 135 us -> 78 us  [shift(): return lax.ppermute(value, SEQ_AXES, pairs)]
    convert_element_type x0 -> x6, other arithmetic: none -> 11.1 us  [the longest x1 4.11 us: shards(): remote = remote_f32.astype(jnp.bfloat16)]
    slice x2 -> x5, local copies, waits for them, and re-layouts: 2.84 us -> 13.6 us  [the longest x3 7.58 us: shards(): dvalue_win[:behind]]
    convert_element_type x2 -> x0, local copies, waits for them, and re-layouts: 7.61 us -> none  [the longest x1 4.18 us: shards(): dvalue_win[:behind].astype(jnp.bfloat16)]
    convert_element_type x8 -> x2, other arithmetic: 9.06 us -> 2.33 us  [shards(): moved = moved.astype(jnp.float32)]
    unnamed x91 -> x105, local copies, waits for them, and re-layouts: 28.4 us -> 29.1 us
  transfers between devices with their start and end apart: 16 -> 16, of which waited for: 5 -> 8; matrix products, arithmetic and copies ran while one was open for 9% -> 13% of each run, Pallas kernels for 0% -> 0%
where the time goes in v4:
time: 427 us; the launch traced here: 422 us
  blocking collectives  145 us (34%)
  waiting for transfers between devices  78 us (18%)
  other arithmetic  62.7 us (15%)
  local copies, waits for them, and re-layouts  60.8 us (14%)
  starting transfers between devices  51.5 us (12%)
  matrix products  22.4 us (5%)
    psum x5, blocking collectives, shards(): gains = lax.psum(gains, axis)  145 us
    ppermute x16, waiting for transfers between devices, shift(): return lax.ppermute(value, SEQ_AXES, pairs)  78 us
    ppermute x16, starting transfers between devices, shift(): return lax.ppermute(value, SEQ_AXES, pairs)  51.5 us
    unnamed x105, local copies, waits for them, and re-layouts  29.1 us
    add_any x3, other arithmetic, rotary(): second * sine  10.2 us
  transfers between devices with their start and end apart: 16, of which 8 were waited for; matrix products, arithmetic and copies ran while one was open for 13% of the time, Pallas kernels for 0%

profile of v4, /device:TPU:1, one launch (start us, length us, event | category | flops | bytes accessed | tf_op | source)
XLA Modules:
  0.0 422.2 jit_solution(5530279323471053999)
XLA Ops:
  3.2 3.9 collective-permute-start
  7.2 4.0 collective-permute-start.4
  20.2 15.3 %collective-permute-done = bf16[144,2048]{1,0:T(8,128)(2,1)} collective-permute-done((bf16[144,2048]{1,0:T(8,128)(2,1)}, bf16[144,2048]{1,0:T(8,128)(2,1)}, u32[]{:S(2)}, u32[]{:S(2)}) %collective-permute-start) | collective-permute-done | bytes 589856 | tf_op jit(solution)/shard_map/ppermute | solution.py:27
  37.4 3.4 collective-permute-start.5
  40.8 3.3 multiply_cosine_fusion
  44.1 5.3 %collective-permute-done.1 = bf16[144,2048]{1,0:T(8,128)(2,1)S(1)} collective-permute-done((bf16[144,2048]{1,0:T(8,128)(2,1)}, bf16[144,2048]{1,0:T(8,128)(2,1)S(1)}, u32[]{:S(2)}, u32[]{:S(2)}) %collective-permute-start.1) | collective-permute-done | bytes 589856 | tf_op jit(solution)/shard_map/ppermute | solution.py:27
  49.4 8.5 %collective-permute-start.2 = (bf16[144,2048]{1,0:T(8,128)(2,1)S(1)}, bf16[144,2048]{1,0:T(8,128)(2,1)S(1)}, u32[]{:S(2)}, u32[]{:S(2)}) collective-permute-start(bf16[144,2048]{1,0:T(8,128)(2,1)S(1)} %collective-permute-done.1), channel_id=1, source_target_pairs={{0,508},{4,0},{8,4},{12,8},{16,12},{20,16},{24,20},{28,24},{32,28}... | collective-permute-start | bytes 1769480 | tf_op jit(solution)/shard_map/ppermute | solution.py:27
  61.1 11.6 %collective-permute-done.2 = bf16[144,2048]{1,0:T(8,128)(2,1)S(1)} collective-permute-done((bf16[144,2048]{1,0:T(8,128)(2,1)S(1)}, bf16[144,2048]{1,0:T(8,128)(2,1)S(1)}, u32[]{:S(2)}, u32[]{:S(2)}) %collective-permute-start.2) | collective-permute-done | bytes 589856 | tf_op jit(solution)/shard_map/ppermute | solution.py:27
  72.8 10.4 %collective-permute-start.3 = (bf16[144,2048]{1,0:T(8,128)(2,1)S(1)}, bf16[144,2048]{1,0:T(8,128)(2,1)S(1)}, u32[]{:S(2)}, u32[]{:S(2)}) collective-permute-start(bf16[144,2048]{1,0:T(8,128)(2,1)S(1)} %collective-permute-done.2), channel_id=1, source_target_pairs={{0,508},{4,0},{8,4},{12,8},{16,12},{20,16},{24,20},{28,24},{32,28}... | collective-permute-start | bytes 1769480 | tf_op jit(solution)/shard_map/ppermute | solution.py:27
  85.2 10.2 %collective-permute-done.3 = bf16[144,2048]{1,0:T(8,128)(2,1)S(1)} collective-permute-done((bf16[144,2048]{1,0:T(8,128)(2,1)S(1)}, bf16[144,2048]{1,0:T(8,128)(2,1)S(1)}, u32[]{:S(2)}, u32[]{:S(2)}) %collective-permute-start.3) | collective-permute-done | bytes 589856 | tf_op jit(solution)/shard_map/ppermute | solution.py:27
  96.8 3.0 slice_convert_fusion
  101.1 2.8 copy.140
  103.9 3.5 copy.166
  107.4 2.2 copy-done.2
  109.6 2.0 multiply_reduce_fusion.1
  111.9 4.2 %fusion.6 = f32[1152,8,128]{2,0,1:T(8,128)S(1)} fusion(f32[1152,8,128]{2,1,0:T(8,128)} %bitcast.165, f32[128]{0:T(128)S(1)} %copy-done.31, f32[1152,8]{0,1:T(8,128)S(1)} %add_rsqrt_fusion), kind=kLoop, calls=%fused_computation.31 | loop fusion | flops 2359296 | bytes 9474560 | tf_op jit(solution)/shard_map/jvp()/mul | solution.py:45
  119.2 3.3 fusion.4
  122.5 3.6 copy-done.37
  126.1 3.4 fusion.10
  129.5 1.9 copy.147
  131.5 2.0 multiply_reduce_fusion.2
  134.8 8.3 %convolution_bitcast_fusion = f32[1152,8,128]{0,2,1:T(8,128)} fusion(bf16[128,8,2,128]{0,3,2,1:T(8,128)(2,1)} %copy.125, f32[8,1152,128,2]{2,1,3,0:T(8,128)} %copy-done.37, f32[8,2,128]{2,1,0:T(2,128)S(1)} %get-tuple-element.59, pred[128,1152]{0,1:T(8,128)(4,1)S(1)} %fusion.42), kind=kOutput, calls=%fused_computation.30 | convolution fusion | flops 613416960 | bytes 14835712 | tf_op jit(solution)/shard_map/grtw,tgrd->wgd/dot_general | solution.py:71
  143.1 3.4 fusion.1
  149.3 3.0 copy.169
  152.3 5.4 %copy.126 = f32[8,128,1024]{2,1,0:T(8,128)} copy(f32[8,128,1024]{1,0,2:T(8,128)} %bitcast.175) | data formatting | bytes 8388608 | tf_op jit(solution)/shard_map/slice | solution.py:142
  157.7 2.2 slice-done.2
  159.9 3.0 copy.170
  162.9 5.4 %copy.127 = f32[8,128,1024]{2,1,0:T(8,128)} copy(f32[8,128,1024]{1,0,2:T(8,128)} %bitcast.176) | data formatting | bytes 8388608 | tf_op jit(solution)/shard_map/slice | solution.py:142
  168.2 4.1 fusion.2
  174.5 4.2 collective-permute-start.12
  179.0 2.8 convert_convert_fusion
  187.3 4.3 %fusion.59 = (f32[1152,8,64]{2,1,0:T(8,128)}, f32[1152,8,64]{2,1,0:T(8,128)}) fusion(f32[1152,8,128]{2,1,0:T(8,128)S(1)} %bitcast.167), kind=kLoop, calls=%fused_computation.134 | loop fusion | bytes 9437184 | tf_op jit(solution)/shard_map/transpose(jvp())/split | solution.py:38
  191.6 7.7 %collective-permute-done.9 = bf16[128,2048]{1,0:T(8,128)(2,1)S(1)} collective-permute-done((bf16[128,2048]{1,0:T(8,128)(2,1)S(1)}, bf16[128,2048]{1,0:T(8,128)(2,1)S(1)}, u32[]{:S(2)}, u32[]{:S(2)}) %collective-permute-start.9) | collective-permute-done | bytes 524320 | tf_op jit(solution)/shard_map/ppermute | solution.py:27
  201.5 9.7 %multiply_add_fusion.1 = (f32[1152,8,64]{2,0,1:T(8,128)}, f32[1152,8,64]{2,0,1:T(8,128)}) fusion(f32[1152,8,64]{2,1,0:T(8,128)} %get-tuple-element.40, f32[1152,8,64]{2,1,0:T(8,128)} %get-tuple-element.39, f32[1152,64]{1,0:T(8,128)} %get-tuple-element.54, f32[1152,64]{1,0:T(8,128)} %get-tuple-element.53), kind=kLoop, calls=%fused_computation.26 | loop fusion | flops 4128768 | bytes 10027008 | tf_op jit(solution)/shard_map/transpose(jvp())/add_any | solution.py:39
  213.1 2.5 fusion.26
  215.6 2.2 collective-permute-start.13
  217.8 2.2 convolution_multiply_fusion
  222.9 9.2 %collective-permute-done.13 = bf16[128,2048]{1,0:T(8,128)(2,1)} collective-permute-done((bf16[128,2048]{1,0:T(8,128)(2,1)}, bf16[128,2048]{1,0:T(8,128)(2,1)}, u32[]{:S(2)}, u32[]{:S(2)}) %collective-permute-start.13) | collective-permute-done | bytes 524320 | tf_op jit(solution)/shard_map/ppermute | solution.py:27
  239.4 16.6 %collective-permute-done.14 = bf16[128,2048]{1,0:T(8,128)(2,1)S(1)} collective-permute-done((bf16[128,2048]{1,0:T(8,128)(2,1)S(1)}, bf16[128,2048]{1,0:T(8,128)(2,1)S(1)}, u32[]{:S(2)}, u32[]{:S(2)}) %collective-permute-start.14) | collective-permute-done | bytes 524320 | tf_op jit(solution)/shard_map/ppermute | solution.py:27
  256.0 2.1 fusion.38
  258.1 2.3 collective-permute-start.15
  262.2 2.1 reshape.260
  264.7 6.5 %multiply_reduce_fusion = f32[128]{0:T(128)S(1)} fusion(f32[1152,8,64]{2,0,1:T(8,128)} %get-tuple-element.32, f32[1152,8,64]{2,0,1:T(8,128)} %get-tuple-element.31, f32[1152,8,128]{2,1,0:T(8,128)} %bitcast.166, f32[1152,8]{0,1:T(8,128)S(1)} %add_rsqrt_fusion), kind=kLoop, calls=%fused_computation.24 | loop fusion | flops 4718464 | bytes 9474560 | tf_op jit(solution)/shard_map/transpose(jvp())/reduce_sum | solution.py:45
  271.1 10.7 %all-reduce.7 = (f32[128]{0:T(128)S(1)}, f32[128]{0:T(128)S(1)}) all-reduce(f32[128]{0:T(128)S(1)} %get-tuple-element.17, f32[128]{0:T(128)S(1)} %multiply_reduce_fusion), channel_id=1, replica_groups=mesh['zh'=4,'x'=4,'y'=8,'zl'=2,'c'=2] {'y'}, use_global_device_ids=true, to_apply=%region_7.8 | all-reduce | flops 256 | bytes 2048 | tf_op jit(solution)/shard_map/psum | solution.py:158
  281.8 51.5 %all-reduce.8 = (f32[128]{0:T(128)S(1)}, f32[128]{0:T(128)S(1)}) all-reduce(f32[128]{0:T(128)S(1)} %get-tuple-element.21, f32[128]{0:T(128)S(1)} %get-tuple-element.22), channel_id=1, replica_groups=mesh['zh'=4,'x'=4,'y'=8,'zl'=2,'c'=2] {'x'}, use_global_device_ids=true, to_apply=%region_8.9 | all-reduce | flops 256 | bytes 2048 | tf_op jit(solution)/shard_map/psum | solution.py:158
  333.3 44.5 %all-reduce.9 = (f32[128]{0:T(128)S(1)}, f32[128]{0:T(128)S(1)}) all-reduce(f32[128]{0:T(128)S(1)} %get-tuple-element.23, f32[128]{0:T(128)S(1)} %get-tuple-element.24), channel_id=1, replica_groups=mesh['zh'=4,'x'=4,'y'=8,'zl'=2,'c'=2] {'zh'}, use_global_device_ids=true, to_apply=%region_9.10 | all-reduce | flops 256 | bytes 2048 | tf_op jit(solution)/shard_map/psum | solution.py:158
  377.9 13.9 %all-reduce.11 = (f32[128]{0:T(128)S(1)}, f32[128]{0:T(128)S(1)}) all-reduce(f32[128]{0:T(128)S(1)} %get-tuple-element.25, f32[128]{0:T(128)S(1)} %get-tuple-element.26), channel_id=1, replica_groups=mesh['zh'=4,'x'=4,'y'=8,'zl'=2,'c'=2] {'zl'}, use_global_device_ids=true, to_apply=%region_10.11 | all-reduce | flops 256 | bytes 2048 | tf_op jit(solution)/shard_map/psum | solution.py:158
  391.7 24.2 %all-reduce.10 = (f32[128]{0:T(128)}, f32[128]{0:T(128)}) all-reduce(f32[128]{0:T(128)S(1)} %get-tuple-element.29, f32[128]{0:T(128)S(1)} %get-tuple-element.30), channel_id=1, replica_groups=mesh['zh'=4,'x'=4,'y'=8,'zl'=2,'c'=2] {'c'}, use_global_device_ids=true, to_apply=%region_11.12 | all-reduce | flops 256 | bytes 2048 | tf_op jit(solution)/shard_map/psum | solution.py:158
  (177 shorter events, 58.3 us)
Async XLA Ops:
  0.6 13.0 %copy-start.33 = (f32[128]{0:T(128)S(1)}, f32[128]{0:T(128)}, u32[]{:S(2)}) copy-start(f32[128]{0:T(128)} %param.14) | copy-start | bytes 1540
  3.2 32.3 %collective-permute-start = (bf16[144,2048]{1,0:T(8,128)(2,1)}, bf16[144,2048]{1,0:T(8,128)(2,1)}, u32[]{:S(2)}, u32[]{:S(2)}) collective-permute-start(bf16[144,2048]{1,0:T(8,128)(2,1)} %fusion.39), channel_id=1, source_target_pairs={{0,32},{4,36},{8,40},{12,44},{16,48},{20,52},{24,56},{28,60},{32,6... | collective-permute-start | bytes 1769480 | tf_op jit(solution)/shard_map/ppermute | solution.py:27
  7.2 30.3 %collective-permute-start.4 = (bf16[144,2048]{1,0:T(8,128)(2,1)}, bf16[144,2048]{1,0:T(8,128)(2,1)}, u32[]{:S(2)}, u32[]{:S(2)}) collective-permute-start(bf16[144,2048]{1,0:T(8,128)(2,1)} %fusion.39), channel_id=1, source_target_pairs={{0,4},{4,8},{8,12},{12,16},{16,20},{20,24},{24,28},{28,32},{32,36}... | collective-permute-start | bytes 1769480 | tf_op jit(solution)/shard_map/ppermute | solution.py:27
  13.6 5.6 %copy-start.21 = (bf16[1,128,1024]{2,1,0:T(8,128)(2,1)S(1)}, bf16[1,128,1024]{2,1,0:T(8,128)(2,1)}, u32[]{:S(2)}) copy-start(bf16[1,128,1024]{2,1,0:T(8,128)(2,1)} %param.10) | copy-start | bytes 786436
  14.3 29.8 %copy-start.25 = (f32[128,64]{1,0:T(8,128)}, f32[128,64]{1,0:T(8,128)S(1)}, u32[]{:S(2)}) copy-start(f32[128,64]{1,0:T(8,128)S(1)} %get-tuple-element.58) | copy-start | bytes 98308
  15.7 28.4 %copy-start.15 = (bf16[128,8,2,128]{3,2,1,0:T(2,128)(2,1)}, bf16[128,8,2,128]{3,2,1,0:T(2,128)(2,1)S(1)}, u32[]{:S(2)}) copy-start(bf16[128,8,2,128]{3,2,1,0:T(2,128)(2,1)S(1)} %reshape_squeeze.4) | copy-start | bytes 1572868
  35.5 14.0 %collective-permute-start.1 = (bf16[144,2048]{1,0:T(8,128)(2,1)}, bf16[144,2048]{1,0:T(8,128)(2,1)S(1)}, u32[]{:S(2)}, u32[]{:S(2)}) collective-permute-start(bf16[144,2048]{1,0:T(8,128)(2,1)} %collective-permute-done), channel_id=1, source_target_pairs={{0,508},{4,0},{8,4},{12,8},{16,12},{20,16},{24,20},{28,24},{32,28}... | collective-permute-start | bytes 1769480 | tf_op jit(solution)/shard_map/ppermute | solution.py:27
  37.4 21.1 %collective-permute-start.5 = (bf16[144,2048]{1,0:T(8,128)(2,1)}, bf16[144,2048]{1,0:T(8,128)(2,1)S(1)}, u32[]{:S(2)}, u32[]{:S(2)}) collective-permute-start(bf16[144,2048]{1,0:T(8,128)(2,1)} %collective-permute-done.4), channel_id=1, source_target_pairs={{0,4},{4,8},{8,12},{12,16},{16,20},{20,24},{24,28},{28,32},{32,36}... | collective-permute-start | bytes 1769480 | tf_op jit(solution)/shard_map/ppermute | solution.py:27
  49.4 23.3 %collective-permute-start.2 = (bf16[144,2048]{1,0:T(8,128)(2,1)S(1)}, bf16[144,2048]{1,0:T(8,128)(2,1)S(1)}, u32[]{:S(2)}, u32[]{:S(2)}) collective-permute-start(bf16[144,2048]{1,0:T(8,128)(2,1)S(1)} %collective-permute-done.1), channel_id=1, source_target_pairs={{0,508},{4,0},{8,4},{12,8},{16,12},{20,16},{24,20},{28,24},{32,28}... | collective-permute-start | bytes 1769480 | tf_op jit(solution)/shard_map/ppermute | solution.py:27
  58.6 38.2 %copy-start.27 = (bf16[1,128,1024]{2,1,0:T(8,128)(2,1)S(1)}, bf16[1,128,1024]{2,1,0:T(8,128)(2,1)}, u32[]{:S(2)}) copy-start(bf16[1,128,1024]{2,1,0:T(8,128)(2,1)} %param.11) | copy-start | bytes 786436
  58.6 24.7 %collective-permute-start.6 = (bf16[144,2048]{1,0:T(8,128)(2,1)S(1)}, bf16[144,2048]{1,0:T(8,128)(2,1)S(1)}, u32[]{:S(2)}, u32[]{:S(2)}) collective-permute-start(bf16[144,2048]{1,0:T(8,128)(2,1)S(1)} %collective-permute-done.5), channel_id=1, source_target_pairs={{0,4},{4,8},{8,12},{12,16},{16,20},{20,24},{24,28},{28,32},{32,36}... | collective-permute-start | bytes 1769480 | tf_op jit(solution)/shard_map/ppermute | solution.py:27
  72.8 22.6 %collective-permute-start.3 = (bf16[144,2048]{1,0:T(8,128)(2,1)S(1)}, bf16[144,2048]{1,0:T(8,128)(2,1)S(1)}, u32[]{:S(2)}, u32[]{:S(2)}) collective-permute-start(bf16[144,2048]{1,0:T(8,128)(2,1)S(1)} %collective-permute-done.2), channel_id=1, source_target_pairs={{0,508},{4,0},{8,4},{12,8},{16,12},{20,16},{24,20},{28,24},{32,28}... | collective-permute-start | bytes 1769480 | tf_op jit(solution)/shard_map/ppermute | solution.py:27
  83.3 12.2 %collective-permute-start.7 = (bf16[144,2048]{1,0:T(8,128)(2,1)S(1)}, bf16[144,2048]{1,0:T(8,128)(2,1)S(1)}, u32[]{:S(2)}, u32[]{:S(2)}) collective-permute-start(bf16[144,2048]{1,0:T(8,128)(2,1)S(1)} %collective-permute-done.6), channel_id=1, source_target_pairs={{0,4},{4,8},{8,12},{12,16},{16,20},{20,24},{24,28},{28,32},{32,36}... | collective-permute-start | bytes 1769480 | tf_op jit(solution)/shard_map/ppermute | solution.py:27
  107.4 4.5 %copy-start.31 = (f32[128]{0:T(128)S(1)}, f32[128]{0:T(128)}, u32[]{:S(2)}) copy-start(f32[128]{0:T(128)} %param.15) | copy-start | bytes 1540
  111.9 4.3 %copy-start.10 = (f32[1152,64]{1,0:T(8,128)S(1)}, f32[1152,64]{1,0:T(8,128)}, u32[]{:S(2)}) copy-start(f32[1152,64]{1,0:T(8,128)} %get-tuple-element.53) | copy-start | bytes 884740
  111.9 4.3 %copy-start.11 = (f32[1152,64]{1,0:T(8,128)S(1)}, f32[1152,64]{1,0:T(8,128)}, u32[]{:S(2)}) copy-start(f32[1152,64]{1,0:T(8,128)} %get-tuple-element.54) | copy-start | bytes 884740
  118.0 4.5 %copy-start.6 = (bf16[1152,8,64]{2,0,1:T(8,128)(2,1)}, bf16[1152,8,64]{2,0,1:T(8,128)(2,1)S(1)}, u32[]{:S(2)}) copy-start(bf16[1152,8,64]{2,0,1:T(8,128)(2,1)S(1)} %get-tuple-element.35) | copy-start | bytes 3538948
  118.0 4.5 %copy-start.8 = (bf16[1152,8,64]{2,0,1:T(8,128)(2,1)}, bf16[1152,8,64]{2,0,1:T(8,128)(2,1)S(1)}, u32[]{:S(2)}) copy-start(bf16[1152,8,64]{2,0,1:T(8,128)(2,1)S(1)} %get-tuple-element.36) | copy-start | bytes 3538948
  119.2 7.0 %copy-start.19 = (bf16[1152,8,128,1]{0,2,3,1:T(8,128)(2,1)S(1)}, bf16[1152,8,128,1]{0,2,3,1:T(8,128)(2,1)}, u32[]{:S(2)}) copy-start(bf16[1152,8,128,1]{0,2,3,1:T(8,128)(2,1)} %copy.140) | copy-start | bytes 7077892
  122.5 3.6 copy-start.37
  126.1 5.3 %copy-start.16 = (bf16[128,8,2,128]{3,2,1,0:T(2,128)(2,1)S(1)}, bf16[128,8,2,128]{3,2,1,0:T(2,128)(2,1)}, u32[]{:S(2)}) copy-start(bf16[128,8,2,128]{3,2,1,0:T(2,128)(2,1)} %copy-done.15) | copy-start | bytes 1572868
  133.4 9.6 %slice-start.4 = ((s8[9437184]{0:T(1024)(128)(4,1)}), s8[1048576]{0:T(1024)(128)(4,1)S(1)}, s32[]{:S(2)}) async-start(s8[9437184]{0:T(1024)(128)(4,1)} %bitcast.196), calls=%async_computation.4 | async-start | bytes 2097152
  134.8 8.3 %copy-start.20 = (bf16[1152,8,128,1]{0,2,3,1:T(8,128)(2,1)S(1)}, bf16[1152,8,128,1]{0,2,3,1:T(8,128)(2,1)}, u32[]{:S(2)}) copy-start(bf16[1152,8,128,1]{0,2,3,1:T(8,128)(2,1)} %copy.140) | copy-start | bytes 7077892
  134.8 8.3 %copy-start.28 = (bf16[128,8,2,128]{0,3,2,1:T(8,128)(2,1)S(1)}, bf16[128,8,2,128]{0,3,2,1:T(8,128)(2,1)}, u32[]{:S(2)}) copy-start(bf16[128,8,2,128]{0,3,2,1:T(8,128)(2,1)} %copy.125) | copy-start | bytes 1572868
  134.8 8.3 %slice-start.5 = ((s8[9437184]{0:T(1024)(128)(4,1)}), s8[4194304]{0:T(1024)(128)(4,1)S(1)}, s32[]{:S(2)}) async-start(s8[9437184]{0:T(1024)(128)(4,1)} %bitcast.196), calls=%async_computation.5 | async-start | bytes 8388608
  134.8 8.3 %slice-start.6 = ((s8[9437184]{0:T(1024)(128)(4,1)}), s8[4194304]{0:T(1024)(128)(4,1)S(1)}, s32[]{:S(2)}) async-start(s8[9437184]{0:T(1024)(128)(4,1)} %bitcast.196), calls=%async_computation.6 | async-start | bytes 8388608
  143.1 3.4 copy-start.24
  149.3 29.5 %copy-start.13 = (f32[128,8,128]{0,2,1:T(8,128)}, f32[128,8,128]{0,2,1:T(8,128)S(1)}, u32[]{:S(2)}) copy-start(f32[128,8,128]{0,2,1:T(8,128)S(1)} %slice.130) | copy-start | bytes 1572868
  173.3 10.4 %collective-permute-start.8 = (bf16[128,2048]{1,0:T(8,128)(2,1)S(1)}, bf16[128,2048]{1,0:T(8,128)(2,1)S(1)}, u32[]{:S(2)}, u32[]{:S(2)}) collective-permute-start(bf16[128,2048]{1,0:T(8,128)(2,1)S(1)} %get-tuple-element.41), channel_id=1, source_target_pairs={{4,0},{8,4},{12,8},{16,12},{20,16},{24,20},{28,24},{32,28},{36,32}... | collective-permute-start | bytes 1572872 | tf_op jit(solution)/shard_map/ppermute | solution.py:27
  174.5 36.6 %collective-permute-start.12 = (bf16[128,2048]{1,0:T(8,128)(2,1)}, bf16[128,2048]{1,0:T(8,128)(2,1)}, u32[]{:S(2)}, u32[]{:S(2)}) collective-permute-start(bf16[128,2048]{1,0:T(8,128)(2,1)} %get-tuple-element.42), channel_id=1, source_target_pairs={{0,4},{4,8},{8,12},{12,16},{16,20},{20,24},{24,28},{28,32},{32,36}... | collective-permute-start | bytes 1572872 | tf_op jit(solution)/shard_map/ppermute | solution.py:27
  182.4 3.5 copy-start.1
  186.0 13.3 %collective-permute-start.9 = (bf16[128,2048]{1,0:T(8,128)(2,1)S(1)}, bf16[128,2048]{1,0:T(8,128)(2,1)S(1)}, u32[]{:S(2)}, u32[]{:S(2)}) collective-permute-start(bf16[128,2048]{1,0:T(8,128)(2,1)S(1)} %fusion.18), channel_id=1, source_target_pairs={{4,0},{8,4},{12,8},{16,12},{20,16},{24,20},{28,24},{32,28},{36,32}... | collective-permute-start | bytes 1572872 | tf_op jit(solution)/shard_map/ppermute | solution.py:27
  200.2 12.9 %collective-permute-start.10 = (bf16[128,2048]{1,0:T(8,128)(2,1)}, bf16[128,2048]{1,0:T(8,128)(2,1)}, u32[]{:S(2)}, u32[]{:S(2)}) collective-permute-start(bf16[128,2048]{1,0:T(8,128)(2,1)} %fusion.22), channel_id=1, source_target_pairs={{4,0},{8,4},{12,8},{16,12},{20,16},{24,20},{28,24},{32,28},{36,32}... | collective-permute-start | bytes 1572872 | tf_op jit(solution)/shard_map/ppermute | solution.py:27
  201.5 16.3 %slice-start = ((s8[4718592]{0:T(1024)(128)(4,1)}), s8[4194304]{0:T(1024)(128)(4,1)S(1)}, s32[]{:S(2)}) async-start(s8[4718592]{0:T(1024)(128)(4,1)} %bitcast.170), calls=%async_computation | async-start | bytes 8388608
  201.5 16.3 %slice-start.1 = ((s8[4718592]{0:T(1024)(128)(4,1)}), s8[524288]{0:T(1024)(128)(4,1)S(1)}, s32[]{:S(2)}) async-start(s8[4718592]{0:T(1024)(128)(4,1)} %bitcast.170), calls=%async_computation.1 | async-start | bytes 1048576
  211.2 6.6 %copy-start.7 = (bf16[1152,8,64]{2,0,1:T(8,128)(2,1)S(1)}, bf16[1152,8,64]{2,0,1:T(8,128)(2,1)}, u32[]{:S(2)}) copy-start(bf16[1152,8,64]{2,0,1:T(8,128)(2,1)} %copy-done.6) | copy-start | bytes 3538948
  211.2 6.6 %copy-start.9 = (bf16[1152,8,64]{2,0,1:T(8,128)(2,1)S(1)}, bf16[1152,8,64]{2,0,1:T(8,128)(2,1)}, u32[]{:S(2)}) copy-start(bf16[1152,8,64]{2,0,1:T(8,128)(2,1)} %copy-done.8) | copy-start | bytes 3538948
  215.6 16.6 %collective-permute-start.13 = (bf16[128,2048]{1,0:T(8,128)(2,1)}, bf16[128,2048]{1,0:T(8,128)(2,1)}, u32[]{:S(2)}, u32[]{:S(2)}) collective-permute-start(bf16[128,2048]{1,0:T(8,128)(2,1)} %get-tuple-element.34), channel_id=1, source_target_pairs={{0,4},{4,8},{8,12},{12,16},{16,20},{20,24},{24,28},{28,32},{32,36}... | collective-permute-start | bytes 1572872 | tf_op jit(solution)/shard_map/ppermute | solution.py:27
  222.9 12.6 %copy-start.17 = (f32[128,16,64]{2,1,0:T(8,128)S(1)}, f32[128,16,64]{2,1,0:T(8,128)}, u32[]{:S(2)}) copy-start(f32[128,16,64]{2,1,0:T(8,128)} %copy.163) | copy-start | bytes 1572868
  222.9 12.6 %copy-start.18 = (f32[128,16,64]{2,1,0:T(8,128)S(1)}, f32[128,16,64]{2,1,0:T(8,128)}, u32[]{:S(2)}) copy-start(f32[128,16,64]{2,1,0:T(8,128)} %copy.162) | copy-start | bytes 1572868
  222.9 12.6 %copy-start.26 = (f32[128,64]{1,0:T(8,128)S(1)}, f32[128,64]{1,0:T(8,128)}, u32[]{:S(2)}) copy-start(f32[128,64]{1,0:T(8,128)} %copy-done.25) | copy-start | bytes 98308
  222.9 13.9 %copy-start.34 = (f32[128]{0:T(128)S(1)}, f32[128]{0:T(128)}, u32[]{:S(2)}) copy-start(f32[128]{0:T(128)} %param.14) | copy-start | bytes 1540
  233.6 22.4 %collective-permute-start.14 = (bf16[128,2048]{1,0:T(8,128)(2,1)S(1)}, bf16[128,2048]{1,0:T(8,128)(2,1)S(1)}, u32[]{:S(2)}, u32[]{:S(2)}) collective-permute-start(bf16[128,2048]{1,0:T(8,128)(2,1)S(1)} %fusion.34), channel_id=1, source_target_pairs={{0,4},{4,8},{8,12},{12,16},{16,20},{20,24},{24,28},{28,32},{32,36}... | collective-permute-start | bytes 1572872 | tf_op jit(solution)/shard_map/ppermute | solution.py:27
  237.9 22.5 %copy-start.5 = (f32[128,16,64]{2,1,0:T(8,128)S(1)}, f32[128,16,64]{2,1,0:T(8,128)}, u32[]{:S(2)}) copy-start(f32[128,16,64]{2,1,0:T(8,128)} %copy-done.4) | copy-start | bytes 1572868
  237.9 178.1 %collective-permute-start.11 = (bf16[128,2048]{1,0:T(8,128)(2,1)}, bf16[128,2048]{1,0:T(8,128)(2,1)}, u32[]{:S(2)}, u32[]{:S(2)}) collective-permute-start(bf16[128,2048]{1,0:T(8,128)(2,1)} %get-tuple-element.33), channel_id=1, source_target_pairs={{4,0},{8,4},{12,8},{16,12},{20,16},{24,20},{28,24},{32,28},{36,32}... | collective-permute-start | bytes 1572872 | tf_op jit(solution)/shard_map/ppermute | solution.py:27
  258.1 6.1 %slice-start.3 = ((f32[1152,8,128]{0,2,1:T(8,128)}), f32[128,8,128]{0,2,1:T(8,128)S(1)}, s32[]{:S(2)}) async-start(f32[1152,8,128]{0,2,1:T(8,128)} %convolution_bitcast_fusion), calls=%async_computation.3 | async-start | bytes 1048576 | tf_op jit(solution)/shard_map/slice | solution.py:161
  258.1 6.4 %copy-start.14 = (f32[128,8,128]{0,2,1:T(8,128)S(1)}, f32[128,8,128]{0,2,1:T(8,128)}, u32[]{:S(2)}) copy-start(f32[128,8,128]{0,2,1:T(8,128)} %copy-done.13) | copy-start | bytes 1572868
  258.1 159.1 %collective-permute-start.15 = (bf16[128,2048]{1,0:T(8,128)(2,1)}, bf16[128,2048]{1,0:T(8,128)(2,1)}, u32[]{:S(2)}, u32[]{:S(2)}) collective-permute-start(bf16[128,2048]{1,0:T(8,128)(2,1)} %fusion.38), channel_id=1, source_target_pairs={{0,480},{4,484},{8,488},{12,492},{16,496},{20,500},{24,504},{28,50... | collective-permute-start | bytes 1572872 | tf_op jit(solution)/shard_map/ppermute | solution.py:27
  (13 other events, 28.3 us)

commit v5 on v4

--- a/solution.py
+++ b/solution.py
@@ -66,10 +66,10 @@
         "grtw,wgd->tgrd", dscores, key_blk, preferred_element_type=jnp.float32
     )
     dkey = score_scale * jnp.einsum(
-        "grtw,tgrd->wgd", dscores, query_blk, preferred_element_type=jnp.float32
+        "grtw,tgrd->gwd", dscores, query_blk, preferred_element_type=jnp.float32
     )
     dvalue = jnp.einsum(
-        "grtw,tgrd->wgd", weights_b, gradient_block, preferred_element_type=jnp.float32
+        "grtw,tgrd->gwd", weights_b, gradient_block, preferred_element_type=jnp.float32
     )
     return (dquery, dkey, dvalue)
 
@@ -136,33 +136,33 @@
         allowed,
     )
     dquery_rot = dquery_rot.reshape(row_count, QUERY_HEADS, HEAD_SIZE)
-    dkey_win = dkey_win.reshape(behind + 1, row_count, key_span_width)
-    dvalue_win = dvalue_win.reshape(behind + 1, row_count, key_span_width)
-    remote_key = dkey_win[:behind].astype(jnp.bfloat16)
-    remote_f32 = jnp.concatenate([dkey_win[:behind], dvalue_win[:behind]], axis=2)
-    remote = remote_f32.astype(jnp.bfloat16)
-    owned = jnp.concatenate([remote_key.astype(jnp.float32), dkey_win[behind:]], axis=0)
-    _, key_gain_gradient = key_window_back(owned.reshape(width, KEY_VALUE_HEADS, HEAD_SIZE))
+    slots = jnp.stack([dkey_win, dvalue_win]).reshape(
+        2, KEY_VALUE_HEADS, behind + 1, row_count, HEAD_SIZE
+    )
+    remote = slots[:, :, :behind].astype(jnp.bfloat16)
+    owned = jnp.concatenate(
+        [remote[0].astype(jnp.float32), slots[0, :, behind:]], axis=1
+    ).reshape(KEY_VALUE_HEADS, width, HEAD_SIZE)
+    _, key_gain_gradient = key_window_back(owned.transpose(1, 0, 2))
     query_raw_gradient, query_gain_gradient = query_back(dquery_rot)
-    carry_near = remote[behind - half]
+    carry_near = remote[:, :, behind - half]
     for offset in range(half - 1, 0, -1):
         got = shift(carry_near, -1, False).astype(jnp.float32)
-        carry_near = (got + remote_f32[behind - offset]).astype(jnp.bfloat16)
-    carry_far = remote[behind - half - 1]
+        carry_near = (got + slots[:, :, behind - offset]).astype(jnp.bfloat16)
+    carry_far = remote[:, :, behind - half - 1]
     for offset in range(half + 2, behind + 1):
         got = shift(carry_far, 1, True).astype(jnp.float32)
-        carry_far = (got + remote_f32[behind - offset]).astype(jnp.bfloat16)
+        carry_far = (got + slots[:, :, behind - offset]).astype(jnp.bfloat16)
     sent = [shift(carry_near, -1, False), shift(carry_far, -behind, True)]
     gains = (query_gain_gradient, key_gain_gradient)
     for axis in ("y", "x", "zh", "zl", "c"):
         gains = lax.psum(gains, axis)
     gain_query, gain_key = gains
-    key_full_length = dkey_win[behind]
-    value_total = dvalue_win[behind]
+    total = slots[:, :, behind]
     for moved in sent:
-        moved = moved.astype(jnp.float32)
-        key_full_length = key_full_length + moved[:, :key_span_width]
-        value_total = value_total + moved[:, key_span_width:]
+        total = total + moved.astype(jnp.float32)
+    key_full_length = total[0].transpose(1, 0, 2).reshape(row_count, key_span_width)
+    value_total = total[1].transpose(1, 0, 2).reshape(row_count, key_span_width)
     _, key_backward = jax.vjp(
         prepare_function,
         key_projection[0].astype(jnp.float32).reshape(row_count, KEY_VALUE_HEADS, HEAD_SIZE),

time: 427 us -> 391 us (0.916)
  local copies, waits for them, and re-layouts: 60.8 us -> 37 us
  blocking collectives: 145 us -> 122 us
  other arithmetic: 62.7 us -> 50.9 us
  starting transfers between devices: 51.5 us -> 60.5 us
  matrix products: 22.4 us -> 28 us
  waiting for transfers between devices: 78 us -> 83.1 us
    psum x5, blocking collectives: 145 us -> 122 us  [shards(): gains = lax.psum(gains, axis)]
    slice x9 -> x1, local copies, waits for them, and re-layouts: 13.8 us -> 0.03 us  [shards(): slots[0, :, behind:]]
    unnamed x105 -> x103, local copies, waits for them, and re-layouts: 29.1 us -> 18.7 us
    ppermute x16, starting transfers between devices: 51.5 us -> 60.5 us  [shift(): return lax.ppermute(value, SEQ_AXES, pairs)]
    convert_element_type x9 -> x4, other arithmetic: 16.2 us -> 7.58 us  [the longest x3 7.3 us: shards(): carry_near = (got + slots[:, :, behind - offset]).astype(jnp.bfloat16)]
    ppermute x16, waiting for transfers between devices: 78 us -> 83.1 us  [shift(): return lax.ppermute(value, SEQ_AXES, pairs)]
  transfers between devices with their start and end apart: 16 -> 16, of which waited for: 8 -> 8; matrix products, arithmetic and copies ran while one was open for 13% -> 10% of each run, Pallas kernels for 0% -> 0%
where the time goes in v5:
time: 391 us; the launch traced here: 383 us
  blocking collectives  122 us (31%)
  waiting for transfers between devices  83.1 us (21%)
  starting transfers between devices  60.5 us (15%)
  other arithmetic  50.9 us (13%)
  local copies, waits for them, and re-layouts  37 us (9%)
  matrix products  28 us (7%)
    psum x5, blocking collectives, shards(): gains = lax.psum(gains, axis)  122 us
    ppermute x16, waiting for transfers between devices, shift(): return lax.ppermute(value, SEQ_AXES, pairs)  83.1 us
    ppermute x16, starting transfers between devices, shift(): return lax.ppermute(value, SEQ_AXES, pairs)  60.5 us
    unnamed x103, local copies, waits for them, and re-layouts  18.7 us
    dot_general x1, matrix products, attend(): jnp.einsum('grtw,tgrd->gwd', weights_b, gradient_block, preferred_element...  7.99 us
  transfers between devices with their start and end apart: 16, of which 8 were waited for; matrix products, arithmetic and copies ran while one was open for 10% of the time, Pallas kernels for 0%

profile of v5, /device:TPU:1, one launch (start us, length us, event | category | flops | bytes accessed | tf_op | source)
XLA Modules:
  0.0 383.0 jit_solution(12597133114225669374)
XLA Ops:
  2.4 4.1 %collective-permute-start.4 = (bf16[144,2048]{1,0:T(8,128)(2,1)S(1)}, bf16[144,2048]{1,0:T(8,128)(2,1)S(1)}, u32[]{:S(2)}, u32[]{:S(2)}) collective-permute-start(bf16[144,2048]{1,0:T(8,128)(2,1)S(1)} %fusion.29), channel_id=1, source_target_pairs={{0,4},{4,8},{8,12},{12,16},{16,20},{20,24},{24,28},{28,32},{32,36}... | collective-permute-start | bytes 1769480 | tf_op jit(solution)/shard_map/ppermute | solution.py:27
  6.5 3.1 collective-permute-start
  11.1 2.2 reshape_squeeze.4
  19.2 24.3 %collective-permute-done = bf16[144,2048]{1,0:T(8,128)(2,1)} collective-permute-done((bf16[144,2048]{1,0:T(8,128)(2,1)S(1)}, bf16[144,2048]{1,0:T(8,128)(2,1)}, u32[]{:S(2)}, u32[]{:S(2)}) %collective-permute-start) | collective-permute-done | bytes 589856 | tf_op jit(solution)/shard_map/ppermute | solution.py:27
  43.5 1.9 collective-permute-start.1
  46.1 3.4 collective-permute-start.5
  49.5 2.1 multiply_cosine_fusion
  51.6 8.6 %collective-permute-done.1 = bf16[144,2048]{1,0:T(8,128)(2,1)S(1)} collective-permute-done((bf16[144,2048]{1,0:T(8,128)(2,1)}, bf16[144,2048]{1,0:T(8,128)(2,1)S(1)}, u32[]{:S(2)}, u32[]{:S(2)}) %collective-permute-start.1) | collective-permute-done | bytes 589856 | tf_op jit(solution)/shard_map/ppermute | solution.py:27
  60.2 12.2 %collective-permute-start.2 = (bf16[144,2048]{1,0:T(8,128)(2,1)S(1)}, bf16[144,2048]{1,0:T(8,128)(2,1)S(1)}, u32[]{:S(2)}, u32[]{:S(2)}) collective-permute-start(bf16[144,2048]{1,0:T(8,128)(2,1)S(1)} %collective-permute-done.1), channel_id=1, source_target_pairs={{0,508},{4,0},{8,4},{12,8},{16,12},{20,16},{24,20},{28,24},{32,28}... | collective-permute-start | bytes 1769480 | tf_op jit(solution)/shard_map/ppermute | solution.py:27
  75.6 7.5 %collective-permute-done.2 = bf16[144,2048]{1,0:T(8,128)(2,1)S(1)} collective-permute-done((bf16[144,2048]{1,0:T(8,128)(2,1)S(1)}, bf16[144,2048]{1,0:T(8,128)(2,1)S(1)}, u32[]{:S(2)}, u32[]{:S(2)}) %collective-permute-start.2) | collective-permute-done | bytes 589856 | tf_op jit(solution)/shard_map/ppermute | solution.py:27
  83.1 13.7 %collective-permute-start.3 = (bf16[144,2048]{1,0:T(8,128)(2,1)S(1)}, bf16[144,2048]{1,0:T(8,128)(2,1)S(1)}, u32[]{:S(2)}, u32[]{:S(2)}) collective-permute-start(bf16[144,2048]{1,0:T(8,128)(2,1)S(1)} %collective-permute-done.2), channel_id=1, source_target_pairs={{0,508},{4,0},{8,4},{12,8},{16,12},{20,16},{24,20},{28,24},{32,28}... | collective-permute-start | bytes 1769480 | tf_op jit(solution)/shard_map/ppermute | solution.py:27
  98.3 8.6 %collective-permute-done.3 = bf16[144,2048]{1,0:T(8,128)(2,1)S(1)} collective-permute-done((bf16[144,2048]{1,0:T(8,128)(2,1)S(1)}, bf16[144,2048]{1,0:T(8,128)(2,1)S(1)}, u32[]{:S(2)}, u32[]{:S(2)}) %collective-permute-start.3) | collective-permute-done | bytes 589856 | tf_op jit(solution)/shard_map/ppermute | solution.py:27
  108.6 3.3 copy.141
  112.7 3.2 copy.119
  115.9 3.7 multiply_reduce_fusion.1
  119.8 4.1 %fusion.4 = f32[1152,8,128]{2,0,1:T(8,128)S(1)} fusion(f32[1152,8,128]{2,1,0:T(8,128)} %bitcast.163, f32[128]{0:T(128)S(1)} %copy-done.33, f32[1152,8]{0,1:T(8,128)S(1)} %add_rsqrt_fusion), kind=kLoop, calls=%fused_computation.17 | loop fusion | flops 2359296 | bytes 9474560 | tf_op jit(solution)/shard_map/jvp()/mul | solution.py:45
  124.1 1.8 subtract_convert_fusion
  127.0 3.3 fusion.3
  130.4 3.6 copy-done.39
  134.0 3.4 fusion.10
  137.4 1.8 copy.126
  139.2 8.0 %fusion.5 = f32[8,1152,128,1]{2,1,3,0:T(8,128)} fusion(bf16[128,8,2,128]{3,2,1,0:T(2,128)(2,1)} %reshape_squeeze.4, f32[8,1152,128,2]{2,1,3,0:T(8,128)} %copy-done.39, f32[8,2,128]{2,1,0:T(2,128)} %copy-done.40, pred[128,1152]{0,1:T(8,128)(4,1)S(1)} %fusion.32), kind=kOutput, calls=%fused_computation.20 | convolution fusion | flops 613416960 | bytes 14835712 | tf_op jit(solution)/shard_map/grtw,tgrd->gwd/dot_general | solution.py:71
  147.2 2.0 multiply_reduce_fusion.2
  150.4 6.5 %fusion.1 = bf16[8,2,128,1152]{2,3,1,0:T(8,128)(2,1)S(1)} fusion(bf16[1152,8,128,1]{0,2,3,1:T(8,128)(2,1)S(1)} %copy-done.12, f32[8,2,128]{2,1,0:T(2,128)S(1)} %copy.127, bf16[128,8,2,128]{3,2,1,0:T(2,128)(2,1)} %reshape_squeeze.4, f32[8,2,128]{2,1,0:T(2,128)} %copy-done.40, f32[8,1152,128,2]{2,1,3,0:T(8,128)} %copy-done.39, pred[128,1152]{0,1:T(8,128)(4,1)S(1)} %fusion.32), kind=kOutput, calls=%fused_computation.2 | convolution fusion | flops 618135552 | bytes 17203200 | tf_op jit(solution)/shard_map/tgrd,wgd->grtw/dot_general | solution.py:61
  159.1 2.7 copy_dynamic-update-slice_fusion.1
  161.9 2.7 copy_dynamic-update-slice_fusion
  165.6 1.5 slice_bitcast_fusion.10
  170.3 4.2 %collective-permute-start.12 = (bf16[2,8,128,128]{3,1,2,0:T(8,128)(2,1)}, bf16[2,8,128,128]{3,1,2,0:T(8,128)(2,1)}, u32[]{:S(2)}, u32[]{:S(2)}) collective-permute-start(bf16[2,8,128,128]{3,1,2,0:T(8,128)(2,1)} %get-tuple-element.44), channel_id=1, source_target_pairs={{0,4},{4,8},{8,12},{12,16},{16,20},{20,24},{24,28},{28,32},{32,36}... | collective-permute-start | bytes 1572872 | tf_op jit(solution)/shard_map/ppermute | solution.py:27
  174.5 6.3 %multiply_add_fusion.1 = (f32[1152,8,64]{2,0,1:T(8,128)}, f32[1152,8,64]{2,0,1:T(8,128)}) fusion(f32[1152,8,128]{2,0,1:T(8,128)S(1)} %bitcast.165, f32[1152,64]{1,0:T(8,128)} %copy-done.8, f32[1152,64]{1,0:T(8,128)} %copy-done.7), kind=kLoop, calls=%fused_computation.13 | loop fusion | flops 4128768 | bytes 10027008 | tf_op jit(solution)/shard_map/transpose(jvp())/add_any | solution.py:39
  180.7 9.5 %collective-permute-done.12 = bf16[2,8,128,128]{3,1,2,0:T(8,128)(2,1)} collective-permute-done((bf16[2,8,128,128]{3,1,2,0:T(8,128)(2,1)}, bf16[2,8,128,128]{3,1,2,0:T(8,128)(2,1)}, u32[]{:S(2)}, u32[]{:S(2)}) %collective-permute-start.12) | collective-permute-done | bytes 524320 | tf_op jit(solution)/shard_map/ppermute | solution.py:27
  193.0 4.0 %collective-permute-start.13 = (bf16[2,8,128,128]{3,1,2,0:T(8,128)(2,1)S(1)}, bf16[2,8,128,128]{3,1,2,0:T(8,128)(2,1)}, u32[]{:S(2)}, u32[]{:S(2)}) collective-permute-start(bf16[2,8,128,128]{3,1,2,0:T(8,128)(2,1)S(1)} %get-tuple-element.36), channel_id=1, source_target_pairs={{0,4},{4,8},{8,12},{12,16},{16,20},{20,24},{24,28},{28,32},{32,36}... | collective-permute-start | bytes 1572872 | tf_op jit(solution)/shard_map/ppermute | solution.py:27
  197.0 5.3 %convolution_multiply_fusion = f32[8,128,2,128]{3,1,2,0:T(8,128)S(1)} fusion(bf16[8,2,128,1152]{2,3,1,0:T(8,128)(2,1)} %copy-done.3, bf16[1152,8,64]{2,0,1:T(8,128)(2,1)} %copy-done.6, bf16[1152,8,64]{2,0,1:T(8,128)(2,1)S(1)} %copy-done.5), kind=kOutput, calls=%fused_computation.28 | convolution fusion | flops 608960512 | bytes 8126464 | tf_op jit(solution)/shard_map/grtw,wgd->tgrd/dot_general | solution.py:65
  205.2 11.1 %collective-permute-done.13 = bf16[2,8,128,128]{3,1,2,0:T(8,128)(2,1)} collective-permute-done((bf16[2,8,128,128]{3,1,2,0:T(8,128)(2,1)S(1)}, bf16[2,8,128,128]{3,1,2,0:T(8,128)(2,1)}, u32[]{:S(2)}, u32[]{:S(2)}) %collective-permute-start.13) | collective-permute-done | bytes 524320 | tf_op jit(solution)/shard_map/ppermute | solution.py:27
  216.3 2.9 fusion.24
  220.6 4.0 %collective-permute-start.14 = (bf16[2,8,128,128]{3,1,2,0:T(8,128)(2,1)}, bf16[2,8,128,128]{3,1,2,0:T(8,128)(2,1)}, u32[]{:S(2)}, u32[]{:S(2)}) collective-permute-start(bf16[2,8,128,128]{3,1,2,0:T(8,128)(2,1)} %get-tuple-element.34), channel_id=1, source_target_pairs={{0,4},{4,8},{8,12},{12,16},{16,20},{20,24},{24,28},{28,32},{32,36}... | collective-permute-start | bytes 1572872 | tf_op jit(solution)/shard_map/ppermute | solution.py:27
  226.1 3.5 collective-permute-done.10
  229.5 10.0 %collective-permute-done.14 = bf16[2,8,128,128]{3,1,2,0:T(8,128)(2,1)} collective-permute-done((bf16[2,8,128,128]{3,1,2,0:T(8,128)(2,1)}, bf16[2,8,128,128]{3,1,2,0:T(8,128)(2,1)}, u32[]{:S(2)}, u32[]{:S(2)}) %collective-permute-start.14) | collective-permute-done | bytes 524320 | tf_op jit(solution)/shard_map/ppermute | solution.py:27
  239.5 3.0 fusion.22
  243.8 1.9 collective-permute-start.15
  245.8 1.8 fusion.14
  247.5 2.1 reshape.269
  249.6 6.5 %multiply_reduce_fusion = f32[128]{0:T(128)S(1)} fusion(f32[1152,8,64]{2,0,1:T(8,128)} %get-tuple-element.38, f32[1152,8,64]{2,0,1:T(8,128)} %get-tuple-element.37, f32[1152,8,128]{2,1,0:T(8,128)} %bitcast.164, f32[1152,8]{0,1:T(8,128)S(1)} %copy-done.27), kind=kLoop, calls=%fused_computation.11 | loop fusion | flops 4718464 | bytes 9474560 | tf_op jit(solution)/shard_map/transpose(jvp())/reduce_sum | solution.py:45
  256.1 12.9 %all-reduce.7 = (f32[128]{0:T(128)S(1)}, f32[128]{0:T(128)S(1)}) all-reduce(f32[128]{0:T(128)S(1)} %get-tuple-element.17, f32[128]{0:T(128)S(1)} %multiply_reduce_fusion), channel_id=1, replica_groups=mesh['zh'=4,'x'=4,'y'=8,'zl'=2,'c'=2] {'y'}, use_global_device_ids=true, to_apply=%region_7.8 | all-reduce | flops 256 | bytes 2048 | tf_op jit(solution)/shard_map/psum | solution.py:159
  269.0 39.6 %all-reduce.8 = (f32[128]{0:T(128)S(1)}, f32[128]{0:T(128)S(1)}) all-reduce(f32[128]{0:T(128)S(1)} %get-tuple-element.21, f32[128]{0:T(128)S(1)} %get-tuple-element.22), channel_id=1, replica_groups=mesh['zh'=4,'x'=4,'y'=8,'zl'=2,'c'=2] {'x'}, use_global_device_ids=true, to_apply=%region_8.9 | all-reduce | flops 256 | bytes 2048 | tf_op jit(solution)/shard_map/psum | solution.py:159
  308.5 42.1 %all-reduce.9 = (f32[128]{0:T(128)S(1)}, f32[128]{0:T(128)S(1)}) all-reduce(f32[128]{0:T(128)S(1)} %get-tuple-element.23, f32[128]{0:T(128)S(1)} %get-tuple-element.24), channel_id=1, replica_groups=mesh['zh'=4,'x'=4,'y'=8,'zl'=2,'c'=2] {'zh'}, use_global_device_ids=true, to_apply=%region_9.10 | all-reduce | flops 256 | bytes 2048 | tf_op jit(solution)/shard_map/psum | solution.py:159
  350.6 3.8 all-reduce.11
  354.4 23.4 %all-reduce.10 = (f32[128]{0:T(128)}, f32[128]{0:T(128)}) all-reduce(f32[128]{0:T(128)S(1)} %get-tuple-element.29, f32[128]{0:T(128)S(1)} %get-tuple-element.30), channel_id=1, replica_groups=mesh['zh'=4,'x'=4,'y'=8,'zl'=2,'c'=2] {'c'}, use_global_device_ids=true, to_apply=%region_11.12 | all-reduce | flops 256 | bytes 2048 | tf_op jit(solution)/shard_map/psum | solution.py:159
  377.8 1.7 fusion.28
  (163 shorter events, 38.5 us)
Async XLA Ops:
  0.6 15.5 %copy-start.35 = (f32[128]{0:T(128)S(1)}, f32[128]{0:T(128)}, u32[]{:S(2)}) copy-start(f32[128]{0:T(128)} %param.14) | copy-start | bytes 1540
  2.4 43.7 %collective-permute-start.4 = (bf16[144,2048]{1,0:T(8,128)(2,1)S(1)}, bf16[144,2048]{1,0:T(8,128)(2,1)S(1)}, u32[]{:S(2)}, u32[]{:S(2)}) collective-permute-start(bf16[144,2048]{1,0:T(8,128)(2,1)S(1)} %fusion.29), channel_id=1, source_target_pairs={{0,4},{4,8},{8,12},{12,16},{16,20},{20,24},{24,28},{28,32},{32,36}... | collective-permute-start | bytes 1769480 | tf_op jit(solution)/shard_map/ppermute | solution.py:27
  6.5 37.1 %collective-permute-start = (bf16[144,2048]{1,0:T(8,128)(2,1)S(1)}, bf16[144,2048]{1,0:T(8,128)(2,1)}, u32[]{:S(2)}, u32[]{:S(2)}) collective-permute-start(bf16[144,2048]{1,0:T(8,128)(2,1)S(1)} %fusion.29), channel_id=1, source_target_pairs={{0,32},{4,36},{8,40},{12,44},{16,48},{20,52},{24,56},{28,60},{32,6... | collective-permute-start | bytes 1769480 | tf_op jit(solution)/shard_map/ppermute | solution.py:27
  15.5 36.0 %copy-start.1 = (f32[16,8,16,128]{3,2,1,0:T(8,128)}, f32[16,8,16,128]{3,2,1,0:T(8,128)S(1)}, u32[]{:S(2)}) copy-start(f32[16,8,16,128]{3,2,1,0:T(8,128)S(1)} %copy.142) | copy-start | bytes 3145732
  15.9 56.5 %copy-start.28 = (f32[128,16]{0,1:T(8,128)}, f32[128,16]{0,1:T(8,128)S(1)}, u32[]{:S(2)}) copy-start(f32[128,16]{0,1:T(8,128)S(1)} %copy.94) | copy-start | bytes 24580
  16.1 59.5 %copy-start.19 = (f32[128,16]{1,0:T(8,128)}, f32[128,16]{1,0:T(8,128)S(1)}, u32[]{:S(2)}) copy-start(f32[128,16]{1,0:T(8,128)S(1)} %copy.95) | copy-start | bytes 24580
  16.8 81.5 %copy-start.21 = (f32[128,64]{1,0:T(8,128)}, f32[128,64]{1,0:T(8,128)S(1)}, u32[]{:S(2)}) copy-start(f32[128,64]{1,0:T(8,128)S(1)} %get-tuple-element.57) | copy-start | bytes 98308
  16.8 81.5 %copy-start.23 = (f32[128,64]{1,0:T(8,128)}, f32[128,64]{1,0:T(8,128)S(1)}, u32[]{:S(2)}) copy-start(f32[128,64]{1,0:T(8,128)S(1)} %get-tuple-element.58) | copy-start | bytes 98308
  43.5 16.7 %collective-permute-start.1 = (bf16[144,2048]{1,0:T(8,128)(2,1)}, bf16[144,2048]{1,0:T(8,128)(2,1)S(1)}, u32[]{:S(2)}, u32[]{:S(2)}) collective-permute-start(bf16[144,2048]{1,0:T(8,128)(2,1)} %collective-permute-done), channel_id=1, source_target_pairs={{0,508},{4,0},{8,4},{12,8},{16,12},{20,16},{24,20},{28,24},{32,28}... | collective-permute-start | bytes 1769480 | tf_op jit(solution)/shard_map/ppermute | solution.py:27
  46.1 27.0 %collective-permute-start.5 = (bf16[144,2048]{1,0:T(8,128)(2,1)S(1)}, bf16[144,2048]{1,0:T(8,128)(2,1)S(1)}, u32[]{:S(2)}, u32[]{:S(2)}) collective-permute-start(bf16[144,2048]{1,0:T(8,128)(2,1)S(1)} %collective-permute-done.4), channel_id=1, source_target_pairs={{0,4},{4,8},{8,12},{12,16},{16,20},{20,24},{24,28},{28,32},{32,36}... | collective-permute-start | bytes 1769480 | tf_op jit(solution)/shard_map/ppermute | solution.py:27
  51.6 72.4 %copy-start.7 = (f32[1152,64]{1,0:T(8,128)}, f32[1152,64]{1,0:T(8,128)S(1)}, u32[]{:S(2)}) copy-start(f32[1152,64]{1,0:T(8,128)S(1)} %get-tuple-element.53) | copy-start | bytes 884740
  51.6 72.4 %copy-start.8 = (f32[1152,64]{1,0:T(8,128)}, f32[1152,64]{1,0:T(8,128)S(1)}, u32[]{:S(2)}) copy-start(f32[1152,64]{1,0:T(8,128)S(1)} %get-tuple-element.54) | copy-start | bytes 884740
  60.2 22.9 %collective-permute-start.2 = (bf16[144,2048]{1,0:T(8,128)(2,1)S(1)}, bf16[144,2048]{1,0:T(8,128)(2,1)S(1)}, u32[]{:S(2)}, u32[]{:S(2)}) collective-permute-start(bf16[144,2048]{1,0:T(8,128)(2,1)S(1)} %collective-permute-done.1), channel_id=1, source_target_pairs={{0,508},{4,0},{8,4},{12,8},{16,12},{20,16},{24,20},{28,24},{32,28}... | collective-permute-start | bytes 1769480 | tf_op jit(solution)/shard_map/ppermute | solution.py:27
  73.1 34.0 %copy-start.13 = (bf16[1,128,1024]{2,1,0:T(8,128)(2,1)S(1)}, bf16[1,128,1024]{2,1,0:T(8,128)(2,1)}, u32[]{:S(2)}) copy-start(bf16[1,128,1024]{2,1,0:T(8,128)(2,1)} %param.10) | copy-start | bytes 786436
  73.1 34.0 %copy-start.25 = (bf16[1,128,1024]{2,1,0:T(8,128)(2,1)S(1)}, bf16[1,128,1024]{2,1,0:T(8,128)(2,1)}, u32[]{:S(2)}) copy-start(bf16[1,128,1024]{2,1,0:T(8,128)(2,1)} %param.11) | copy-start | bytes 786436
  73.1 23.8 %collective-permute-start.6 = (bf16[144,2048]{1,0:T(8,128)(2,1)S(1)}, bf16[144,2048]{1,0:T(8,128)(2,1)S(1)}, u32[]{:S(2)}, u32[]{:S(2)}) collective-permute-start(bf16[144,2048]{1,0:T(8,128)(2,1)S(1)} %collective-permute-done.5), channel_id=1, source_target_pairs={{0,4},{4,8},{8,12},{12,16},{16,20},{20,24},{24,28},{28,32},{32,36}... | collective-permute-start | bytes 1769480 | tf_op jit(solution)/shard_map/ppermute | solution.py:27
  83.1 23.7 %collective-permute-start.3 = (bf16[144,2048]{1,0:T(8,128)(2,1)S(1)}, bf16[144,2048]{1,0:T(8,128)(2,1)S(1)}, u32[]{:S(2)}, u32[]{:S(2)}) collective-permute-start(bf16[144,2048]{1,0:T(8,128)(2,1)S(1)} %collective-permute-done.2), channel_id=1, source_target_pairs={{0,508},{4,0},{8,4},{12,8},{16,12},{20,16},{24,20},{28,24},{32,28}... | collective-permute-start | bytes 1769480 | tf_op jit(solution)/shard_map/ppermute | solution.py:27
  96.9 10.0 %collective-permute-start.7 = (bf16[144,2048]{1,0:T(8,128)(2,1)S(1)}, bf16[144,2048]{1,0:T(8,128)(2,1)S(1)}, u32[]{:S(2)}, u32[]{:S(2)}) collective-permute-start(bf16[144,2048]{1,0:T(8,128)(2,1)S(1)} %collective-permute-done.6), channel_id=1, source_target_pairs={{0,4},{4,8},{8,12},{12,16},{16,20},{20,24},{24,28},{28,32},{32,36}... | collective-permute-start | bytes 1769480 | tf_op jit(solution)/shard_map/ppermute | solution.py:27
  112.6 7.2 %copy-start.33 = (f32[128]{0:T(128)S(1)}, f32[128]{0:T(128)}, u32[]{:S(2)}) copy-start(f32[128]{0:T(128)} %param.15) | copy-start | bytes 1540
  119.8 4.2 %copy-start.26 = (f32[1152,8]{0,1:T(8,128)}, f32[1152,8]{0,1:T(8,128)S(1)}, u32[]{:S(2)}) copy-start(f32[1152,8]{0,1:T(8,128)S(1)} %add_rsqrt_fusion) | copy-start | bytes 110596
  125.9 4.5 %copy-start.4 = (bf16[1152,8,64]{2,0,1:T(8,128)(2,1)}, bf16[1152,8,64]{2,0,1:T(8,128)(2,1)S(1)}, u32[]{:S(2)}) copy-start(bf16[1152,8,64]{2,0,1:T(8,128)(2,1)S(1)} %get-tuple-element.39) | copy-start | bytes 3538948
  125.9 4.5 %copy-start.6 = (bf16[1152,8,64]{2,0,1:T(8,128)(2,1)}, bf16[1152,8,64]{2,0,1:T(8,128)(2,1)S(1)}, u32[]{:S(2)}) copy-start(bf16[1152,8,64]{2,0,1:T(8,128)(2,1)S(1)} %get-tuple-element.40) | copy-start | bytes 3538948
  127.0 7.0 %copy-start.12 = (bf16[1152,8,128,1]{0,2,3,1:T(8,128)(2,1)S(1)}, bf16[1152,8,128,1]{0,2,3,1:T(8,128)(2,1)}, u32[]{:S(2)}) copy-start(bf16[1152,8,128,1]{0,2,3,1:T(8,128)(2,1)} %copy.119) | copy-start | bytes 7077892
  130.4 3.6 copy-start.40
  139.2 8.0 %copy-start.14 = (bf16[128,8,2,128]{3,2,1,0:T(2,128)(2,1)S(1)}, bf16[128,8,2,128]{3,2,1,0:T(2,128)(2,1)}, u32[]{:S(2)}) copy-start(bf16[128,8,2,128]{3,2,1,0:T(2,128)(2,1)} %reshape_squeeze.4) | copy-start | bytes 1572868
  150.4 6.6 %copy-start.16 = (bf16[128,16,64]{2,0,1:T(8,128)(2,1)S(1)}, bf16[128,16,64]{2,0,1:T(8,128)(2,1)}, u32[]{:S(2)}) copy-start(bf16[128,16,64]{2,0,1:T(8,128)(2,1)} %copy.96) | copy-start | bytes 786436
  150.4 6.6 %copy-start.18 = (bf16[128,16,64]{2,0,1:T(8,128)(2,1)S(1)}, bf16[128,16,64]{2,0,1:T(8,128)(2,1)}, u32[]{:S(2)}) copy-start(bf16[128,16,64]{2,0,1:T(8,128)(2,1)} %copy.97) | copy-start | bytes 786436
  164.7 25.6 %copy-start = (f32[2,8,9,128,128]{4,1,3,0,2:T(8,128)}, f32[2,8,9,128,128]{4,1,3,0,2:T(8,128)S(1)}, u32[]{:S(2)}) copy-start(f32[2,8,9,128,128]{4,1,3,0,2:T(8,128)S(1)} %copy_dynamic-update-slice_fusion) | copy-start | bytes 28311556
  169.0 11.8 %collective-permute-start.8 = (bf16[2,8,128,128]{3,1,2,0:T(8,128)(2,1)}, bf16[2,8,128,128]{3,1,2,0:T(8,128)(2,1)}, u32[]{:S(2)}, u32[]{:S(2)}) collective-permute-start(bf16[2,8,128,128]{3,1,2,0:T(8,128)(2,1)} %get-tuple-element.43), channel_id=1, source_target_pairs={{4,0},{8,4},{12,8},{16,12},{20,16},{24,20},{28,24},{32,28},{36,32}... | collective-permute-start | bytes 1572872 | tf_op jit(solution)/shard_map/ppermute | solution.py:27
  170.3 20.0 %collective-permute-start.12 = (bf16[2,8,128,128]{3,1,2,0:T(8,128)(2,1)}, bf16[2,8,128,128]{3,1,2,0:T(8,128)(2,1)}, u32[]{:S(2)}, u32[]{:S(2)}) collective-permute-start(bf16[2,8,128,128]{3,1,2,0:T(8,128)(2,1)} %get-tuple-element.44), channel_id=1, source_target_pairs={{0,4},{4,8},{8,12},{12,16},{16,20},{20,24},{24,28},{28,32},{32,36}... | collective-permute-start | bytes 1572872 | tf_op jit(solution)/shard_map/ppermute | solution.py:27
  180.7 16.2 %copy-start.5 = (bf16[1152,8,64]{2,0,1:T(8,128)(2,1)S(1)}, bf16[1152,8,64]{2,0,1:T(8,128)(2,1)}, u32[]{:S(2)}) copy-start(bf16[1152,8,64]{2,0,1:T(8,128)(2,1)} %copy-done.4) | copy-start | bytes 3538948
  191.7 13.6 %collective-permute-start.9 = (bf16[2,8,128,128]{3,1,2,0:T(8,128)(2,1)S(1)}, bf16[2,8,128,128]{3,1,2,0:T(8,128)(2,1)S(1)}, u32[]{:S(2)}, u32[]{:S(2)}) collective-permute-start(bf16[2,8,128,128]{3,1,2,0:T(8,128)(2,1)S(1)} %get-tuple-element.35), channel_id=1, source_target_pairs={{4,0},{8,4},{12,8},{16,12},{20,16},{24,20},{28,24},{32,28},{36,32}... | collective-permute-start | bytes 1572872 | tf_op jit(solution)/shard_map/ppermute | solution.py:27
  193.0 23.4 %collective-permute-start.13 = (bf16[2,8,128,128]{3,1,2,0:T(8,128)(2,1)S(1)}, bf16[2,8,128,128]{3,1,2,0:T(8,128)(2,1)}, u32[]{:S(2)}, u32[]{:S(2)}) collective-permute-start(bf16[2,8,128,128]{3,1,2,0:T(8,128)(2,1)S(1)} %get-tuple-element.36), channel_id=1, source_target_pairs={{0,4},{4,8},{8,12},{12,16},{16,20},{20,24},{24,28},{28,32},{32,36}... | collective-permute-start | bytes 1572872 | tf_op jit(solution)/shard_map/ppermute | solution.py:27
  202.3 22.3 %copy-start.22 = (f32[128,64]{1,0:T(8,128)S(1)}, f32[128,64]{1,0:T(8,128)}, u32[]{:S(2)}) copy-start(f32[128,64]{1,0:T(8,128)} %copy-done.21) | copy-start | bytes 98308
  202.3 22.3 %copy-start.24 = (f32[128,64]{1,0:T(8,128)S(1)}, f32[128,64]{1,0:T(8,128)}, u32[]{:S(2)}) copy-start(f32[128,64]{1,0:T(8,128)} %copy-done.23) | copy-start | bytes 98308
  203.8 21.1 %copy-start.2 = (f32[16,8,16,128]{3,2,1,0:T(8,128)S(1)}, f32[16,8,16,128]{3,2,1,0:T(8,128)}, u32[]{:S(2)}) copy-start(f32[16,8,16,128]{3,2,1,0:T(8,128)} %copy-done.1) | copy-start | bytes 3145732
  203.8 21.1 %copy-start.20 = (f32[128,16]{1,0:T(8,128)S(1)}, f32[128,16]{1,0:T(8,128)}, u32[]{:S(2)}) copy-start(f32[128,16]{1,0:T(8,128)} %copy-done.19) | copy-start | bytes 24580
  203.8 21.1 %copy-start.36 = (f32[128]{0:T(128)S(1)}, f32[128]{0:T(128)}, u32[]{:S(2)}) copy-start(f32[128]{0:T(128)} %param.14) | copy-start | bytes 1540
  205.2 19.4 %copy-start.10 = (f32[128,16,64]{2,1,0:T(8,128)S(1)}, f32[128,16,64]{2,1,0:T(8,128)}, u32[]{:S(2)}) copy-start(f32[128,16,64]{2,1,0:T(8,128)} %copy.138) | copy-start | bytes 1572868
  205.2 19.4 %copy-start.11 = (f32[128,16,64]{2,1,0:T(8,128)S(1)}, f32[128,16,64]{2,1,0:T(8,128)}, u32[]{:S(2)}) copy-start(f32[128,16,64]{2,1,0:T(8,128)} %copy.139) | copy-start | bytes 1572868
  219.2 6.7 %copy-start.29 = (f32[128,16]{0,1:T(8,128)S(1)}, f32[128,16]{0,1:T(8,128)}, u32[]{:S(2)}) copy-start(f32[128,16]{0,1:T(8,128)} %copy-done.28) | copy-start | bytes 24580
  219.2 10.4 %collective-permute-start.10 = (bf16[2,8,128,128]{3,1,2,0:T(8,128)(2,1)}, bf16[2,8,128,128]{3,1,2,0:T(8,128)(2,1)}, u32[]{:S(2)}, u32[]{:S(2)}) collective-permute-start(bf16[2,8,128,128]{3,1,2,0:T(8,128)(2,1)} %get-tuple-element.33), channel_id=1, source_target_pairs={{4,0},{8,4},{12,8},{16,12},{20,16},{24,20},{28,24},{32,28},{36,32}... | collective-permute-start | bytes 1572872 | tf_op jit(solution)/shard_map/ppermute | solution.py:27
  220.6 18.9 %collective-permute-start.14 = (bf16[2,8,128,128]{3,1,2,0:T(8,128)(2,1)}, bf16[2,8,128,128]{3,1,2,0:T(8,128)(2,1)}, u32[]{:S(2)}, u32[]{:S(2)}) collective-permute-start(bf16[2,8,128,128]{3,1,2,0:T(8,128)(2,1)} %get-tuple-element.34), channel_id=1, source_target_pairs={{0,4},{4,8},{8,12},{12,16},{16,20},{20,24},{24,28},{28,32},{32,36}... | collective-permute-start | bytes 1572872 | tf_op jit(solution)/shard_map/ppermute | solution.py:27
  225.9 23.7 %copy-start.27 = (f32[1152,8]{0,1:T(8,128)S(1)}, f32[1152,8]{0,1:T(8,128)}, u32[]{:S(2)}) copy-start(f32[1152,8]{0,1:T(8,128)} %copy-done.26) | copy-start | bytes 110596
  242.6 135.2 %collective-permute-start.11 = (bf16[2,8,128,128]{3,1,2,0:T(8,128)(2,1)}, bf16[2,8,128,128]{3,1,2,0:T(8,128)(2,1)}, u32[]{:S(2)}, u32[]{:S(2)}) collective-permute-start(bf16[2,8,128,128]{3,1,2,0:T(8,128)(2,1)} %get-tuple-element.31), channel_id=1, source_target_pairs={{4,0},{8,4},{12,8},{16,12},{20,16},{24,20},{28,24},{32,28},{36,32}... | collective-permute-start | bytes 1572872 | tf_op jit(solution)/shard_map/ppermute | solution.py:27
  243.8 133.9 %collective-permute-start.15 = (bf16[2,8,128,128]{3,1,2,0:T(8,128)(2,1)}, bf16[2,8,128,128]{3,1,2,0:T(8,128)(2,1)}, u32[]{:S(2)}, u32[]{:S(2)}) collective-permute-start(bf16[2,8,128,128]{3,1,2,0:T(8,128)(2,1)} %get-tuple-element.32), channel_id=1, source_target_pairs={{0,480},{4,484},{8,488},{12,492},{16,496},{20,500},{24,504},{28,50... | collective-permute-start | bytes 1572872 | tf_op jit(solution)/shard_map/ppermute | solution.py:27
  256.1 124.5 %copy-start.9 = (f32[16,8,8,128]{3,2,1,0:T(8,128)S(1)}, f32[16,8,8,128]{3,2,1,0:T(8,128)}, u32[]{:S(2)}) copy-start(f32[16,8,8,128]{3,2,1,0:T(8,128)} %copy.144) | copy-start | bytes 1572868
  256.1 124.5 %copy-start.34 = (f32[128]{0:T(128)S(1)}, f32[128]{0:T(128)}, u32[]{:S(2)}) copy-start(f32[128]{0:T(128)} %param.15) | copy-start | bytes 1540
  (11 other events, 26.8 us)

commit v6 on v5

--- a/solution.py
+++ b/solution.py
@@ -153,12 +153,14 @@
     for offset in range(half + 2, behind + 1):
         got = shift(carry_far, 1, True).astype(jnp.float32)
         carry_far = (got + slots[:, :, behind - offset]).astype(jnp.bfloat16)
+    gains, carry_near, carry_far = lax.optimization_barrier(
+        ((query_gain_gradient, key_gain_gradient), carry_near, carry_far)
+    )
     sent = [shift(carry_near, -1, False), shift(carry_far, -behind, True)]
-    gains = (query_gain_gradient, key_gain_gradient)
     for axis in ("y", "x", "zh", "zl", "c"):
         gains = lax.psum(gains, axis)
+    gains, total = lax.optimization_barrier((gains, slots[:, :, behind]))
     gain_query, gain_key = gains
-    total = slots[:, :, behind]
     for moved in sent:
         total = total + moved.astype(jnp.float32)
     key_full_length = total[0].transpose(1, 0, 2).reshape(row_count, key_span_width)

time: 391 us -> 396 us (1.013)
  blocking collectives: 122 us -> 135 us
  starting transfers between devices: 60.5 us -> 54.7 us
    psum x5, blocking collectives: 122 us -> 135 us  [shards(): gains = lax.psum(gains, axis)]
    ppermute x16, starting transfers between devices: 60.5 us -> 54.7 us  [shift(): return lax.ppermute(value, SEQ_AXES, pairs)]
    unnamed x103 -> x97, local copies, waits for them, and re-layouts: 18.7 us -> 21 us
  transfers between devices with their start and end apart: 16 -> 16, of which waited for: 8 -> 7; matrix products, arithmetic and copies ran while one was open for 10% -> 10% of each run, Pallas kernels for 0% -> 0%
where the time goes in v6:
time: 396 us; the launch traced here: 391 us
  blocking collectives  135 us (34%)
  waiting for transfers between devices  80 us (20%)
  starting transfers between devices  54.7 us (14%)
  other arithmetic  52 us (13%)
  local copies, waits for them, and re-layouts  40.1 us (10%)
  matrix products  27.9 us (7%)
    psum x5, blocking collectives, shards(): gains = lax.psum(gains, axis)  135 us
    ppermute x16, waiting for transfers between devices, shift(): return lax.ppermute(value, SEQ_AXES, pairs)  80 us
    ppermute x16, starting transfers between devices, shift(): return lax.ppermute(value, SEQ_AXES, pairs)  54.7 us
    unnamed x97, local copies, waits for them, and re-layouts  21 us
    convert_element_type x3, other arithmetic, shards(): carry_far = (got + slots[:, :, behind - offset]).astype(jnp.bfloat16)  9.15 us
    dot_general x1, matrix products, attend(): jnp.einsum('grtw,tgrd->gwd', weights_b, gradient_block, preferred_element...  8.11 us
  transfers between devices with their start and end apart: 16, of which 7 were waited for; matrix products, arithmetic and copies ran while one was open for 10% of the time, Pallas kernels for 0%

profile of v6, /device:TPU:1, one launch (start us, length us, event | category | flops | bytes accessed | tf_op | source)
XLA Modules:
  0.0 391.0 jit_solution(14561487281252060463)
XLA Ops:
  2.4 4.1 %collective-permute-start.4 = (bf16[144,2048]{1,0:T(8,128)(2,1)S(1)}, bf16[144,2048]{1,0:T(8,128)(2,1)S(1)}, u32[]{:S(2)}, u32[]{:S(2)}) collective-permute-start(bf16[144,2048]{1,0:T(8,128)(2,1)S(1)} %fusion.27), channel_id=1, source_target_pairs={{0,4},{4,8},{8,12},{12,16},{16,20},{20,24},{24,28},{28,32},{32,36}... | collective-permute-start | bytes 1769480 | tf_op jit(solution)/shard_map/ppermute | solution.py:27
  6.5 3.1 collective-permute-start
  11.1 2.2 reshape_squeeze.4
  19.2 24.2 %collective-permute-done = bf16[144,2048]{1,0:T(8,128)(2,1)S(1)} collective-permute-done((bf16[144,2048]{1,0:T(8,128)(2,1)S(1)}, bf16[144,2048]{1,0:T(8,128)(2,1)S(1)}, u32[]{:S(2)}, u32[]{:S(2)}) %collective-permute-start) | collective-permute-done | bytes 589856 | tf_op jit(solution)/shard_map/ppermute | solution.py:27
  43.4 1.9 collective-permute-start.1
  45.4 3.4 collective-permute-start.5
  48.8 3.3 multiply_cosine_fusion
  52.1 7.6 %collective-permute-done.1 = bf16[144,2048]{1,0:T(8,128)(2,1)S(1)} collective-permute-done((bf16[144,2048]{1,0:T(8,128)(2,1)S(1)}, bf16[144,2048]{1,0:T(8,128)(2,1)S(1)}, u32[]{:S(2)}, u32[]{:S(2)}) %collective-permute-start.1) | collective-permute-done | bytes 589856 | tf_op jit(solution)/shard_map/ppermute | solution.py:27
  59.7 12.3 %collective-permute-start.2 = (bf16[144,2048]{1,0:T(8,128)(2,1)S(1)}, bf16[144,2048]{1,0:T(8,128)(2,1)S(1)}, u32[]{:S(2)}, u32[]{:S(2)}) collective-permute-start(bf16[144,2048]{1,0:T(8,128)(2,1)S(1)} %collective-permute-done.1), channel_id=1, source_target_pairs={{0,508},{4,0},{8,4},{12,8},{16,12},{20,16},{24,20},{28,24},{32,28}... | collective-permute-start | bytes 1769480 | tf_op jit(solution)/shard_map/ppermute | solution.py:27
  74.2 8.7 %collective-permute-done.2 = bf16[144,2048]{1,0:T(8,128)(2,1)S(1)} collective-permute-done((bf16[144,2048]{1,0:T(8,128)(2,1)S(1)}, bf16[144,2048]{1,0:T(8,128)(2,1)S(1)}, u32[]{:S(2)}, u32[]{:S(2)}) %collective-permute-start.2) | collective-permute-done | bytes 589856 | tf_op jit(solution)/shard_map/ppermute | solution.py:27
  82.8 13.6 %collective-permute-start.3 = (bf16[144,2048]{1,0:T(8,128)(2,1)S(1)}, bf16[144,2048]{1,0:T(8,128)(2,1)S(1)}, u32[]{:S(2)}, u32[]{:S(2)}) collective-permute-start(bf16[144,2048]{1,0:T(8,128)(2,1)S(1)} %collective-permute-done.2), channel_id=1, source_target_pairs={{0,508},{4,0},{8,4},{12,8},{16,12},{20,16},{24,20},{28,24},{32,28}... | collective-permute-start | bytes 1769480 | tf_op jit(solution)/shard_map/ppermute | solution.py:27
  96.5 1.9 collective-permute-start.7
  98.5 8.0 %collective-permute-done.3 = bf16[144,2048]{1,0:T(8,128)(2,1)S(1)} collective-permute-done((bf16[144,2048]{1,0:T(8,128)(2,1)S(1)}, bf16[144,2048]{1,0:T(8,128)(2,1)S(1)}, u32[]{:S(2)}, u32[]{:S(2)}) %collective-permute-start.3) | collective-permute-done | bytes 589856 | tf_op jit(solution)/shard_map/ppermute | solution.py:27
  108.3 3.4 copy.141
  112.3 2.8 copy.119
  115.2 3.7 multiply_reduce_fusion.1
  119.1 4.2 %fusion.4 = f32[1152,8,128]{2,0,1:T(8,128)S(1)} fusion(f32[1152,8,128]{2,1,0:T(8,128)} %bitcast.159, f32[128]{0:T(128)S(1)} %copy-done.26, f32[1152,8]{0,1:T(8,128)S(1)} %add_rsqrt_fusion), kind=kLoop, calls=%fused_computation.17 | loop fusion | flops 2359296 | bytes 9474560 | tf_op jit(solution)/shard_map/jvp()/mul | solution.py:45
  123.5 1.7 subtract_convert_fusion
  126.3 3.3 fusion.3
  129.6 3.6 copy-done.34
  133.3 3.4 fusion.10
  136.6 2.4 copy.126
  139.1 8.1 %fusion.5 = f32[8,1152,128,1]{2,1,3,0:T(8,128)} fusion(bf16[128,8,2,128]{3,2,1,0:T(2,128)(2,1)} %reshape_squeeze.4, f32[8,1152,128,2]{2,1,3,0:T(8,128)} %copy-done.34, f32[8,2,128]{2,1,0:T(2,128)S(1)} %get-tuple-element.73, pred[128,1152]{0,1:T(8,128)(4,1)} %copy-done.23), kind=kOutput, calls=%fused_computation.20 | convolution fusion | flops 613416960 | bytes 14835712 | tf_op jit(solution)/shard_map/grtw,tgrd->gwd/dot_general | solution.py:71
  147.2 1.9 multiply_reduce_fusion.2
  150.4 7.8 %fusion.1 = bf16[8,2,128,1152]{2,3,1,0:T(8,128)(2,1)S(1)} fusion(bf16[1152,8,128,1]{0,2,3,1:T(8,128)(2,1)} %copy.119, f32[8,2,128]{2,1,0:T(2,128)S(1)} %copy.127, bf16[128,8,2,128]{3,2,1,0:T(2,128)(2,1)} %reshape_squeeze.4, f32[8,2,128]{2,1,0:T(2,128)} %copy-done.35, f32[8,1152,128,2]{2,1,3,0:T(8,128)} %copy-done.34, pred[128,1152]{0,1:T(8,128)(4,1)} %copy-done.23), kind=kOutput, calls=%fused_computation.2 | convolution fusion | flops 618135552 | bytes 17203200 | tf_op jit(solution)/shard_map/tgrd,wgd->grtw/dot_general | solution.py:61
  160.5 2.7 copy_dynamic-update-slice_fusion.1
  163.3 3.0 copy_dynamic-update-slice_fusion
  167.1 2.7 copy-done
  172.8 2.1 collective-permute-start.11
  176.2 5.0 %multiply_add_fusion.1 = (f32[1152,8,64]{2,0,1:T(8,128)}, f32[1152,8,64]{2,0,1:T(8,128)}) fusion(f32[1152,8,128]{2,0,1:T(8,128)S(1)} %bitcast.161, f32[1152,64]{1,0:T(8,128)S(1)} %copy-done.6, f32[1152,64]{1,0:T(8,128)S(1)} %copy-done.4), kind=kLoop, calls=%fused_computation.13 | loop fusion | flops 4128768 | bytes 10027008 | tf_op jit(solution)/shard_map/transpose(jvp())/add_any | solution.py:39
  181.2 3.8 convolution_multiply_fusion
  188.0 4.1 %collective-permute-done.11 = bf16[2,8,128,128]{3,1,2,0:T(8,128)(2,1)} collective-permute-done((bf16[2,8,128,128]{3,1,2,0:T(8,128)(2,1)}, bf16[2,8,128,128]{3,1,2,0:T(8,128)(2,1)}, u32[]{:S(2)}, u32[]{:S(2)}) %collective-permute-start.11) | collective-permute-done | bytes 524320 | tf_op jit(solution)/shard_map/ppermute | solution.py:27
  192.1 3.0 fusion.20
  195.1 1.9 collective-permute-start.12
  199.6 18.7 %collective-permute-done.12 = bf16[2,8,128,128]{3,1,2,0:T(8,128)(2,1)} collective-permute-done((bf16[2,8,128,128]{3,1,2,0:T(8,128)(2,1)}, bf16[2,8,128,128]{3,1,2,0:T(8,128)(2,1)}, u32[]{:S(2)}, u32[]{:S(2)}) %collective-permute-start.12) | collective-permute-done | bytes 524320 | tf_op jit(solution)/shard_map/ppermute | solution.py:27
  218.4 3.0 fusion.18
  221.3 1.9 collective-permute-start.13
  224.7 6.7 %multiply_reduce_fusion = f32[128]{0:T(128)S(1)} fusion(f32[1152,8,64]{2,0,1:T(8,128)} %get-tuple-element.52, f32[1152,8,64]{2,0,1:T(8,128)} %get-tuple-element.51, f32[1152,8,128]{2,1,0:T(8,128)} %bitcast.160, f32[1152,8]{0,1:T(8,128)S(1)} %copy-done.22), kind=kLoop, calls=%fused_computation.11 | loop fusion | flops 4718464 | bytes 9474560 | tf_op jit(solution)/shard_map/transpose(jvp())/reduce_sum | solution.py:45
  231.4 8.5 %collective-permute-done.13 = bf16[2,8,128,128]{3,1,2,0:T(8,128)(2,1)} collective-permute-done((bf16[2,8,128,128]{3,1,2,0:T(8,128)(2,1)}, bf16[2,8,128,128]{3,1,2,0:T(8,128)(2,1)}, u32[]{:S(2)}, u32[]{:S(2)}) %collective-permute-start.13) | collective-permute-done | bytes 524320 | tf_op jit(solution)/shard_map/ppermute | solution.py:27
  240.0 3.2 fusion.16
  244.4 1.9 collective-permute-start.15
  246.3 1.8 fusion.14
  248.1 2.1 reshape.269
  251.5 13.1 %all-reduce.7 = (f32[128]{0:T(128)S(1)}, f32[128]{0:T(128)S(1)}) all-reduce(f32[128]{0:T(128)S(1)} %get-tuple-element.24, f32[128]{0:T(128)S(1)} %multiply_reduce_fusion), channel_id=1, replica_groups=mesh['zh'=4,'x'=4,'y'=8,'zl'=2,'c'=2] {'y'}, use_global_device_ids=true, to_apply=%region_6.7 | all-reduce | flops 256 | bytes 2048 | tf_op jit(solution)/shard_map/psum | solution.py:161
  264.6 49.3 %all-reduce.8 = (f32[128]{0:T(128)S(1)}, f32[128]{0:T(128)S(1)}) all-reduce(f32[128]{0:T(128)S(1)} %get-tuple-element.35, f32[128]{0:T(128)S(1)} %get-tuple-element.36), channel_id=1, replica_groups=mesh['zh'=4,'x'=4,'y'=8,'zl'=2,'c'=2] {'x'}, use_global_device_ids=true, to_apply=%region_7.8 | all-reduce | flops 256 | bytes 2048 | tf_op jit(solution)/shard_map/psum | solution.py:161
  313.9 41.0 %all-reduce.9 = (f32[128]{0:T(128)S(1)}, f32[128]{0:T(128)S(1)}) all-reduce(f32[128]{0:T(128)S(1)} %get-tuple-element.37, f32[128]{0:T(128)S(1)} %get-tuple-element.38), channel_id=1, replica_groups=mesh['zh'=4,'x'=4,'y'=8,'zl'=2,'c'=2] {'zh'}, use_global_device_ids=true, to_apply=%region_8.9 | all-reduce | flops 256 | bytes 2048 | tf_op jit(solution)/shard_map/psum | solution.py:161
  354.9 3.8 all-reduce.11
  358.7 27.4 %all-reduce.10 = (f32[128]{0:T(128)}, f32[128]{0:T(128)}) all-reduce(f32[128]{0:T(128)S(1)} %get-tuple-element.43, f32[128]{0:T(128)S(1)} %get-tuple-element.44), channel_id=1, replica_groups=mesh['zh'=4,'x'=4,'y'=8,'zl'=2,'c'=2] {'c'}, use_global_device_ids=true, to_apply=%region_10.11 | all-reduce | flops 256 | bytes 2048 | tf_op jit(solution)/shard_map/psum | solution.py:161
  (159 shorter events, 37.7 us)
Async XLA Ops:
  0.6 15.5 %copy-start.28 = (f32[128]{0:T(128)S(1)}, f32[128]{0:T(128)}, u32[]{:S(2)}) copy-start(f32[128]{0:T(128)} %param.14) | copy-start | bytes 1540
  1.3 14.2 %copy-start.30 = (bf16[1,128]{1,0:T(2,128)(2,1)}, bf16[1,128]{1,0:T(2,128)(2,1)S(1)}, u32[]{:S(2)}) copy-start(bf16[1,128]{1,0:T(2,128)(2,1)S(1)} %convert_element_type.139) | copy-start | bytes 772
  2.4 43.0 %collective-permute-start.4 = (bf16[144,2048]{1,0:T(8,128)(2,1)S(1)}, bf16[144,2048]{1,0:T(8,128)(2,1)S(1)}, u32[]{:S(2)}, u32[]{:S(2)}) collective-permute-start(bf16[144,2048]{1,0:T(8,128)(2,1)S(1)} %fusion.27), channel_id=1, source_target_pairs={{0,4},{4,8},{8,12},{12,16},{16,20},{20,24},{24,28},{28,32},{32,36}... | collective-permute-start | bytes 1769480 | tf_op jit(solution)/shard_map/ppermute | solution.py:27
  6.5 37.0 %collective-permute-start = (bf16[144,2048]{1,0:T(8,128)(2,1)S(1)}, bf16[144,2048]{1,0:T(8,128)(2,1)S(1)}, u32[]{:S(2)}, u32[]{:S(2)}) collective-permute-start(bf16[144,2048]{1,0:T(8,128)(2,1)S(1)} %fusion.27), channel_id=1, source_target_pairs={{0,32},{4,36},{8,40},{12,44},{16,48},{20,52},{24,56},{28,60},{32,6... | collective-permute-start | bytes 1769480 | tf_op jit(solution)/shard_map/ppermute | solution.py:27
  16.8 81.7 %copy-start.18 = (f32[128,64]{1,0:T(8,128)}, f32[128,64]{1,0:T(8,128)S(1)}, u32[]{:S(2)}) copy-start(f32[128,64]{1,0:T(8,128)S(1)} %get-tuple-element.72) | copy-start | bytes 98308
  43.4 16.3 %collective-permute-start.1 = (bf16[144,2048]{1,0:T(8,128)(2,1)S(1)}, bf16[144,2048]{1,0:T(8,128)(2,1)S(1)}, u32[]{:S(2)}, u32[]{:S(2)}) collective-permute-start(bf16[144,2048]{1,0:T(8,128)(2,1)S(1)} %collective-permute-done), channel_id=1, source_target_pairs={{0,508},{4,0},{8,4},{12,8},{16,12},{20,16},{24,20},{28,24},{32,28}... | collective-permute-start | bytes 1769480 | tf_op jit(solution)/shard_map/ppermute | solution.py:27
  45.4 27.3 %collective-permute-start.5 = (bf16[144,2048]{1,0:T(8,128)(2,1)S(1)}, bf16[144,2048]{1,0:T(8,128)(2,1)S(1)}, u32[]{:S(2)}, u32[]{:S(2)}) collective-permute-start(bf16[144,2048]{1,0:T(8,128)(2,1)S(1)} %collective-permute-done.4), channel_id=1, source_target_pairs={{0,4},{4,8},{8,12},{12,16},{16,20},{20,24},{24,28},{28,32},{32,36}... | collective-permute-start | bytes 1769480 | tf_op jit(solution)/shard_map/ppermute | solution.py:27
  59.7 23.1 %collective-permute-start.2 = (bf16[144,2048]{1,0:T(8,128)(2,1)S(1)}, bf16[144,2048]{1,0:T(8,128)(2,1)S(1)}, u32[]{:S(2)}, u32[]{:S(2)}) collective-permute-start(bf16[144,2048]{1,0:T(8,128)(2,1)S(1)} %collective-permute-done.1), channel_id=1, source_target_pairs={{0,508},{4,0},{8,4},{12,8},{16,12},{20,16},{24,20},{28,24},{32,28}... | collective-permute-start | bytes 1769480 | tf_op jit(solution)/shard_map/ppermute | solution.py:27
  72.6 34.1 %copy-start.12 = (bf16[1,128,1024]{2,1,0:T(8,128)(2,1)S(1)}, bf16[1,128,1024]{2,1,0:T(8,128)(2,1)}, u32[]{:S(2)}) copy-start(bf16[1,128,1024]{2,1,0:T(8,128)(2,1)} %param.10) | copy-start | bytes 786436
  72.6 34.1 %copy-start.20 = (bf16[1,128,1024]{2,1,0:T(8,128)(2,1)S(1)}, bf16[1,128,1024]{2,1,0:T(8,128)(2,1)}, u32[]{:S(2)}) copy-start(bf16[1,128,1024]{2,1,0:T(8,128)(2,1)} %param.11) | copy-start | bytes 786436
  72.6 34.1 %copy-start.31 = (bf16[1,128]{1,0:T(2,128)(2,1)S(1)}, bf16[1,128]{1,0:T(2,128)(2,1)}, u32[]{:S(2)}) copy-start(bf16[1,128]{1,0:T(2,128)(2,1)} %copy-done.30) | copy-start | bytes 772
  72.6 23.9 %collective-permute-start.6 = (bf16[144,2048]{1,0:T(8,128)(2,1)S(1)}, bf16[144,2048]{1,0:T(8,128)(2,1)S(1)}, u32[]{:S(2)}, u32[]{:S(2)}) collective-permute-start(bf16[144,2048]{1,0:T(8,128)(2,1)S(1)} %collective-permute-done.5), channel_id=1, source_target_pairs={{0,4},{4,8},{8,12},{12,16},{16,20},{20,24},{24,28},{28,32},{32,36}... | collective-permute-start | bytes 1769480 | tf_op jit(solution)/shard_map/ppermute | solution.py:27
  82.8 23.7 %collective-permute-start.3 = (bf16[144,2048]{1,0:T(8,128)(2,1)S(1)}, bf16[144,2048]{1,0:T(8,128)(2,1)S(1)}, u32[]{:S(2)}, u32[]{:S(2)}) collective-permute-start(bf16[144,2048]{1,0:T(8,128)(2,1)S(1)} %collective-permute-done.2), channel_id=1, source_target_pairs={{0,508},{4,0},{8,4},{12,8},{16,12},{20,16},{24,20},{28,24},{32,28}... | collective-permute-start | bytes 1769480 | tf_op jit(solution)/shard_map/ppermute | solution.py:27
  96.5 10.0 %collective-permute-start.7 = (bf16[144,2048]{1,0:T(8,128)(2,1)S(1)}, bf16[144,2048]{1,0:T(8,128)(2,1)S(1)}, u32[]{:S(2)}, u32[]{:S(2)}) collective-permute-start(bf16[144,2048]{1,0:T(8,128)(2,1)S(1)} %collective-permute-done.6), channel_id=1, source_target_pairs={{0,4},{4,8},{8,12},{12,16},{16,20},{20,24},{24,28},{28,32},{32,36}... | collective-permute-start | bytes 1769480 | tf_op jit(solution)/shard_map/ppermute | solution.py:27
  115.2 3.9 %copy-start.26 = (f32[128]{0:T(128)S(1)}, f32[128]{0:T(128)}, u32[]{:S(2)}) copy-start(f32[128]{0:T(128)} %param.15) | copy-start | bytes 1540
  119.1 4.3 %copy-start.21 = (f32[1152,8]{0,1:T(8,128)}, f32[1152,8]{0,1:T(8,128)S(1)}, u32[]{:S(2)}) copy-start(f32[1152,8]{0,1:T(8,128)S(1)} %add_rsqrt_fusion) | copy-start | bytes 110596
  119.1 4.3 %copy-start.3 = (f32[1152,64]{1,0:T(8,128)S(1)}, f32[1152,64]{1,0:T(8,128)}, u32[]{:S(2)}) copy-start(f32[1152,64]{1,0:T(8,128)} %get-tuple-element.67) | copy-start | bytes 884740
  119.1 4.3 %copy-start.5 = (f32[1152,64]{1,0:T(8,128)S(1)}, f32[1152,64]{1,0:T(8,128)}, u32[]{:S(2)}) copy-start(f32[1152,64]{1,0:T(8,128)} %get-tuple-element.68) | copy-start | bytes 884740
  123.4 2.8 copy-start.14
  125.1 4.5 %copy-start.2 = (bf16[1152,8,64]{2,0,1:T(8,128)(2,1)}, bf16[1152,8,64]{2,0,1:T(8,128)(2,1)S(1)}, u32[]{:S(2)}) copy-start(bf16[1152,8,64]{2,0,1:T(8,128)(2,1)S(1)} %get-tuple-element.54) | copy-start | bytes 3538948
  126.3 3.4 copy-start.23
  126.3 7.0 %copy-start.11 = (bf16[1152,8,128,1]{0,2,3,1:T(8,128)(2,1)S(1)}, bf16[1152,8,128,1]{0,2,3,1:T(8,128)(2,1)}, u32[]{:S(2)}) copy-start(bf16[1152,8,128,1]{0,2,3,1:T(8,128)(2,1)} %copy.119) | copy-start | bytes 7077892
  129.6 3.6 copy-start.34
  129.6 9.5 %copy-start.35 = (f32[8,2,128]{2,1,0:T(2,128)}, f32[8,2,128]{2,1,0:T(2,128)S(1)}, u32[]{:S(2)}) copy-start(f32[8,2,128]{2,1,0:T(2,128)S(1)} %get-tuple-element.73) | copy-start | bytes 24580
  139.1 8.1 %copy-start.8 = (f32[8,2,128,128]{3,1,0,2:T(2,128)S(1)}, f32[8,2,128,128]{3,1,0,2:T(2,128)}, u32[]{:S(2)}) copy-start(f32[8,2,128,128]{3,1,0,2:T(2,128)} %copy.126) | copy-start | bytes 3145732
  139.1 8.1 %copy-start.13 = (bf16[128,8,2,128]{3,2,1,0:T(2,128)(2,1)S(1)}, bf16[128,8,2,128]{3,2,1,0:T(2,128)(2,1)}, u32[]{:S(2)}) copy-start(bf16[128,8,2,128]{3,2,1,0:T(2,128)(2,1)} %reshape_squeeze.4) | copy-start | bytes 1572868
  150.4 7.8 %copy-start.15 = (bf16[128,16,64]{2,0,1:T(8,128)(2,1)S(1)}, bf16[128,16,64]{2,0,1:T(8,128)(2,1)}, u32[]{:S(2)}) copy-start(bf16[128,16,64]{2,0,1:T(8,128)(2,1)} %copy.96) | copy-start | bytes 786436
  150.4 7.9 %copy-start.17 = (bf16[128,16,64]{2,0,1:T(8,128)(2,1)S(1)}, bf16[128,16,64]{2,0,1:T(8,128)(2,1)}, u32[]{:S(2)}) copy-start(bf16[128,16,64]{2,0,1:T(8,128)(2,1)} %copy.97) | copy-start | bytes 786436
  166.2 3.6 copy-start
  171.8 4.3 %copy-start.4 = (f32[1152,64]{1,0:T(8,128)S(1)}, f32[1152,64]{1,0:T(8,128)}, u32[]{:S(2)}) copy-start(f32[1152,64]{1,0:T(8,128)} %get-tuple-element.67) | copy-start | bytes 884740
  171.9 4.3 %copy-start.6 = (f32[1152,64]{1,0:T(8,128)S(1)}, f32[1152,64]{1,0:T(8,128)}, u32[]{:S(2)}) copy-start(f32[1152,64]{1,0:T(8,128)} %get-tuple-element.68) | copy-start | bytes 884740
  171.9 9.3 %slice-start = ((s8[4718592]{0:T(1024)(128)(4,1)}), s8[4194304]{0:T(1024)(128)(4,1)S(1)}, s32[]{:S(2)}) async-start(s8[4718592]{0:T(1024)(128)(4,1)} %bitcast.166), calls=%async_computation | async-start | bytes 8388608
  172.8 19.3 %collective-permute-start.11 = (bf16[2,8,128,128]{3,1,2,0:T(8,128)(2,1)}, bf16[2,8,128,128]{3,1,2,0:T(8,128)(2,1)}, u32[]{:S(2)}, u32[]{:S(2)}) collective-permute-start(bf16[2,8,128,128]{3,1,2,0:T(8,128)(2,1)} %get-tuple-element.57), channel_id=1, source_target_pairs={{0,4},{4,8},{8,12},{12,16},{16,20},{20,24},{24,28},{28,32},{32,36}... | collective-permute-start | bytes 1572872 | tf_op jit(solution)/shard_map/ppermute | solution.py:27
  174.9 17.3 %collective-permute-start.8 = (bf16[2,8,128,128]{3,1,2,0:T(8,128)(2,1)}, bf16[2,8,128,128]{3,1,2,0:T(8,128)(2,1)}, u32[]{:S(2)}, u32[]{:S(2)}) collective-permute-start(bf16[2,8,128,128]{3,1,2,0:T(8,128)(2,1)} %get-tuple-element.58), channel_id=1, source_target_pairs={{4,0},{8,4},{12,8},{16,12},{20,16},{24,20},{28,24},{32,28},{36,32}... | collective-permute-start | bytes 1572872 | tf_op jit(solution)/shard_map/ppermute | solution.py:27
  176.2 5.0 %slice-start.1 = ((s8[4718592]{0:T(1024)(128)(4,1)}), s8[524288]{0:T(1024)(128)(4,1)S(1)}, s32[]{:S(2)}) async-start(s8[4718592]{0:T(1024)(128)(4,1)} %bitcast.166), calls=%async_computation.1 | async-start | bytes 1048576
  185.0 13.3 %copy-start.19 = (f32[128,64]{1,0:T(8,128)S(1)}, f32[128,64]{1,0:T(8,128)}, u32[]{:S(2)}) copy-start(f32[128,64]{1,0:T(8,128)} %copy-done.18) | copy-start | bytes 98308
  186.6 12.0 %copy-start.29 = (f32[128]{0:T(128)S(1)}, f32[128]{0:T(128)}, u32[]{:S(2)}) copy-start(f32[128]{0:T(128)} %param.14) | copy-start | bytes 1540
  188.0 10.3 %copy-start.9 = (f32[128,16,64]{2,1,0:T(8,128)S(1)}, f32[128,16,64]{2,1,0:T(8,128)}, u32[]{:S(2)}) copy-start(f32[128,16,64]{2,1,0:T(8,128)} %copy.138) | copy-start | bytes 1572868
  188.0 10.3 %copy-start.10 = (f32[128,16,64]{2,1,0:T(8,128)S(1)}, f32[128,16,64]{2,1,0:T(8,128)}, u32[]{:S(2)}) copy-start(f32[128,16,64]{2,1,0:T(8,128)} %copy.139) | copy-start | bytes 1572868
  195.1 23.2 %collective-permute-start.12 = (bf16[2,8,128,128]{3,1,2,0:T(8,128)(2,1)}, bf16[2,8,128,128]{3,1,2,0:T(8,128)(2,1)}, u32[]{:S(2)}, u32[]{:S(2)}) collective-permute-start(bf16[2,8,128,128]{3,1,2,0:T(8,128)(2,1)} %get-tuple-element.49), channel_id=1, source_target_pairs={{0,4},{4,8},{8,12},{12,16},{16,20},{20,24},{24,28},{28,32},{32,36}... | collective-permute-start | bytes 1572872 | tf_op jit(solution)/shard_map/ppermute | solution.py:27
  197.0 21.3 %collective-permute-start.9 = (bf16[2,8,128,128]{3,1,2,0:T(8,128)(2,1)}, bf16[2,8,128,128]{3,1,2,0:T(8,128)(2,1)}, u32[]{:S(2)}, u32[]{:S(2)}) collective-permute-start(bf16[2,8,128,128]{3,1,2,0:T(8,128)(2,1)} %get-tuple-element.50), channel_id=1, source_target_pairs={{4,0},{8,4},{12,8},{16,12},{20,16},{24,20},{28,24},{32,28},{36,32}... | collective-permute-start | bytes 1572872 | tf_op jit(solution)/shard_map/ppermute | solution.py:27
  198.7 26.0 %copy-start.22 = (f32[1152,8]{0,1:T(8,128)S(1)}, f32[1152,8]{0,1:T(8,128)}, u32[]{:S(2)}) copy-start(f32[1152,8]{0,1:T(8,128)} %copy-done.21) | copy-start | bytes 110596
  221.3 18.6 %collective-permute-start.13 = (bf16[2,8,128,128]{3,1,2,0:T(8,128)(2,1)}, bf16[2,8,128,128]{3,1,2,0:T(8,128)(2,1)}, u32[]{:S(2)}, u32[]{:S(2)}) collective-permute-start(bf16[2,8,128,128]{3,1,2,0:T(8,128)(2,1)} %get-tuple-element.47), channel_id=1, source_target_pairs={{0,4},{4,8},{8,12},{12,16},{16,20},{20,24},{24,28},{28,32},{32,36}... | collective-permute-start | bytes 1572872 | tf_op jit(solution)/shard_map/ppermute | solution.py:27
  223.3 16.7 %collective-permute-start.10 = (bf16[2,8,128,128]{3,1,2,0:T(8,128)(2,1)}, bf16[2,8,128,128]{3,1,2,0:T(8,128)(2,1)}, u32[]{:S(2)}, u32[]{:S(2)}) collective-permute-start(bf16[2,8,128,128]{3,1,2,0:T(8,128)(2,1)} %get-tuple-element.48), channel_id=1, source_target_pairs={{4,0},{8,4},{12,8},{16,12},{20,16},{24,20},{28,24},{32,28},{36,32}... | collective-permute-start | bytes 1572872 | tf_op jit(solution)/shard_map/ppermute | solution.py:27
  243.1 142.9 %collective-permute-start.14 = (bf16[2,8,128,128]{3,1,2,0:T(8,128)(2,1)}, bf16[2,8,128,128]{3,1,2,0:T(8,128)(2,1)}, u32[]{:S(2)}, u32[]{:S(2)}) collective-permute-start(bf16[2,8,128,128]{3,1,2,0:T(8,128)(2,1)} %get-tuple-element.27), channel_id=1, source_target_pairs={{4,0},{8,4},{12,8},{16,12},{20,16},{24,20},{28,24},{32,28},{36,32}... | collective-permute-start | bytes 1572872 | tf_op jit(solution)/shard_map/ppermute | solution.py:27
  244.4 141.6 %collective-permute-start.15 = (bf16[2,8,128,128]{3,1,2,0:T(8,128)(2,1)}, bf16[2,8,128,128]{3,1,2,0:T(8,128)(2,1)}, u32[]{:S(2)}, u32[]{:S(2)}) collective-permute-start(bf16[2,8,128,128]{3,1,2,0:T(8,128)(2,1)} %get-tuple-element.28), channel_id=1, source_target_pairs={{0,480},{4,484},{8,488},{12,492},{16,496},{20,500},{24,504},{28,50... | collective-permute-start | bytes 1572872 | tf_op jit(solution)/shard_map/ppermute | solution.py:27
  250.2 138.4 %copy-start.7 = (f32[16,8,8,128]{3,2,1,0:T(8,128)S(1)}, f32[16,8,8,128]{3,2,1,0:T(8,128)}, u32[]{:S(2)}) copy-start(f32[16,8,8,128]{3,2,1,0:T(8,128)} %copy.144) | copy-start | bytes 1572868
  250.2 138.4 %copy-start.27 = (f32[128]{0:T(128)S(1)}, f32[128]{0:T(128)}, u32[]{:S(2)}) copy-start(f32[128]{0:T(128)} %param.15) | copy-start | bytes 1540
  (8 other events, 17.6 us)

commit v7 on v5

--- a/solution.py
+++ b/solution.py
@@ -108,20 +108,27 @@
         b_slot = shift(b_slot, behind if step == 0 else -1, True)
         near.append(a_slot)
         far.append(b_slot)
-    stacked = jnp.stack(far + near[::-1] + [packed])
+    window = far + near[::-1] + [packed]
     width = (behind + 1) * row_count
-    key_raw_win = stacked[:, :row_count, :key_span_width].reshape(width, KEY_VALUE_HEADS, HEAD_SIZE)
-    value_win = stacked[:, :row_count, key_span_width:].reshape(width, KEY_VALUE_HEADS, HEAD_SIZE)
-    key_doc = stacked[:, row_count, :row_count].reshape(width).astype(jnp.int32)
     key_pos = base - behind * row_count + jnp.arange(width, dtype=jnp.int32)
-
-    def prepare_window(raw, gain):
-        return prepare(raw, gain, key_pos)
-
-    key_normalized_win, key_window_back = jax.vjp(
-        prepare_window, key_raw_win.astype(jnp.float32), key_norm_gain
-    )
-    key_win = key_normalized_win.astype(jnp.bfloat16)
+    key_parts, key_backs = [], []
+    for index, slab in enumerate(window):
+        slab_pos = key_pos[index * row_count:(index + 1) * row_count]
+
+        def prepare_slab(raw, gain, slab_pos=slab_pos):
+            return prepare(raw, gain, slab_pos)
+
+        raw = slab[:row_count, :key_span_width].astype(jnp.float32)
+        normalized, back = jax.vjp(
+            prepare_slab, raw.reshape(row_count, KEY_VALUE_HEADS, HEAD_SIZE), key_norm_gain
+        )
+        key_parts.append(normalized.astype(jnp.bfloat16))
+        key_backs.append(back)
+    key_win = jnp.concatenate(key_parts, axis=0)
+    value_win = jnp.concatenate(
+        [slab[:row_count, key_span_width:] for slab in window], axis=0
+    ).reshape(width, KEY_VALUE_HEADS, HEAD_SIZE)
+    key_doc = jnp.concatenate([slab[row_count, :row_count] for slab in window]).astype(jnp.int32)
     allowed = (
         (key_pos[None, :] <= positions[:, None])
         & (positions[:, None] - key_pos[None, :] < WINDOW_LENGTH)
@@ -136,38 +143,39 @@
         allowed,
     )
     dquery_rot = dquery_rot.reshape(row_count, QUERY_HEADS, HEAD_SIZE)
-    slots = jnp.stack([dkey_win, dvalue_win]).reshape(
-        2, KEY_VALUE_HEADS, behind + 1, row_count, HEAD_SIZE
-    )
-    remote = slots[:, :, :behind].astype(jnp.bfloat16)
-    owned = jnp.concatenate(
-        [remote[0].astype(jnp.float32), slots[0, :, behind:]], axis=1
-    ).reshape(KEY_VALUE_HEADS, width, HEAD_SIZE)
-    _, key_gain_gradient = key_window_back(owned.transpose(1, 0, 2))
+    dkey_slots = dkey_win.reshape(KEY_VALUE_HEADS, behind + 1, row_count, HEAD_SIZE)
+    dvalue_slots = dvalue_win.reshape(KEY_VALUE_HEADS, behind + 1, row_count, HEAD_SIZE)
+
+    def part(slot):
+        return jnp.stack([dkey_slots[:, slot], dvalue_slots[:, slot]])
+
+    key_gain_gradient = None
+    for slot in range(behind + 1):
+        owned = dkey_slots[:, slot]
+        if slot < behind:
+            owned = owned.astype(jnp.bfloat16).astype(jnp.float32)
+        _, gain_part = key_backs[slot](owned.transpose(1, 0, 2))
+        key_gain_gradient = gain_part if key_gain_gradient is None else key_gain_gradient + gain_part
     query_raw_gradient, query_gain_gradient = query_back(dquery_rot)
-    carry_near = remote[:, :, behind - half]
+    carry_near = part(behind - half).astype(jnp.bfloat16)
     for offset in range(half - 1, 0, -1):
         got = shift(carry_near, -1, False).astype(jnp.float32)
-        carry_near = (got + slots[:, :, behind - offset]).astype(jnp.bfloat16)
-    carry_far = remote[:, :, behind - half - 1]
+        carry_near = (got + part(behind - offset)).astype(jnp.bfloat16)
+    carry_far = part(behind - half - 1).astype(jnp.bfloat16)
     for offset in range(half + 2, behind + 1):
         got = shift(carry_far, 1, True).astype(jnp.float32)
-        carry_far = (got + slots[:, :, behind - offset]).astype(jnp.bfloat16)
+        carry_far = (got + part(behind - offset)).astype(jnp.bfloat16)
     sent = [shift(carry_near, -1, False), shift(carry_far, -behind, True)]
     gains = (query_gain_gradient, key_gain_gradient)
     for axis in ("y", "x", "zh", "zl", "c"):
         gains = lax.psum(gains, axis)
     gain_query, gain_key = gains
-    total = slots[:, :, behind]
+    total = part(behind)
     for moved in sent:
         total = total + moved.astype(jnp.float32)
     key_full_length = total[0].transpose(1, 0, 2).reshape(row_count, key_span_width)
     value_total = total[1].transpose(1, 0, 2).reshape(row_count, key_span_width)
-    _, key_backward = jax.vjp(
-        prepare_function,
-        key_projection[0].astype(jnp.float32).reshape(row_count, KEY_VALUE_HEADS, HEAD_SIZE),
-        key_norm_gain,
-    )
+    key_backward = key_backs[behind]
     key_raw_gradient, _ = key_backward(
         key_full_length.reshape(row_count, KEY_VALUE_HEADS, HEAD_SIZE)
     )

time: 391 us -> 462 us (1.18)
  local copies, waits for them, and re-layouts: 37 us -> 104 us
  blocking collectives: 122 us -> 155 us
  waiting for transfers between devices: 83.1 us -> 58.8 us
  starting transfers between devices: 60.5 us -> 51.8 us
  other arithmetic: 50.9 us -> 56.2 us
    unnamed x103 -> x298, local copies, waits for them, and re-layouts: 18.7 us -> 53.1 us
    psum x5, blocking collectives: 122 us -> 155 us  [shards(): gains = lax.psum(gains, axis)]
    ppermute x16, waiting for transfers between devices: 83.1 us -> 58.8 us  [shift(): return lax.ppermute(value, SEQ_AXES, pairs)]
    concatenate x1 -> x18, local copies, waits for them, and re-layouts: 0.91 us -> 18.6 us  [the longest x10 10.6 us: shards(): jnp.concatenate([slab[:row_count, key_span_width:] for slab in window], a...]
    slice x1 -> x8, local copies, waits for them, and re-layouts: 0.03 us -> 12.1 us  [shards(): raw = slab[:row_count, :key_span_width].astype(jnp.float32)]
    ppermute x16, starting transfers between devices: 60.5 us -> 51.8 us  [shift(): return lax.ppermute(value, SEQ_AXES, pairs)]
  transfers between devices with their start and end apart: 16 -> 16, of which waited for: 8 -> 7; matrix products, arithmetic and copies ran while one was open for 10% -> 16% of each run, Pallas kernels for 0% -> 0%
where the time goes in v7:
time: 462 us; the launch traced here: 454 us
  blocking collectives  155 us (34%)
  local copies, waits for them, and re-layouts  104 us (23%)
  waiting for transfers between devices  58.8 us (13%)
  other arithmetic  56.2 us (12%)
  starting transfers between devices  51.8 us (11%)
  matrix products  23.9 us (5%)
    psum x5, blocking collectives, shards(): gains = lax.psum(gains, axis)  155 us
    ppermute x16, waiting for transfers between devices, shift(): return lax.ppermute(value, SEQ_AXES, pairs)  58.8 us
    unnamed x298, local copies, waits for them, and re-layouts  53.1 us
    ppermute x16, starting transfers between devices, shift(): return lax.ppermute(value, SEQ_AXES, pairs)  51.8 us
    slice x8, local copies, waits for them, and re-layouts, shards(): raw = slab[:row_count, :key_span_width].astype(jnp.float32)  12.1 us
    concatenate x10, local copies, waits for them, and re-layouts, shards(): jnp.concatenate([slab[:row_count, key_span_width:] for slab in window], a...  10.6 us
  transfers between devices with their start and end apart: 16, of which 7 were waited for; matrix products, arithmetic and copies ran while one was open for 16% of the time, Pallas kernels for 0%

profile of v7, /device:TPU:1, one launch (start us, length us, event | category | flops | bytes accessed | tf_op | source)
XLA Modules:
  0.0 453.5 jit_solution(3298010373761354804)
XLA Ops:
  1.3 1.9 fusion.31
  3.2 3.9 collective-permute-start
  7.1 4.0 collective-permute-start.4
  14.2 3.4 multiply_cosine_fusion
  23.9 11.5 %collective-permute-done = bf16[144,2048]{1,0:T(8,128)(2,1)} collective-permute-done((bf16[144,2048]{1,0:T(8,128)(2,1)}, bf16[144,2048]{1,0:T(8,128)(2,1)}, u32[]{:S(2)}, u32[]{:S(2)}) %collective-permute-start) | collective-permute-done | bytes 589856 | tf_op jit(solution)/shard_map/ppermute | solution.py:27
  41.8 1.9 collective-permute-start.1
  43.7 4.2 collective-permute-start.5
  51.2 4.6 %collective-permute-done.1 = bf16[144,2048]{1,0:T(8,128)(2,1)S(1)} collective-permute-done((bf16[144,2048]{1,0:T(8,128)(2,1)}, bf16[144,2048]{1,0:T(8,128)(2,1)S(1)}, u32[]{:S(2)}, u32[]{:S(2)}) %collective-permute-start.1) | collective-permute-done | bytes 589856 | tf_op jit(solution)/shard_map/ppermute | solution.py:27
  60.8 8.5 %collective-permute-start.2 = (bf16[144,2048]{1,0:T(8,128)(2,1)}, bf16[144,2048]{1,0:T(8,128)(2,1)}, u32[]{:S(2)}, u32[]{:S(2)}) collective-permute-start(bf16[144,2048]{1,0:T(8,128)(2,1)} %copy-done.89), channel_id=1, source_target_pairs={{0,508},{4,0},{8,4},{12,8},{16,12},{20,16},{24,20},{28,24},{32,28}... | collective-permute-start | bytes 1769480 | tf_op jit(solution)/shard_map/ppermute | solution.py:27
  69.3 2.1 collective-permute-start.6
  78.6 2.1 copy.290
  85.1 1.9 fusion.62
  88.1 1.8 fusion.59
  91.7 10.8 %collective-permute-start.3 = (bf16[144,2048]{1,0:T(8,128)(2,1)}, bf16[144,2048]{1,0:T(8,128)(2,1)}, u32[]{:S(2)}, u32[]{:S(2)}) collective-permute-start(bf16[144,2048]{1,0:T(8,128)(2,1)} %collective-permute-done.2), channel_id=1, source_target_pairs={{0,508},{4,0},{8,4},{12,8},{16,12},{20,16},{24,20},{28,24},{32,28}... | collective-permute-start | bytes 1769480 | tf_op jit(solution)/shard_map/ppermute | solution.py:27
  102.5 2.6 collective-permute-start.7
  110.3 1.8 copy.310
  112.1 1.8 copy.382
  116.6 1.9 copy.288
  122.8 1.9 fusion.61
  126.7 1.8 fusion.60
  147.1 1.8 constant_dynamic-update-slice_fusion.5
  165.4 2.3 fusion.3
  167.8 3.7 copy-done.125
  171.4 3.5 fusion.14
  175.0 2.4 copy.359
  177.4 8.1 %fusion.11 = f32[8,1152,128,1]{2,1,3,0:T(8,128)} fusion(bf16[128,8,2,128]{3,2,1,0:T(2,128)(2,1)} %reshape_squeeze.3, f32[8,1152,128,2]{2,1,3,0:T(8,128)} %copy-done.125, f32[8,2,128]{2,1,0:T(2,128)} %copy-done.126, pred[128,1152]{0,1:T(8,128)(4,1)} %copy-done.90), kind=kOutput, calls=%fused_computation.14 | convolution fusion | flops 613416960 | bytes 14835712 | tf_op jit(solution)/shard_map/grtw,tgrd->gwd/dot_general | solution.py:71
  185.6 2.0 multiply_reduce_fusion
  187.5 1.8 copy.360
  189.4 7.5 %fusion.1 = bf16[8,2,128,1152]{2,3,1,0:T(8,128)(2,1)S(1)} fusion(f32[8,2,128]{2,1,0:T(2,128)} %copy.360, bf16[1152,8,128]{2,0,1:T(8,128)(2,1)} %constant_dynamic-update-slice_fusion, bf16[128,8,2,128]{3,2,1,0:T(2,128)(2,1)} %reshape_squeeze.3, f32[8,2,128]{2,1,0:T(2,128)} %copy-done.126, f32[8,1152,128,2]{2,1,3,0:T(8,128)} %copy-done.125, ...), kind=kOutput, calls=%fused_computation.2 | convolution fusion | flops 618135552 | bytes 17203200 | tf_op jit(solution)/shard_map/tgrd,wgd->grtw/dot_general | solution.py:61
  199.6 1.9 slice_bitcast_fusion.7
  202.3 2.2 slice_bitcast_fusion.15
  204.5 2.3 convert_bitcast_fusion.7
  209.6 1.8 multiply_add_fusion.1
  217.0 2.1 collective-permute-start.12
  227.5 6.0 %collective-permute-done.12 = bf16[2,8,128,128]{3,2,1,0:T(8,128)(2,1)S(1)} collective-permute-done((bf16[2,8,128,128]{3,2,1,0:T(8,128)(2,1)S(1)}, bf16[2,8,128,128]{3,2,1,0:T(8,128)(2,1)S(1)}, u32[]{:S(2)}, u32[]{:S(2)}) %collective-permute-start.12) | collective-permute-done | bytes 524320 | tf_op jit(solution)/shard_map/ppermute | solution.py:27
  234.4 2.0 collective-permute-start.13
  241.0 16.0 %collective-permute-done.13 = bf16[2,8,128,128]{3,2,1,0:T(8,128)(2,1)} collective-permute-done((bf16[2,8,128,128]{3,2,1,0:T(8,128)(2,1)}, bf16[2,8,128,128]{3,2,1,0:T(8,128)(2,1)}, u32[]{:S(2)}, u32[]{:S(2)}) %collective-permute-start.13) | collective-permute-done | bytes 524320 | tf_op jit(solution)/shard_map/ppermute | solution.py:27
  258.2 2.1 collective-permute-start.14
  260.4 2.1 fusion.26
  265.5 13.1 %collective-permute-done.14 = bf16[2,8,128,128]{3,2,1,0:T(8,128)(2,1)} collective-permute-done((bf16[2,8,128,128]{3,2,1,0:T(8,128)(2,1)S(1)}, bf16[2,8,128,128]{3,2,1,0:T(8,128)(2,1)}, u32[]{:S(2)}, u32[]{:S(2)}) %collective-permute-start.14) | collective-permute-done | bytes 524320 | tf_op jit(solution)/shard_map/ppermute | solution.py:27
  279.8 2.1 collective-permute-start.15
  285.6 4.3 collective-permute-done.15
  289.9 3.3 collective-permute-done.11
  298.0 13.7 %all-reduce.23 = (f32[128]{0:T(128)S(1)}, f32[128]{0:T(128)S(1)}) all-reduce(f32[128]{0:T(128)S(1)} %copy-done.124, f32[128]{0:T(128)S(1)} %add_add_fusion.2), channel_id=1, replica_groups=mesh['zh'=4,'x'=4,'y'=8,'zl'=2,'c'=2] {'y'}, use_global_device_ids=true, to_apply=%region_14.15 | all-reduce | flops 256 | bytes 2048 | tf_op jit(solution)/shard_map/psum | solution.py:171
  311.6 77.4 %all-reduce.24 = (f32[128]{0:T(128)S(1)}, f32[128]{0:T(128)S(1)}) all-reduce(f32[128]{0:T(128)S(1)} %get-tuple-element.46, f32[128]{0:T(128)S(1)} %get-tuple-element.47), channel_id=1, replica_groups=mesh['zh'=4,'x'=4,'y'=8,'zl'=2,'c'=2] {'x'}, use_global_device_ids=true, to_apply=%region_15.16 | all-reduce | flops 256 | bytes 2048 | tf_op jit(solution)/shard_map/psum | solution.py:171
  389.0 48.0 %all-reduce.25 = (f32[128]{0:T(128)S(1)}, f32[128]{0:T(128)S(1)}) all-reduce(f32[128]{0:T(128)S(1)} %get-tuple-element.48, f32[128]{0:T(128)S(1)} %get-tuple-element.49), channel_id=1, replica_groups=mesh['zh'=4,'x'=4,'y'=8,'zl'=2,'c'=2] {'zh'}, use_global_device_ids=true, to_apply=%region_16.17 | all-reduce | flops 256 | bytes 2048 | tf_op jit(solution)/shard_map/psum | solution.py:171
  437.0 3.8 all-reduce.27
  440.7 12.5 %all-reduce.26 = (f32[128]{0:T(128)}, f32[128]{0:T(128)}) all-reduce(f32[128]{0:T(128)S(1)} %get-tuple-element.54, f32[128]{0:T(128)S(1)} %get-tuple-element.55), channel_id=1, replica_groups=mesh['zh'=4,'x'=4,'y'=8,'zl'=2,'c'=2] {'c'}, use_global_device_ids=true, to_apply=%region_18.19 | all-reduce | flops 256 | bytes 2048 | tf_op jit(solution)/shard_map/psum | solution.py:171
  (432 shorter events, 126.3 us)
Async XLA Ops:
  3.2 32.3 %collective-permute-start = (bf16[144,2048]{1,0:T(8,128)(2,1)}, bf16[144,2048]{1,0:T(8,128)(2,1)}, u32[]{:S(2)}, u32[]{:S(2)}) collective-permute-start(bf16[144,2048]{1,0:T(8,128)(2,1)} %fusion.31), channel_id=1, source_target_pairs={{0,32},{4,36},{8,40},{12,44},{16,48},{20,52},{24,56},{28,60},{32,6... | collective-permute-start | bytes 1769480 | tf_op jit(solution)/shard_map/ppermute | solution.py:27
  7.1 29.8 %collective-permute-start.4 = (bf16[144,2048]{1,0:T(8,128)(2,1)}, bf16[144,2048]{1,0:T(8,128)(2,1)}, u32[]{:S(2)}, u32[]{:S(2)}) collective-permute-start(bf16[144,2048]{1,0:T(8,128)(2,1)} %fusion.31), channel_id=1, source_target_pairs={{0,4},{4,8},{8,12},{12,16},{16,20},{20,24},{24,28},{28,32},{32,36}... | collective-permute-start | bytes 1769480 | tf_op jit(solution)/shard_map/ppermute | solution.py:27
  22.1 135.4 %copy-start = (f32[128,8,128]{2,0,1:T(8,128)}, f32[128,8,128]{2,0,1:T(8,128)S(1)}, u32[]{:S(2)}) copy-start(f32[128,8,128]{2,0,1:T(8,128)S(1)} %copy.294) | copy-start | bytes 1572868
  23.9 13.0 %copy-start.107 = (f32[128,8]{0,1:T(8,128)}, f32[128,8]{0,1:T(8,128)S(1)}, u32[]{:S(2)}) copy-start(f32[128,8]{0,1:T(8,128)S(1)} %multiply_reduce_fusion.14) | copy-start | bytes 12292
  39.6 117.9 %copy-start.6 = (f32[128,8,128]{2,0,1:T(8,128)}, f32[128,8,128]{2,0,1:T(8,128)S(1)}, u32[]{:S(2)}) copy-start(f32[128,8,128]{2,0,1:T(8,128)S(1)} %copy.292) | copy-start | bytes 1572868
  39.7 117.8 %copy-start.2 = (f32[128,8,128]{2,0,1:T(8,128)}, f32[128,8,128]{2,0,1:T(8,128)S(1)}, u32[]{:S(2)}) copy-start(f32[128,8,128]{2,0,1:T(8,128)S(1)} %copy.278) | copy-start | bytes 1572868
  41.8 14.0 %collective-permute-start.1 = (bf16[144,2048]{1,0:T(8,128)(2,1)}, bf16[144,2048]{1,0:T(8,128)(2,1)S(1)}, u32[]{:S(2)}, u32[]{:S(2)}) collective-permute-start(bf16[144,2048]{1,0:T(8,128)(2,1)} %collective-permute-done), channel_id=1, source_target_pairs={{0,508},{4,0},{8,4},{12,8},{16,12},{20,16},{24,20},{28,24},{32,28}... | collective-permute-start | bytes 1769480 | tf_op jit(solution)/shard_map/ppermute | solution.py:27
  43.7 13.8 %collective-permute-start.5 = (bf16[144,2048]{1,0:T(8,128)(2,1)}, bf16[144,2048]{1,0:T(8,128)(2,1)}, u32[]{:S(2)}, u32[]{:S(2)}) collective-permute-start(bf16[144,2048]{1,0:T(8,128)(2,1)} %collective-permute-done.4), channel_id=1, source_target_pairs={{0,4},{4,8},{8,12},{12,16},{16,20},{20,24},{24,28},{28,32},{32,36}... | collective-permute-start | bytes 1769480 | tf_op jit(solution)/shard_map/ppermute | solution.py:27
  59.5 19.0 %copy-start.28 = (bf16[128,1024]{0,1:T(8,128)(2,1)}, bf16[128,1024]{0,1:T(8,128)(2,1)S(1)}, u32[]{:S(2)}) copy-start(bf16[128,1024]{0,1:T(8,128)(2,1)S(1)} %copy.375) | copy-start | bytes 786436
  60.8 24.3 %collective-permute-start.2 = (bf16[144,2048]{1,0:T(8,128)(2,1)}, bf16[144,2048]{1,0:T(8,128)(2,1)}, u32[]{:S(2)}, u32[]{:S(2)}) collective-permute-start(bf16[144,2048]{1,0:T(8,128)(2,1)} %copy-done.89), channel_id=1, source_target_pairs={{0,508},{4,0},{8,4},{12,8},{16,12},{20,16},{24,20},{28,24},{32,28}... | collective-permute-start | bytes 1769480 | tf_op jit(solution)/shard_map/ppermute | solution.py:27
  69.3 18.8 %collective-permute-start.6 = (bf16[144,2048]{1,0:T(8,128)(2,1)}, bf16[144,2048]{1,0:T(8,128)(2,1)}, u32[]{:S(2)}, u32[]{:S(2)}) collective-permute-start(bf16[144,2048]{1,0:T(8,128)(2,1)} %collective-permute-done.5), channel_id=1, source_target_pairs={{0,4},{4,8},{8,12},{12,16},{16,20},{20,24},{24,28},{28,32},{32,36}... | collective-permute-start | bytes 1769480 | tf_op jit(solution)/shard_map/ppermute | solution.py:27
  78.6 78.9 %copy-start.4 = (f32[128,8,128]{2,0,1:T(8,128)}, f32[128,8,128]{2,0,1:T(8,128)S(1)}, u32[]{:S(2)}) copy-start(f32[128,8,128]{2,0,1:T(8,128)S(1)} %copy.280) | copy-start | bytes 1572868
  91.7 31.1 %collective-permute-start.3 = (bf16[144,2048]{1,0:T(8,128)(2,1)}, bf16[144,2048]{1,0:T(8,128)(2,1)}, u32[]{:S(2)}, u32[]{:S(2)}) collective-permute-start(bf16[144,2048]{1,0:T(8,128)(2,1)} %collective-permute-done.2), channel_id=1, source_target_pairs={{0,508},{4,0},{8,4},{12,8},{16,12},{20,16},{24,20},{28,24},{32,28}... | collective-permute-start | bytes 1769480 | tf_op jit(solution)/shard_map/ppermute | solution.py:27
  102.5 24.1 %collective-permute-start.7 = (bf16[144,2048]{1,0:T(8,128)(2,1)}, bf16[144,2048]{1,0:T(8,128)(2,1)}, u32[]{:S(2)}, u32[]{:S(2)}) collective-permute-start(bf16[144,2048]{1,0:T(8,128)(2,1)} %collective-permute-done.6), channel_id=1, source_target_pairs={{0,4},{4,8},{8,12},{12,16},{16,20},{20,24},{24,28},{28,32},{32,36}... | collective-permute-start | bytes 1769480 | tf_op jit(solution)/shard_map/ppermute | solution.py:27
  147.0 10.5 %copy-start.115 = (f32[128,8]{0,1:T(8,128)S(1)}, f32[128,8]{0,1:T(8,128)}, u32[]{:S(2)}) copy-start(f32[128,8]{0,1:T(8,128)} %multiply_reduce_fusion.18) | copy-start | bytes 12292
  147.0 10.6 %copy-start.8 = (f32[128,8,128]{2,0,1:T(8,128)S(1)}, f32[128,8,128]{2,0,1:T(8,128)}, u32[]{:S(2)}) copy-start(f32[128,8,128]{2,0,1:T(8,128)} %copy.282) | copy-start | bytes 1572868
  147.0 10.6 %copy-start.10 = (f32[128,8,128]{2,0,1:T(8,128)S(1)}, f32[128,8,128]{2,0,1:T(8,128)}, u32[]{:S(2)}) copy-start(f32[128,8,128]{2,0,1:T(8,128)} %copy.290) | copy-start | bytes 1572868
  147.0 10.6 %copy-start.12 = (f32[128,8,128]{2,0,1:T(8,128)S(1)}, f32[128,8,128]{2,0,1:T(8,128)}, u32[]{:S(2)}) copy-start(f32[128,8,128]{2,0,1:T(8,128)} %copy.288) | copy-start | bytes 1572868
  147.0 10.6 %copy-start.14 = (f32[128,8,128]{2,0,1:T(8,128)S(1)}, f32[128,8,128]{2,0,1:T(8,128)}, u32[]{:S(2)}) copy-start(f32[128,8,128]{2,0,1:T(8,128)} %copy.284) | copy-start | bytes 1572868
  147.0 10.6 %copy-start.16 = (f32[128,8,128]{2,0,1:T(8,128)S(1)}, f32[128,8,128]{2,0,1:T(8,128)}, u32[]{:S(2)}) copy-start(f32[128,8,128]{2,0,1:T(8,128)} %copy.286) | copy-start | bytes 1572868
  147.0 10.6 %copy-start.93 = (f32[128,8]{0,1:T(8,128)S(1)}, f32[128,8]{0,1:T(8,128)}, u32[]{:S(2)}) copy-start(f32[128,8]{0,1:T(8,128)} %get-tuple-element.212) | copy-start | bytes 12292
  147.0 10.6 %copy-start.95 = (f32[128,8]{0,1:T(8,128)S(1)}, f32[128,8]{0,1:T(8,128)}, u32[]{:S(2)}) copy-start(f32[128,8]{0,1:T(8,128)} %get-tuple-element.206) | copy-start | bytes 12292
  147.0 10.6 %copy-start.97 = (f32[128,8]{0,1:T(8,128)S(1)}, f32[128,8]{0,1:T(8,128)}, u32[]{:S(2)}) copy-start(f32[128,8]{0,1:T(8,128)} %get-tuple-element.205) | copy-start | bytes 12292
  147.0 10.6 %copy-start.120 = (f32[128]{0:T(128)S(1)}, f32[128]{0:T(128)}, u32[]{:S(2)}) copy-start(f32[128]{0:T(128)} %param.15) | copy-start | bytes 1540
  217.0 16.5 %collective-permute-start.12 = (bf16[2,8,128,128]{3,2,1,0:T(8,128)(2,1)S(1)}, bf16[2,8,128,128]{3,2,1,0:T(8,128)(2,1)S(1)}, u32[]{:S(2)}, u32[]{:S(2)}) collective-permute-start(bf16[2,8,128,128]{3,2,1,0:T(8,128)(2,1)S(1)} %pad_maximum_fusion.2), channel_id=1, source_target_pairs={{0,4},{4,8},{8,12},{12,16},{16,20},{20,24},{24,28},{28,32},{32,36}... | collective-permute-start | bytes 1572872 | tf_op jit(solution)/shard_map/ppermute | solution.py:27
  220.2 16.3 %collective-permute-start.8 = (bf16[2,8,128,128]{3,2,1,0:T(8,128)(2,1)S(1)}, bf16[2,8,128,128]{3,2,1,0:T(8,128)(2,1)S(1)}, u32[]{:S(2)}, u32[]{:S(2)}) collective-permute-start(bf16[2,8,128,128]{3,2,1,0:T(8,128)(2,1)S(1)} %pad_maximum_fusion.1), channel_id=1, source_target_pairs={{4,0},{8,4},{12,8},{16,12},{20,16},{24,20},{28,24},{32,28},{36,32}... | collective-permute-start | bytes 1572872 | tf_op jit(solution)/shard_map/ppermute | solution.py:27
  227.5 11.2 %copy-start.15 = (f32[128,8,128]{2,0,1:T(8,128)S(1)}, f32[128,8,128]{2,0,1:T(8,128)}, u32[]{:S(2)}) copy-start(f32[128,8,128]{2,0,1:T(8,128)} %copy.284) | copy-start | bytes 1572868
  227.5 11.2 %copy-start.102 = (f32[128,8]{0,1:T(8,128)S(1)}, f32[128,8]{0,1:T(8,128)}, u32[]{:S(2)}) copy-start(f32[128,8]{0,1:T(8,128)} %copy-done.101) | copy-start | bytes 12292
  234.4 22.6 %collective-permute-start.13 = (bf16[2,8,128,128]{3,2,1,0:T(8,128)(2,1)}, bf16[2,8,128,128]{3,2,1,0:T(8,128)(2,1)}, u32[]{:S(2)}, u32[]{:S(2)}) collective-permute-start(bf16[2,8,128,128]{3,2,1,0:T(8,128)(2,1)} %fusion.28), channel_id=1, source_target_pairs={{0,4},{4,8},{8,12},{12,16},{16,20},{20,24},{24,28},{28,32},{32,36}... | collective-permute-start | bytes 1572872 | tf_op jit(solution)/shard_map/ppermute | solution.py:27
  237.4 22.9 %collective-permute-start.9 = (bf16[2,8,128,128]{3,2,1,0:T(8,128)(2,1)}, bf16[2,8,128,128]{3,2,1,0:T(8,128)(2,1)}, u32[]{:S(2)}, u32[]{:S(2)}) collective-permute-start(bf16[2,8,128,128]{3,2,1,0:T(8,128)(2,1)} %fusion.25), channel_id=1, source_target_pairs={{4,0},{8,4},{12,8},{16,12},{20,16},{24,20},{28,24},{32,28},{36,32}... | collective-permute-start | bytes 1572872 | tf_op jit(solution)/shard_map/ppermute | solution.py:27
  239.2 17.8 %copy-start.33 = (f32[1,8,128,128]{3,2,1,0:T(8,128)S(1)}, f32[1,8,128,128]{3,2,1,0:T(8,128)}, u32[]{:S(2)}) copy-start(f32[1,8,128,128]{3,2,1,0:T(8,128)} %get-tuple-element.75) | copy-start | bytes 1572868
  239.2 17.8 %copy-start.44 = (f32[1,8,128,128]{3,2,1,0:T(8,128)S(1)}, f32[1,8,128,128]{3,2,1,0:T(8,128)}, u32[]{:S(2)}) copy-start(f32[1,8,128,128]{3,2,1,0:T(8,128)} %get-tuple-element.71) | copy-start | bytes 1572868
  239.2 21.1 %copy-start.32 = (f32[1,8,128,128]{3,2,1,0:T(8,128)S(1)}, f32[1,8,128,128]{3,2,1,0:T(8,128)}, u32[]{:S(2)}) copy-start(f32[1,8,128,128]{3,2,1,0:T(8,128)} %get-tuple-element.78) | copy-start | bytes 1572868
  239.2 21.1 %copy-start.43 = (f32[1,8,128,128]{3,2,1,0:T(8,128)S(1)}, f32[1,8,128,128]{3,2,1,0:T(8,128)}, u32[]{:S(2)}) copy-start(f32[1,8,128,128]{3,2,1,0:T(8,128)} %get-tuple-element.68) | copy-start | bytes 1572868
  241.0 22.7 %copy-start.9 = (f32[128,8,128]{2,0,1:T(8,128)S(1)}, f32[128,8,128]{2,0,1:T(8,128)}, u32[]{:S(2)}) copy-start(f32[128,8,128]{2,0,1:T(8,128)} %copy.282) | copy-start | bytes 1572868
  241.0 22.7 %copy-start.36 = (f32[128,8,64]{2,0,1:T(8,128)S(1)}, f32[128,8,64]{2,0,1:T(8,128)}, u32[]{:S(2)}) copy-start(f32[128,8,64]{2,0,1:T(8,128)} %get-tuple-element.93) | copy-start | bytes 786436
  241.0 22.7 %copy-start.37 = (f32[128,8,64]{2,0,1:T(8,128)S(1)}, f32[128,8,64]{2,0,1:T(8,128)}, u32[]{:S(2)}) copy-start(f32[128,8,64]{2,0,1:T(8,128)} %get-tuple-element.94) | copy-start | bytes 786436
  241.0 22.7 %copy-start.100 = (f32[128,8]{0,1:T(8,128)S(1)}, f32[128,8]{0,1:T(8,128)}, u32[]{:S(2)}) copy-start(f32[128,8]{0,1:T(8,128)} %copy-done.99) | copy-start | bytes 12292
  258.2 20.4 %collective-permute-start.14 = (bf16[2,8,128,128]{3,2,1,0:T(8,128)(2,1)S(1)}, bf16[2,8,128,128]{3,2,1,0:T(8,128)(2,1)}, u32[]{:S(2)}, u32[]{:S(2)}) collective-permute-start(bf16[2,8,128,128]{3,2,1,0:T(8,128)(2,1)S(1)} %fusion.29), channel_id=1, source_target_pairs={{0,4},{4,8},{8,12},{12,16},{16,20},{20,24},{24,28},{28,32},{32,36}... | collective-permute-start | bytes 1572872 | tf_op jit(solution)/shard_map/ppermute | solution.py:27
  262.4 19.4 %collective-permute-start.10 = (bf16[2,8,128,128]{3,2,1,0:T(8,128)(2,1)}, bf16[2,8,128,128]{3,2,1,0:T(8,128)(2,1)}, u32[]{:S(2)}, u32[]{:S(2)}) collective-permute-start(bf16[2,8,128,128]{3,2,1,0:T(8,128)(2,1)} %fusion.26), channel_id=1, source_target_pairs={{4,0},{8,4},{12,8},{16,12},{20,16},{24,20},{28,24},{32,28},{36,32}... | collective-permute-start | bytes 1572872 | tf_op jit(solution)/shard_map/ppermute | solution.py:27
  263.8 14.8 %copy-start.31 = (f32[1,8,128,128]{3,2,1,0:T(8,128)S(1)}, f32[1,8,128,128]{3,2,1,0:T(8,128)}, u32[]{:S(2)}) copy-start(f32[1,8,128,128]{3,2,1,0:T(8,128)} %get-tuple-element.79) | copy-start | bytes 1572868
  263.8 14.8 %copy-start.42 = (f32[1,8,128,128]{3,2,1,0:T(8,128)S(1)}, f32[1,8,128,128]{3,2,1,0:T(8,128)}, u32[]{:S(2)}) copy-start(f32[1,8,128,128]{3,2,1,0:T(8,128)} %get-tuple-element.72) | copy-start | bytes 1572868
  265.2 16.7 %copy-start.30 = (f32[1,8,128,128]{3,2,1,0:T(8,128)S(1)}, f32[1,8,128,128]{3,2,1,0:T(8,128)}, u32[]{:S(2)}) copy-start(f32[1,8,128,128]{3,2,1,0:T(8,128)} %get-tuple-element.77) | copy-start | bytes 1572868
  265.2 16.7 %copy-start.41 = (f32[1,8,128,128]{3,2,1,0:T(8,128)S(1)}, f32[1,8,128,128]{3,2,1,0:T(8,128)}, u32[]{:S(2)}) copy-start(f32[1,8,128,128]{3,2,1,0:T(8,128)} %get-tuple-element.69) | copy-start | bytes 1572868
  265.4 19.1 %copy-start.3 = (f32[128,8,128]{2,0,1:T(8,128)S(1)}, f32[128,8,128]{2,0,1:T(8,128)}, u32[]{:S(2)}) copy-start(f32[128,8,128]{2,0,1:T(8,128)} %copy-done.2) | copy-start | bytes 1572868
  265.4 19.1 %copy-start.94 = (f32[128,8]{0,1:T(8,128)S(1)}, f32[128,8]{0,1:T(8,128)}, u32[]{:S(2)}) copy-start(f32[128,8]{0,1:T(8,128)} %get-tuple-element.212) | copy-start | bytes 12292
  279.8 10.1 %collective-permute-start.15 = (bf16[2,8,128,128]{3,2,1,0:T(8,128)(2,1)S(1)}, bf16[2,8,128,128]{3,2,1,0:T(8,128)(2,1)S(1)}, u32[]{:S(2)}, u32[]{:S(2)}) collective-permute-start(bf16[2,8,128,128]{3,2,1,0:T(8,128)(2,1)S(1)} %fusion.30), channel_id=1, source_target_pairs={{0,480},{4,484},{8,488},{12,492},{16,496},{20,500},{24,504},{28,50... | collective-permute-start | bytes 1572872 | tf_op jit(solution)/shard_map/ppermute | solution.py:27
  283.1 10.1 %collective-permute-start.11 = (bf16[2,8,128,128]{3,2,1,0:T(8,128)(2,1)S(1)}, bf16[2,8,128,128]{3,2,1,0:T(8,128)(2,1)S(1)}, u32[]{:S(2)}, u32[]{:S(2)}) collective-permute-start(bf16[2,8,128,128]{3,2,1,0:T(8,128)(2,1)S(1)} %fusion.27), channel_id=1, source_target_pairs={{4,0},{8,4},{12,8},{16,12},{20,16},{24,20},{28,24},{32,28},{36,32}... | collective-permute-start | bytes 1572872 | tf_op jit(solution)/shard_map/ppermute | solution.py:27
  (97 other events, 297.7 us)

commit v8 on v5

--- a/solution.py
+++ b/solution.py
@@ -95,11 +95,9 @@
     )
     query_rot = query_normalized.astype(jnp.bfloat16)
     value_flat = value_proj[0]
-    doc_rows = jnp.zeros((16, 2 * key_span_width), jnp.bfloat16)
-    doc_rows = doc_rows.at[0, :row_count].set(doc_row.astype(jnp.bfloat16))
-    packed = jnp.concatenate(
-        [jnp.concatenate([key_projection[0], value_flat], axis=1), doc_rows], axis=0
-    )
+    doc_columns = jnp.zeros((row_count, 128), jnp.bfloat16)
+    doc_columns = doc_columns.at[:, 0].set(doc_row.astype(jnp.bfloat16))
+    packed = jnp.concatenate([key_projection[0], value_flat, doc_columns], axis=1)
     half = behind // 2
     near, far = [], []
     a_slot, b_slot = packed, packed
@@ -110,9 +108,11 @@
         far.append(b_slot)
     stacked = jnp.stack(far + near[::-1] + [packed])
     width = (behind + 1) * row_count
-    key_raw_win = stacked[:, :row_count, :key_span_width].reshape(width, KEY_VALUE_HEADS, HEAD_SIZE)
-    value_win = stacked[:, :row_count, key_span_width:].reshape(width, KEY_VALUE_HEADS, HEAD_SIZE)
-    key_doc = stacked[:, row_count, :row_count].reshape(width).astype(jnp.int32)
+    key_raw_win = stacked[:, :, :key_span_width].reshape(width, KEY_VALUE_HEADS, HEAD_SIZE)
+    value_win = stacked[:, :, key_span_width:2 * key_span_width].reshape(
+        width, KEY_VALUE_HEADS, HEAD_SIZE
+    )
+    key_doc = stacked[:, :, 2 * key_span_width].reshape(width).astype(jnp.int32)
     key_pos = base - behind * row_count + jnp.arange(width, dtype=jnp.int32)
 
     def prepare_window(raw, gain):

time: 391 us -> 406 us (1.038)
  waiting for transfers between devices: 83.1 us -> 93.6 us
    ppermute x16, waiting for transfers between devices: 83.1 us -> 93.6 us  [shift(): return lax.ppermute(value, SEQ_AXES, pairs)]
    unnamed x103 -> x110, local copies, waits for them, and re-layouts: 18.7 us -> 20 us
where the time goes in v8:
time: 406 us; the launch traced here: 399 us
  blocking collectives  123 us (30%)
  waiting for transfers between devices  93.6 us (23%)
  starting transfers between devices  61.3 us (15%)
  other arithmetic  53.1 us (13%)
  local copies, waits for them, and re-layouts  37.3 us (9%)
  matrix products  28 us (7%)
    psum x5, blocking collectives, shards(): gains = lax.psum(gains, axis)  123 us
    ppermute x16, waiting for transfers between devices, shift(): return lax.ppermute(value, SEQ_AXES, pairs)  93.6 us
    ppermute x16, starting transfers between devices, shift(): return lax.ppermute(value, SEQ_AXES, pairs)  61.3 us
    unnamed x110, local copies, waits for them, and re-layouts  20 us
  transfers between devices with their start and end apart: 16, of which 8 were waited for; matrix products, arithmetic and copies ran while one was open for 10% of the time, Pallas kernels for 0%

profile of v8, /device:TPU:1, one launch (start us, length us, event | category | flops | bytes accessed | tf_op | source)
XLA Modules:
  0.0 398.5 jit_solution(10162232181078550958)
XLA Ops:
  2.7 1.9 fusion.32
  4.7 4.8 %collective-permute-start.4 = (bf16[128,2176]{1,0:T(8,128)(2,1)}, bf16[128,2176]{1,0:T(8,128)(2,1)}, u32[]{:S(2)}, u32[]{:S(2)}) collective-permute-start(bf16[128,2176]{1,0:T(8,128)(2,1)} %fusion.32), channel_id=1, source_target_pairs={{0,4},{4,8},{8,12},{12,16},{16,20},{20,24},{24,28},{28,32},{32,36}... | collective-permute-start | bytes 1671176 | tf_op jit(solution)/shard_map/ppermute | solution.py:27
  9.5 2.3 collective-permute-start
  21.7 2.1 multiply_cosine_fusion
  23.9 3.4 collective-permute-start.5
  27.2 20.0 %collective-permute-done = bf16[128,2176]{1,0:T(8,128)(2,1)} collective-permute-done((bf16[128,2176]{1,0:T(8,128)(2,1)}, bf16[128,2176]{1,0:T(8,128)(2,1)}, u32[]{:S(2)}, u32[]{:S(2)}) %collective-permute-start) | collective-permute-done | bytes 557088 | tf_op jit(solution)/shard_map/ppermute | solution.py:27
  47.2 1.9 collective-permute-start.1
  50.3 3.4 collective-permute-start.6
  53.7 14.5 %collective-permute-done.1 = bf16[128,2176]{1,0:T(8,128)(2,1)S(1)} collective-permute-done((bf16[128,2176]{1,0:T(8,128)(2,1)}, bf16[128,2176]{1,0:T(8,128)(2,1)S(1)}, u32[]{:S(2)}, u32[]{:S(2)}) %collective-permute-start.1) | collective-permute-done | bytes 557088 | tf_op jit(solution)/shard_map/ppermute | solution.py:27
  68.2 12.2 %collective-permute-start.2 = (bf16[128,2176]{1,0:T(8,128)(2,1)S(1)}, bf16[128,2176]{1,0:T(8,128)(2,1)S(1)}, u32[]{:S(2)}, u32[]{:S(2)}) collective-permute-start(bf16[128,2176]{1,0:T(8,128)(2,1)S(1)} %collective-permute-done.1), channel_id=1, source_target_pairs={{0,508},{4,0},{8,4},{12,8},{16,12},{20,16},{24,20},{28,24},{32,28}... | collective-permute-start | bytes 1671176 | tf_op jit(solution)/shard_map/ppermute | solution.py:27
  81.8 12.2 %collective-permute-done.2 = bf16[128,2176]{1,0:T(8,128)(2,1)S(1)} collective-permute-done((bf16[128,2176]{1,0:T(8,128)(2,1)S(1)}, bf16[128,2176]{1,0:T(8,128)(2,1)S(1)}, u32[]{:S(2)}, u32[]{:S(2)}) %collective-permute-start.2) | collective-permute-done | bytes 557088 | tf_op jit(solution)/shard_map/ppermute | solution.py:27
  94.0 12.5 %collective-permute-start.3 = (bf16[128,2176]{1,0:T(8,128)(2,1)S(1)}, bf16[128,2176]{1,0:T(8,128)(2,1)S(1)}, u32[]{:S(2)}, u32[]{:S(2)}) collective-permute-start(bf16[128,2176]{1,0:T(8,128)(2,1)S(1)} %collective-permute-done.2), channel_id=1, source_target_pairs={{0,508},{4,0},{8,4},{12,8},{16,12},{20,16},{24,20},{28,24},{32,28}... | collective-permute-start | bytes 1671176 | tf_op jit(solution)/shard_map/ppermute | solution.py:27
  106.6 8.6 %collective-permute-done.3 = bf16[128,2176]{1,0:T(8,128)(2,1)S(1)} collective-permute-done((bf16[128,2176]{1,0:T(8,128)(2,1)S(1)}, bf16[128,2176]{1,0:T(8,128)(2,1)S(1)}, u32[]{:S(2)}, u32[]{:S(2)}) %collective-permute-start.3) | collective-permute-done | bytes 557088 | tf_op jit(solution)/shard_map/ppermute | solution.py:27
  118.3 3.4 copy.182
  122.3 3.2 copy.159
  125.5 3.7 multiply_reduce_fusion.1
  129.5 4.1 %fusion.4 = f32[1152,8,128]{2,0,1:T(8,128)S(1)} fusion(f32[1152,8,128]{2,1,0:T(8,128)} %bitcast.165, f32[128]{0:T(128)S(1)} %copy-done.36, f32[1152,8]{0,1:T(8,128)S(1)} %add_rsqrt_fusion), kind=kLoop, calls=%fused_computation.17 | loop fusion | flops 2359296 | bytes 9474560 | tf_op jit(solution)/shard_map/jvp()/mul | solution.py:45
  133.7 1.8 subtract_convert_fusion
  136.7 3.3 fusion.3
  140.0 3.6 copy-done.42
  143.7 3.4 fusion.10
  147.1 1.8 copy.166
  148.8 8.0 %fusion.5 = f32[8,1152,128,1]{2,1,3,0:T(8,128)} fusion(bf16[128,8,2,128]{3,2,1,0:T(2,128)(2,1)} %reshape_squeeze.4, f32[8,1152,128,2]{2,1,3,0:T(8,128)} %copy-done.42, f32[8,2,128]{2,1,0:T(2,128)} %copy-done.43, pred[128,1152]{0,1:T(8,128)(4,1)S(1)} %fusion.31), kind=kOutput, calls=%fused_computation.20 | convolution fusion | flops 613416960 | bytes 14835712 | tf_op jit(solution)/shard_map/grtw,tgrd->gwd/dot_general | solution.py:71
  156.8 2.0 multiply_reduce_fusion.2
  160.0 6.5 %fusion.1 = bf16[8,2,128,1152]{2,3,1,0:T(8,128)(2,1)S(1)} fusion(bf16[1152,8,128,1]{0,2,3,1:T(8,128)(2,1)S(1)} %copy-done.13, f32[8,2,128]{2,1,0:T(2,128)S(1)} %copy.167, bf16[128,8,2,128]{3,2,1,0:T(2,128)(2,1)} %reshape_squeeze.4, f32[8,2,128]{2,1,0:T(2,128)} %copy-done.43, f32[8,1152,128,2]{2,1,3,0:T(8,128)} %copy-done.42, pred[128,1152]{0,1:T(8,128)(4,1)S(1)} %fusion.31), kind=kOutput, calls=%fused_computation.2 | convolution fusion | flops 618135552 | bytes 17203200 | tf_op jit(solution)/shard_map/tgrd,wgd->grtw/dot_general | solution.py:61
  168.8 2.7 copy_dynamic-update-slice_fusion.1
  171.6 2.7 copy_dynamic-update-slice_fusion
  179.9 4.2 %collective-permute-start.12 = (bf16[2,8,128,128]{3,1,2,0:T(8,128)(2,1)}, bf16[2,8,128,128]{3,1,2,0:T(8,128)(2,1)}, u32[]{:S(2)}, u32[]{:S(2)}) collective-permute-start(bf16[2,8,128,128]{3,1,2,0:T(8,128)(2,1)} %get-tuple-element.44), channel_id=1, source_target_pairs={{0,4},{4,8},{8,12},{12,16},{16,20},{20,24},{24,28},{28,32},{32,36}... | collective-permute-start | bytes 1572872 | tf_op jit(solution)/shard_map/ppermute | solution.py:27
  184.1 6.3 %multiply_add_fusion.1 = (f32[1152,8,64]{2,0,1:T(8,128)}, f32[1152,8,64]{2,0,1:T(8,128)}) fusion(f32[1152,8,128]{2,0,1:T(8,128)S(1)} %bitcast.167, f32[1152,64]{1,0:T(8,128)} %copy-done.8, f32[1152,64]{1,0:T(8,128)} %copy-done.7), kind=kLoop, calls=%fused_computation.13 | loop fusion | flops 4128768 | bytes 10027008 | tf_op jit(solution)/shard_map/transpose(jvp())/add_any | solution.py:39
  190.4 10.6 %collective-permute-done.12 = bf16[2,8,128,128]{3,1,2,0:T(8,128)(2,1)} collective-permute-done((bf16[2,8,128,128]{3,1,2,0:T(8,128)(2,1)}, bf16[2,8,128,128]{3,1,2,0:T(8,128)(2,1)}, u32[]{:S(2)}, u32[]{:S(2)}) %collective-permute-start.12) | collective-permute-done | bytes 524320 | tf_op jit(solution)/shard_map/ppermute | solution.py:27
  203.7 4.0 %collective-permute-start.13 = (bf16[2,8,128,128]{3,1,2,0:T(8,128)(2,1)S(1)}, bf16[2,8,128,128]{3,1,2,0:T(8,128)(2,1)}, u32[]{:S(2)}, u32[]{:S(2)}) collective-permute-start(bf16[2,8,128,128]{3,1,2,0:T(8,128)(2,1)S(1)} %get-tuple-element.36), channel_id=1, source_target_pairs={{0,4},{4,8},{8,12},{12,16},{16,20},{20,24},{24,28},{28,32},{32,36}... | collective-permute-start | bytes 1572872 | tf_op jit(solution)/shard_map/ppermute | solution.py:27
  207.7 5.3 %convolution_multiply_fusion = f32[8,128,2,128]{3,1,2,0:T(8,128)S(1)} fusion(bf16[8,2,128,1152]{2,3,1,0:T(8,128)(2,1)} %copy-done.3, bf16[1152,8,64]{2,0,1:T(8,128)(2,1)} %copy-done.6, bf16[1152,8,64]{2,0,1:T(8,128)(2,1)S(1)} %copy-done.5), kind=kOutput, calls=%fused_computation.28 | convolution fusion | flops 608960512 | bytes 8126464 | tf_op jit(solution)/shard_map/grtw,wgd->tgrd/dot_general | solution.py:65
  216.0 12.2 %collective-permute-done.13 = bf16[2,8,128,128]{3,1,2,0:T(8,128)(2,1)} collective-permute-done((bf16[2,8,128,128]{3,1,2,0:T(8,128)(2,1)S(1)}, bf16[2,8,128,128]{3,1,2,0:T(8,128)(2,1)}, u32[]{:S(2)}, u32[]{:S(2)}) %collective-permute-start.13) | collective-permute-done | bytes 524320 | tf_op jit(solution)/shard_map/ppermute | solution.py:27
  228.2 2.9 fusion.24
  232.4 4.0 %collective-permute-start.14 = (bf16[2,8,128,128]{3,1,2,0:T(8,128)(2,1)}, bf16[2,8,128,128]{3,1,2,0:T(8,128)(2,1)}, u32[]{:S(2)}, u32[]{:S(2)}) collective-permute-start(bf16[2,8,128,128]{3,1,2,0:T(8,128)(2,1)} %get-tuple-element.34), channel_id=1, source_target_pairs={{0,4},{4,8},{8,12},{12,16},{16,20},{20,24},{24,28},{28,32},{32,36}... | collective-permute-start | bytes 1572872 | tf_op jit(solution)/shard_map/ppermute | solution.py:27
  237.9 3.5 collective-permute-done.10
  241.4 12.0 %collective-permute-done.14 = bf16[2,8,128,128]{3,1,2,0:T(8,128)(2,1)} collective-permute-done((bf16[2,8,128,128]{3,1,2,0:T(8,128)(2,1)}, bf16[2,8,128,128]{3,1,2,0:T(8,128)(2,1)}, u32[]{:S(2)}, u32[]{:S(2)}) %collective-permute-start.14) | collective-permute-done | bytes 524320 | tf_op jit(solution)/shard_map/ppermute | solution.py:27
  253.4 3.0 fusion.22
  257.7 1.9 collective-permute-start.15
  259.7 1.8 fusion.14
  261.4 2.1 reshape.283
  263.5 6.5 %multiply_reduce_fusion = f32[128]{0:T(128)S(1)} fusion(f32[1152,8,64]{2,0,1:T(8,128)} %get-tuple-element.38, f32[1152,8,64]{2,0,1:T(8,128)} %get-tuple-element.37, f32[1152,8,128]{2,1,0:T(8,128)} %bitcast.166, f32[1152,8]{0,1:T(8,128)S(1)} %copy-done.28), kind=kLoop, calls=%fused_computation.11 | loop fusion | flops 4718464 | bytes 9474560 | tf_op jit(solution)/shard_map/transpose(jvp())/reduce_sum | solution.py:45
  270.0 12.9 %all-reduce.7 = (f32[128]{0:T(128)S(1)}, f32[128]{0:T(128)S(1)}) all-reduce(f32[128]{0:T(128)S(1)} %get-tuple-element.17, f32[128]{0:T(128)S(1)} %multiply_reduce_fusion), channel_id=1, replica_groups=mesh['zh'=4,'x'=4,'y'=8,'zl'=2,'c'=2] {'y'}, use_global_device_ids=true, to_apply=%region_8.9 | all-reduce | flops 256 | bytes 2048 | tf_op jit(solution)/shard_map/psum | solution.py:159
  282.9 43.2 %all-reduce.8 = (f32[128]{0:T(128)S(1)}, f32[128]{0:T(128)S(1)}) all-reduce(f32[128]{0:T(128)S(1)} %get-tuple-element.21, f32[128]{0:T(128)S(1)} %get-tuple-element.22), channel_id=1, replica_groups=mesh['zh'=4,'x'=4,'y'=8,'zl'=2,'c'=2] {'x'}, use_global_device_ids=true, to_apply=%region_9.10 | all-reduce | flops 256 | bytes 2048 | tf_op jit(solution)/shard_map/psum | solution.py:159
  326.1 40.0 %all-reduce.9 = (f32[128]{0:T(128)S(1)}, f32[128]{0:T(128)S(1)}) all-reduce(f32[128]{0:T(128)S(1)} %get-tuple-element.23, f32[128]{0:T(128)S(1)} %get-tuple-element.24), channel_id=1, replica_groups=mesh['zh'=4,'x'=4,'y'=8,'zl'=2,'c'=2] {'zh'}, use_global_device_ids=true, to_apply=%region_10.11 | all-reduce | flops 256 | bytes 2048 | tf_op jit(solution)/shard_map/psum | solution.py:159
  366.1 3.8 all-reduce.11
  369.8 23.5 %all-reduce.10 = (f32[128]{0:T(128)}, f32[128]{0:T(128)}) all-reduce(f32[128]{0:T(128)S(1)} %get-tuple-element.29, f32[128]{0:T(128)S(1)} %get-tuple-element.30), channel_id=1, replica_groups=mesh['zh'=4,'x'=4,'y'=8,'zl'=2,'c'=2] {'c'}, use_global_device_ids=true, to_apply=%region_12.13 | all-reduce | flops 256 | bytes 2048 | tf_op jit(solution)/shard_map/psum | solution.py:159
  393.3 1.7 fusion.28
  (171 shorter events, 41.4 us)
Async XLA Ops:
  0.6 15.6 %copy-start.38 = (f32[128]{0:T(128)S(1)}, f32[128]{0:T(128)}, u32[]{:S(2)}) copy-start(f32[128]{0:T(128)} %param.14) | copy-start | bytes 1540
  2.7 11.2 %copy-start.29 = (bf16[128,1]{1,0:T(8,128)(2,1)}, bf16[128,1]{1,0:T(8,128)(2,1)S(1)}, u32[]{:S(2)}) copy-start(bf16[128,1]{1,0:T(8,128)(2,1)S(1)} %copy.181) | copy-start | bytes 772
  4.7 19.2 %collective-permute-start.4 = (bf16[128,2176]{1,0:T(8,128)(2,1)}, bf16[128,2176]{1,0:T(8,128)(2,1)}, u32[]{:S(2)}, u32[]{:S(2)}) collective-permute-start(bf16[128,2176]{1,0:T(8,128)(2,1)} %fusion.32), channel_id=1, source_target_pairs={{0,4},{4,8},{8,12},{12,16},{16,20},{20,24},{24,28},{28,32},{32,36}... | collective-permute-start | bytes 1671176 | tf_op jit(solution)/shard_map/ppermute | solution.py:27
  9.5 37.7 %collective-permute-start = (bf16[128,2176]{1,0:T(8,128)(2,1)}, bf16[128,2176]{1,0:T(8,128)(2,1)}, u32[]{:S(2)}, u32[]{:S(2)}) collective-permute-start(bf16[128,2176]{1,0:T(8,128)(2,1)} %fusion.32), channel_id=1, source_target_pairs={{0,32},{4,36},{8,40},{12,44},{16,48},{20,52},{24,56},{28,60},{32,6... | collective-permute-start | bytes 1671176 | tf_op jit(solution)/shard_map/ppermute | solution.py:27
  15.3 5.4 %copy-start.1 = (f32[16,8,16,128]{3,2,1,0:T(8,128)}, f32[16,8,16,128]{3,2,1,0:T(8,128)S(1)}, u32[]{:S(2)}) copy-start(f32[16,8,16,128]{3,2,1,0:T(8,128)S(1)} %copy.183) | copy-start | bytes 3145732
  23.8 109.8 %copy-start.7 = (f32[1152,64]{1,0:T(8,128)}, f32[1152,64]{1,0:T(8,128)S(1)}, u32[]{:S(2)}) copy-start(f32[1152,64]{1,0:T(8,128)S(1)} %get-tuple-element.53) | copy-start | bytes 884740
  23.8 109.8 %copy-start.8 = (f32[1152,64]{1,0:T(8,128)}, f32[1152,64]{1,0:T(8,128)S(1)}, u32[]{:S(2)}) copy-start(f32[1152,64]{1,0:T(8,128)S(1)} %get-tuple-element.54) | copy-start | bytes 884740
  23.8 92.7 %copy-start.12 = (bf16[1,128,1024]{2,1,0:T(8,128)(2,1)S(1)}, bf16[1,128,1024]{2,1,0:T(8,128)(2,1)}, u32[]{:S(2)}) copy-start(bf16[1,128,1024]{2,1,0:T(8,128)(2,1)} %param.10) | copy-start | bytes 786436
  23.8 92.7 %copy-start.25 = (bf16[1,128,1024]{2,1,0:T(8,128)(2,1)S(1)}, bf16[1,128,1024]{2,1,0:T(8,128)(2,1)}, u32[]{:S(2)}) copy-start(bf16[1,128,1024]{2,1,0:T(8,128)(2,1)} %param.11) | copy-start | bytes 786436
  23.8 92.7 %copy-start.30 = (bf16[128,1]{1,0:T(8,128)(2,1)S(1)}, bf16[128,1]{1,0:T(8,128)(2,1)}, u32[]{:S(2)}) copy-start(bf16[128,1]{1,0:T(8,128)(2,1)} %copy-done.29) | copy-start | bytes 772
  23.9 26.4 %collective-permute-start.5 = (bf16[128,2176]{1,0:T(8,128)(2,1)}, bf16[128,2176]{1,0:T(8,128)(2,1)S(1)}, u32[]{:S(2)}, u32[]{:S(2)}) collective-permute-start(bf16[128,2176]{1,0:T(8,128)(2,1)} %collective-permute-done.4), channel_id=1, source_target_pairs={{0,4},{4,8},{8,12},{12,16},{16,20},{20,24},{24,28},{28,32},{32,36}... | collective-permute-start | bytes 1671176 | tf_op jit(solution)/shard_map/ppermute | solution.py:27
  47.2 20.9 %collective-permute-start.1 = (bf16[128,2176]{1,0:T(8,128)(2,1)}, bf16[128,2176]{1,0:T(8,128)(2,1)S(1)}, u32[]{:S(2)}, u32[]{:S(2)}) collective-permute-start(bf16[128,2176]{1,0:T(8,128)(2,1)} %collective-permute-done), channel_id=1, source_target_pairs={{0,508},{4,0},{8,4},{12,8},{16,12},{20,16},{24,20},{28,24},{32,28}... | collective-permute-start | bytes 1671176 | tf_op jit(solution)/shard_map/ppermute | solution.py:27
  50.3 30.2 %collective-permute-start.6 = (bf16[128,2176]{1,0:T(8,128)(2,1)S(1)}, bf16[128,2176]{1,0:T(8,128)(2,1)S(1)}, u32[]{:S(2)}, u32[]{:S(2)}) collective-permute-start(bf16[128,2176]{1,0:T(8,128)(2,1)S(1)} %collective-permute-done.5), channel_id=1, source_target_pairs={{0,4},{4,8},{8,12},{12,16},{16,20},{20,24},{24,28},{28,32},{32,36}... | collective-permute-start | bytes 1671176 | tf_op jit(solution)/shard_map/ppermute | solution.py:27
  68.2 25.8 %collective-permute-start.2 = (bf16[128,2176]{1,0:T(8,128)(2,1)S(1)}, bf16[128,2176]{1,0:T(8,128)(2,1)S(1)}, u32[]{:S(2)}, u32[]{:S(2)}) collective-permute-start(bf16[128,2176]{1,0:T(8,128)(2,1)S(1)} %collective-permute-done.1), channel_id=1, source_target_pairs={{0,508},{4,0},{8,4},{12,8},{16,12},{20,16},{24,20},{28,24},{32,28}... | collective-permute-start | bytes 1671176 | tf_op jit(solution)/shard_map/ppermute | solution.py:27
  80.4 34.8 %collective-permute-start.7 = (bf16[128,2176]{1,0:T(8,128)(2,1)S(1)}, bf16[128,2176]{1,0:T(8,128)(2,1)S(1)}, u32[]{:S(2)}, u32[]{:S(2)}) collective-permute-start(bf16[128,2176]{1,0:T(8,128)(2,1)S(1)} %collective-permute-done.6), channel_id=1, source_target_pairs={{0,4},{4,8},{8,12},{12,16},{16,20},{20,24},{24,28},{28,32},{32,36}... | collective-permute-start | bytes 1671176 | tf_op jit(solution)/shard_map/ppermute | solution.py:27
  94.0 21.2 %collective-permute-start.3 = (bf16[128,2176]{1,0:T(8,128)(2,1)S(1)}, bf16[128,2176]{1,0:T(8,128)(2,1)S(1)}, u32[]{:S(2)}, u32[]{:S(2)}) collective-permute-start(bf16[128,2176]{1,0:T(8,128)(2,1)S(1)} %collective-permute-done.2), channel_id=1, source_target_pairs={{0,508},{4,0},{8,4},{12,8},{16,12},{20,16},{24,20},{28,24},{32,28}... | collective-permute-start | bytes 1671176 | tf_op jit(solution)/shard_map/ppermute | solution.py:27
  122.3 7.2 %copy-start.36 = (f32[128]{0:T(128)S(1)}, f32[128]{0:T(128)}, u32[]{:S(2)}) copy-start(f32[128]{0:T(128)} %param.15) | copy-start | bytes 1540
  129.5 4.2 %copy-start.27 = (f32[1152,8]{0,1:T(8,128)}, f32[1152,8]{0,1:T(8,128)S(1)}, u32[]{:S(2)}) copy-start(f32[1152,8]{0,1:T(8,128)S(1)} %add_rsqrt_fusion) | copy-start | bytes 110596
  133.7 3.0 copy-start.15
  135.5 4.5 %copy-start.4 = (bf16[1152,8,64]{2,0,1:T(8,128)(2,1)}, bf16[1152,8,64]{2,0,1:T(8,128)(2,1)S(1)}, u32[]{:S(2)}) copy-start(bf16[1152,8,64]{2,0,1:T(8,128)(2,1)S(1)} %get-tuple-element.39) | copy-start | bytes 3538948
  135.5 4.5 %copy-start.6 = (bf16[1152,8,64]{2,0,1:T(8,128)(2,1)}, bf16[1152,8,64]{2,0,1:T(8,128)(2,1)S(1)}, u32[]{:S(2)}) copy-start(bf16[1152,8,64]{2,0,1:T(8,128)(2,1)S(1)} %get-tuple-element.40) | copy-start | bytes 3538948
  136.7 7.0 %copy-start.13 = (bf16[1152,8,128,1]{0,2,3,1:T(8,128)(2,1)S(1)}, bf16[1152,8,128,1]{0,2,3,1:T(8,128)(2,1)}, u32[]{:S(2)}) copy-start(bf16[1152,8,128,1]{0,2,3,1:T(8,128)(2,1)} %copy.159) | copy-start | bytes 7077892
  140.0 3.6 copy-start.42
  140.0 3.6 copy-start.43
  148.8 8.0 %copy-start.14 = (bf16[128,8,2,128]{3,2,1,0:T(2,128)(2,1)S(1)}, bf16[128,8,2,128]{3,2,1,0:T(2,128)(2,1)}, u32[]{:S(2)}) copy-start(bf16[128,8,2,128]{3,2,1,0:T(2,128)(2,1)} %reshape_squeeze.4) | copy-start | bytes 1572868
  160.0 6.6 %copy-start.16 = (bf16[128,16,64]{2,0,1:T(8,128)(2,1)S(1)}, bf16[128,16,64]{2,0,1:T(8,128)(2,1)}, u32[]{:S(2)}) copy-start(bf16[128,16,64]{2,0,1:T(8,128)(2,1)} %copy.136) | copy-start | bytes 786436
  160.0 6.6 %copy-start.18 = (bf16[128,16,64]{2,0,1:T(8,128)(2,1)S(1)}, bf16[128,16,64]{2,0,1:T(8,128)(2,1)}, u32[]{:S(2)}) copy-start(bf16[128,16,64]{2,0,1:T(8,128)(2,1)} %copy.137) | copy-start | bytes 786436
  174.3 26.7 %copy-start = (f32[2,8,9,128,128]{4,1,3,0,2:T(8,128)}, f32[2,8,9,128,128]{4,1,3,0,2:T(8,128)S(1)}, u32[]{:S(2)}) copy-start(f32[2,8,9,128,128]{4,1,3,0,2:T(8,128)S(1)} %copy_dynamic-update-slice_fusion) | copy-start | bytes 28311556
  178.6 11.8 %collective-permute-start.8 = (bf16[2,8,128,128]{3,1,2,0:T(8,128)(2,1)}, bf16[2,8,128,128]{3,1,2,0:T(8,128)(2,1)}, u32[]{:S(2)}, u32[]{:S(2)}) collective-permute-start(bf16[2,8,128,128]{3,1,2,0:T(8,128)(2,1)} %get-tuple-element.43), channel_id=1, source_target_pairs={{4,0},{8,4},{12,8},{16,12},{20,16},{24,20},{28,24},{32,28},{36,32}... | collective-permute-start | bytes 1572872 | tf_op jit(solution)/shard_map/ppermute | solution.py:27
  179.9 21.1 %collective-permute-start.12 = (bf16[2,8,128,128]{3,1,2,0:T(8,128)(2,1)}, bf16[2,8,128,128]{3,1,2,0:T(8,128)(2,1)}, u32[]{:S(2)}, u32[]{:S(2)}) collective-permute-start(bf16[2,8,128,128]{3,1,2,0:T(8,128)(2,1)} %get-tuple-element.44), channel_id=1, source_target_pairs={{0,4},{4,8},{8,12},{12,16},{16,20},{20,24},{24,28},{28,32},{32,36}... | collective-permute-start | bytes 1572872 | tf_op jit(solution)/shard_map/ppermute | solution.py:27
  190.4 17.3 %copy-start.5 = (bf16[1152,8,64]{2,0,1:T(8,128)(2,1)S(1)}, bf16[1152,8,64]{2,0,1:T(8,128)(2,1)}, u32[]{:S(2)}) copy-start(bf16[1152,8,64]{2,0,1:T(8,128)(2,1)} %copy-done.4) | copy-start | bytes 3538948
  202.4 13.6 %collective-permute-start.9 = (bf16[2,8,128,128]{3,1,2,0:T(8,128)(2,1)S(1)}, bf16[2,8,128,128]{3,1,2,0:T(8,128)(2,1)S(1)}, u32[]{:S(2)}, u32[]{:S(2)}) collective-permute-start(bf16[2,8,128,128]{3,1,2,0:T(8,128)(2,1)S(1)} %get-tuple-element.35), channel_id=1, source_target_pairs={{4,0},{8,4},{12,8},{16,12},{20,16},{24,20},{28,24},{32,28},{36,32}... | collective-permute-start | bytes 1572872 | tf_op jit(solution)/shard_map/ppermute | solution.py:27
  203.7 24.5 %collective-permute-start.13 = (bf16[2,8,128,128]{3,1,2,0:T(8,128)(2,1)S(1)}, bf16[2,8,128,128]{3,1,2,0:T(8,128)(2,1)}, u32[]{:S(2)}, u32[]{:S(2)}) collective-permute-start(bf16[2,8,128,128]{3,1,2,0:T(8,128)(2,1)S(1)} %get-tuple-element.36), channel_id=1, source_target_pairs={{0,4},{4,8},{8,12},{12,16},{16,20},{20,24},{24,28},{28,32},{32,36}... | collective-permute-start | bytes 1572872 | tf_op jit(solution)/shard_map/ppermute | solution.py:27
  213.0 23.5 %copy-start.22 = (f32[128,64]{1,0:T(8,128)S(1)}, f32[128,64]{1,0:T(8,128)}, u32[]{:S(2)}) copy-start(f32[128,64]{1,0:T(8,128)} %copy-done.21) | copy-start | bytes 98308
  213.0 23.5 %copy-start.24 = (f32[128,64]{1,0:T(8,128)S(1)}, f32[128,64]{1,0:T(8,128)}, u32[]{:S(2)}) copy-start(f32[128,64]{1,0:T(8,128)} %copy-done.23) | copy-start | bytes 98308
  214.6 22.2 %copy-start.2 = (f32[16,8,16,128]{3,2,1,0:T(8,128)S(1)}, f32[16,8,16,128]{3,2,1,0:T(8,128)}, u32[]{:S(2)}) copy-start(f32[16,8,16,128]{3,2,1,0:T(8,128)} %copy-done.1) | copy-start | bytes 3145732
  214.6 22.2 %copy-start.20 = (f32[128,16]{1,0:T(8,128)S(1)}, f32[128,16]{1,0:T(8,128)}, u32[]{:S(2)}) copy-start(f32[128,16]{1,0:T(8,128)} %copy-done.19) | copy-start | bytes 24580
  214.6 22.2 %copy-start.39 = (f32[128]{0:T(128)S(1)}, f32[128]{0:T(128)}, u32[]{:S(2)}) copy-start(f32[128]{0:T(128)} %param.14) | copy-start | bytes 1540
  216.0 20.5 %copy-start.10 = (f32[128,16,64]{2,1,0:T(8,128)S(1)}, f32[128,16,64]{2,1,0:T(8,128)}, u32[]{:S(2)}) copy-start(f32[128,16,64]{2,1,0:T(8,128)} %copy.178) | copy-start | bytes 1572868
  216.0 20.5 %copy-start.11 = (f32[128,16,64]{2,1,0:T(8,128)S(1)}, f32[128,16,64]{2,1,0:T(8,128)}, u32[]{:S(2)}) copy-start(f32[128,16,64]{2,1,0:T(8,128)} %copy.179) | copy-start | bytes 1572868
  231.0 6.7 %copy-start.32 = (f32[128,16]{0,1:T(8,128)S(1)}, f32[128,16]{0,1:T(8,128)}, u32[]{:S(2)}) copy-start(f32[128,16]{0,1:T(8,128)} %copy-done.31) | copy-start | bytes 24580
  231.0 10.4 %collective-permute-start.10 = (bf16[2,8,128,128]{3,1,2,0:T(8,128)(2,1)}, bf16[2,8,128,128]{3,1,2,0:T(8,128)(2,1)}, u32[]{:S(2)}, u32[]{:S(2)}) collective-permute-start(bf16[2,8,128,128]{3,1,2,0:T(8,128)(2,1)} %get-tuple-element.33), channel_id=1, source_target_pairs={{4,0},{8,4},{12,8},{16,12},{20,16},{24,20},{28,24},{32,28},{36,32}... | collective-permute-start | bytes 1572872 | tf_op jit(solution)/shard_map/ppermute | solution.py:27
  232.4 21.0 %collective-permute-start.14 = (bf16[2,8,128,128]{3,1,2,0:T(8,128)(2,1)}, bf16[2,8,128,128]{3,1,2,0:T(8,128)(2,1)}, u32[]{:S(2)}, u32[]{:S(2)}) collective-permute-start(bf16[2,8,128,128]{3,1,2,0:T(8,128)(2,1)} %get-tuple-element.34), channel_id=1, source_target_pairs={{0,4},{4,8},{8,12},{12,16},{16,20},{20,24},{24,28},{28,32},{32,36}... | collective-permute-start | bytes 1572872 | tf_op jit(solution)/shard_map/ppermute | solution.py:27
  237.7 25.8 %copy-start.28 = (f32[1152,8]{0,1:T(8,128)S(1)}, f32[1152,8]{0,1:T(8,128)}, u32[]{:S(2)}) copy-start(f32[1152,8]{0,1:T(8,128)} %copy-done.27) | copy-start | bytes 110596
  256.5 136.8 %collective-permute-start.11 = (bf16[2,8,128,128]{3,1,2,0:T(8,128)(2,1)}, bf16[2,8,128,128]{3,1,2,0:T(8,128)(2,1)}, u32[]{:S(2)}, u32[]{:S(2)}) collective-permute-start(bf16[2,8,128,128]{3,1,2,0:T(8,128)(2,1)} %get-tuple-element.31), channel_id=1, source_target_pairs={{4,0},{8,4},{12,8},{16,12},{20,16},{24,20},{28,24},{32,28},{36,32}... | collective-permute-start | bytes 1572872 | tf_op jit(solution)/shard_map/ppermute | solution.py:27
  257.7 135.6 %collective-permute-start.15 = (bf16[2,8,128,128]{3,1,2,0:T(8,128)(2,1)}, bf16[2,8,128,128]{3,1,2,0:T(8,128)(2,1)}, u32[]{:S(2)}, u32[]{:S(2)}) collective-permute-start(bf16[2,8,128,128]{3,1,2,0:T(8,128)(2,1)} %get-tuple-element.32), channel_id=1, source_target_pairs={{0,480},{4,484},{8,488},{12,492},{16,496},{20,500},{24,504},{28,50... | collective-permute-start | bytes 1572872 | tf_op jit(solution)/shard_map/ppermute | solution.py:27
  270.0 126.2 %copy-start.9 = (f32[16,8,8,128]{3,2,1,0:T(8,128)S(1)}, f32[16,8,8,128]{3,2,1,0:T(8,128)}, u32[]{:S(2)}) copy-start(f32[16,8,8,128]{3,2,1,0:T(8,128)} %copy.185) | copy-start | bytes 1572868
  270.0 126.2 %copy-start.37 = (f32[128]{0:T(128)S(1)}, f32[128]{0:T(128)}, u32[]{:S(2)}) copy-start(f32[128]{0:T(128)} %param.15) | copy-start | bytes 1540
  (14 other events, 26.2 us)

commit v9 on v5

--- a/solution.py
+++ b/solution.py
@@ -155,7 +155,7 @@
         carry_far = (got + slots[:, :, behind - offset]).astype(jnp.bfloat16)
     sent = [shift(carry_near, -1, False), shift(carry_far, -behind, True)]
     gains = (query_gain_gradient, key_gain_gradient)
-    for axis in ("y", "x", "zh", "zl", "c"):
+    for axis in ("c", "zl", "y", "x", "zh"):
         gains = lax.psum(gains, axis)
     gain_query, gain_key = gains
     total = slots[:, :, behind]

time: 391 us -> 399 us (1.020)
  the two profiles are of different devices: /device:TPU:1 before, /device:TPU:2 now
where the time goes in v9:
time: 399 us; the launch traced here: 391 us
  blocking collectives  116 us (29%)
  starting transfers between devices  88.7 us (22%)
  waiting for transfers between devices  68.9 us (17%)
  other arithmetic  50.9 us (13%)
  local copies, waits for them, and re-layouts  37 us (9%)
  matrix products  27.9 us (7%)
    psum x5, blocking collectives, shards(): gains = lax.psum(gains, axis)  116 us
    ppermute x16, starting transfers between devices, shift(): return lax.ppermute(value, SEQ_AXES, pairs)  88.7 us
    ppermute x16, waiting for transfers between devices, shift(): return lax.ppermute(value, SEQ_AXES, pairs)  68.9 us
    unnamed x103, local copies, waits for them, and re-layouts  18.7 us
    dot_general x1, matrix products, attend(): jnp.einsum('grtw,tgrd->gwd', weights_b, gradient_block, preferred_element...  7.99 us
  transfers between devices with their start and end apart: 16, of which 11 were waited for; matrix products, arithmetic and copies ran while one was open for 10% of the time, Pallas kernels for 0%

profile of v9, /device:TPU:2, one launch (start us, length us, event | category | flops | bytes accessed | tf_op | source)
XLA Modules:
  0.0 391.1 jit_solution(10049692266502726247)
XLA Ops:
  2.4 3.5 collective-permute-start.4
  5.9 3.4 collective-permute-start
  10.8 2.2 reshape_squeeze.4
  18.9 15.3 %collective-permute-done = bf16[144,2048]{1,0:T(8,128)(2,1)} collective-permute-done((bf16[144,2048]{1,0:T(8,128)(2,1)S(1)}, bf16[144,2048]{1,0:T(8,128)(2,1)}, u32[]{:S(2)}, u32[]{:S(2)}) %collective-permute-start) | collective-permute-done | bytes 589856 | tf_op jit(solution)/shard_map/ppermute | solution.py:27
  36.7 3.9 collective-permute-start.5
  40.6 2.1 multiply_cosine_fusion
  42.8 8.8 %collective-permute-done.1 = bf16[144,2048]{1,0:T(8,128)(2,1)S(1)} collective-permute-done((bf16[144,2048]{1,0:T(8,128)(2,1)}, bf16[144,2048]{1,0:T(8,128)(2,1)S(1)}, u32[]{:S(2)}, u32[]{:S(2)}) %collective-permute-start.1) | collective-permute-done | bytes 589856 | tf_op jit(solution)/shard_map/ppermute | solution.py:27
  51.6 4.3 %collective-permute-start.2 = (bf16[144,2048]{1,0:T(8,128)(2,1)S(1)}, bf16[144,2048]{1,0:T(8,128)(2,1)S(1)}, u32[]{:S(2)}, u32[]{:S(2)}) collective-permute-start(bf16[144,2048]{1,0:T(8,128)(2,1)S(1)} %collective-permute-done.1), channel_id=1, source_target_pairs={{0,508},{4,0},{8,4},{12,8},{16,12},{20,16},{24,20},{28,24},{32,28}... | collective-permute-start | bytes 1769480 | tf_op jit(solution)/shard_map/ppermute | solution.py:27
  56.5 2.0 collective-permute-start.6
  59.6 8.4 %collective-permute-done.2 = bf16[144,2048]{1,0:T(8,128)(2,1)S(1)} collective-permute-done((bf16[144,2048]{1,0:T(8,128)(2,1)S(1)}, bf16[144,2048]{1,0:T(8,128)(2,1)S(1)}, u32[]{:S(2)}, u32[]{:S(2)}) %collective-permute-start.2) | collective-permute-done | bytes 589856 | tf_op jit(solution)/shard_map/ppermute | solution.py:27
  68.1 6.5 %collective-permute-start.3 = (bf16[144,2048]{1,0:T(8,128)(2,1)S(1)}, bf16[144,2048]{1,0:T(8,128)(2,1)S(1)}, u32[]{:S(2)}, u32[]{:S(2)}) collective-permute-start(bf16[144,2048]{1,0:T(8,128)(2,1)S(1)} %collective-permute-done.2), channel_id=1, source_target_pairs={{0,508},{4,0},{8,4},{12,8},{16,12},{20,16},{24,20},{28,24},{32,28}... | collective-permute-start | bytes 1769480 | tf_op jit(solution)/shard_map/ppermute | solution.py:27
  77.0 8.8 %collective-permute-done.3 = bf16[144,2048]{1,0:T(8,128)(2,1)S(1)} collective-permute-done((bf16[144,2048]{1,0:T(8,128)(2,1)S(1)}, bf16[144,2048]{1,0:T(8,128)(2,1)S(1)}, u32[]{:S(2)}, u32[]{:S(2)}) %collective-permute-start.3) | collective-permute-done | bytes 589856 | tf_op jit(solution)/shard_map/ppermute | solution.py:27
  85.9 6.6 %collective-permute-done.7 = bf16[144,2048]{1,0:T(8,128)(2,1)S(1)} collective-permute-done((bf16[144,2048]{1,0:T(8,128)(2,1)S(1)}, bf16[144,2048]{1,0:T(8,128)(2,1)S(1)}, u32[]{:S(2)}, u32[]{:S(2)}) %collective-permute-start.7) | collective-permute-done | bytes 589856 | tf_op jit(solution)/shard_map/ppermute | solution.py:27
  94.3 3.3 copy.141
  98.3 3.2 copy.119
  101.6 3.7 multiply_reduce_fusion.1
  105.5 4.1 %fusion.4 = f32[1152,8,128]{2,0,1:T(8,128)S(1)} fusion(f32[1152,8,128]{2,1,0:T(8,128)} %bitcast.163, f32[128]{0:T(128)S(1)} %copy-done.33, f32[1152,8]{0,1:T(8,128)S(1)} %add_rsqrt_fusion), kind=kLoop, calls=%fused_computation.17 | loop fusion | flops 2359296 | bytes 9474560 | tf_op jit(solution)/shard_map/jvp()/mul | solution.py:45
  112.7 3.3 fusion.3
  116.1 3.6 copy-done.39
  119.7 3.4 fusion.10
  124.9 8.0 %fusion.5 = f32[8,1152,128,1]{2,1,3,0:T(8,128)} fusion(bf16[128,8,2,128]{3,2,1,0:T(2,128)(2,1)} %reshape_squeeze.4, f32[8,1152,128,2]{2,1,3,0:T(8,128)} %copy-done.39, f32[8,2,128]{2,1,0:T(2,128)} %copy-done.40, pred[128,1152]{0,1:T(8,128)(4,1)S(1)} %fusion.32), kind=kOutput, calls=%fused_computation.20 | convolution fusion | flops 613416960 | bytes 14835712 | tf_op jit(solution)/shard_map/grtw,tgrd->gwd/dot_general | solution.py:71
  132.9 2.0 multiply_reduce_fusion.2
  136.0 6.5 %fusion.1 = bf16[8,2,128,1152]{2,3,1,0:T(8,128)(2,1)S(1)} fusion(bf16[1152,8,128,1]{0,2,3,1:T(8,128)(2,1)S(1)} %copy-done.12, f32[8,2,128]{2,1,0:T(2,128)S(1)} %copy.127, bf16[128,8,2,128]{3,2,1,0:T(2,128)(2,1)} %reshape_squeeze.4, f32[8,2,128]{2,1,0:T(2,128)} %copy-done.40, f32[8,1152,128,2]{2,1,3,0:T(8,128)} %copy-done.39, pred[128,1152]{0,1:T(8,128)(4,1)S(1)} %fusion.32), kind=kOutput, calls=%fused_computation.2 | convolution fusion | flops 618135552 | bytes 17203200 | tf_op jit(solution)/shard_map/tgrd,wgd->grtw/dot_general | solution.py:61
  144.8 2.7 copy_dynamic-update-slice_fusion.1
  147.6 2.7 copy_dynamic-update-slice_fusion
  154.7 1.9 collective-permute-start.8
  156.6 4.1 %collective-permute-start.12 = (bf16[2,8,128,128]{3,1,2,0:T(8,128)(2,1)}, bf16[2,8,128,128]{3,1,2,0:T(8,128)(2,1)}, u32[]{:S(2)}, u32[]{:S(2)}) collective-permute-start(bf16[2,8,128,128]{3,1,2,0:T(8,128)(2,1)} %get-tuple-element.44), channel_id=1, source_target_pairs={{0,4},{4,8},{8,12},{12,16},{16,20},{20,24},{24,28},{28,32},{32,36}... | collective-permute-start | bytes 1572872 | tf_op jit(solution)/shard_map/ppermute | solution.py:27
  160.7 6.3 %multiply_add_fusion.1 = (f32[1152,8,64]{2,0,1:T(8,128)}, f32[1152,8,64]{2,0,1:T(8,128)}) fusion(f32[1152,8,128]{2,0,1:T(8,128)S(1)} %bitcast.165, f32[1152,64]{1,0:T(8,128)} %copy-done.8, f32[1152,64]{1,0:T(8,128)} %copy-done.7), kind=kLoop, calls=%fused_computation.13 | loop fusion | flops 4128768 | bytes 10027008 | tf_op jit(solution)/shard_map/transpose(jvp())/add_any | solution.py:39
  168.1 4.0 %collective-permute-done.12 = bf16[2,8,128,128]{3,1,2,0:T(8,128)(2,1)} collective-permute-done((bf16[2,8,128,128]{3,1,2,0:T(8,128)(2,1)}, bf16[2,8,128,128]{3,1,2,0:T(8,128)(2,1)}, u32[]{:S(2)}, u32[]{:S(2)}) %collective-permute-start.12) | collective-permute-done | bytes 524320 | tf_op jit(solution)/shard_map/ppermute | solution.py:27
  173.5 1.9 collective-permute-start.9
  175.5 3.9 %collective-permute-start.13 = (bf16[2,8,128,128]{3,1,2,0:T(8,128)(2,1)S(1)}, bf16[2,8,128,128]{3,1,2,0:T(8,128)(2,1)}, u32[]{:S(2)}, u32[]{:S(2)}) collective-permute-start(bf16[2,8,128,128]{3,1,2,0:T(8,128)(2,1)S(1)} %get-tuple-element.36), channel_id=1, source_target_pairs={{0,4},{4,8},{8,12},{12,16},{16,20},{20,24},{24,28},{28,32},{32,36}... | collective-permute-start | bytes 1572872 | tf_op jit(solution)/shard_map/ppermute | solution.py:27
  179.4 5.3 %convolution_multiply_fusion = f32[8,128,2,128]{3,1,2,0:T(8,128)S(1)} fusion(bf16[8,2,128,1152]{2,3,1,0:T(8,128)(2,1)} %copy-done.3, bf16[1152,8,64]{2,0,1:T(8,128)(2,1)} %copy-done.6, bf16[1152,8,64]{2,0,1:T(8,128)(2,1)S(1)} %copy-done.5), kind=kOutput, calls=%fused_computation.28 | convolution fusion | flops 608960512 | bytes 8126464 | tf_op jit(solution)/shard_map/grtw,wgd->tgrd/dot_general | solution.py:65
  187.7 2.2 collective-permute-done.13
  189.8 2.9 fusion.24
  192.7 2.1 collective-permute-start.10
  194.8 3.8 collective-permute-start.14
  200.1 4.2 %collective-permute-done.10 = bf16[2,8,128,128]{3,1,2,0:T(8,128)(2,1)} collective-permute-done((bf16[2,8,128,128]{3,1,2,0:T(8,128)(2,1)}, bf16[2,8,128,128]{3,1,2,0:T(8,128)(2,1)}, u32[]{:S(2)}, u32[]{:S(2)}) %collective-permute-start.10) | collective-permute-done | bytes 524320 | tf_op jit(solution)/shard_map/ppermute | solution.py:27
  204.4 8.9 %collective-permute-done.14 = bf16[2,8,128,128]{3,1,2,0:T(8,128)(2,1)} collective-permute-done((bf16[2,8,128,128]{3,1,2,0:T(8,128)(2,1)}, bf16[2,8,128,128]{3,1,2,0:T(8,128)(2,1)}, u32[]{:S(2)}, u32[]{:S(2)}) %collective-permute-start.14) | collective-permute-done | bytes 524320 | tf_op jit(solution)/shard_map/ppermute | solution.py:27
  213.3 3.0 fusion.22
  216.4 19.2 %collective-permute-start.11 = (bf16[2,8,128,128]{3,1,2,0:T(8,128)(2,1)}, bf16[2,8,128,128]{3,1,2,0:T(8,128)(2,1)}, u32[]{:S(2)}, u32[]{:S(2)}) collective-permute-start(bf16[2,8,128,128]{3,1,2,0:T(8,128)(2,1)} %get-tuple-element.31), channel_id=1, source_target_pairs={{4,0},{8,4},{12,8},{16,12},{20,16},{24,20},{28,24},{32,28},{36,32}... | collective-permute-start | bytes 1572872 | tf_op jit(solution)/shard_map/ppermute | solution.py:27
  235.6 24.2 %collective-permute-start.15 = (bf16[2,8,128,128]{3,1,2,0:T(8,128)(2,1)}, bf16[2,8,128,128]{3,1,2,0:T(8,128)(2,1)}, u32[]{:S(2)}, u32[]{:S(2)}) collective-permute-start(bf16[2,8,128,128]{3,1,2,0:T(8,128)(2,1)} %get-tuple-element.32), channel_id=1, source_target_pairs={{0,480},{4,484},{8,488},{12,492},{16,496},{20,500},{24,504},{28,50... | collective-permute-start | bytes 1572872 | tf_op jit(solution)/shard_map/ppermute | solution.py:27
  261.5 2.1 reshape.269
  263.6 6.5 %multiply_reduce_fusion = f32[128]{0:T(128)S(1)} fusion(f32[1152,8,64]{2,0,1:T(8,128)} %get-tuple-element.38, f32[1152,8,64]{2,0,1:T(8,128)} %get-tuple-element.37, f32[1152,8,128]{2,1,0:T(8,128)} %bitcast.164, f32[1152,8]{0,1:T(8,128)S(1)} %copy-done.27), kind=kLoop, calls=%fused_computation.11 | loop fusion | flops 4718464 | bytes 9474560 | tf_op jit(solution)/shard_map/transpose(jvp())/reduce_sum | solution.py:45
  270.1 2.6 all-reduce.10
  272.7 25.9 %all-reduce.11 = (f32[128]{0:T(128)S(1)}, f32[128]{0:T(128)S(1)}) all-reduce(f32[128]{0:T(128)S(1)} %get-tuple-element.27, f32[128]{0:T(128)S(1)} %get-tuple-element.28), channel_id=1, replica_groups=mesh['zh'=4,'x'=4,'y'=8,'zl'=2,'c'=2] {'zl'}, use_global_device_ids=true, to_apply=%region_8.9 | all-reduce | flops 256 | bytes 2048 | tf_op jit(solution)/shard_map/psum | solution.py:159
  298.6 16.8 %all-reduce.7 = (f32[128]{0:T(128)S(1)}, f32[128]{0:T(128)S(1)}) all-reduce(f32[128]{0:T(128)S(1)} %get-tuple-element.29, f32[128]{0:T(128)S(1)} %get-tuple-element.30), channel_id=1, replica_groups=mesh['zh'=4,'x'=4,'y'=8,'zl'=2,'c'=2] {'y'}, use_global_device_ids=true, to_apply=%region_9.10 | all-reduce | flops 256 | bytes 2048 | tf_op jit(solution)/shard_map/psum | solution.py:159
  315.4 30.2 %all-reduce.8 = (f32[128]{0:T(128)S(1)}, f32[128]{0:T(128)S(1)}) all-reduce(f32[128]{0:T(128)S(1)} %get-tuple-element.21, f32[128]{0:T(128)S(1)} %get-tuple-element.22), channel_id=1, replica_groups=mesh['zh'=4,'x'=4,'y'=8,'zl'=2,'c'=2] {'x'}, use_global_device_ids=true, to_apply=%region_10.11 | all-reduce | flops 256 | bytes 2048 | tf_op jit(solution)/shard_map/psum | solution.py:159
  345.5 40.4 %all-reduce.9 = (f32[128]{0:T(128)}, f32[128]{0:T(128)}) all-reduce(f32[128]{0:T(128)S(1)} %get-tuple-element.23, f32[128]{0:T(128)S(1)} %get-tuple-element.24), channel_id=1, replica_groups=mesh['zh'=4,'x'=4,'y'=8,'zl'=2,'c'=2] {'zh'}, use_global_device_ids=true, to_apply=%region_11.12 | all-reduce | flops 256 | bytes 2048 | tf_op jit(solution)/shard_map/psum | solution.py:159
  (163 shorter events, 44.2 us)
Async XLA Ops:
  0.6 15.2 %copy-start.35 = (f32[128]{0:T(128)S(1)}, f32[128]{0:T(128)}, u32[]{:S(2)}) copy-start(f32[128]{0:T(128)} %param.14) | copy-start | bytes 1540
  2.4 34.3 %collective-permute-start.4 = (bf16[144,2048]{1,0:T(8,128)(2,1)S(1)}, bf16[144,2048]{1,0:T(8,128)(2,1)S(1)}, u32[]{:S(2)}, u32[]{:S(2)}) collective-permute-start(bf16[144,2048]{1,0:T(8,128)(2,1)S(1)} %fusion.29), channel_id=1, source_target_pairs={{0,4},{4,8},{8,12},{12,16},{16,20},{20,24},{24,28},{28,32},{32,36}... | collective-permute-start | bytes 1769480 | tf_op jit(solution)/shard_map/ppermute | solution.py:27
  5.9 28.3 %collective-permute-start = (bf16[144,2048]{1,0:T(8,128)(2,1)S(1)}, bf16[144,2048]{1,0:T(8,128)(2,1)}, u32[]{:S(2)}, u32[]{:S(2)}) collective-permute-start(bf16[144,2048]{1,0:T(8,128)(2,1)S(1)} %fusion.29), channel_id=1, source_target_pairs={{0,32},{4,36},{8,40},{12,44},{16,48},{20,52},{24,56},{28,60},{32,6... | collective-permute-start | bytes 1769480 | tf_op jit(solution)/shard_map/ppermute | solution.py:27
  15.3 27.5 %copy-start.1 = (f32[16,8,16,128]{3,2,1,0:T(8,128)}, f32[16,8,16,128]{3,2,1,0:T(8,128)S(1)}, u32[]{:S(2)}) copy-start(f32[16,8,16,128]{3,2,1,0:T(8,128)S(1)} %copy.142) | copy-start | bytes 3145732
  15.7 40.2 %copy-start.28 = (f32[128,16]{0,1:T(8,128)}, f32[128,16]{0,1:T(8,128)S(1)}, u32[]{:S(2)}) copy-start(f32[128,16]{0,1:T(8,128)S(1)} %copy.94) | copy-start | bytes 24580
  15.8 43.8 %copy-start.19 = (f32[128,16]{1,0:T(8,128)}, f32[128,16]{1,0:T(8,128)S(1)}, u32[]{:S(2)}) copy-start(f32[128,16]{1,0:T(8,128)S(1)} %copy.95) | copy-start | bytes 24580
  16.5 60.5 %copy-start.21 = (f32[128,64]{1,0:T(8,128)}, f32[128,64]{1,0:T(8,128)S(1)}, u32[]{:S(2)}) copy-start(f32[128,64]{1,0:T(8,128)S(1)} %get-tuple-element.57) | copy-start | bytes 98308
  16.5 60.5 %copy-start.23 = (f32[128,64]{1,0:T(8,128)}, f32[128,64]{1,0:T(8,128)S(1)}, u32[]{:S(2)}) copy-start(f32[128,64]{1,0:T(8,128)S(1)} %get-tuple-element.58) | copy-start | bytes 98308
  34.2 17.3 %collective-permute-start.1 = (bf16[144,2048]{1,0:T(8,128)(2,1)}, bf16[144,2048]{1,0:T(8,128)(2,1)S(1)}, u32[]{:S(2)}, u32[]{:S(2)}) collective-permute-start(bf16[144,2048]{1,0:T(8,128)(2,1)} %collective-permute-done), channel_id=1, source_target_pairs={{0,508},{4,0},{8,4},{12,8},{16,12},{20,16},{24,20},{28,24},{32,28}... | collective-permute-start | bytes 1769480 | tf_op jit(solution)/shard_map/ppermute | solution.py:27
  36.7 19.7 %collective-permute-start.5 = (bf16[144,2048]{1,0:T(8,128)(2,1)S(1)}, bf16[144,2048]{1,0:T(8,128)(2,1)S(1)}, u32[]{:S(2)}, u32[]{:S(2)}) collective-permute-start(bf16[144,2048]{1,0:T(8,128)(2,1)S(1)} %collective-permute-done.4), channel_id=1, source_target_pairs={{0,4},{4,8},{8,12},{12,16},{16,20},{20,24},{24,28},{28,32},{32,36}... | collective-permute-start | bytes 1769480 | tf_op jit(solution)/shard_map/ppermute | solution.py:27
  42.8 66.9 %copy-start.7 = (f32[1152,64]{1,0:T(8,128)}, f32[1152,64]{1,0:T(8,128)S(1)}, u32[]{:S(2)}) copy-start(f32[1152,64]{1,0:T(8,128)S(1)} %get-tuple-element.53) | copy-start | bytes 884740
  42.8 66.9 %copy-start.8 = (f32[1152,64]{1,0:T(8,128)}, f32[1152,64]{1,0:T(8,128)S(1)}, u32[]{:S(2)}) copy-start(f32[1152,64]{1,0:T(8,128)S(1)} %get-tuple-element.54) | copy-start | bytes 884740
  51.6 16.5 %collective-permute-start.2 = (bf16[144,2048]{1,0:T(8,128)(2,1)S(1)}, bf16[144,2048]{1,0:T(8,128)(2,1)S(1)}, u32[]{:S(2)}, u32[]{:S(2)}) collective-permute-start(bf16[144,2048]{1,0:T(8,128)(2,1)S(1)} %collective-permute-done.1), channel_id=1, source_target_pairs={{0,508},{4,0},{8,4},{12,8},{16,12},{20,16},{24,20},{28,24},{32,28}... | collective-permute-start | bytes 1769480 | tf_op jit(solution)/shard_map/ppermute | solution.py:27
  56.5 36.3 %copy-start.13 = (bf16[1,128,1024]{2,1,0:T(8,128)(2,1)S(1)}, bf16[1,128,1024]{2,1,0:T(8,128)(2,1)}, u32[]{:S(2)}) copy-start(bf16[1,128,1024]{2,1,0:T(8,128)(2,1)} %param.10) | copy-start | bytes 786436
  56.5 36.3 %copy-start.25 = (bf16[1,128,1024]{2,1,0:T(8,128)(2,1)S(1)}, bf16[1,128,1024]{2,1,0:T(8,128)(2,1)}, u32[]{:S(2)}) copy-start(bf16[1,128,1024]{2,1,0:T(8,128)(2,1)} %param.11) | copy-start | bytes 786436
  56.5 18.6 %collective-permute-start.6 = (bf16[144,2048]{1,0:T(8,128)(2,1)S(1)}, bf16[144,2048]{1,0:T(8,128)(2,1)S(1)}, u32[]{:S(2)}, u32[]{:S(2)}) collective-permute-start(bf16[144,2048]{1,0:T(8,128)(2,1)S(1)} %collective-permute-done.5), channel_id=1, source_target_pairs={{0,4},{4,8},{8,12},{12,16},{16,20},{20,24},{24,28},{28,32},{32,36}... | collective-permute-start | bytes 1769480 | tf_op jit(solution)/shard_map/ppermute | solution.py:27
  68.1 17.8 %collective-permute-start.3 = (bf16[144,2048]{1,0:T(8,128)(2,1)S(1)}, bf16[144,2048]{1,0:T(8,128)(2,1)S(1)}, u32[]{:S(2)}, u32[]{:S(2)}) collective-permute-start(bf16[144,2048]{1,0:T(8,128)(2,1)S(1)} %collective-permute-done.2), channel_id=1, source_target_pairs={{0,508},{4,0},{8,4},{12,8},{16,12},{20,16},{24,20},{28,24},{32,28}... | collective-permute-start | bytes 1769480 | tf_op jit(solution)/shard_map/ppermute | solution.py:27
  75.0 17.5 %collective-permute-start.7 = (bf16[144,2048]{1,0:T(8,128)(2,1)S(1)}, bf16[144,2048]{1,0:T(8,128)(2,1)S(1)}, u32[]{:S(2)}, u32[]{:S(2)}) collective-permute-start(bf16[144,2048]{1,0:T(8,128)(2,1)S(1)} %collective-permute-done.6), channel_id=1, source_target_pairs={{0,4},{4,8},{8,12},{12,16},{16,20},{20,24},{24,28},{28,32},{32,36}... | collective-permute-start | bytes 1769480 | tf_op jit(solution)/shard_map/ppermute | solution.py:27
  98.3 7.2 %copy-start.33 = (f32[128]{0:T(128)S(1)}, f32[128]{0:T(128)}, u32[]{:S(2)}) copy-start(f32[128]{0:T(128)} %param.15) | copy-start | bytes 1540
  105.5 4.2 %copy-start.26 = (f32[1152,8]{0,1:T(8,128)}, f32[1152,8]{0,1:T(8,128)S(1)}, u32[]{:S(2)}) copy-start(f32[1152,8]{0,1:T(8,128)S(1)} %add_rsqrt_fusion) | copy-start | bytes 110596
  111.6 4.5 %copy-start.4 = (bf16[1152,8,64]{2,0,1:T(8,128)(2,1)}, bf16[1152,8,64]{2,0,1:T(8,128)(2,1)S(1)}, u32[]{:S(2)}) copy-start(bf16[1152,8,64]{2,0,1:T(8,128)(2,1)S(1)} %get-tuple-element.39) | copy-start | bytes 3538948
  111.6 4.5 %copy-start.6 = (bf16[1152,8,64]{2,0,1:T(8,128)(2,1)}, bf16[1152,8,64]{2,0,1:T(8,128)(2,1)S(1)}, u32[]{:S(2)}) copy-start(bf16[1152,8,64]{2,0,1:T(8,128)(2,1)S(1)} %get-tuple-element.40) | copy-start | bytes 3538948
  112.7 7.0 %copy-start.12 = (bf16[1152,8,128,1]{0,2,3,1:T(8,128)(2,1)S(1)}, bf16[1152,8,128,1]{0,2,3,1:T(8,128)(2,1)}, u32[]{:S(2)}) copy-start(bf16[1152,8,128,1]{0,2,3,1:T(8,128)(2,1)} %copy.119) | copy-start | bytes 7077892
  116.1 3.6 copy-start.40
  124.9 8.0 %copy-start.14 = (bf16[128,8,2,128]{3,2,1,0:T(2,128)(2,1)S(1)}, bf16[128,8,2,128]{3,2,1,0:T(2,128)(2,1)}, u32[]{:S(2)}) copy-start(bf16[128,8,2,128]{3,2,1,0:T(2,128)(2,1)} %reshape_squeeze.4) | copy-start | bytes 1572868
  136.0 6.6 %copy-start.16 = (bf16[128,16,64]{2,0,1:T(8,128)(2,1)S(1)}, bf16[128,16,64]{2,0,1:T(8,128)(2,1)}, u32[]{:S(2)}) copy-start(bf16[128,16,64]{2,0,1:T(8,128)(2,1)} %copy.96) | copy-start | bytes 786436
  136.0 6.6 %copy-start.18 = (bf16[128,16,64]{2,0,1:T(8,128)(2,1)S(1)}, bf16[128,16,64]{2,0,1:T(8,128)(2,1)}, u32[]{:S(2)}) copy-start(bf16[128,16,64]{2,0,1:T(8,128)(2,1)} %copy.97) | copy-start | bytes 786436
  150.4 21.7 %copy-start = (f32[2,8,9,128,128]{4,1,3,0,2:T(8,128)}, f32[2,8,9,128,128]{4,1,3,0,2:T(8,128)S(1)}, u32[]{:S(2)}) copy-start(f32[2,8,9,128,128]{4,1,3,0,2:T(8,128)S(1)} %copy_dynamic-update-slice_fusion) | copy-start | bytes 28311556
  154.7 13.4 %collective-permute-start.8 = (bf16[2,8,128,128]{3,1,2,0:T(8,128)(2,1)}, bf16[2,8,128,128]{3,1,2,0:T(8,128)(2,1)}, u32[]{:S(2)}, u32[]{:S(2)}) collective-permute-start(bf16[2,8,128,128]{3,1,2,0:T(8,128)(2,1)} %get-tuple-element.43), channel_id=1, source_target_pairs={{4,0},{8,4},{12,8},{16,12},{20,16},{24,20},{28,24},{32,28},{36,32}... | collective-permute-start | bytes 1572872 | tf_op jit(solution)/shard_map/ppermute | solution.py:27
  156.6 15.5 %collective-permute-start.12 = (bf16[2,8,128,128]{3,1,2,0:T(8,128)(2,1)}, bf16[2,8,128,128]{3,1,2,0:T(8,128)(2,1)}, u32[]{:S(2)}, u32[]{:S(2)}) collective-permute-start(bf16[2,8,128,128]{3,1,2,0:T(8,128)(2,1)} %get-tuple-element.44), channel_id=1, source_target_pairs={{0,4},{4,8},{8,12},{12,16},{16,20},{20,24},{24,28},{28,32},{32,36}... | collective-permute-start | bytes 1572872 | tf_op jit(solution)/shard_map/ppermute | solution.py:27
  167.0 12.4 %copy-start.5 = (bf16[1152,8,64]{2,0,1:T(8,128)(2,1)S(1)}, bf16[1152,8,64]{2,0,1:T(8,128)(2,1)}, u32[]{:S(2)}) copy-start(bf16[1152,8,64]{2,0,1:T(8,128)(2,1)} %copy-done.4) | copy-start | bytes 3538948
  173.5 14.1 %collective-permute-start.9 = (bf16[2,8,128,128]{3,1,2,0:T(8,128)(2,1)S(1)}, bf16[2,8,128,128]{3,1,2,0:T(8,128)(2,1)S(1)}, u32[]{:S(2)}, u32[]{:S(2)}) collective-permute-start(bf16[2,8,128,128]{3,1,2,0:T(8,128)(2,1)S(1)} %get-tuple-element.35), channel_id=1, source_target_pairs={{4,0},{8,4},{12,8},{16,12},{20,16},{24,20},{28,24},{32,28},{36,32}... | collective-permute-start | bytes 1572872 | tf_op jit(solution)/shard_map/ppermute | solution.py:27
  175.5 14.4 %collective-permute-start.13 = (bf16[2,8,128,128]{3,1,2,0:T(8,128)(2,1)S(1)}, bf16[2,8,128,128]{3,1,2,0:T(8,128)(2,1)}, u32[]{:S(2)}, u32[]{:S(2)}) collective-permute-start(bf16[2,8,128,128]{3,1,2,0:T(8,128)(2,1)S(1)} %get-tuple-element.36), channel_id=1, source_target_pairs={{0,4},{4,8},{8,12},{12,16},{16,20},{20,24},{24,28},{28,32},{32,36}... | collective-permute-start | bytes 1572872 | tf_op jit(solution)/shard_map/ppermute | solution.py:27
  184.7 14.0 %copy-start.22 = (f32[128,64]{1,0:T(8,128)S(1)}, f32[128,64]{1,0:T(8,128)}, u32[]{:S(2)}) copy-start(f32[128,64]{1,0:T(8,128)} %copy-done.21) | copy-start | bytes 98308
  184.7 14.0 %copy-start.24 = (f32[128,64]{1,0:T(8,128)S(1)}, f32[128,64]{1,0:T(8,128)}, u32[]{:S(2)}) copy-start(f32[128,64]{1,0:T(8,128)} %copy-done.23) | copy-start | bytes 98308
  186.2 12.8 %copy-start.2 = (f32[16,8,16,128]{3,2,1,0:T(8,128)S(1)}, f32[16,8,16,128]{3,2,1,0:T(8,128)}, u32[]{:S(2)}) copy-start(f32[16,8,16,128]{3,2,1,0:T(8,128)} %copy-done.1) | copy-start | bytes 3145732
  186.2 12.8 %copy-start.20 = (f32[128,16]{1,0:T(8,128)S(1)}, f32[128,16]{1,0:T(8,128)}, u32[]{:S(2)}) copy-start(f32[128,16]{1,0:T(8,128)} %copy-done.19) | copy-start | bytes 24580
  186.2 12.8 %copy-start.36 = (f32[128]{0:T(128)S(1)}, f32[128]{0:T(128)}, u32[]{:S(2)}) copy-start(f32[128]{0:T(128)} %param.14) | copy-start | bytes 1540
  187.6 11.0 %copy-start.10 = (f32[128,16,64]{2,1,0:T(8,128)S(1)}, f32[128,16,64]{2,1,0:T(8,128)}, u32[]{:S(2)}) copy-start(f32[128,16,64]{2,1,0:T(8,128)} %copy.138) | copy-start | bytes 1572868
  187.7 11.1 %copy-start.11 = (f32[128,16,64]{2,1,0:T(8,128)S(1)}, f32[128,16,64]{2,1,0:T(8,128)}, u32[]{:S(2)}) copy-start(f32[128,16,64]{2,1,0:T(8,128)} %copy.139) | copy-start | bytes 1572868
  192.7 7.3 %copy-start.29 = (f32[128,16]{0,1:T(8,128)S(1)}, f32[128,16]{0,1:T(8,128)}, u32[]{:S(2)}) copy-start(f32[128,16]{0,1:T(8,128)} %copy-done.28) | copy-start | bytes 24580
  192.7 11.7 %collective-permute-start.10 = (bf16[2,8,128,128]{3,1,2,0:T(8,128)(2,1)}, bf16[2,8,128,128]{3,1,2,0:T(8,128)(2,1)}, u32[]{:S(2)}, u32[]{:S(2)}) collective-permute-start(bf16[2,8,128,128]{3,1,2,0:T(8,128)(2,1)} %get-tuple-element.33), channel_id=1, source_target_pairs={{4,0},{8,4},{12,8},{16,12},{20,16},{24,20},{28,24},{32,28},{36,32}... | collective-permute-start | bytes 1572872 | tf_op jit(solution)/shard_map/ppermute | solution.py:27
  194.8 18.5 %collective-permute-start.14 = (bf16[2,8,128,128]{3,1,2,0:T(8,128)(2,1)}, bf16[2,8,128,128]{3,1,2,0:T(8,128)(2,1)}, u32[]{:S(2)}, u32[]{:S(2)}) collective-permute-start(bf16[2,8,128,128]{3,1,2,0:T(8,128)(2,1)} %get-tuple-element.34), channel_id=1, source_target_pairs={{0,4},{4,8},{8,12},{12,16},{16,20},{20,24},{24,28},{28,32},{32,36}... | collective-permute-start | bytes 1572872 | tf_op jit(solution)/shard_map/ppermute | solution.py:27
  199.9 63.6 %copy-start.27 = (f32[1152,8]{0,1:T(8,128)S(1)}, f32[1152,8]{0,1:T(8,128)}, u32[]{:S(2)}) copy-start(f32[1152,8]{0,1:T(8,128)} %copy-done.26) | copy-start | bytes 110596
  216.4 169.5 %collective-permute-start.11 = (bf16[2,8,128,128]{3,1,2,0:T(8,128)(2,1)}, bf16[2,8,128,128]{3,1,2,0:T(8,128)(2,1)}, u32[]{:S(2)}, u32[]{:S(2)}) collective-permute-start(bf16[2,8,128,128]{3,1,2,0:T(8,128)(2,1)} %get-tuple-element.31), channel_id=1, source_target_pairs={{4,0},{8,4},{12,8},{16,12},{20,16},{24,20},{28,24},{32,28},{36,32}... | collective-permute-start | bytes 1572872 | tf_op jit(solution)/shard_map/ppermute | solution.py:27
  235.6 150.3 %collective-permute-start.15 = (bf16[2,8,128,128]{3,1,2,0:T(8,128)(2,1)}, bf16[2,8,128,128]{3,1,2,0:T(8,128)(2,1)}, u32[]{:S(2)}, u32[]{:S(2)}) collective-permute-start(bf16[2,8,128,128]{3,1,2,0:T(8,128)(2,1)} %get-tuple-element.32), channel_id=1, source_target_pairs={{0,480},{4,484},{8,488},{12,492},{16,496},{20,500},{24,504},{28,50... | collective-permute-start | bytes 1572872 | tf_op jit(solution)/shard_map/ppermute | solution.py:27
  270.0 118.7 %copy-start.9 = (f32[16,8,8,128]{3,2,1,0:T(8,128)S(1)}, f32[16,8,8,128]{3,2,1,0:T(8,128)}, u32[]{:S(2)}) copy-start(f32[16,8,8,128]{3,2,1,0:T(8,128)} %copy.144) | copy-start | bytes 1572868
  270.0 118.7 %copy-start.34 = (f32[128]{0:T(128)S(1)}, f32[128]{0:T(128)}, u32[]{:S(2)}) copy-start(f32[128]{0:T(128)} %param.15) | copy-start | bytes 1540
  (11 other events, 26.8 us)

commit v10 on v9

--- a/solution.py
+++ b/solution.py
@@ -155,7 +155,7 @@
         carry_far = (got + slots[:, :, behind - offset]).astype(jnp.bfloat16)
     sent = [shift(carry_near, -1, False), shift(carry_far, -behind, True)]
     gains = (query_gain_gradient, key_gain_gradient)
-    for axis in ("c", "zl", "y", "x", "zh"):
+    for axis in ("y", "x", "zh", DP_AXES):
         gains = lax.psum(gains, axis)
     gain_query, gain_key = gains
     total = slots[:, :, behind]

time: 399 us -> 389 us (0.975)
  the two profiles are of different devices: /device:TPU:2 before, /device:TPU:1 now
where the time goes in v10:
time: 389 us; the launch traced here: 381 us
  blocking collectives  120 us (31%)
  waiting for transfers between devices  83.1 us (21%)
  starting transfers between devices  60.5 us (16%)
  other arithmetic  50.8 us (13%)
  local copies, waits for them, and re-layouts  36.8 us (9%)
  matrix products  28 us (7%)
    psum x4, blocking collectives, shards(): gains = lax.psum(gains, axis)  120 us
    ppermute x16, waiting for transfers between devices, shift(): return lax.ppermute(value, SEQ_AXES, pairs)  83.1 us
    ppermute x16, starting transfers between devices, shift(): return lax.ppermute(value, SEQ_AXES, pairs)  60.5 us
    unnamed x103, local copies, waits for them, and re-layouts  18.6 us
    dot_general x1, matrix products, attend(): jnp.einsum('grtw,tgrd->gwd', weights_b, gradient_block, preferred_element...  7.99 us
  transfers between devices with their start and end apart: 16, of which 8 were waited for; matrix products, arithmetic and copies ran while one was open for 11% of the time, Pallas kernels for 0%

profile of v10, /device:TPU:1, one launch (start us, length us, event | category | flops | bytes accessed | tf_op | source)
XLA Modules:
  0.0 380.9 jit_solution(6507494451450765539)
XLA Ops:
  2.4 4.1 %collective-permute-start.4 = (bf16[144,2048]{1,0:T(8,128)(2,1)S(1)}, bf16[144,2048]{1,0:T(8,128)(2,1)S(1)}, u32[]{:S(2)}, u32[]{:S(2)}) collective-permute-start(bf16[144,2048]{1,0:T(8,128)(2,1)S(1)} %fusion.29), channel_id=1, source_target_pairs={{0,4},{4,8},{8,12},{12,16},{16,20},{20,24},{24,28},{28,32},{32,36}... | collective-permute-start | bytes 1769480 | tf_op jit(solution)/shard_map/ppermute | solution.py:27
  6.5 3.1 collective-permute-start
  11.1 2.2 reshape_squeeze.4
  19.2 24.3 %collective-permute-done = bf16[144,2048]{1,0:T(8,128)(2,1)} collective-permute-done((bf16[144,2048]{1,0:T(8,128)(2,1)S(1)}, bf16[144,2048]{1,0:T(8,128)(2,1)}, u32[]{:S(2)}, u32[]{:S(2)}) %collective-permute-start) | collective-permute-done | bytes 589856 | tf_op jit(solution)/shard_map/ppermute | solution.py:27
  43.5 1.9 collective-permute-start.1
  46.1 3.4 collective-permute-start.5
  49.5 2.1 multiply_cosine_fusion
  51.6 8.6 %collective-permute-done.1 = bf16[144,2048]{1,0:T(8,128)(2,1)S(1)} collective-permute-done((bf16[144,2048]{1,0:T(8,128)(2,1)}, bf16[144,2048]{1,0:T(8,128)(2,1)S(1)}, u32[]{:S(2)}, u32[]{:S(2)}) %collective-permute-start.1) | collective-permute-done | bytes 589856 | tf_op jit(solution)/shard_map/ppermute | solution.py:27
  60.2 12.2 %collective-permute-start.2 = (bf16[144,2048]{1,0:T(8,128)(2,1)S(1)}, bf16[144,2048]{1,0:T(8,128)(2,1)S(1)}, u32[]{:S(2)}, u32[]{:S(2)}) collective-permute-start(bf16[144,2048]{1,0:T(8,128)(2,1)S(1)} %collective-permute-done.1), channel_id=1, source_target_pairs={{0,508},{4,0},{8,4},{12,8},{16,12},{20,16},{24,20},{28,24},{32,28}... | collective-permute-start | bytes 1769480 | tf_op jit(solution)/shard_map/ppermute | solution.py:27
  75.6 7.6 %collective-permute-done.2 = bf16[144,2048]{1,0:T(8,128)(2,1)S(1)} collective-permute-done((bf16[144,2048]{1,0:T(8,128)(2,1)S(1)}, bf16[144,2048]{1,0:T(8,128)(2,1)S(1)}, u32[]{:S(2)}, u32[]{:S(2)}) %collective-permute-start.2) | collective-permute-done | bytes 589856 | tf_op jit(solution)/shard_map/ppermute | solution.py:27
  83.1 13.7 %collective-permute-start.3 = (bf16[144,2048]{1,0:T(8,128)(2,1)S(1)}, bf16[144,2048]{1,0:T(8,128)(2,1)S(1)}, u32[]{:S(2)}, u32[]{:S(2)}) collective-permute-start(bf16[144,2048]{1,0:T(8,128)(2,1)S(1)} %collective-permute-done.2), channel_id=1, source_target_pairs={{0,508},{4,0},{8,4},{12,8},{16,12},{20,16},{24,20},{28,24},{32,28}... | collective-permute-start | bytes 1769480 | tf_op jit(solution)/shard_map/ppermute | solution.py:27
  98.3 8.6 %collective-permute-done.3 = bf16[144,2048]{1,0:T(8,128)(2,1)S(1)} collective-permute-done((bf16[144,2048]{1,0:T(8,128)(2,1)S(1)}, bf16[144,2048]{1,0:T(8,128)(2,1)S(1)}, u32[]{:S(2)}, u32[]{:S(2)}) %collective-permute-start.3) | collective-permute-done | bytes 589856 | tf_op jit(solution)/shard_map/ppermute | solution.py:27
  108.6 3.4 copy.141
  112.7 3.0 copy.119
  115.7 3.7 multiply_reduce_fusion.1
  119.6 4.1 %fusion.4 = f32[1152,8,128]{2,0,1:T(8,128)S(1)} fusion(f32[1152,8,128]{2,1,0:T(8,128)} %bitcast.163, f32[128]{0:T(128)S(1)} %copy-done.33, f32[1152,8]{0,1:T(8,128)S(1)} %add_rsqrt_fusion), kind=kLoop, calls=%fused_computation.17 | loop fusion | flops 2359296 | bytes 9474560 | tf_op jit(solution)/shard_map/jvp()/mul | solution.py:45
  123.9 1.8 subtract_convert_fusion
  126.8 3.3 fusion.3
  130.1 3.6 copy-done.39
  133.8 3.4 fusion.10
  137.2 1.8 copy.126
  138.9 8.0 %fusion.5 = f32[8,1152,128,1]{2,1,3,0:T(8,128)} fusion(bf16[128,8,2,128]{3,2,1,0:T(2,128)(2,1)} %reshape_squeeze.4, f32[8,1152,128,2]{2,1,3,0:T(8,128)} %copy-done.39, f32[8,2,128]{2,1,0:T(2,128)} %copy-done.40, pred[128,1152]{0,1:T(8,128)(4,1)S(1)} %fusion.32), kind=kOutput, calls=%fused_computation.20 | convolution fusion | flops 613416960 | bytes 14835712 | tf_op jit(solution)/shard_map/grtw,tgrd->gwd/dot_general | solution.py:71
  146.9 2.0 multiply_reduce_fusion.2
  150.1 6.6 %fusion.1 = bf16[8,2,128,1152]{2,3,1,0:T(8,128)(2,1)S(1)} fusion(bf16[1152,8,128,1]{0,2,3,1:T(8,128)(2,1)S(1)} %copy-done.12, f32[8,2,128]{2,1,0:T(2,128)S(1)} %copy.127, bf16[128,8,2,128]{3,2,1,0:T(2,128)(2,1)} %reshape_squeeze.4, f32[8,2,128]{2,1,0:T(2,128)} %copy-done.40, f32[8,1152,128,2]{2,1,3,0:T(8,128)} %copy-done.39, pred[128,1152]{0,1:T(8,128)(4,1)S(1)} %fusion.32), kind=kOutput, calls=%fused_computation.2 | convolution fusion | flops 618135552 | bytes 17203200 | tf_op jit(solution)/shard_map/tgrd,wgd->grtw/dot_general | solution.py:61
  156.7 1.5 bitcast_multiply_fusion
  158.9 2.7 copy_dynamic-update-slice_fusion.1
  161.7 2.7 copy_dynamic-update-slice_fusion
  165.4 1.5 slice_bitcast_fusion.10
  170.1 4.2 %collective-permute-start.12 = (bf16[2,8,128,128]{3,1,2,0:T(8,128)(2,1)}, bf16[2,8,128,128]{3,1,2,0:T(8,128)(2,1)}, u32[]{:S(2)}, u32[]{:S(2)}) collective-permute-start(bf16[2,8,128,128]{3,1,2,0:T(8,128)(2,1)} %get-tuple-element.42), channel_id=1, source_target_pairs={{0,4},{4,8},{8,12},{12,16},{16,20},{20,24},{24,28},{28,32},{32,36}... | collective-permute-start | bytes 1572872 | tf_op jit(solution)/shard_map/ppermute | solution.py:27
  174.3 6.2 %multiply_add_fusion.1 = (f32[1152,8,64]{2,0,1:T(8,128)}, f32[1152,8,64]{2,0,1:T(8,128)}) fusion(f32[1152,8,128]{2,0,1:T(8,128)S(1)} %bitcast.165, f32[1152,64]{1,0:T(8,128)} %copy-done.8, f32[1152,64]{1,0:T(8,128)} %copy-done.7), kind=kLoop, calls=%fused_computation.13 | loop fusion | flops 4128768 | bytes 10027008 | tf_op jit(solution)/shard_map/transpose(jvp())/add_any | solution.py:39
  180.6 9.5 %collective-permute-done.12 = bf16[2,8,128,128]{3,1,2,0:T(8,128)(2,1)} collective-permute-done((bf16[2,8,128,128]{3,1,2,0:T(8,128)(2,1)}, bf16[2,8,128,128]{3,1,2,0:T(8,128)(2,1)}, u32[]{:S(2)}, u32[]{:S(2)}) %collective-permute-start.12) | collective-permute-done | bytes 524320 | tf_op jit(solution)/shard_map/ppermute | solution.py:27
  192.8 4.0 %collective-permute-start.13 = (bf16[2,8,128,128]{3,1,2,0:T(8,128)(2,1)S(1)}, bf16[2,8,128,128]{3,1,2,0:T(8,128)(2,1)}, u32[]{:S(2)}, u32[]{:S(2)}) collective-permute-start(bf16[2,8,128,128]{3,1,2,0:T(8,128)(2,1)S(1)} %get-tuple-element.34), channel_id=1, source_target_pairs={{0,4},{4,8},{8,12},{12,16},{16,20},{20,24},{24,28},{28,32},{32,36}... | collective-permute-start | bytes 1572872 | tf_op jit(solution)/shard_map/ppermute | solution.py:27
  196.8 5.3 %convolution_multiply_fusion = f32[8,128,2,128]{3,1,2,0:T(8,128)S(1)} fusion(bf16[8,2,128,1152]{2,3,1,0:T(8,128)(2,1)} %copy-done.3, bf16[1152,8,64]{2,0,1:T(8,128)(2,1)} %copy-done.6, bf16[1152,8,64]{2,0,1:T(8,128)(2,1)S(1)} %copy-done.5), kind=kOutput, calls=%fused_computation.28 | convolution fusion | flops 608960512 | bytes 8126464 | tf_op jit(solution)/shard_map/grtw,wgd->tgrd/dot_general | solution.py:65
  205.1 11.0 %collective-permute-done.13 = bf16[2,8,128,128]{3,1,2,0:T(8,128)(2,1)} collective-permute-done((bf16[2,8,128,128]{3,1,2,0:T(8,128)(2,1)S(1)}, bf16[2,8,128,128]{3,1,2,0:T(8,128)(2,1)}, u32[]{:S(2)}, u32[]{:S(2)}) %collective-permute-start.13) | collective-permute-done | bytes 524320 | tf_op jit(solution)/shard_map/ppermute | solution.py:27
  216.1 2.9 fusion.24
  220.4 4.0 %collective-permute-start.14 = (bf16[2,8,128,128]{3,1,2,0:T(8,128)(2,1)}, bf16[2,8,128,128]{3,1,2,0:T(8,128)(2,1)}, u32[]{:S(2)}, u32[]{:S(2)}) collective-permute-start(bf16[2,8,128,128]{3,1,2,0:T(8,128)(2,1)} %get-tuple-element.32), channel_id=1, source_target_pairs={{0,4},{4,8},{8,12},{12,16},{16,20},{20,24},{24,28},{28,32},{32,36}... | collective-permute-start | bytes 1572872 | tf_op jit(solution)/shard_map/ppermute | solution.py:27
  225.9 3.5 collective-permute-done.10
  229.3 10.0 %collective-permute-done.14 = bf16[2,8,128,128]{3,1,2,0:T(8,128)(2,1)} collective-permute-done((bf16[2,8,128,128]{3,1,2,0:T(8,128)(2,1)}, bf16[2,8,128,128]{3,1,2,0:T(8,128)(2,1)}, u32[]{:S(2)}, u32[]{:S(2)}) %collective-permute-start.14) | collective-permute-done | bytes 524320 | tf_op jit(solution)/shard_map/ppermute | solution.py:27
  239.3 3.1 fusion.22
  243.6 1.9 collective-permute-start.15
  245.6 1.8 fusion.14
  247.4 2.1 reshape.269
  249.4 6.5 %multiply_reduce_fusion = f32[128]{0:T(128)S(1)} fusion(f32[1152,8,64]{2,0,1:T(8,128)} %get-tuple-element.36, f32[1152,8,64]{2,0,1:T(8,128)} %get-tuple-element.35, f32[1152,8,128]{2,1,0:T(8,128)} %bitcast.164, f32[1152,8]{0,1:T(8,128)S(1)} %copy-done.27), kind=kLoop, calls=%fused_computation.11 | loop fusion | flops 4718464 | bytes 9474560 | tf_op jit(solution)/shard_map/transpose(jvp())/reduce_sum | solution.py:45
  255.9 12.9 %all-reduce.7 = (f32[128]{0:T(128)S(1)}, f32[128]{0:T(128)S(1)}) all-reduce(f32[128]{0:T(128)S(1)} %get-tuple-element.17, f32[128]{0:T(128)S(1)} %multiply_reduce_fusion), channel_id=1, replica_groups=mesh['zh'=4,'x'=4,'y'=8,'zl'=2,'c'=2] {'y'}, use_global_device_ids=true, to_apply=%region_7.8 | all-reduce | flops 256 | bytes 2048 | tf_op jit(solution)/shard_map/psum | solution.py:159
  268.8 39.6 %all-reduce.9 = (f32[128]{0:T(128)S(1)}, f32[128]{0:T(128)S(1)}) all-reduce(f32[128]{0:T(128)S(1)} %get-tuple-element.21, f32[128]{0:T(128)S(1)} %get-tuple-element.22), channel_id=1, replica_groups=mesh['zh'=4,'x'=4,'y'=8,'zl'=2,'c'=2] {'x'}, use_global_device_ids=true, to_apply=%region_8.9 | all-reduce | flops 256 | bytes 2048 | tf_op jit(solution)/shard_map/psum | solution.py:159
  308.3 42.0 %all-reduce.10 = (f32[128]{0:T(128)S(1)}, f32[128]{0:T(128)S(1)}) all-reduce(f32[128]{0:T(128)S(1)} %get-tuple-element.25, f32[128]{0:T(128)S(1)} %get-tuple-element.26), channel_id=1, replica_groups=mesh['zh'=4,'x'=4,'y'=8,'zl'=2,'c'=2] {'zh'}, use_global_device_ids=true, to_apply=%region_9.10 | all-reduce | flops 256 | bytes 2048 | tf_op jit(solution)/shard_map/psum | solution.py:159
  350.3 25.1 %all-reduce.8 = (f32[128]{0:T(128)}, f32[128]{0:T(128)}) all-reduce(f32[128]{0:T(128)S(1)} %get-tuple-element.27, f32[128]{0:T(128)S(1)} %get-tuple-element.28), channel_id=1, replica_groups=mesh['zh'=4,'x'=4,'y'=8,'zl'=2,'c'=2] {'zl','c'}, use_global_device_ids=true, to_apply=%region_10.11 | all-reduce | flops 256 | bytes 2048 | tf_op jit(solution)/shard_map/psum | solution.py:159
  375.5 1.7 fusion.28
  (162 shorter events, 37.0 us)
Async XLA Ops:
  0.6 15.4 %copy-start.35 = (f32[128]{0:T(128)S(1)}, f32[128]{0:T(128)}, u32[]{:S(2)}) copy-start(f32[128]{0:T(128)} %param.14) | copy-start | bytes 1540
  2.4 43.7 %collective-permute-start.4 = (bf16[144,2048]{1,0:T(8,128)(2,1)S(1)}, bf16[144,2048]{1,0:T(8,128)(2,1)S(1)}, u32[]{:S(2)}, u32[]{:S(2)}) collective-permute-start(bf16[144,2048]{1,0:T(8,128)(2,1)S(1)} %fusion.29), channel_id=1, source_target_pairs={{0,4},{4,8},{8,12},{12,16},{16,20},{20,24},{24,28},{28,32},{32,36}... | collective-permute-start | bytes 1769480 | tf_op jit(solution)/shard_map/ppermute | solution.py:27
  6.5 37.1 %collective-permute-start = (bf16[144,2048]{1,0:T(8,128)(2,1)S(1)}, bf16[144,2048]{1,0:T(8,128)(2,1)}, u32[]{:S(2)}, u32[]{:S(2)}) collective-permute-start(bf16[144,2048]{1,0:T(8,128)(2,1)S(1)} %fusion.29), channel_id=1, source_target_pairs={{0,32},{4,36},{8,40},{12,44},{16,48},{20,52},{24,56},{28,60},{32,6... | collective-permute-start | bytes 1769480 | tf_op jit(solution)/shard_map/ppermute | solution.py:27
  15.5 36.0 %copy-start.1 = (f32[16,8,16,128]{3,2,1,0:T(8,128)}, f32[16,8,16,128]{3,2,1,0:T(8,128)S(1)}, u32[]{:S(2)}) copy-start(f32[16,8,16,128]{3,2,1,0:T(8,128)S(1)} %copy.142) | copy-start | bytes 3145732
  15.9 56.5 %copy-start.28 = (f32[128,16]{0,1:T(8,128)}, f32[128,16]{0,1:T(8,128)S(1)}, u32[]{:S(2)}) copy-start(f32[128,16]{0,1:T(8,128)S(1)} %copy.94) | copy-start | bytes 24580
  16.1 59.5 %copy-start.19 = (f32[128,16]{1,0:T(8,128)}, f32[128,16]{1,0:T(8,128)S(1)}, u32[]{:S(2)}) copy-start(f32[128,16]{1,0:T(8,128)S(1)} %copy.95) | copy-start | bytes 24580
  16.8 81.5 %copy-start.21 = (f32[128,64]{1,0:T(8,128)}, f32[128,64]{1,0:T(8,128)S(1)}, u32[]{:S(2)}) copy-start(f32[128,64]{1,0:T(8,128)S(1)} %get-tuple-element.55) | copy-start | bytes 98308
  16.8 81.5 %copy-start.23 = (f32[128,64]{1,0:T(8,128)}, f32[128,64]{1,0:T(8,128)S(1)}, u32[]{:S(2)}) copy-start(f32[128,64]{1,0:T(8,128)S(1)} %get-tuple-element.56) | copy-start | bytes 98308
  43.5 16.7 %collective-permute-start.1 = (bf16[144,2048]{1,0:T(8,128)(2,1)}, bf16[144,2048]{1,0:T(8,128)(2,1)S(1)}, u32[]{:S(2)}, u32[]{:S(2)}) collective-permute-start(bf16[144,2048]{1,0:T(8,128)(2,1)} %collective-permute-done), channel_id=1, source_target_pairs={{0,508},{4,0},{8,4},{12,8},{16,12},{20,16},{24,20},{28,24},{32,28}... | collective-permute-start | bytes 1769480 | tf_op jit(solution)/shard_map/ppermute | solution.py:27
  46.1 26.9 %collective-permute-start.5 = (bf16[144,2048]{1,0:T(8,128)(2,1)S(1)}, bf16[144,2048]{1,0:T(8,128)(2,1)S(1)}, u32[]{:S(2)}, u32[]{:S(2)}) collective-permute-start(bf16[144,2048]{1,0:T(8,128)(2,1)S(1)} %collective-permute-done.4), channel_id=1, source_target_pairs={{0,4},{4,8},{8,12},{12,16},{16,20},{20,24},{24,28},{28,32},{32,36}... | collective-permute-start | bytes 1769480 | tf_op jit(solution)/shard_map/ppermute | solution.py:27
  51.6 72.2 %copy-start.7 = (f32[1152,64]{1,0:T(8,128)}, f32[1152,64]{1,0:T(8,128)S(1)}, u32[]{:S(2)}) copy-start(f32[1152,64]{1,0:T(8,128)S(1)} %get-tuple-element.51) | copy-start | bytes 884740
  51.6 72.2 %copy-start.8 = (f32[1152,64]{1,0:T(8,128)}, f32[1152,64]{1,0:T(8,128)S(1)}, u32[]{:S(2)}) copy-start(f32[1152,64]{1,0:T(8,128)S(1)} %get-tuple-element.52) | copy-start | bytes 884740
  60.2 22.9 %collective-permute-start.2 = (bf16[144,2048]{1,0:T(8,128)(2,1)S(1)}, bf16[144,2048]{1,0:T(8,128)(2,1)S(1)}, u32[]{:S(2)}, u32[]{:S(2)}) collective-permute-start(bf16[144,2048]{1,0:T(8,128)(2,1)S(1)} %collective-permute-done.1), channel_id=1, source_target_pairs={{0,508},{4,0},{8,4},{12,8},{16,12},{20,16},{24,20},{28,24},{32,28}... | collective-permute-start | bytes 1769480 | tf_op jit(solution)/shard_map/ppermute | solution.py:27
  73.0 34.1 %copy-start.13 = (bf16[1,128,1024]{2,1,0:T(8,128)(2,1)S(1)}, bf16[1,128,1024]{2,1,0:T(8,128)(2,1)}, u32[]{:S(2)}) copy-start(bf16[1,128,1024]{2,1,0:T(8,128)(2,1)} %param.10) | copy-start | bytes 786436
  73.0 34.1 %copy-start.25 = (bf16[1,128,1024]{2,1,0:T(8,128)(2,1)S(1)}, bf16[1,128,1024]{2,1,0:T(8,128)(2,1)}, u32[]{:S(2)}) copy-start(bf16[1,128,1024]{2,1,0:T(8,128)(2,1)} %param.11) | copy-start | bytes 786436
  73.0 23.8 %collective-permute-start.6 = (bf16[144,2048]{1,0:T(8,128)(2,1)S(1)}, bf16[144,2048]{1,0:T(8,128)(2,1)S(1)}, u32[]{:S(2)}, u32[]{:S(2)}) collective-permute-start(bf16[144,2048]{1,0:T(8,128)(2,1)S(1)} %collective-permute-done.5), channel_id=1, source_target_pairs={{0,4},{4,8},{8,12},{12,16},{16,20},{20,24},{24,28},{28,32},{32,36}... | collective-permute-start | bytes 1769480 | tf_op jit(solution)/shard_map/ppermute | solution.py:27
  83.1 23.7 %collective-permute-start.3 = (bf16[144,2048]{1,0:T(8,128)(2,1)S(1)}, bf16[144,2048]{1,0:T(8,128)(2,1)S(1)}, u32[]{:S(2)}, u32[]{:S(2)}) collective-permute-start(bf16[144,2048]{1,0:T(8,128)(2,1)S(1)} %collective-permute-done.2), channel_id=1, source_target_pairs={{0,508},{4,0},{8,4},{12,8},{16,12},{20,16},{24,20},{28,24},{32,28}... | collective-permute-start | bytes 1769480 | tf_op jit(solution)/shard_map/ppermute | solution.py:27
  96.9 10.0 %collective-permute-start.7 = (bf16[144,2048]{1,0:T(8,128)(2,1)S(1)}, bf16[144,2048]{1,0:T(8,128)(2,1)S(1)}, u32[]{:S(2)}, u32[]{:S(2)}) collective-permute-start(bf16[144,2048]{1,0:T(8,128)(2,1)S(1)} %collective-permute-done.6), channel_id=1, source_target_pairs={{0,4},{4,8},{8,12},{12,16},{16,20},{20,24},{24,28},{28,32},{32,36}... | collective-permute-start | bytes 1769480 | tf_op jit(solution)/shard_map/ppermute | solution.py:27
  112.7 6.9 %copy-start.33 = (f32[128]{0:T(128)S(1)}, f32[128]{0:T(128)}, u32[]{:S(2)}) copy-start(f32[128]{0:T(128)} %param.15) | copy-start | bytes 1540
  119.6 4.2 %copy-start.26 = (f32[1152,8]{0,1:T(8,128)}, f32[1152,8]{0,1:T(8,128)S(1)}, u32[]{:S(2)}) copy-start(f32[1152,8]{0,1:T(8,128)S(1)} %add_rsqrt_fusion) | copy-start | bytes 110596
  125.7 4.5 %copy-start.4 = (bf16[1152,8,64]{2,0,1:T(8,128)(2,1)}, bf16[1152,8,64]{2,0,1:T(8,128)(2,1)S(1)}, u32[]{:S(2)}) copy-start(bf16[1152,8,64]{2,0,1:T(8,128)(2,1)S(1)} %get-tuple-element.37) | copy-start | bytes 3538948
  125.7 4.5 %copy-start.6 = (bf16[1152,8,64]{2,0,1:T(8,128)(2,1)}, bf16[1152,8,64]{2,0,1:T(8,128)(2,1)S(1)}, u32[]{:S(2)}) copy-start(bf16[1152,8,64]{2,0,1:T(8,128)(2,1)S(1)} %get-tuple-element.38) | copy-start | bytes 3538948
  126.8 7.0 %copy-start.12 = (bf16[1152,8,128,1]{0,2,3,1:T(8,128)(2,1)S(1)}, bf16[1152,8,128,1]{0,2,3,1:T(8,128)(2,1)}, u32[]{:S(2)}) copy-start(bf16[1152,8,128,1]{0,2,3,1:T(8,128)(2,1)} %copy.119) | copy-start | bytes 7077892
  130.1 3.6 copy-start.39
  138.9 8.0 %copy-start.14 = (bf16[128,8,2,128]{3,2,1,0:T(2,128)(2,1)S(1)}, bf16[128,8,2,128]{3,2,1,0:T(2,128)(2,1)}, u32[]{:S(2)}) copy-start(bf16[128,8,2,128]{3,2,1,0:T(2,128)(2,1)} %reshape_squeeze.4) | copy-start | bytes 1572868
  150.1 6.6 %copy-start.16 = (bf16[128,16,64]{2,0,1:T(8,128)(2,1)S(1)}, bf16[128,16,64]{2,0,1:T(8,128)(2,1)}, u32[]{:S(2)}) copy-start(bf16[128,16,64]{2,0,1:T(8,128)(2,1)} %copy.96) | copy-start | bytes 786436
  150.1 6.6 %copy-start.18 = (bf16[128,16,64]{2,0,1:T(8,128)(2,1)S(1)}, bf16[128,16,64]{2,0,1:T(8,128)(2,1)}, u32[]{:S(2)}) copy-start(bf16[128,16,64]{2,0,1:T(8,128)(2,1)} %copy.97) | copy-start | bytes 786436
  164.5 25.6 %copy-start = (f32[2,8,9,128,128]{4,1,3,0,2:T(8,128)}, f32[2,8,9,128,128]{4,1,3,0,2:T(8,128)S(1)}, u32[]{:S(2)}) copy-start(f32[2,8,9,128,128]{4,1,3,0,2:T(8,128)S(1)} %copy_dynamic-update-slice_fusion) | copy-start | bytes 28311556
  168.8 11.8 %collective-permute-start.8 = (bf16[2,8,128,128]{3,1,2,0:T(8,128)(2,1)}, bf16[2,8,128,128]{3,1,2,0:T(8,128)(2,1)}, u32[]{:S(2)}, u32[]{:S(2)}) collective-permute-start(bf16[2,8,128,128]{3,1,2,0:T(8,128)(2,1)} %get-tuple-element.41), channel_id=1, source_target_pairs={{4,0},{8,4},{12,8},{16,12},{20,16},{24,20},{28,24},{32,28},{36,32}... | collective-permute-start | bytes 1572872 | tf_op jit(solution)/shard_map/ppermute | solution.py:27
  170.1 20.0 %collective-permute-start.12 = (bf16[2,8,128,128]{3,1,2,0:T(8,128)(2,1)}, bf16[2,8,128,128]{3,1,2,0:T(8,128)(2,1)}, u32[]{:S(2)}, u32[]{:S(2)}) collective-permute-start(bf16[2,8,128,128]{3,1,2,0:T(8,128)(2,1)} %get-tuple-element.42), channel_id=1, source_target_pairs={{0,4},{4,8},{8,12},{12,16},{16,20},{20,24},{24,28},{28,32},{32,36}... | collective-permute-start | bytes 1572872 | tf_op jit(solution)/shard_map/ppermute | solution.py:27
  180.6 16.2 %copy-start.5 = (bf16[1152,8,64]{2,0,1:T(8,128)(2,1)S(1)}, bf16[1152,8,64]{2,0,1:T(8,128)(2,1)}, u32[]{:S(2)}) copy-start(bf16[1152,8,64]{2,0,1:T(8,128)(2,1)} %copy-done.4) | copy-start | bytes 3538948
  191.5 13.6 %collective-permute-start.9 = (bf16[2,8,128,128]{3,1,2,0:T(8,128)(2,1)S(1)}, bf16[2,8,128,128]{3,1,2,0:T(8,128)(2,1)S(1)}, u32[]{:S(2)}, u32[]{:S(2)}) collective-permute-start(bf16[2,8,128,128]{3,1,2,0:T(8,128)(2,1)S(1)} %get-tuple-element.33), channel_id=1, source_target_pairs={{4,0},{8,4},{12,8},{16,12},{20,16},{24,20},{28,24},{32,28},{36,32}... | collective-permute-start | bytes 1572872 | tf_op jit(solution)/shard_map/ppermute | solution.py:27
  192.8 23.3 %collective-permute-start.13 = (bf16[2,8,128,128]{3,1,2,0:T(8,128)(2,1)S(1)}, bf16[2,8,128,128]{3,1,2,0:T(8,128)(2,1)}, u32[]{:S(2)}, u32[]{:S(2)}) collective-permute-start(bf16[2,8,128,128]{3,1,2,0:T(8,128)(2,1)S(1)} %get-tuple-element.34), channel_id=1, source_target_pairs={{0,4},{4,8},{8,12},{12,16},{16,20},{20,24},{24,28},{28,32},{32,36}... | collective-permute-start | bytes 1572872 | tf_op jit(solution)/shard_map/ppermute | solution.py:27
  202.1 22.3 %copy-start.22 = (f32[128,64]{1,0:T(8,128)S(1)}, f32[128,64]{1,0:T(8,128)}, u32[]{:S(2)}) copy-start(f32[128,64]{1,0:T(8,128)} %copy-done.21) | copy-start | bytes 98308
  202.1 22.3 %copy-start.24 = (f32[128,64]{1,0:T(8,128)S(1)}, f32[128,64]{1,0:T(8,128)}, u32[]{:S(2)}) copy-start(f32[128,64]{1,0:T(8,128)} %copy-done.23) | copy-start | bytes 98308
  203.6 21.1 %copy-start.2 = (f32[16,8,16,128]{3,2,1,0:T(8,128)S(1)}, f32[16,8,16,128]{3,2,1,0:T(8,128)}, u32[]{:S(2)}) copy-start(f32[16,8,16,128]{3,2,1,0:T(8,128)} %copy-done.1) | copy-start | bytes 3145732
  203.6 21.1 %copy-start.20 = (f32[128,16]{1,0:T(8,128)S(1)}, f32[128,16]{1,0:T(8,128)}, u32[]{:S(2)}) copy-start(f32[128,16]{1,0:T(8,128)} %copy-done.19) | copy-start | bytes 24580
  203.6 21.1 %copy-start.36 = (f32[128]{0:T(128)S(1)}, f32[128]{0:T(128)}, u32[]{:S(2)}) copy-start(f32[128]{0:T(128)} %param.14) | copy-start | bytes 1540
  205.1 19.3 %copy-start.10 = (f32[128,16,64]{2,1,0:T(8,128)S(1)}, f32[128,16,64]{2,1,0:T(8,128)}, u32[]{:S(2)}) copy-start(f32[128,16,64]{2,1,0:T(8,128)} %copy.138) | copy-start | bytes 1572868
  205.1 19.4 %copy-start.11 = (f32[128,16,64]{2,1,0:T(8,128)S(1)}, f32[128,16,64]{2,1,0:T(8,128)}, u32[]{:S(2)}) copy-start(f32[128,16,64]{2,1,0:T(8,128)} %copy.139) | copy-start | bytes 1572868
  219.0 6.7 %copy-start.29 = (f32[128,16]{0,1:T(8,128)S(1)}, f32[128,16]{0,1:T(8,128)}, u32[]{:S(2)}) copy-start(f32[128,16]{0,1:T(8,128)} %copy-done.28) | copy-start | bytes 24580
  219.0 10.4 %collective-permute-start.10 = (bf16[2,8,128,128]{3,1,2,0:T(8,128)(2,1)}, bf16[2,8,128,128]{3,1,2,0:T(8,128)(2,1)}, u32[]{:S(2)}, u32[]{:S(2)}) collective-permute-start(bf16[2,8,128,128]{3,1,2,0:T(8,128)(2,1)} %get-tuple-element.31), channel_id=1, source_target_pairs={{4,0},{8,4},{12,8},{16,12},{20,16},{24,20},{28,24},{32,28},{36,32}... | collective-permute-start | bytes 1572872 | tf_op jit(solution)/shard_map/ppermute | solution.py:27
  220.4 18.9 %collective-permute-start.14 = (bf16[2,8,128,128]{3,1,2,0:T(8,128)(2,1)}, bf16[2,8,128,128]{3,1,2,0:T(8,128)(2,1)}, u32[]{:S(2)}, u32[]{:S(2)}) collective-permute-start(bf16[2,8,128,128]{3,1,2,0:T(8,128)(2,1)} %get-tuple-element.32), channel_id=1, source_target_pairs={{0,4},{4,8},{8,12},{12,16},{16,20},{20,24},{24,28},{28,32},{32,36}... | collective-permute-start | bytes 1572872 | tf_op jit(solution)/shard_map/ppermute | solution.py:27
  225.7 23.8 %copy-start.27 = (f32[1152,8]{0,1:T(8,128)S(1)}, f32[1152,8]{0,1:T(8,128)}, u32[]{:S(2)}) copy-start(f32[1152,8]{0,1:T(8,128)} %copy-done.26) | copy-start | bytes 110596
  242.4 133.1 %collective-permute-start.11 = (bf16[2,8,128,128]{3,1,2,0:T(8,128)(2,1)}, bf16[2,8,128,128]{3,1,2,0:T(8,128)(2,1)}, u32[]{:S(2)}, u32[]{:S(2)}) collective-permute-start(bf16[2,8,128,128]{3,1,2,0:T(8,128)(2,1)} %get-tuple-element.29), channel_id=1, source_target_pairs={{4,0},{8,4},{12,8},{16,12},{20,16},{24,20},{28,24},{32,28},{36,32}... | collective-permute-start | bytes 1572872 | tf_op jit(solution)/shard_map/ppermute | solution.py:27
  243.6 131.8 %collective-permute-start.15 = (bf16[2,8,128,128]{3,1,2,0:T(8,128)(2,1)}, bf16[2,8,128,128]{3,1,2,0:T(8,128)(2,1)}, u32[]{:S(2)}, u32[]{:S(2)}) collective-permute-start(bf16[2,8,128,128]{3,1,2,0:T(8,128)(2,1)} %get-tuple-element.30), channel_id=1, source_target_pairs={{0,480},{4,484},{8,488},{12,492},{16,496},{20,500},{24,504},{28,50... | collective-permute-start | bytes 1572872 | tf_op jit(solution)/shard_map/ppermute | solution.py:27
  255.9 122.4 %copy-start.9 = (f32[16,8,8,128]{3,2,1,0:T(8,128)S(1)}, f32[16,8,8,128]{3,2,1,0:T(8,128)}, u32[]{:S(2)}) copy-start(f32[16,8,8,128]{3,2,1,0:T(8,128)} %copy.144) | copy-start | bytes 1572868
  255.9 122.4 %copy-start.34 = (f32[128]{0:T(128)S(1)}, f32[128]{0:T(128)}, u32[]{:S(2)}) copy-start(f32[128]{0:T(128)} %param.15) | copy-start | bytes 1540
  (11 other events, 26.8 us)

commit v11 on v10

--- a/solution.py
+++ b/solution.py
@@ -155,7 +155,7 @@
         carry_far = (got + slots[:, :, behind - offset]).astype(jnp.bfloat16)
     sent = [shift(carry_near, -1, False), shift(carry_far, -behind, True)]
     gains = (query_gain_gradient, key_gain_gradient)
-    for axis in ("y", "x", "zh", DP_AXES):
+    for axis in ("y", "x", ("zh",) + DP_AXES):
         gains = lax.psum(gains, axis)
     gain_query, gain_key = gains
     total = slots[:, :, behind]

time: 389 us -> 392 us (level)
  the two profiles are of different devices: /device:TPU:1 before, /device:TPU:193 now
where the time goes in v11:
time: 392 us; the launch traced here: 384 us
  waiting for transfers between devices  132 us (34%)
  blocking collectives  76.1 us (19%)
  starting transfers between devices  58.7 us (15%)
  other arithmetic  50.8 us (13%)
  local copies, waits for them, and re-layouts  36.8 us (9%)
  matrix products  28 us (7%)
    ppermute x16, waiting for transfers between devices, shift(): return lax.ppermute(value, SEQ_AXES, pairs)  132 us
    psum x3, blocking collectives, shards(): gains = lax.psum(gains, axis)  76.1 us
    ppermute x16, starting transfers between devices, shift(): return lax.ppermute(value, SEQ_AXES, pairs)  58.7 us
    unnamed x103, local copies, waits for them, and re-layouts  18.6 us
    dot_general x1, matrix products, attend(): jnp.einsum('grtw,tgrd->gwd', weights_b, gradient_block, preferred_element...  7.98 us
  transfers between devices with their start and end apart: 16, of which 9 were waited for; matrix products, arithmetic and copies ran while one was open for 10% of the time, Pallas kernels for 0%

profile of v11, /device:TPU:193, one launch (start us, length us, event | category | flops | bytes accessed | tf_op | source)
XLA Modules:
  0.0 384.3 jit_solution(1247719684394809004)
XLA Ops:
  2.4 3.2 collective-permute-start.4
  5.6 3.1 collective-permute-start
  10.3 2.2 reshape_squeeze.4
  18.4 43.4 %collective-permute-done = bf16[144,2048]{1,0:T(8,128)(2,1)} collective-permute-done((bf16[144,2048]{1,0:T(8,128)(2,1)S(1)}, bf16[144,2048]{1,0:T(8,128)(2,1)}, u32[]{:S(2)}, u32[]{:S(2)}) %collective-permute-start) | collective-permute-done | bytes 589856 | tf_op jit(solution)/shard_map/ppermute | solution.py:27
  61.8 1.9 collective-permute-start.1
  64.3 3.4 collective-permute-start.5
  67.7 2.1 multiply_cosine_fusion
  69.8 16.5 %collective-permute-done.1 = bf16[144,2048]{1,0:T(8,128)(2,1)S(1)} collective-permute-done((bf16[144,2048]{1,0:T(8,128)(2,1)}, bf16[144,2048]{1,0:T(8,128)(2,1)S(1)}, u32[]{:S(2)}, u32[]{:S(2)}) %collective-permute-start.1) | collective-permute-done | bytes 589856 | tf_op jit(solution)/shard_map/ppermute | solution.py:27
  86.3 11.4 %collective-permute-start.2 = (bf16[144,2048]{1,0:T(8,128)(2,1)S(1)}, bf16[144,2048]{1,0:T(8,128)(2,1)S(1)}, u32[]{:S(2)}, u32[]{:S(2)}) collective-permute-start(bf16[144,2048]{1,0:T(8,128)(2,1)S(1)} %collective-permute-done.1), channel_id=1, source_target_pairs={{0,508},{4,0},{8,4},{12,8},{16,12},{20,16},{24,20},{28,24},{32,28}... | collective-permute-start | bytes 1769480 | tf_op jit(solution)/shard_map/ppermute | solution.py:27
  98.3 2.0 collective-permute-start.6
  101.5 14.1 %collective-permute-done.2 = bf16[144,2048]{1,0:T(8,128)(2,1)S(1)} collective-permute-done((bf16[144,2048]{1,0:T(8,128)(2,1)S(1)}, bf16[144,2048]{1,0:T(8,128)(2,1)S(1)}, u32[]{:S(2)}, u32[]{:S(2)}) %collective-permute-start.2) | collective-permute-done | bytes 589856 | tf_op jit(solution)/shard_map/ppermute | solution.py:27
  115.6 11.7 %collective-permute-start.3 = (bf16[144,2048]{1,0:T(8,128)(2,1)S(1)}, bf16[144,2048]{1,0:T(8,128)(2,1)S(1)}, u32[]{:S(2)}, u32[]{:S(2)}) collective-permute-start(bf16[144,2048]{1,0:T(8,128)(2,1)S(1)} %collective-permute-done.2), channel_id=1, source_target_pairs={{0,508},{4,0},{8,4},{12,8},{16,12},{20,16},{24,20},{28,24},{32,28}... | collective-permute-start | bytes 1769480 | tf_op jit(solution)/shard_map/ppermute | solution.py:27
  127.4 1.9 collective-permute-start.7
  129.4 11.2 %collective-permute-done.3 = bf16[144,2048]{1,0:T(8,128)(2,1)S(1)} collective-permute-done((bf16[144,2048]{1,0:T(8,128)(2,1)S(1)}, bf16[144,2048]{1,0:T(8,128)(2,1)S(1)}, u32[]{:S(2)}, u32[]{:S(2)}) %collective-permute-start.3) | collective-permute-done | bytes 589856 | tf_op jit(solution)/shard_map/ppermute | solution.py:27
  140.6 11.6 %collective-permute-done.7 = bf16[144,2048]{1,0:T(8,128)(2,1)S(1)} collective-permute-done((bf16[144,2048]{1,0:T(8,128)(2,1)S(1)}, bf16[144,2048]{1,0:T(8,128)(2,1)S(1)}, u32[]{:S(2)}, u32[]{:S(2)}) %collective-permute-start.7) | collective-permute-done | bytes 589856 | tf_op jit(solution)/shard_map/ppermute | solution.py:27
  154.0 3.3 copy.141
  158.0 3.0 copy.119
  161.0 3.7 multiply_reduce_fusion.1
  164.9 4.1 %fusion.4 = f32[1152,8,128]{2,0,1:T(8,128)S(1)} fusion(f32[1152,8,128]{2,1,0:T(8,128)} %bitcast.163, f32[128]{0:T(128)S(1)} %copy-done.33, f32[1152,8]{0,1:T(8,128)S(1)} %add_rsqrt_fusion), kind=kLoop, calls=%fused_computation.17 | loop fusion | flops 2359296 | bytes 9474560 | tf_op jit(solution)/shard_map/jvp()/mul | solution.py:45
  172.1 3.3 fusion.3
  175.5 3.6 copy-done.39
  179.1 3.4 fusion.10
  184.3 8.0 %fusion.5 = f32[8,1152,128,1]{2,1,3,0:T(8,128)} fusion(bf16[128,8,2,128]{3,2,1,0:T(2,128)(2,1)} %reshape_squeeze.4, f32[8,1152,128,2]{2,1,3,0:T(8,128)} %copy-done.39, f32[8,2,128]{2,1,0:T(2,128)} %copy-done.40, pred[128,1152]{0,1:T(8,128)(4,1)S(1)} %fusion.32), kind=kOutput, calls=%fused_computation.20 | convolution fusion | flops 613416960 | bytes 14835712 | tf_op jit(solution)/shard_map/grtw,tgrd->gwd/dot_general | solution.py:71
  192.3 2.0 multiply_reduce_fusion.2
  195.5 6.6 %fusion.1 = bf16[8,2,128,1152]{2,3,1,0:T(8,128)(2,1)S(1)} fusion(bf16[1152,8,128,1]{0,2,3,1:T(8,128)(2,1)S(1)} %copy-done.12, f32[8,2,128]{2,1,0:T(2,128)S(1)} %copy.127, bf16[128,8,2,128]{3,2,1,0:T(2,128)(2,1)} %reshape_squeeze.4, f32[8,2,128]{2,1,0:T(2,128)} %copy-done.40, f32[8,1152,128,2]{2,1,3,0:T(8,128)} %copy-done.39, pred[128,1152]{0,1:T(8,128)(4,1)S(1)} %fusion.32), kind=kOutput, calls=%fused_computation.2 | convolution fusion | flops 618135552 | bytes 17203200 | tf_op jit(solution)/shard_map/tgrd,wgd->grtw/dot_general | solution.py:61
  204.3 2.7 copy_dynamic-update-slice_fusion.1
  207.1 2.7 copy_dynamic-update-slice_fusion
  214.1 1.9 collective-permute-start.8
  216.0 3.6 collective-permute-start.12
  219.7 6.2 %multiply_add_fusion.1 = (f32[1152,8,64]{2,0,1:T(8,128)}, f32[1152,8,64]{2,0,1:T(8,128)}) fusion(f32[1152,8,128]{2,0,1:T(8,128)S(1)} %bitcast.165, f32[1152,64]{1,0:T(8,128)} %copy-done.8, f32[1152,64]{1,0:T(8,128)} %copy-done.7), kind=kLoop, calls=%fused_computation.13 | loop fusion | flops 4128768 | bytes 10027008 | tf_op jit(solution)/shard_map/transpose(jvp())/add_any | solution.py:39
  225.9 9.5 %collective-permute-done.12 = bf16[2,8,128,128]{3,1,2,0:T(8,128)(2,1)} collective-permute-done((bf16[2,8,128,128]{3,1,2,0:T(8,128)(2,1)}, bf16[2,8,128,128]{3,1,2,0:T(8,128)(2,1)}, u32[]{:S(2)}, u32[]{:S(2)}) %collective-permute-start.12) | collective-permute-done | bytes 524320 | tf_op jit(solution)/shard_map/ppermute | solution.py:27
  236.9 1.9 collective-permute-start.9
  238.8 3.4 collective-permute-start.13
  242.2 5.3 %convolution_multiply_fusion = f32[8,128,2,128]{3,1,2,0:T(8,128)S(1)} fusion(bf16[8,2,128,1152]{2,3,1,0:T(8,128)(2,1)} %copy-done.3, bf16[1152,8,64]{2,0,1:T(8,128)(2,1)} %copy-done.6, bf16[1152,8,64]{2,0,1:T(8,128)(2,1)S(1)} %copy-done.5), kind=kOutput, calls=%fused_computation.28 | convolution fusion | flops 608960512 | bytes 8126464 | tf_op jit(solution)/shard_map/grtw,wgd->tgrd/dot_general | solution.py:65
  250.4 9.2 %collective-permute-done.13 = bf16[2,8,128,128]{3,1,2,0:T(8,128)(2,1)} collective-permute-done((bf16[2,8,128,128]{3,1,2,0:T(8,128)(2,1)S(1)}, bf16[2,8,128,128]{3,1,2,0:T(8,128)(2,1)}, u32[]{:S(2)}, u32[]{:S(2)}) %collective-permute-start.13) | collective-permute-done | bytes 524320 | tf_op jit(solution)/shard_map/ppermute | solution.py:27
  259.6 2.9 fusion.24
  262.4 2.0 collective-permute-start.10
  264.5 3.4 collective-permute-start.14
  269.3 4.6 %collective-permute-done.10 = bf16[2,8,128,128]{3,1,2,0:T(8,128)(2,1)} collective-permute-done((bf16[2,8,128,128]{3,1,2,0:T(8,128)(2,1)}, bf16[2,8,128,128]{3,1,2,0:T(8,128)(2,1)}, u32[]{:S(2)}, u32[]{:S(2)}) %collective-permute-start.10) | collective-permute-done | bytes 524320 | tf_op jit(solution)/shard_map/ppermute | solution.py:27
  273.9 11.6 %collective-permute-done.14 = bf16[2,8,128,128]{3,1,2,0:T(8,128)(2,1)} collective-permute-done((bf16[2,8,128,128]{3,1,2,0:T(8,128)(2,1)}, bf16[2,8,128,128]{3,1,2,0:T(8,128)(2,1)}, u32[]{:S(2)}, u32[]{:S(2)}) %collective-permute-start.14) | collective-permute-done | bytes 524320 | tf_op jit(solution)/shard_map/ppermute | solution.py:27
  285.5 3.0 fusion.22
  288.6 1.9 collective-permute-start.11
  290.5 1.9 collective-permute-start.15
  294.2 2.1 reshape.269
  296.3 6.5 %multiply_reduce_fusion = f32[128]{0:T(128)S(1)} fusion(f32[1152,8,64]{2,0,1:T(8,128)} %get-tuple-element.34, f32[1152,8,64]{2,0,1:T(8,128)} %get-tuple-element.33, f32[1152,8,128]{2,1,0:T(8,128)} %bitcast.164, f32[1152,8]{0,1:T(8,128)S(1)} %copy-done.27), kind=kLoop, calls=%fused_computation.11 | loop fusion | flops 4718464 | bytes 9474560 | tf_op jit(solution)/shard_map/transpose(jvp())/reduce_sum | solution.py:45
  302.8 12.4 %all-reduce.8 = (f32[128]{0:T(128)S(1)}, f32[128]{0:T(128)S(1)}) all-reduce(f32[128]{0:T(128)S(1)} %get-tuple-element.17, f32[128]{0:T(128)S(1)} %multiply_reduce_fusion), channel_id=1, replica_groups=mesh['zh'=4,'x'=4,'y'=8,'zl'=2,'c'=2] {'y'}, use_global_device_ids=true, to_apply=%region_7.8 | all-reduce | flops 256 | bytes 2048 | tf_op jit(solution)/shard_map/psum | solution.py:159
  315.1 10.3 %all-reduce.9 = (f32[128]{0:T(128)S(1)}, f32[128]{0:T(128)S(1)}) all-reduce(f32[128]{0:T(128)S(1)} %get-tuple-element.23, f32[128]{0:T(128)S(1)} %get-tuple-element.24), channel_id=1, replica_groups=mesh['zh'=4,'x'=4,'y'=8,'zl'=2,'c'=2] {'x'}, use_global_device_ids=true, to_apply=%region_8.9 | all-reduce | flops 256 | bytes 2048 | tf_op jit(solution)/shard_map/psum | solution.py:159
  325.4 53.4 %all-reduce.7 = (f32[128]{0:T(128)}, f32[128]{0:T(128)}) all-reduce(f32[128]{0:T(128)S(1)} %get-tuple-element.25, f32[128]{0:T(128)S(1)} %get-tuple-element.26), channel_id=1, replica_groups=mesh['zh'=4,'x'=4,'y'=8,'zl'=2,'c'=2] {'zh','zl','c'}, use_global_device_ids=true, to_apply=%region_9.10 | all-reduce | flops 256 | bytes 2048 | tf_op jit(solution)/shard_map/psum | solution.py:159
  (161 shorter events, 38.9 us)
Async XLA Ops:
  0.6 14.6 %copy-start.35 = (f32[128]{0:T(128)S(1)}, f32[128]{0:T(128)}, u32[]{:S(2)}) copy-start(f32[128]{0:T(128)} %param.14) | copy-start | bytes 1540
  2.4 61.9 %collective-permute-start.4 = (bf16[144,2048]{1,0:T(8,128)(2,1)S(1)}, bf16[144,2048]{1,0:T(8,128)(2,1)S(1)}, u32[]{:S(2)}, u32[]{:S(2)}) collective-permute-start(bf16[144,2048]{1,0:T(8,128)(2,1)S(1)} %fusion.29), channel_id=1, source_target_pairs={{0,4},{4,8},{8,12},{12,16},{16,20},{20,24},{24,28},{28,32},{32,36}... | collective-permute-start | bytes 1769480 | tf_op jit(solution)/shard_map/ppermute | solution.py:27
  5.6 56.2 %collective-permute-start = (bf16[144,2048]{1,0:T(8,128)(2,1)S(1)}, bf16[144,2048]{1,0:T(8,128)(2,1)}, u32[]{:S(2)}, u32[]{:S(2)}) collective-permute-start(bf16[144,2048]{1,0:T(8,128)(2,1)S(1)} %fusion.29), channel_id=1, source_target_pairs={{0,32},{4,36},{8,40},{12,44},{16,48},{20,52},{24,56},{28,60},{32,6... | collective-permute-start | bytes 1769480 | tf_op jit(solution)/shard_map/ppermute | solution.py:27
  14.7 55.1 %copy-start.1 = (f32[16,8,16,128]{3,2,1,0:T(8,128)}, f32[16,8,16,128]{3,2,1,0:T(8,128)S(1)}, u32[]{:S(2)}) copy-start(f32[16,8,16,128]{3,2,1,0:T(8,128)S(1)} %copy.142) | copy-start | bytes 3145732
  15.1 82.6 %copy-start.28 = (f32[128,16]{0,1:T(8,128)}, f32[128,16]{0,1:T(8,128)S(1)}, u32[]{:S(2)}) copy-start(f32[128,16]{0,1:T(8,128)S(1)} %copy.94) | copy-start | bytes 24580
  15.3 86.2 %copy-start.19 = (f32[128,16]{1,0:T(8,128)}, f32[128,16]{1,0:T(8,128)S(1)}, u32[]{:S(2)}) copy-start(f32[128,16]{1,0:T(8,128)S(1)} %copy.95) | copy-start | bytes 24580
  15.9 113.4 %copy-start.21 = (f32[128,64]{1,0:T(8,128)}, f32[128,64]{1,0:T(8,128)S(1)}, u32[]{:S(2)}) copy-start(f32[128,64]{1,0:T(8,128)S(1)} %get-tuple-element.53) | copy-start | bytes 98308
  16.0 113.4 %copy-start.23 = (f32[128,64]{1,0:T(8,128)}, f32[128,64]{1,0:T(8,128)S(1)}, u32[]{:S(2)}) copy-start(f32[128,64]{1,0:T(8,128)S(1)} %get-tuple-element.54) | copy-start | bytes 98308
  61.8 24.5 %collective-permute-start.1 = (bf16[144,2048]{1,0:T(8,128)(2,1)}, bf16[144,2048]{1,0:T(8,128)(2,1)S(1)}, u32[]{:S(2)}, u32[]{:S(2)}) collective-permute-start(bf16[144,2048]{1,0:T(8,128)(2,1)} %collective-permute-done), channel_id=1, source_target_pairs={{0,508},{4,0},{8,4},{12,8},{16,12},{20,16},{24,20},{28,24},{32,28}... | collective-permute-start | bytes 1769480 | tf_op jit(solution)/shard_map/ppermute | solution.py:27
  64.3 34.0 %collective-permute-start.5 = (bf16[144,2048]{1,0:T(8,128)(2,1)S(1)}, bf16[144,2048]{1,0:T(8,128)(2,1)S(1)}, u32[]{:S(2)}, u32[]{:S(2)}) collective-permute-start(bf16[144,2048]{1,0:T(8,128)(2,1)S(1)} %collective-permute-done.4), channel_id=1, source_target_pairs={{0,4},{4,8},{8,12},{12,16},{16,20},{20,24},{24,28},{28,32},{32,36}... | collective-permute-start | bytes 1769480 | tf_op jit(solution)/shard_map/ppermute | solution.py:27
  69.8 99.3 %copy-start.7 = (f32[1152,64]{1,0:T(8,128)}, f32[1152,64]{1,0:T(8,128)S(1)}, u32[]{:S(2)}) copy-start(f32[1152,64]{1,0:T(8,128)S(1)} %get-tuple-element.49) | copy-start | bytes 884740
  69.8 99.3 %copy-start.8 = (f32[1152,64]{1,0:T(8,128)}, f32[1152,64]{1,0:T(8,128)S(1)}, u32[]{:S(2)}) copy-start(f32[1152,64]{1,0:T(8,128)S(1)} %get-tuple-element.50) | copy-start | bytes 884740
  86.3 29.3 %collective-permute-start.2 = (bf16[144,2048]{1,0:T(8,128)(2,1)S(1)}, bf16[144,2048]{1,0:T(8,128)(2,1)S(1)}, u32[]{:S(2)}, u32[]{:S(2)}) collective-permute-start(bf16[144,2048]{1,0:T(8,128)(2,1)S(1)} %collective-permute-done.1), channel_id=1, source_target_pairs={{0,508},{4,0},{8,4},{12,8},{16,12},{20,16},{24,20},{28,24},{32,28}... | collective-permute-start | bytes 1769480 | tf_op jit(solution)/shard_map/ppermute | solution.py:27
  98.3 54.1 %copy-start.13 = (bf16[1,128,1024]{2,1,0:T(8,128)(2,1)S(1)}, bf16[1,128,1024]{2,1,0:T(8,128)(2,1)}, u32[]{:S(2)}) copy-start(bf16[1,128,1024]{2,1,0:T(8,128)(2,1)} %param.10) | copy-start | bytes 786436
  98.3 54.1 %copy-start.25 = (bf16[1,128,1024]{2,1,0:T(8,128)(2,1)S(1)}, bf16[1,128,1024]{2,1,0:T(8,128)(2,1)}, u32[]{:S(2)}) copy-start(bf16[1,128,1024]{2,1,0:T(8,128)(2,1)} %param.11) | copy-start | bytes 786436
  98.3 29.1 %collective-permute-start.6 = (bf16[144,2048]{1,0:T(8,128)(2,1)S(1)}, bf16[144,2048]{1,0:T(8,128)(2,1)S(1)}, u32[]{:S(2)}, u32[]{:S(2)}) collective-permute-start(bf16[144,2048]{1,0:T(8,128)(2,1)S(1)} %collective-permute-done.5), channel_id=1, source_target_pairs={{0,4},{4,8},{8,12},{12,16},{16,20},{20,24},{24,28},{28,32},{32,36}... | collective-permute-start | bytes 1769480 | tf_op jit(solution)/shard_map/ppermute | solution.py:27
  115.6 25.0 %collective-permute-start.3 = (bf16[144,2048]{1,0:T(8,128)(2,1)S(1)}, bf16[144,2048]{1,0:T(8,128)(2,1)S(1)}, u32[]{:S(2)}, u32[]{:S(2)}) collective-permute-start(bf16[144,2048]{1,0:T(8,128)(2,1)S(1)} %collective-permute-done.2), channel_id=1, source_target_pairs={{0,508},{4,0},{8,4},{12,8},{16,12},{20,16},{24,20},{28,24},{32,28}... | collective-permute-start | bytes 1769480 | tf_op jit(solution)/shard_map/ppermute | solution.py:27
  127.4 24.8 %collective-permute-start.7 = (bf16[144,2048]{1,0:T(8,128)(2,1)S(1)}, bf16[144,2048]{1,0:T(8,128)(2,1)S(1)}, u32[]{:S(2)}, u32[]{:S(2)}) collective-permute-start(bf16[144,2048]{1,0:T(8,128)(2,1)S(1)} %collective-permute-done.6), channel_id=1, source_target_pairs={{0,4},{4,8},{8,12},{12,16},{16,20},{20,24},{24,28},{28,32},{32,36}... | collective-permute-start | bytes 1769480 | tf_op jit(solution)/shard_map/ppermute | solution.py:27
  158.0 6.9 %copy-start.33 = (f32[128]{0:T(128)S(1)}, f32[128]{0:T(128)}, u32[]{:S(2)}) copy-start(f32[128]{0:T(128)} %param.15) | copy-start | bytes 1540
  164.9 4.2 %copy-start.26 = (f32[1152,8]{0,1:T(8,128)}, f32[1152,8]{0,1:T(8,128)S(1)}, u32[]{:S(2)}) copy-start(f32[1152,8]{0,1:T(8,128)S(1)} %add_rsqrt_fusion) | copy-start | bytes 110596
  171.0 4.5 %copy-start.4 = (bf16[1152,8,64]{2,0,1:T(8,128)(2,1)}, bf16[1152,8,64]{2,0,1:T(8,128)(2,1)S(1)}, u32[]{:S(2)}) copy-start(bf16[1152,8,64]{2,0,1:T(8,128)(2,1)S(1)} %get-tuple-element.35) | copy-start | bytes 3538948
  171.0 4.5 %copy-start.6 = (bf16[1152,8,64]{2,0,1:T(8,128)(2,1)}, bf16[1152,8,64]{2,0,1:T(8,128)(2,1)S(1)}, u32[]{:S(2)}) copy-start(bf16[1152,8,64]{2,0,1:T(8,128)(2,1)S(1)} %get-tuple-element.36) | copy-start | bytes 3538948
  172.1 7.0 %copy-start.12 = (bf16[1152,8,128,1]{0,2,3,1:T(8,128)(2,1)S(1)}, bf16[1152,8,128,1]{0,2,3,1:T(8,128)(2,1)}, u32[]{:S(2)}) copy-start(bf16[1152,8,128,1]{0,2,3,1:T(8,128)(2,1)} %copy.119) | copy-start | bytes 7077892
  175.5 3.6 copy-start.39
  184.3 8.0 %copy-start.14 = (bf16[128,8,2,128]{3,2,1,0:T(2,128)(2,1)S(1)}, bf16[128,8,2,128]{3,2,1,0:T(2,128)(2,1)}, u32[]{:S(2)}) copy-start(bf16[128,8,2,128]{3,2,1,0:T(2,128)(2,1)} %reshape_squeeze.4) | copy-start | bytes 1572868
  195.5 6.6 %copy-start.16 = (bf16[128,16,64]{2,0,1:T(8,128)(2,1)S(1)}, bf16[128,16,64]{2,0,1:T(8,128)(2,1)}, u32[]{:S(2)}) copy-start(bf16[128,16,64]{2,0,1:T(8,128)(2,1)} %copy.96) | copy-start | bytes 786436
  195.5 6.6 %copy-start.18 = (bf16[128,16,64]{2,0,1:T(8,128)(2,1)S(1)}, bf16[128,16,64]{2,0,1:T(8,128)(2,1)}, u32[]{:S(2)}) copy-start(bf16[128,16,64]{2,0,1:T(8,128)(2,1)} %copy.97) | copy-start | bytes 786436
  209.8 25.6 %copy-start = (f32[2,8,9,128,128]{4,1,3,0,2:T(8,128)}, f32[2,8,9,128,128]{4,1,3,0,2:T(8,128)S(1)}, u32[]{:S(2)}) copy-start(f32[2,8,9,128,128]{4,1,3,0,2:T(8,128)S(1)} %copy_dynamic-update-slice_fusion) | copy-start | bytes 28311556
  214.1 11.8 %collective-permute-start.8 = (bf16[2,8,128,128]{3,1,2,0:T(8,128)(2,1)}, bf16[2,8,128,128]{3,1,2,0:T(8,128)(2,1)}, u32[]{:S(2)}, u32[]{:S(2)}) collective-permute-start(bf16[2,8,128,128]{3,1,2,0:T(8,128)(2,1)} %get-tuple-element.39), channel_id=1, source_target_pairs={{4,0},{8,4},{12,8},{16,12},{20,16},{24,20},{28,24},{32,28},{36,32}... | collective-permute-start | bytes 1572872 | tf_op jit(solution)/shard_map/ppermute | solution.py:27
  216.0 19.4 %collective-permute-start.12 = (bf16[2,8,128,128]{3,1,2,0:T(8,128)(2,1)}, bf16[2,8,128,128]{3,1,2,0:T(8,128)(2,1)}, u32[]{:S(2)}, u32[]{:S(2)}) collective-permute-start(bf16[2,8,128,128]{3,1,2,0:T(8,128)(2,1)} %get-tuple-element.40), channel_id=1, source_target_pairs={{0,4},{4,8},{8,12},{12,16},{16,20},{20,24},{24,28},{28,32},{32,36}... | collective-permute-start | bytes 1572872 | tf_op jit(solution)/shard_map/ppermute | solution.py:27
  225.9 16.2 %copy-start.5 = (bf16[1152,8,64]{2,0,1:T(8,128)(2,1)S(1)}, bf16[1152,8,64]{2,0,1:T(8,128)(2,1)}, u32[]{:S(2)}) copy-start(bf16[1152,8,64]{2,0,1:T(8,128)(2,1)} %copy-done.4) | copy-start | bytes 3538948
  236.9 13.6 %collective-permute-start.9 = (bf16[2,8,128,128]{3,1,2,0:T(8,128)(2,1)S(1)}, bf16[2,8,128,128]{3,1,2,0:T(8,128)(2,1)S(1)}, u32[]{:S(2)}, u32[]{:S(2)}) collective-permute-start(bf16[2,8,128,128]{3,1,2,0:T(8,128)(2,1)S(1)} %get-tuple-element.31), channel_id=1, source_target_pairs={{4,0},{8,4},{12,8},{16,12},{20,16},{24,20},{28,24},{32,28},{36,32}... | collective-permute-start | bytes 1572872 | tf_op jit(solution)/shard_map/ppermute | solution.py:27
  238.8 20.8 %collective-permute-start.13 = (bf16[2,8,128,128]{3,1,2,0:T(8,128)(2,1)S(1)}, bf16[2,8,128,128]{3,1,2,0:T(8,128)(2,1)}, u32[]{:S(2)}, u32[]{:S(2)}) collective-permute-start(bf16[2,8,128,128]{3,1,2,0:T(8,128)(2,1)S(1)} %get-tuple-element.32), channel_id=1, source_target_pairs={{0,4},{4,8},{8,12},{12,16},{16,20},{20,24},{24,28},{28,32},{32,36}... | collective-permute-start | bytes 1572872 | tf_op jit(solution)/shard_map/ppermute | solution.py:27
  247.4 20.4 %copy-start.22 = (f32[128,64]{1,0:T(8,128)S(1)}, f32[128,64]{1,0:T(8,128)}, u32[]{:S(2)}) copy-start(f32[128,64]{1,0:T(8,128)} %copy-done.21) | copy-start | bytes 98308
  247.5 20.4 %copy-start.24 = (f32[128,64]{1,0:T(8,128)S(1)}, f32[128,64]{1,0:T(8,128)}, u32[]{:S(2)}) copy-start(f32[128,64]{1,0:T(8,128)} %copy-done.23) | copy-start | bytes 98308
  249.0 19.2 %copy-start.2 = (f32[16,8,16,128]{3,2,1,0:T(8,128)S(1)}, f32[16,8,16,128]{3,2,1,0:T(8,128)}, u32[]{:S(2)}) copy-start(f32[16,8,16,128]{3,2,1,0:T(8,128)} %copy-done.1) | copy-start | bytes 3145732
  249.0 19.2 %copy-start.20 = (f32[128,16]{1,0:T(8,128)S(1)}, f32[128,16]{1,0:T(8,128)}, u32[]{:S(2)}) copy-start(f32[128,16]{1,0:T(8,128)} %copy-done.19) | copy-start | bytes 24580
  249.0 19.2 %copy-start.36 = (f32[128]{0:T(128)S(1)}, f32[128]{0:T(128)}, u32[]{:S(2)}) copy-start(f32[128]{0:T(128)} %param.14) | copy-start | bytes 1540
  250.4 17.5 %copy-start.10 = (f32[128,16,64]{2,1,0:T(8,128)S(1)}, f32[128,16,64]{2,1,0:T(8,128)}, u32[]{:S(2)}) copy-start(f32[128,16,64]{2,1,0:T(8,128)} %copy.138) | copy-start | bytes 1572868
  250.4 17.5 %copy-start.11 = (f32[128,16,64]{2,1,0:T(8,128)S(1)}, f32[128,16,64]{2,1,0:T(8,128)}, u32[]{:S(2)}) copy-start(f32[128,16,64]{2,1,0:T(8,128)} %copy.139) | copy-start | bytes 1572868
  262.4 6.7 %copy-start.29 = (f32[128,16]{0,1:T(8,128)S(1)}, f32[128,16]{0,1:T(8,128)}, u32[]{:S(2)}) copy-start(f32[128,16]{0,1:T(8,128)} %copy-done.28) | copy-start | bytes 24580
  262.4 11.5 %collective-permute-start.10 = (bf16[2,8,128,128]{3,1,2,0:T(8,128)(2,1)}, bf16[2,8,128,128]{3,1,2,0:T(8,128)(2,1)}, u32[]{:S(2)}, u32[]{:S(2)}) collective-permute-start(bf16[2,8,128,128]{3,1,2,0:T(8,128)(2,1)} %get-tuple-element.29), channel_id=1, source_target_pairs={{4,0},{8,4},{12,8},{16,12},{20,16},{24,20},{28,24},{32,28},{36,32}... | collective-permute-start | bytes 1572872 | tf_op jit(solution)/shard_map/ppermute | solution.py:27
  264.5 21.0 %collective-permute-start.14 = (bf16[2,8,128,128]{3,1,2,0:T(8,128)(2,1)}, bf16[2,8,128,128]{3,1,2,0:T(8,128)(2,1)}, u32[]{:S(2)}, u32[]{:S(2)}) collective-permute-start(bf16[2,8,128,128]{3,1,2,0:T(8,128)(2,1)} %get-tuple-element.30), channel_id=1, source_target_pairs={{0,4},{4,8},{8,12},{12,16},{16,20},{20,24},{24,28},{28,32},{32,36}... | collective-permute-start | bytes 1572872 | tf_op jit(solution)/shard_map/ppermute | solution.py:27
  269.1 27.1 %copy-start.27 = (f32[1152,8]{0,1:T(8,128)S(1)}, f32[1152,8]{0,1:T(8,128)}, u32[]{:S(2)}) copy-start(f32[1152,8]{0,1:T(8,128)} %copy-done.26) | copy-start | bytes 110596
  288.6 90.3 %collective-permute-start.11 = (bf16[2,8,128,128]{3,1,2,0:T(8,128)(2,1)}, bf16[2,8,128,128]{3,1,2,0:T(8,128)(2,1)}, u32[]{:S(2)}, u32[]{:S(2)}) collective-permute-start(bf16[2,8,128,128]{3,1,2,0:T(8,128)(2,1)} %get-tuple-element.27), channel_id=1, source_target_pairs={{4,0},{8,4},{12,8},{16,12},{20,16},{24,20},{28,24},{32,28},{36,32}... | collective-permute-start | bytes 1572872 | tf_op jit(solution)/shard_map/ppermute | solution.py:27
  290.5 88.4 %collective-permute-start.15 = (bf16[2,8,128,128]{3,1,2,0:T(8,128)(2,1)}, bf16[2,8,128,128]{3,1,2,0:T(8,128)(2,1)}, u32[]{:S(2)}, u32[]{:S(2)}) collective-permute-start(bf16[2,8,128,128]{3,1,2,0:T(8,128)(2,1)} %get-tuple-element.28), channel_id=1, source_target_pairs={{0,480},{4,484},{8,488},{12,492},{16,496},{20,500},{24,504},{28,50... | collective-permute-start | bytes 1572872 | tf_op jit(solution)/shard_map/ppermute | solution.py:27
  302.7 79.0 %copy-start.9 = (f32[16,8,8,128]{3,2,1,0:T(8,128)S(1)}, f32[16,8,8,128]{3,2,1,0:T(8,128)}, u32[]{:S(2)}) copy-start(f32[16,8,8,128]{3,2,1,0:T(8,128)} %copy.144) | copy-start | bytes 1572868
  302.7 79.0 %copy-start.34 = (f32[128]{0:T(128)S(1)}, f32[128]{0:T(128)}, u32[]{:S(2)}) copy-start(f32[128]{0:T(128)} %param.15) | copy-start | bytes 1540
  (11 other events, 26.8 us)
